TPU v7x, 32 devices: a whole 2x2x4 slice. The times are simulated.
32 devices in a mesh: group: 2 (over y), inp: 4 (over z), tm: 2 (over x), pol: 2 (over core).
Axes of the slice: x: 2, y: 2, z: 4, core: 2. Of those that a mesh axis runs over, the one named last changes fastest.
Arguments:
- voltages: bfloat16 [1024, 65536], P(('group', 'inp'), ('tm', 'pol')), parts along dimension 0, may hold values from -6 to 6
Outputs:
- visibilities: float32 [1024, 2, 512, 512], P(('group', 'inp', 'tm'), None, 'pol'), parts along dimension 0
There are 2 independent parts, one for each index of `group`. A program takes and returns all parts, laid end to end along the dimension named above; each array names one. Nothing has to cross between parts.
All inputs are finite; a program needn't handle non-finite values.
Results may differ from a plain program's by a relative error of at most 0.0054.
Values may be sent and summed in bfloat16 or wider, within the bound.
No kernel may reach another device: no remote copies, remote signals or barrier semaphores. Data moves between devices by JAX's collectives and lax.ppermute only.
A program may use at most 256 MiB of HBM per device.

v0:
```python
import math

import jax
import jax.numpy as jnp
from jax import lax
from jax.sharding import PartitionSpec as P

CH = 512
TAPS = 16


def shifted(block, axis, distance):
    devices = range(lax.axis_size(axis))
    route = [(i - distance, i) for i in devices if i - distance in devices]
    return lax.ppermute(block, axis, route)


def prototype(tap_count, frame_len):
    length = tap_count * frame_len
    sample = lax.broadcasted_iota(jnp.int32, (length,), 0).astype(jnp.float32)
    centred = (sample - (length - 1) / 2.0) / frame_len
    window = 0.5 - 0.5 * jnp.cos(2.0 * math.pi * (sample + 0.5) / length)
    angle = math.pi * centred
    filter_taps = jnp.sin(angle) / angle * window
    filter_taps = filter_taps / jnp.sqrt(jnp.sum(filter_taps * filter_taps))
    return filter_taps.reshape(tap_count, frame_len)


def dft_table(frame_len):
    sample_idx = lax.broadcasted_iota(jnp.int32, (frame_len, frame_len // 2), 0)
    channel_idx = lax.broadcasted_iota(jnp.int32, (frame_len, frame_len // 2), 1)
    phase = (sample_idx * channel_idx % frame_len).astype(jnp.float32) * (2.0 * math.pi / frame_len)
    table = jnp.stack([jnp.cos(phase), -jnp.sin(phase)], axis=2)
    return table.reshape(frame_len, frame_len).astype(jnp.bfloat16)


def per_device(voltages):
    inputs_here = voltages.shape[0]
    frame_len = 2 * CH
    frames = voltages.reshape(inputs_here, voltages.shape[1] // frame_len, frame_len)
    spectra_here = frames.shape[1]
    last_frames = frames[:, spectra_here - (TAPS - 1) :, :]
    history = shifted(last_frames, ("tm", "pol"), 1)
    extended = jnp.concatenate([history, frames], axis=1)
    filter_taps = prototype(TAPS, frame_len)
    filtered = jnp.zeros((inputs_here, spectra_here, frame_len), jnp.float32)
    for tap_index in range(TAPS):
        filtered = filtered + filter_taps[tap_index] * extended[
            :, tap_index : tap_index + spectra_here, :
        ].astype(jnp.float32)
    filtered = filtered.astype(jnp.bfloat16)
    spectra = lax.dot_general(
        dft_table(frame_len),
        filtered.reshape(inputs_here * spectra_here, frame_len),
        (((0,), (1,)), ((), ())),
        preferred_element_type=jnp.float32,
    )
    spectra = spectra.astype(jnp.bfloat16).reshape(CH, 2, inputs_here, spectra_here)
    inp_size = lax.axis_size("inp")
    tm_size = lax.axis_size("tm")
    own_channels = CH // (inp_size * tm_size)
    widened = spectra.reshape(CH, 2, 1, inputs_here, spectra_here)
    received = lax.all_to_all(widened, ("inp", "tm"), split_axis=0, concat_axis=2, tiled=True)
    received = received.reshape(own_channels, 2, inp_size, tm_size, inputs_here, spectra_here)
    turned = received.transpose(0, 1, 2, 4, 3, 5).reshape(
        own_channels, 2, inp_size * inputs_here, tm_size * spectra_here
    )
    pol_size = lax.axis_size("pol")
    rows_here = turned.shape[2] // pol_size
    row_start = lax.axis_index("pol") * rows_here
    segment = lax.all_gather(turned, "pol", axis=3, tiled=True)
    own_rows = lax.dynamic_slice_in_dim(segment, row_start, rows_here, 2)
    left_rows = jnp.concatenate([own_rows[:, 0], own_rows[:, 1]], axis=-1)
    right_real = jnp.concatenate([segment[:, 0], segment[:, 1]], axis=-1)
    right_imag = jnp.concatenate([-segment[:, 1], segment[:, 0]], axis=-1)
    part_real = jnp.einsum(
        "crk,cjk->crj", left_rows, right_real, preferred_element_type=jnp.float32
    )
    part_imag = jnp.einsum(
        "crk,cjk->crj", left_rows, right_imag, preferred_element_type=jnp.float32
    )
    summed = jnp.stack([part_real, part_imag], axis=1)
    return summed * (1.0 / (turned.shape[3] * pol_size))


def solution(mesh):
    return jax.shard_map(
        per_device,
        mesh=mesh,
        in_specs=(P(("group", "inp"), ("tm", "pol")),),
        out_specs=P(("group", "inp", "tm"), None, "pol", None),
        check_vma=False,
    )
```

profile of v0, /device:TPU:0, one launch (start us, length us, event | category | flops | bytes accessed | tf_op | source)
XLA Modules:
  0.0 484.7 jit_solution(11061835007359937390)
XLA Ops:
  6.5 0.0 all-gather.2.cloned.1.call-start
  6.5 6.4 %copy.27 = bf16[128,16384]{0,1:T(8,128)(2,1)} copy(bf16[128,16384]{1,0:T(8,128)(2,1)} %param.1) | data formatting | bytes 8388608 | tf_op args[0]
  12.9 4.3 slice.163
  17.2 6.3 %copy.28 = bf16[128,15,1024]{2,0,1:T(8,128)(2,1)} copy(bf16[128,15,1024]{0,2,1:T(8,128)(2,1)} %slice.163) | data formatting | bytes 7864320 | tf_op jit(solution)/shard_map/slice | solution.py:42
  23.5 4.2 collective-permute-start
  27.8 1.1 multiply_reduce_fusion
  29.5 8.5 %negate_convert_fusion = (bf16[1024,512,1]{1,0,2:T(8,128)(2,1)S(1)}, bf16[1024,512,1]{1,0,2:T(8,128)(2,1)S(1)}) fusion(), kind=kLoop, calls=%fused_computation.62 | loop fusion | flops 8912896 | bytes 2097152 | tf_op jit(solution)/shard_map/convert.1
  38.1 0.2 pad_maximum_fusion.2
  38.3 4.1 copy.26
  42.4 2.7 convert_element_type.86
  45.1 0.5 broadcast_divide_fusion
  45.6 0.0 collective-permute-done
  45.6 6.2 %copy.29 = bf16[128,15,1024]{0,2,1:T(8,128)(2,1)} copy(bf16[128,15,1024]{2,0,1:T(8,128)(2,1)} %collective-permute-done) | data formatting | bytes 7864320 | tf_op jit(solution)/shard_map/ppermute | solution.py:15
  51.8 24.9 %add_convert_fusion = bf16[128,16,1024]{0,2,1:T(8,128)(2,1)} fusion(bf16[128,16,1024]{0,2,1:T(8,128)(2,1)} %bitcast.32, bf16[128,15,1024]{0,2,1:T(8,128)(2,1)} %copy.29, f32[1024]{0:T(1024)S(1)} %get-tuple-element.10, f32[1024]{0:T(1024)S(1)} %get-tuple-element.11, f32[1024]{0:T(1024)S(1)} %get-tuple-element.12, f32[1024]{0:T(1024)S(1)} %get-tuple-element.13, ...), kind=kLoop, calls=%fused_computation.37 | loop fusion | flops 132120576 | bytes 12386304 | tf_op jit(solution)/shard_map/convert_element_type | solution.py:51
  76.7 6.7 %copy.30 = bf16[128,16,1024]{2,1,0:T(8,128)(2,1)} copy(bf16[128,16,1024]{0,2,1:T(8,128)(2,1)} %add_convert_fusion) | data formatting | bytes 8388608 | tf_op jit(solution)/shard_map/convert_element_type | solution.py:51
  83.4 8.3 %convolution_convert_fusion = bf16[1024,2048]{1,0:T(8,128)(2,1)} fusion(bf16[1024,1024]{0,1:T(8,128)(2,1)S(1)} %convert_element_type.86, bf16[2048,1024]{1,0:T(8,128)(2,1)} %bitcast.34), kind=kOutput, calls=%fused_computation.54 | convolution fusion | flops 4297064448 | bytes 10485760 | tf_op jit(solution)/shard_map/dot_general | solution.py:52
  91.7 31.6 %reshape_reshape.3 = bf16[512,2,1,128,16]{4,3,1,0,2:T(8,128)(2,1)} reshape(bf16[1024,2048]{1,0:T(8,128)(2,1)} %convolution_convert_fusion) | data formatting | bytes 8388608 | tf_op jit(solution)/shard_map/reshape;reshape | solution.py:62
  123.2 24.9 %copy.31 = bf16[512,2,1,128,16]{3,4,2,1,0:T(8,128)(2,1)} copy(bf16[512,2,1,128,16]{4,3,1,0,2:T(8,128)(2,1)} %reshape_reshape.3) | data formatting | bytes 8388608 | tf_op jit(solution)/shard_map/reshape;reshape | solution.py:62
  148.1 124.0 %all_to_all.15 = bf16[512,2,1,128,16]{3,4,2,1,0:T(8,128)(2,1)S(1)} all-to-all(bf16[512,2,1,128,16]{3,4,2,1,0:T(8,128)(2,1)} %copy.31), channel_id=1, replica_groups=mesh['group'=2,'inp'=4,'tm'=2,'pol'=2] {'inp','tm'}, dimensions={0} | all-to-all | bytes 8388608 | tf_op jit(solution)/shard_map/all_to_all | solution.py:63
  272.1 5.3 %copy.40 = bf16[64,2,4,128,2,16]{3,2,0,1,5,4:T(4,128)(2,1)} copy(bf16[64,2,4,128,2,16]{3,5,1,0,4,2:T(8,128)(2,1)S(1)} %bitcast.33) | data formatting | bytes 8388608 | tf_op jit(solution)/shard_map/reshape | solution.py:65
  277.4 7.2 %reshape.135 = bf16[64,2,512,32]{2,0,1,3:T(8,128)(2,1)} reshape(bf16[64,2,4,128,2,16]{3,2,0,1,5,4:T(4,128)(2,1)} %copy.40) | data formatting | bytes 8388608 | tf_op jit(solution)/shard_map/reshape | solution.py:65
  284.6 0.0 all-gather.2.cloned.1.call-update
  284.6 19.0 %all-gather.2.cloned.1.call-done = bf16[64,2,512,64]{2,0,1,3:T(8,128)(2,1)} async-done(((bf16[64,2,512,32]{2,0,1,3:T(8,128)(2,1)}), bf16[64,2,512,64]{2,0,1,3:T(8,128)(2,1)}) %all-gather.2.cloned.1.call-update) | async-done | bytes 8388624 | tf_op jit(solution)/shard_map/all_gather | solution.py:71
  303.7 4.0 constant_dynamic-slice_fusion
  307.7 5.3 %copy.43 = bf16[64,1,256,64]{3,2,0,1:T(8,128)(2,1)} copy(bf16[64,1,256,64]{2,0,1,3:T(8,128)(2,1)} %get-tuple-element.5) | data formatting | bytes 4194304
  313.1 6.1 %fusion.29 = (bf16[64,1,512,64]{2,0,1,3:T(8,128)(2,1)}, bf16[64,1,512,64]{2,0,1,3:T(8,128)(2,1)}) fusion(bf16[64,2,512,64]{2,0,1,3:T(8,128)(2,1)} %all-gather.2.cloned.1.call-done), kind=kLoop, calls=%fused_computation.76 | loop fusion | bytes 16777216 | tf_op jit(solution)/shard_map/slice | solution.py:74
  319.2 9.2 %copy.46 = bf16[64,1,512,64]{3,2,0,1:T(8,128)(2,1)} copy(bf16[64,1,512,64]{2,0,1,3:T(8,128)(2,1)} %get-tuple-element.7) | data formatting | bytes 8388608
  328.4 3.8 copy.44
  332.2 7.7 %bitcast_negate_fusion = bf16[64,512,64]{2,1,0:T(8,128)(2,1)} fusion(bf16[64,1,512,64]{3,2,0,1:T(8,128)(2,1)} %copy.46), kind=kLoop, calls=%fused_computation.75 | loop fusion | flops 2097152 | bytes 8388608 | tf_op jit(solution)/shard_map/neg | solution.py:75
  339.9 9.3 %copy.45 = bf16[64,1,512,64]{3,2,0,1:T(8,128)(2,1)} copy(bf16[64,1,512,64]{2,0,1,3:T(8,128)(2,1)} %get-tuple-element.8) | data formatting | bytes 8388608
  349.2 0.0 copy-start
  349.2 22.8 %convolution_bitcast_fusion = f32[64,1,256,512]{3,2,0,1:T(8,128)} fusion(bf16[64,512,64]{2,1,0:T(8,128)(2,1)} %bitcast.24, bf16[64,512,64]{2,1,0:T(8,128)(2,1)} %bitcast_negate_fusion, bf16[64,256,64]{2,1,0:T(8,128)(2,1)} %bitcast.29, bf16[64,256,64]{2,1,0:T(8,128)(2,1)} %bitcast.27), kind=kOutput, calls=%fused_computation.29 | convolution fusion | flops 2172649472 | bytes 46137344 | tf_op jit(solution)/shard_map/crk,cjk->crj/dot_general | solution.py:79
  371.9 0.0 copy-done
  371.9 18.3 %convolution_bitcast_fusion.1 = f32[64,1,256,512]{3,2,0,1:T(8,128)} fusion(bf16[64,512,64]{2,1,0:T(8,128)(2,1)} %bitcast.26, bf16[64,512,64]{2,1,0:T(8,128)(2,1)S(1)} %bitcast.25, bf16[64,256,64]{2,1,0:T(8,128)(2,1)} %bitcast.30, bf16[64,256,64]{2,1,0:T(8,128)(2,1)} %bitcast.28), kind=kOutput, calls=%fused_computation.30 | convolution fusion | flops 2172649472 | bytes 46137344 | tf_op jit(solution)/shard_map/crk,cjk->crj/dot_general | solution.py:76
  390.3 43.6 %maximum_multiply_fusion = f32[64,2,256,512]{3,2,0,1:T(8,128)} fusion(f32[64,1,256,512]{3,2,0,1:T(8,128)} %convolution_bitcast_fusion, f32[64,1,256,512]{3,2,0,1:T(8,128)} %convolution_bitcast_fusion.1), kind=kLoop, calls=%fused_computation | loop fusion | flops 33554432 | bytes 134217728 | tf_op jit(solution)/shard_map/mul | solution.py:83
  433.9 44.0 %copy.38 = f32[64,2,256,512]{3,2,1,0:T(8,128)} copy(f32[64,2,256,512]{3,2,0,1:T(8,128)} %maximum_multiply_fusion) | data formatting | bytes 134217728 | tf_op jit(solution)/shard_map/mul | solution.py:83
  (1 shorter events, 0.0 us)
Async XLA Ops:
  6.5 297.2 %all-gather.2.cloned.1.call-start = ((), (), s32[]{:S(2)}) async-start(), calls=%async_computation.1 | async-start | bytes 12582912 | tf_op jit(solution)/shard_map/all_gather | solution.py:71
  23.5 22.1 %collective-permute-start = (bf16[128,15,1024]{2,0,1:T(8,128)(2,1)}, bf16[128,15,1024]{2,0,1:T(8,128)(2,1)}, u32[]{:S(2)}, u32[]{:S(2)}) collective-permute-start(bf16[128,15,1024]{2,0,1:T(8,128)(2,1)} %copy.28), channel_id=1, source_target_pairs={{0,1},{1,2},{2,3},{4,5},{5,6},{6,7},{8,9},{9,10},{10,11},{12,13},{... | collective-permute-start | bytes 11796488 | tf_op jit(solution)/shard_map/ppermute | solution.py:15
  349.2 22.8 %copy-start = (bf16[64,1,512,64]{3,2,0,1:T(8,128)(2,1)S(1)}, bf16[64,1,512,64]{3,2,0,1:T(8,128)(2,1)}, u32[]{:S(2)}) copy-start(bf16[64,1,512,64]{3,2,0,1:T(8,128)(2,1)} %copy.45) | copy-start | bytes 12582916
Sparse Core Ops, SparseCore 0:
  284.8 18.8 all-gather.1
where the time goes:
time: 488 us; the launch traced here: 485 us
  local copies, waits for them, and re-layouts  187 us (38%)
  blocking collectives  124 us (25%)
  other arithmetic  86.5 us (18%)
  matrix products  49.4 us (10%)
  waiting for transfers between devices  19.1 us (4%)
  between operations  14.1 us (3%)
    all_to_all x1, blocking collectives, per_device(): lax.all_to_all(widened, ('inp', 'tm'), split_axis=0, concat_axis=2, tiled...  124 us
    another operation x2, local copies, waits for them, and re-layouts, per_device(): widened = spectra.reshape(CH, 2, 1, inputs_here, spectra_here)  56.5 us
    mul x1, local copies, waits for them, and re-layouts, per_device(): return summed * (1.0 / (turned.shape[3] * pol_size))  44 us
    mul x1, other arithmetic, per_device(): return summed * (1.0 / (turned.shape[3] * pol_size))  43.6 us
    unnamed x7, local copies, waits for them, and re-layouts  34 us
    convert_element_type x1, other arithmetic, per_device(): filtered = filtered.astype(jnp.bfloat16)  24.9 us
    dot_general x1, matrix products, per_device(): jnp.einsum('crk,cjk->crj', left_rows, right_imag, preferred_element_type=...  22.8 us
    all_gather x1, waiting for transfers between devices, per_device(): segment = lax.all_gather(turned, 'pol', axis=3, tiled=True)  19 us
  transfers between devices with their start and end apart: 2, of which 1 were waited for; matrix products, arithmetic and copies ran while one was open for 4% of the time, Pallas kernels for 0%

commit v1 on v0

v1 whole, which is shorter than its diff:
```python
import math

import jax
import jax.numpy as jnp
from jax import lax
from jax.sharding import PartitionSpec as P

CH = 512
TAPS = 16


def shifted(block, axis, distance):
    devices = range(lax.axis_size(axis))
    route = [(i - distance, i) for i in devices if i - distance in devices]
    return lax.ppermute(block, axis, route)


def prototype(tap_count, frame_len):
    length = tap_count * frame_len
    sample = lax.broadcasted_iota(jnp.int32, (length,), 0).astype(jnp.float32)
    centred = (sample - (length - 1) / 2.0) / frame_len
    window = 0.5 - 0.5 * jnp.cos(2.0 * math.pi * (sample + 0.5) / length)
    angle = math.pi * centred
    filter_taps = jnp.sin(angle) / angle * window
    filter_taps = filter_taps / jnp.sqrt(jnp.sum(filter_taps * filter_taps))
    return filter_taps.reshape(tap_count, frame_len)


def dft_table_t(frame_len):
    channel_idx = lax.broadcasted_iota(jnp.int32, (frame_len // 2, frame_len), 0)
    sample_idx = lax.broadcasted_iota(jnp.int32, (frame_len // 2, frame_len), 1)
    phase = (sample_idx * channel_idx % frame_len).astype(jnp.float32) * (2.0 * math.pi / frame_len)
    table = jnp.stack([jnp.cos(phase), -jnp.sin(phase)], axis=1)
    return table.reshape(frame_len, frame_len).astype(jnp.bfloat16)


def per_device(voltages):
    inputs_here = voltages.shape[0]
    frame_len = 2 * CH
    spectra_here = voltages.shape[1] // frame_len
    frames = voltages.reshape(inputs_here, spectra_here, frame_len).transpose(1, 0, 2)
    last_frames = frames[spectra_here - (TAPS - 1) :]
    history = shifted(last_frames, ("tm", "pol"), 1)
    extended = jnp.concatenate([history, frames], axis=0)
    filter_taps = prototype(TAPS, frame_len)
    filtered = jnp.zeros((spectra_here, inputs_here, frame_len), jnp.float32)
    for tap_index in range(TAPS):
        filtered = filtered + filter_taps[tap_index] * extended[
            tap_index : tap_index + spectra_here
        ].astype(jnp.float32)
    filtered = filtered.astype(jnp.bfloat16)
    spectra = lax.dot_general(
        dft_table_t(frame_len),
        filtered.reshape(spectra_here * inputs_here, frame_len),
        (((1,), (1,)), ((), ())),
        preferred_element_type=jnp.float32,
    )
    spectra = spectra.astype(jnp.bfloat16).reshape(CH, 2, spectra_here, inputs_here)
    inp_size = lax.axis_size("inp")
    tm_size = lax.axis_size("tm")
    pol_size = lax.axis_size("pol")
    own_channels = CH // (inp_size * tm_size)
    received = lax.all_to_all(spectra, ("inp", "tm"), split_axis=0, concat_axis=0, tiled=True)
    received = received.reshape(inp_size, tm_size, own_channels, 2, spectra_here, inputs_here)
    gathered = lax.all_gather(received, "pol", axis=0, tiled=False)
    blocks = gathered.transpose(3, 2, 0, 4, 5, 1, 6)
    depth = tm_size * pol_size * 2 * spectra_here
    cols = inp_size * inputs_here
    left_all = blocks.reshape(own_channels, depth, cols)
    right_imag = jnp.stack([-blocks[:, :, :, 1], blocks[:, :, :, 0]], axis=3).reshape(
        own_channels, depth, cols
    )
    right = jnp.stack([left_all, right_imag], axis=1)
    rows_here = cols // pol_size
    row_start = lax.axis_index("pol") * rows_here
    own_rows = lax.dynamic_slice_in_dim(left_all, row_start, rows_here, 2)
    own_rows = jnp.broadcast_to(own_rows[:, None], (own_channels, 2, depth, rows_here))
    summed = lax.dot_general(
        own_rows,
        right,
        (((2,), (2,)), ((0, 1), (0, 1))),
        preferred_element_type=jnp.float32,
    )
    return summed * (1.0 / (depth // 2))


def solution(mesh):
    return jax.shard_map(
        per_device,
        mesh=mesh,
        in_specs=(P(("group", "inp"), ("tm", "pol")),),
        out_specs=P(("group", "inp", "tm"), None, "pol", None),
        check_vma=False,
    )
```

time: 488 us -> 333 us (0.68)
  local copies, waits for them, and re-layouts: 187 us -> 78.5 us
  other arithmetic: 86.5 us -> 53 us
  matrix products: 49.4 us -> 36.3 us
    mul x1 -> x0, local copies, waits for them, and re-layouts: 44 us -> none  [per_device(): return summed * (1.0 / (turned.shape[3] * pol_size))]
    mul x1 -> x0, other arithmetic: 43.6 us -> none  [per_device(): return summed * (1.0 / (turned.shape[3] * pol_size))]
    another operation x3 -> x4, local copies, waits for them, and re-layouts: 60.5 us -> 35.8 us  [the longest x2 26.2 us: per_device(): right = jnp.stack([left_all, right_imag], axis=1)]
    unnamed x7, local copies, waits for them, and re-layouts: 34 us -> 14.1 us
    slice x4 -> x1, local copies, waits for them, and re-layouts: 20.8 us -> 4.35 us  [per_device(): last_frames = frames[spectra_here - (TAPS - 1):]]
    dot_general x3 -> x2, matrix products: 49.4 us -> 36.3 us  [the longest x1 29.4 us: per_device(): lax.dot_general(own_rows, right, (((2,), (2,)), ((0, 1), (0, 1))), prefer...]
    another operation x2 -> x3, other arithmetic: 8.74 us -> 16.9 us
    ppermute x1 -> x0, local copies, waits for them, and re-layouts: 6.17 us -> none  [shifted(): return lax.ppermute(block, axis, route)]
where the time goes in v1:
time: 333 us; the launch traced here: 332 us
  blocking collectives  126 us (38%)
  local copies, waits for them, and re-layouts  78.5 us (24%)
  other arithmetic  53 us (16%)
  matrix products  36.3 us (11%)
  waiting for transfers between devices  19.1 us (6%)
  between operations  14.1 us (4%)
  starting transfers between devices  4.23 us (1%)
    all_to_all x1, blocking collectives, per_device(): lax.all_to_all(spectra, ('inp', 'tm'), split_axis=0, concat_axis=0, tiled...  126 us
    dot_general x1, matrix products, per_device(): lax.dot_general(own_rows, right, (((2,), (2,)), ((0, 1), (0, 1))), prefer...  29.4 us
    another operation x2, local copies, waits for them, and re-layouts, per_device(): right = jnp.stack([left_all, right_imag], axis=1)  26.2 us
    convert_element_type x1, other arithmetic, per_device(): filtered = filtered.astype(jnp.bfloat16)  25.7 us
    all_gather x1, waiting for transfers between devices, per_device(): gathered = lax.all_gather(received, 'pol', axis=0, tiled=False)  19 us
    unnamed x7, local copies, waits for them, and re-layouts  14.1 us
    reshape x1, local copies, waits for them, and re-layouts, per_device(): left_all = blocks.reshape(own_channels, depth, cols)  13.1 us
    neg x1, other arithmetic, per_device(): -blocks[:, :, :, 1]  8.83 us
  transfers between devices with their start and end apart: 2, of which 1 were waited for; matrix products, arithmetic and copies ran while one was open for 4% of the time, Pallas kernels for 0%

profile of v1, /device:TPU:0, one launch (start us, length us, event | category | flops | bytes accessed | tf_op | source)
XLA Modules:
  0.0 331.6 jit_solution(6252266510471901847)
XLA Ops:
  6.5 0.0 all-gather.2.cloned.1.call-start
  6.5 6.4 %copy.15 = bf16[128,16384]{0,1:T(8,128)(2,1)} copy(bf16[128,16384]{1,0:T(8,128)(2,1)} %param.1) | data formatting | bytes 8388608 | tf_op args[0]
  12.9 4.3 %slice.153 = bf16[15,128,1024]{1,2,0:T(8,128)(2,1)} slice(bf16[16,128,1024]{1,2,0:T(8,128)(2,1)} %bitcast.15), slice={[1:16], [0:128], [0:1024]} | slice | bytes 7864320 | tf_op jit(solution)/shard_map/slice | solution.py:42
  17.2 4.2 %collective-permute-start = (bf16[15,128,1024]{1,2,0:T(8,128)(2,1)}, bf16[15,128,1024]{1,2,0:T(8,128)(2,1)}, u32[]{:S(2)}, u32[]{:S(2)}) collective-permute-start(bf16[15,128,1024]{1,2,0:T(8,128)(2,1)} %slice.153), channel_id=1, source_target_pairs={{0,1},{1,2},{2,3},{4,5},{5,6},{6,7},{8,9},{9,10},{10,11},{12,13},{... | collective-permute-start | bytes 11796488 | tf_op jit(solution)/shard_map/ppermute | solution.py:15
  21.5 1.1 multiply_reduce_fusion
  23.3 8.5 %negate_convert_fusion = (bf16[512,1,1024]{2,0,1:T(8,128)(2,1)S(1)}, bf16[512,1,1024]{2,0,1:T(8,128)(2,1)S(1)}) fusion(), kind=kLoop, calls=%fused_computation.59 | loop fusion | flops 8912896 | bytes 2097152 | tf_op jit(solution)/shard_map/convert.1
  31.8 0.2 pad_maximum_fusion.2
  32.0 2.2 copy.14
  34.1 2.3 convert_element_type.86
  36.4 0.5 broadcast_divide_fusion
  36.9 0.0 collective-permute-done
  36.9 25.7 %add_convert_fusion = bf16[16,128,1024]{1,2,0:T(8,128)(2,1)} fusion(bf16[16,128,1024]{1,2,0:T(8,128)(2,1)} %bitcast.16, bf16[15,128,1024]{1,2,0:T(8,128)(2,1)} %collective-permute-done, f32[1024]{0:T(1024)S(1)} %get-tuple-element.8, f32[1024]{0:T(1024)S(1)} %get-tuple-element.9, f32[1024]{0:T(1024)S(1)} %get-tuple-element.10, ...), kind=kLoop, calls=%fused_computation.33 | loop fusion | flops 132120576 | bytes 12386304 | tf_op jit(solution)/shard_map/convert_element_type | solution.py:51
  62.6 0.0 copy-start.1
  62.6 6.5 %copy.16 = bf16[16,128,1024]{2,1,0:T(8,128)(2,1)} copy(bf16[16,128,1024]{1,2,0:T(8,128)(2,1)} %add_convert_fusion) | data formatting | bytes 8388608 | tf_op jit(solution)/shard_map/convert_element_type | solution.py:51
  69.1 0.0 copy-done.1
  69.1 7.0 %convert_bitcast_fusion = bf16[128,8,16,128]{3,1,2,0:T(8,128)(2,1)S(1)} fusion(bf16[1024,1024]{1,0:T(8,128)(2,1)S(1)} %copy-done.1, bf16[2048,1024]{1,0:T(8,128)(2,1)} %bitcast.19), kind=kOutput, calls=%fused_computation.51 | convolution fusion | flops 4297064448 | bytes 10485760 | tf_op jit(solution)/shard_map/dot_general | solution.py:52
  76.1 1.4 copy.20
  77.5 126.2 %all_to_all.5 = bf16[512,2,16,128]{3,2,1,0:T(8,128)(2,1)S(1)} all-to-all(bf16[512,2,16,128]{3,2,1,0:T(8,128)(2,1)S(1)} %bitcast.17), channel_id=1, replica_groups=mesh['group'=2,'inp'=4,'tm'=2,'pol'=2] {'inp','tm'}, dimensions={0} | all-to-all | bytes 8388608 | tf_op jit(solution)/shard_map/all_to_all | solution.py:63
  203.8 7.4 %copy.17 = bf16[1,4,2,64,2,16,128]{6,1,5,4,0,2,3:T(4,128)(2,1)} copy(bf16[1,4,2,64,2,16,128]{6,5,4,3,2,1,0:T(8,128)(2,1)S(1)} %bitcast.18) | data formatting | bytes 8388608 | tf_op jit(solution)/shard_map/all_gather;reshape | solution.py:65
  211.2 0.0 all-gather.2.cloned.1.call-update
  211.2 19.0 %all-gather.2.cloned.1.call-done = bf16[2,4,2,64,2,16,128]{6,1,5,4,0,2,3:T(4,128)(2,1)} async-done(((bf16[1,4,2,64,2,16,128]{6,1,5,4,0,2,3:T(4,128)(2,1)}), bf16[2,4,2,64,2,16,128]{6,1,5,4,0,2,3:T(4,128)(2,1)}) %all-gather.2.cloned.1.call-update) | async-done | bytes 8388624 | tf_op jit(solution)/shard_map/all_gather | solution.py:65
  230.2 13.1 %stack_reshape.6 = bf16[64,1,128,512]{3,2,1,0:T(8,128)(2,1)} reshape(bf16[64,2,2,2,16,4,128]{6,5,4,3,2,1,0:T(4,128)(2,1)} %bitcast.12) | data formatting | bytes 16777216 | tf_op jit(solution)/shard_map/stack;reshape | solution.py:73
  243.4 13.1 %reshape.134 = bf16[64,128,512]{2,1,0:T(8,128)(2,1)} reshape(bf16[64,2,2,2,16,4,128]{6,5,4,3,2,1,0:T(4,128)(2,1)} %bitcast.13) | data formatting | bytes 16777216 | tf_op jit(solution)/shard_map/reshape | solution.py:69
  256.4 0.0 copy-start
  256.4 8.8 %slice_negate_fusion = (bf16[64,2,2,1,16,4,128]{6,5,4,3,2,1,0:T(4,128)(2,1)}, bf16[64,2,2,1,16,4,128]{6,5,4,3,2,1,0:T(4,128)(2,1)}) fusion(bf16[64,2,2,2,16,4,128]{6,5,4,3,2,1,0:T(4,128)(2,1)} %bitcast.14), kind=kLoop, calls=%fused_computation.48 | loop fusion | flops 2097152 | bytes 16777216 | tf_op jit(solution)/shard_map/neg | solution.py:70
  265.2 0.0 copy-done
  265.2 2.4 constant_dynamic-slice_fusion
  267.6 6.4 %copy.19 = bf16[64,128,256]{1,2,0:T(8,128)(2,1)} copy(bf16[64,128,256]{2,1,0:T(8,128)(2,1)} %constant_dynamic-slice_fusion) | data formatting | bytes 8388608
  274.0 8.2 %pad_maximum_fusion = bf16[64,2,2,2,16,4,128]{6,5,4,3,2,1,0:T(4,128)(2,1)} fusion(bf16[64,2,2,1,16,4,128]{6,5,4,3,2,1,0:T(4,128)(2,1)} %get-tuple-element.6, bf16[64,2,2,1,16,4,128]{6,5,4,3,2,1,0:T(4,128)(2,1)} %get-tuple-element.5), kind=kLoop, calls=%fused_computation.32 | loop fusion | flops 4194304 | bytes 16777216 | tf_op jit(solution)/shard_map/stack | solution.py:70
  282.3 13.1 %stack_reshape.7 = bf16[64,1,128,512]{3,2,1,0:T(8,128)(2,1)} reshape(bf16[64,2,2,2,16,4,128]{6,5,4,3,2,1,0:T(4,128)(2,1)} %pad_maximum_fusion) | data formatting | bytes 16777216 | tf_op jit(solution)/shard_map/stack;reshape | solution.py:73
  295.3 29.4 %broadcast_multiply_fusion = f32[64,2,256,512]{3,2,1,0:T(8,128)} fusion(bf16[64,1,128,512]{3,2,1,0:T(8,128)(2,1)} %stack_reshape.7, bf16[64,1,128,512]{3,2,1,0:T(8,128)(2,1)} %stack_reshape.6, bf16[64,128,256]{1,2,0:T(8,128)(2,1)} %copy.19), kind=kOutput, calls=%fused_computation | convolution fusion | flops 4320133120 | bytes 88080384 | tf_op jit(solution)/shard_map/dot_general | solution.py:78
  (1 shorter events, 0.0 us)
Async XLA Ops:
  6.5 223.7 %all-gather.2.cloned.1.call-start = ((), (), s32[]{:S(2)}) async-start(), calls=%async_computation.1 | async-start | bytes 12582912 | tf_op jit(solution)/shard_map/all_gather | solution.py:65
  17.2 19.7 %collective-permute-start = (bf16[15,128,1024]{1,2,0:T(8,128)(2,1)}, bf16[15,128,1024]{1,2,0:T(8,128)(2,1)}, u32[]{:S(2)}, u32[]{:S(2)}) collective-permute-start(bf16[15,128,1024]{1,2,0:T(8,128)(2,1)} %slice.153), channel_id=1, source_target_pairs={{0,1},{1,2},{2,3},{4,5},{5,6},{6,7},{8,9},{9,10},{10,11},{12,13},{... | collective-permute-start | bytes 11796488 | tf_op jit(solution)/shard_map/ppermute | solution.py:15
  62.6 6.6 %copy-start.1 = (bf16[1024,1024]{1,0:T(8,128)(2,1)S(1)}, bf16[1024,1024]{1,0:T(8,128)(2,1)}, u32[]{:S(2)}) copy-start(bf16[1024,1024]{1,0:T(8,128)(2,1)} %convert_element_type.86) | copy-start | bytes 6291460
  256.4 8.8 %copy-start = (bf16[64,128,512]{2,1,0:T(8,128)(2,1)S(1)}, bf16[64,128,512]{2,1,0:T(8,128)(2,1)}, u32[]{:S(2)}) copy-start(bf16[64,128,512]{2,1,0:T(8,128)(2,1)} %reshape.134) | copy-start | bytes 25165828
Sparse Core Ops, SparseCore 0:
  211.3 18.8 all-gather.1

commit v2 on v1

--- a/solution.py
+++ b/solution.py
@@ -59,26 +59,43 @@
     inp_size = lax.axis_size("inp")
     tm_size = lax.axis_size("tm")
     pol_size = lax.axis_size("pol")
-    own_channels = CH // (inp_size * tm_size)
-    received = lax.all_to_all(spectra, ("inp", "tm"), split_axis=0, concat_axis=0, tiled=True)
-    received = received.reshape(inp_size, tm_size, own_channels, 2, spectra_here, inputs_here)
-    gathered = lax.all_gather(received, "pol", axis=0, tiled=False)
-    blocks = gathered.transpose(3, 2, 0, 4, 5, 1, 6)
-    depth = tm_size * pol_size * 2 * spectra_here
+    group_size = inp_size * tm_size
+    own_channels = CH // group_size
+    blocks = spectra.reshape(group_size, own_channels, 2, spectra_here, inputs_here)
+    inp_at = lax.axis_index("inp")
+    tm_at = lax.axis_index("tm")
     cols = inp_size * inputs_here
-    left_all = blocks.reshape(own_channels, depth, cols)
-    right_imag = jnp.stack([-blocks[:, :, :, 1], blocks[:, :, :, 0]], axis=3).reshape(
-        own_channels, depth, cols
-    )
-    right = jnp.stack([left_all, right_imag], axis=1)
+    half = jnp.zeros((own_channels, 2, tm_size, spectra_here, cols), jnp.bfloat16)
+    for inp_step in range(inp_size):
+        for tm_step in range(tm_size):
+            target = ((inp_at + inp_step) % inp_size) * tm_size + (tm_at + tm_step) % tm_size
+            block = lax.dynamic_index_in_dim(blocks, target, 0, keepdims=False)
+            if inp_step or tm_step:
+                route = [
+                    (g, ((g // tm_size + inp_step) % inp_size) * tm_size + (g % tm_size + tm_step) % tm_size)
+                    for g in range(group_size)
+                ]
+                block = lax.ppermute(block, ("inp", "tm"), route)
+            source_inp = (inp_at + inp_size - inp_step) % inp_size
+            half = lax.dynamic_update_slice(
+                half, block[:, :, None], (0, 0, tm_step, 0, source_inp * inputs_here)
+            )
+    if pol_size == 2:
+        partner = lax.ppermute(half, "pol", [(0, 1), (1, 0)])
+        both = jnp.stack([half, partner], axis=1)
+    else:
+        both = lax.all_gather(half, "pol", axis=1, tiled=False)
+    depth = pol_size * 2 * tm_size * spectra_here
+    left_all = both.reshape(own_channels, depth, cols)
     rows_here = cols // pol_size
     row_start = lax.axis_index("pol") * rows_here
-    own_rows = lax.dynamic_slice_in_dim(left_all, row_start, rows_here, 2)
-    own_rows = jnp.broadcast_to(own_rows[:, None], (own_channels, 2, depth, rows_here))
+    own_rows = lax.dynamic_slice_in_dim(both, row_start, rows_here, 5)
+    swapped = jnp.stack([own_rows[:, :, 1], -own_rows[:, :, 0]], axis=2)
+    lhs = jnp.stack([own_rows, swapped], axis=1).reshape(own_channels, 2, depth, rows_here)
     summed = lax.dot_general(
-        own_rows,
-        right,
-        (((2,), (2,)), ((0, 1), (0, 1))),
+        lhs,
+        left_all,
+        (((2,), (1,)), ((0,), (0,))),
         preferred_element_type=jnp.float32,
     )
     return summed * (1.0 / (depth // 2))

time: 333 us -> 267 us (0.80)
  blocking collectives: 126 us -> 0 us
  starting transfers between devices: 4.23 us -> 66.5 us
  waiting for transfers between devices: 19.1 us -> 58.9 us
  local copies, waits for them, and re-layouts: 78.5 us -> 53 us
  between operations: 14.1 us -> 0.79 us
    all_to_all x1 -> x0, blocking collectives: 126 us -> none  [per_device(): lax.all_to_all(spectra, ('inp', 'tm'), split_axis=0, concat_axis=0, tiled...]
    ppermute x0 -> x8, starting transfers between devices: none -> 62.3 us  [the longest x7 62.3 us: per_device(): block = lax.ppermute(block, ('inp', 'tm'), route)]
    ppermute x0 -> x8, waiting for transfers between devices: none -> 58.9 us  [the longest x7 51.4 us: per_device(): block = lax.ppermute(block, ('inp', 'tm'), route)]
    another operation x3 -> x2, local copies, waits for them, and re-layouts: 33.6 us -> 12.7 us  [per_device(): jnp.stack([own_rows, swapped], axis=1)]
    all_gather x1 -> x0, waiting for transfers between devices: 19 us -> none  [per_device(): gathered = lax.all_gather(received, 'pol', axis=0, tiled=False)]
    reshape x1 -> x0, local copies, waits for them, and re-layouts: 13.1 us -> none  [per_device(): left_all = blocks.reshape(own_channels, depth, cols)]
    dynamic_update_slice x0 -> x8, local copies, waits for them, and re-layouts: none -> 10.2 us  [per_device(): lax.dynamic_update_slice(half, block[:, :, None], (0, 0, tm_step, 0, sour...]
    neg x1 -> x0, other arithmetic: 8.83 us -> none  [per_device(): -blocks[:, :, :, 1]]
  transfers between devices with their start and end apart: 2 -> 9, of which waited for: 1 -> 5; matrix products, arithmetic and copies ran while one was open for 4% -> 10% of each run, Pallas kernels for 0% -> 0%
where the time goes in v2:
time: 267 us; the launch traced here: 266 us
  starting transfers between devices  66.5 us (25%)
  waiting for transfers between devices  58.9 us (22%)
  local copies, waits for them, and re-layouts  53 us (20%)
  other arithmetic  51.3 us (19%)
  matrix products  35.6 us (13%)
    ppermute x7, starting transfers between devices, per_device(): block = lax.ppermute(block, ('inp', 'tm'), route)  62.3 us
    ppermute x7, waiting for transfers between devices, per_device(): block = lax.ppermute(block, ('inp', 'tm'), route)  51.4 us
    dot_general x1, matrix products, per_device(): lax.dot_general(lhs, left_all, (((2,), (1,)), ((0,), (0,))), preferred_el...  28.6 us
    convert_element_type x1, other arithmetic, per_device(): filtered = filtered.astype(jnp.bfloat16)  25 us
    another operation x2, local copies, waits for them, and re-layouts, per_device(): jnp.stack([own_rows, swapped], axis=1)  12.7 us
    unnamed x8, local copies, waits for them, and re-layouts  10.6 us
    another operation x2, other arithmetic, per_device(): both = jnp.stack([half, partner], axis=1)  10.2 us
    dynamic_update_slice x8, local copies, waits for them, and re-layouts, per_device(): lax.dynamic_update_slice(half, block[:, :, None], (0, 0, tm_step, 0, sour...  10.2 us
  transfers between devices with their start and end apart: 9, of which 5 were waited for; matrix products, arithmetic and copies ran while one was open for 10% of the time, Pallas kernels for 0%

profile of v2, /device:TPU:0, one launch (start us, length us, event | category | flops | bytes accessed | tf_op | source)
XLA Modules:
  0.0 266.0 jit_solution(2974697726013550053)
XLA Ops:
  0.0 6.4 %copy.19 = bf16[128,16384]{0,1:T(8,128)(2,1)} copy(bf16[128,16384]{1,0:T(8,128)(2,1)} %param.1) | data formatting | bytes 8388608 | tf_op args[0]
  6.4 4.3 %slice.153 = bf16[15,128,1024]{1,2,0:T(8,128)(2,1)} slice(bf16[16,128,1024]{1,2,0:T(8,128)(2,1)} %bitcast.54), slice={[1:16], [0:128], [0:1024]} | slice | bytes 7864320 | tf_op jit(solution)/shard_map/slice | solution.py:42
  10.7 4.2 %collective-permute-start = (bf16[15,128,1024]{1,2,0:T(8,128)(2,1)}, bf16[15,128,1024]{1,2,0:T(8,128)(2,1)}, u32[]{:S(2)}, u32[]{:S(2)}) collective-permute-start(bf16[15,128,1024]{1,2,0:T(8,128)(2,1)} %slice.153), channel_id=1, source_target_pairs={{0,1},{1,2},{2,3},{4,5},{5,6},{6,7},{8,9},{9,10},{10,11},{12,13},{... | collective-permute-start | bytes 11796488 | tf_op jit(solution)/shard_map/ppermute | solution.py:15
  14.9 1.1 multiply_reduce_fusion
  16.7 8.5 %negate_convert_fusion = (bf16[512,1,1024]{2,0,1:T(8,128)(2,1)S(1)}, bf16[512,1,1024]{2,0,1:T(8,128)(2,1)S(1)}) fusion(), kind=kLoop, calls=%fused_computation.62 | loop fusion | flops 8912896 | bytes 2097152 | tf_op jit(solution)/shard_map/convert.1
  25.2 0.2 pad_maximum_fusion.3
  25.4 2.2 copy.18
  27.6 2.3 convert_element_type.86
  29.8 0.5 broadcast_divide_fusion
  30.3 0.0 collective-permute-done
  30.3 25.0 %add_convert_fusion = bf16[16,128,1024]{1,2,0:T(8,128)(2,1)} fusion(bf16[16,128,1024]{1,2,0:T(8,128)(2,1)} %bitcast.55, bf16[15,128,1024]{1,2,0:T(8,128)(2,1)} %collective-permute-done, f32[1024]{0:T(1024)S(1)} %get-tuple-element.15, f32[1024]{0:T(1024)S(1)} %get-tuple-element.16, f32[1024]{0:T(1024)S(1)} %get-tuple-element.17, ...), kind=kLoop, calls=%fused_computation.35 | loop fusion | flops 132120576 | bytes 12386304 | tf_op jit(solution)/shard_map/convert_element_type | solution.py:51
  55.3 0.0 copy-start.2
  55.4 6.5 %copy.20 = bf16[16,128,1024]{2,1,0:T(8,128)(2,1)} copy(bf16[16,128,1024]{1,2,0:T(8,128)(2,1)} %add_convert_fusion) | data formatting | bytes 8388608 | tf_op jit(solution)/shard_map/convert_element_type | solution.py:51
  61.9 0.0 copy-done.2
  61.9 7.0 %convert_bitcast_fusion = bf16[128,8,16,128]{3,1,2,0:T(8,128)(2,1)S(1)} fusion(bf16[1024,1024]{1,0:T(8,128)(2,1)S(1)} %copy-done.2, bf16[2048,1024]{1,0:T(8,128)(2,1)} %bitcast.59), kind=kOutput, calls=%fused_computation.53 | convolution fusion | flops 4297064448 | bytes 10485760 | tf_op jit(solution)/shard_map/dot_general | solution.py:52
  68.9 1.4 copy.25
  70.3 0.0 copy-start.1
  70.3 1.9 copy-done.1
  72.2 1.7 dynamic-slice_bitcast_fusion
  73.9 30.6 %collective-permute-start.1 = (bf16[64,2,16,128]{3,2,1,0:T(8,128)(2,1)}, bf16[64,2,16,128]{3,2,1,0:T(8,128)(2,1)}, u32[]{:S(2)}, u32[]{:S(2)}) collective-permute-start(bf16[64,2,16,128]{3,2,1,0:T(8,128)(2,1)} %get-tuple-element.13), channel_id=1, source_target_pairs={{0,2},{2,0},{4,6},{6,4},{8,10},{10,8},{12,14},{14,12},{1,3},{3,1},... | collective-permute-start | bytes 1572872 | tf_op jit(solution)/shard_map/ppermute | solution.py:78
  104.5 1.6 collective-permute-start.2
  106.0 1.7 collective-permute-start.7
  107.7 1.8 collective-permute-start.6
  109.5 1.7 collective-permute-start.3
  111.2 2.5 broadcast_in_dim.27
  113.8 1.9 bitcast_dynamic-update-slice_fusion.7
  115.7 1.4 collective-permute-done.1
  117.1 9.8 %collective-permute-start.4 = (bf16[64,2,16,128]{3,2,1,0:T(8,128)(2,1)S(1)}, bf16[64,2,16,128]{3,2,1,0:T(8,128)(2,1)S(1)}, u32[]{:S(2)}, u32[]{:S(2)}) collective-permute-start(bf16[64,2,16,128]{3,2,1,0:T(8,128)(2,1)S(1)} %get-tuple-element.10), channel_id=1, source_target_pairs={{0,8},{2,10},{4,12},{6,14},{8,0},{10,2},{12,4},{14,6},{1,9},{3,11}... | collective-permute-start | bytes 1572872 | tf_op jit(solution)/shard_map/ppermute | solution.py:78
  126.9 1.9 bitcast_dynamic-update-slice_fusion.6
  128.8 0.0 collective-permute-done.2
  128.8 15.1 %collective-permute-start.5 = (bf16[64,2,16,128]{3,2,1,0:T(8,128)(2,1)S(1)}, bf16[64,2,16,128]{3,2,1,0:T(8,128)(2,1)S(1)}, u32[]{:S(2)}, u32[]{:S(2)}) collective-permute-start(bf16[64,2,16,128]{3,2,1,0:T(8,128)(2,1)S(1)} %get-tuple-element.9), channel_id=1, source_target_pairs={{0,10},{2,8},{4,14},{6,12},{8,2},{10,0},{12,6},{14,4},{1,11},{3,9}... | collective-permute-start | bytes 1572872 | tf_op jit(solution)/shard_map/ppermute | solution.py:78
  143.9 1.9 bitcast_dynamic-update-slice_fusion.5
  145.9 8.6 %collective-permute-done.3 = bf16[64,2,16,128]{3,2,1,0:T(8,128)(2,1)S(1)} collective-permute-done((bf16[64,2,16,128]{3,2,1,0:T(8,128)(2,1)S(1)}, bf16[64,2,16,128]{3,2,1,0:T(8,128)(2,1)S(1)}, u32[]{:S(2)}, u32[]{:S(2)}) %collective-permute-start.3) | collective-permute-done | bytes 524320 | tf_op jit(solution)/shard_map/ppermute | solution.py:78
  154.4 0.9 bitcast_dynamic-update-slice_fusion.4
  155.3 30.0 %collective-permute-done.4 = bf16[64,2,16,128]{3,2,1,0:T(8,128)(2,1)S(1)} collective-permute-done((bf16[64,2,16,128]{3,2,1,0:T(8,128)(2,1)S(1)}, bf16[64,2,16,128]{3,2,1,0:T(8,128)(2,1)S(1)}, u32[]{:S(2)}, u32[]{:S(2)}) %collective-permute-start.4) | collective-permute-done | bytes 524320 | tf_op jit(solution)/shard_map/ppermute | solution.py:78
  185.3 0.9 bitcast_dynamic-update-slice_fusion.3
  186.2 11.4 %collective-permute-done.5 = bf16[64,2,16,128]{3,2,1,0:T(8,128)(2,1)S(1)} collective-permute-done((bf16[64,2,16,128]{3,2,1,0:T(8,128)(2,1)S(1)}, bf16[64,2,16,128]{3,2,1,0:T(8,128)(2,1)S(1)}, u32[]{:S(2)}, u32[]{:S(2)}) %collective-permute-start.5) | collective-permute-done | bytes 524320 | tf_op jit(solution)/shard_map/ppermute | solution.py:78
  197.6 0.9 bitcast_dynamic-update-slice_fusion.2
  198.5 0.0 collective-permute-done.6
  198.5 0.9 bitcast_dynamic-update-slice_fusion.1
  199.4 0.0 collective-permute-done.7
  199.4 0.9 bitcast_dynamic-update-slice_fusion
  200.3 0.0 collective-permute-start.8
  200.3 7.5 %collective-permute-done.8 = bf16[64,2,2,16,512]{4,3,2,1,0:T(8,128)(2,1)} collective-permute-done((bf16[64,2,2,16,512]{4,3,2,1,0:T(8,128)(2,1)}, bf16[64,2,2,16,512]{4,3,2,1,0:T(8,128)(2,1)}, u32[]{:S(2)}, u32[]{:S(2)}) %collective-permute-start.8) | collective-permute-done | bytes 4194336 | tf_op jit(solution)/shard_map/ppermute | solution.py:84
  207.8 7.5 %pad_maximum_fusion = bf16[64,2,2,2,16,512]{5,4,3,2,1,0:T(8,128)(2,1)} fusion(bf16[64,1,2,2,16,512]{5,4,3,2,1,0:T(8,128)(2,1)} %bitcast.21, bf16[64,1,2,2,16,512]{5,4,3,2,1,0:T(8,128)(2,1)} %bitcast.20), kind=kLoop, calls=%fused_computation.30 | loop fusion | flops 4194304 | bytes 16777216 | tf_op jit(solution)/shard_map/stack | solution.py:85
  215.2 2.8 %fusion.3 = bf16[64,2,2,2,16,256]{5,4,3,2,1,0:T(8,128)(2,1)S(1)} fusion(s32[]{:T(128)S(6)} %select_n.148, bf16[64,1,2,2,16,512]{5,4,3,2,1,0:T(8,128)(2,1)} %bitcast.20, bf16[64,1,2,2,16,512]{5,4,3,2,1,0:T(8,128)(2,1)} %bitcast.21), kind=kLoop, calls=%fused_computation.36 | loop fusion | flops 8388608 | bytes 12582916 | tf_op jit(solution)/shard_map/stack | solution.py:85
  218.0 0.0 copy-start
  218.0 1.8 fusion.26
  219.8 0.9 copy-done
  220.7 6.4 %copy.22 = bf16[64,1,128,256]{2,3,1,0:T(8,128)(2,1)} copy(bf16[64,1,128,256]{3,2,0,1:T(8,128)(2,1)} %bitcast.53) | data formatting | bytes 8388608 | tf_op jit(solution)/shard_map/stack | solution.py:94
  227.0 4.0 %pad_maximum_fusion.2 = bf16[64,2,2,2,16,256]{5,4,3,2,1,0:T(8,128)(2,1)} fusion(bf16[64,2,1,2,16,256]{5,4,3,2,1,0:T(8,128)(2,1)} %get-tuple-element.6, bf16[64,2,1,2,16,256]{5,4,3,2,1,0:T(8,128)(2,1)S(1)} %get-tuple-element.5), kind=kLoop, calls=%fused_computation.52 | loop fusion | flops 2097152 | bytes 8388608 | tf_op jit(solution)/shard_map/stack | solution.py:93
  231.0 6.4 %copy.23 = bf16[64,1,128,256]{2,3,1,0:T(8,128)(2,1)} copy(bf16[64,1,128,256]{3,2,0,1:T(8,128)(2,1)} %bitcast.58) | data formatting | bytes 8388608 | tf_op jit(solution)/shard_map/stack | solution.py:94
  237.4 28.6 %broadcast_multiply_fusion = f32[64,2,256,512]{3,2,1,0:T(8,128)} fusion(bf16[64,128,512,1]{2,1,3,0:T(8,128)(2,1)} %bitcast.52, bf16[64,1,128,256]{2,3,1,0:T(8,128)(2,1)} %copy.23, bf16[64,1,128,256]{2,3,1,0:T(8,128)(2,1)} %copy.22), kind=kOutput, calls=%fused_computation | convolution fusion | flops 4315938816 | bytes 83886080 | tf_op jit(solution)/shard_map/dot_general | solution.py:95
  (1 shorter events, 0.0 us)
Async XLA Ops:
  10.7 19.7 %collective-permute-start = (bf16[15,128,1024]{1,2,0:T(8,128)(2,1)}, bf16[15,128,1024]{1,2,0:T(8,128)(2,1)}, u32[]{:S(2)}, u32[]{:S(2)}) collective-permute-start(bf16[15,128,1024]{1,2,0:T(8,128)(2,1)} %slice.153), channel_id=1, source_target_pairs={{0,1},{1,2},{2,3},{4,5},{5,6},{6,7},{8,9},{9,10},{10,11},{12,13},{... | collective-permute-start | bytes 11796488 | tf_op jit(solution)/shard_map/ppermute | solution.py:15
  55.3 6.6 %copy-start.2 = (bf16[1024,1024]{1,0:T(8,128)(2,1)S(1)}, bf16[1024,1024]{1,0:T(8,128)(2,1)}, u32[]{:S(2)}) copy-start(bf16[1024,1024]{1,0:T(8,128)(2,1)} %convert_element_type.86) | copy-start | bytes 6291460
  70.3 2.0 copy-start.1
  73.9 43.2 %collective-permute-start.1 = (bf16[64,2,16,128]{3,2,1,0:T(8,128)(2,1)}, bf16[64,2,16,128]{3,2,1,0:T(8,128)(2,1)}, u32[]{:S(2)}, u32[]{:S(2)}) collective-permute-start(bf16[64,2,16,128]{3,2,1,0:T(8,128)(2,1)} %get-tuple-element.13), channel_id=1, source_target_pairs={{0,2},{2,0},{4,6},{6,4},{8,10},{10,8},{12,14},{14,12},{1,3},{3,1},... | collective-permute-start | bytes 1572872 | tf_op jit(solution)/shard_map/ppermute | solution.py:78
  104.5 24.4 %collective-permute-start.2 = (bf16[64,2,16,128]{3,2,1,0:T(8,128)(2,1)S(1)}, bf16[64,2,16,128]{3,2,1,0:T(8,128)(2,1)}, u32[]{:S(2)}, u32[]{:S(2)}) collective-permute-start(bf16[64,2,16,128]{3,2,1,0:T(8,128)(2,1)S(1)} %get-tuple-element.12), channel_id=1, source_target_pairs={{0,4},{2,6},{4,8},{6,10},{8,12},{10,14},{12,0},{14,2},{1,5},{3,7},... | collective-permute-start | bytes 1572872 | tf_op jit(solution)/shard_map/ppermute | solution.py:78
  106.0 93.3 %collective-permute-start.7 = (bf16[64,2,16,128]{3,2,1,0:T(8,128)(2,1)S(1)}, bf16[64,2,16,128]{3,2,1,0:T(8,128)(2,1)S(1)}, u32[]{:S(2)}, u32[]{:S(2)}) collective-permute-start(bf16[64,2,16,128]{3,2,1,0:T(8,128)(2,1)S(1)} %get-tuple-element.7), channel_id=1, source_target_pairs={{0,14},{2,12},{4,2},{6,0},{8,6},{10,4},{12,10},{14,8},{1,15},{3,13... | collective-permute-start | bytes 1572872 | tf_op jit(solution)/shard_map/ppermute | solution.py:78
  107.7 90.8 %collective-permute-start.6 = (bf16[64,2,16,128]{3,2,1,0:T(8,128)(2,1)S(1)}, bf16[64,2,16,128]{3,2,1,0:T(8,128)(2,1)S(1)}, u32[]{:S(2)}, u32[]{:S(2)}) collective-permute-start(bf16[64,2,16,128]{3,2,1,0:T(8,128)(2,1)S(1)} %get-tuple-element.8), channel_id=1, source_target_pairs={{0,12},{2,14},{4,0},{6,2},{8,4},{10,6},{12,8},{14,10},{1,13},{3,15... | collective-permute-start | bytes 1572872 | tf_op jit(solution)/shard_map/ppermute | solution.py:78
  109.5 44.9 %collective-permute-start.3 = (bf16[64,2,16,128]{3,2,1,0:T(8,128)(2,1)S(1)}, bf16[64,2,16,128]{3,2,1,0:T(8,128)(2,1)S(1)}, u32[]{:S(2)}, u32[]{:S(2)}) collective-permute-start(bf16[64,2,16,128]{3,2,1,0:T(8,128)(2,1)S(1)} %get-tuple-element.11), channel_id=1, source_target_pairs={{0,6},{2,4},{4,10},{6,8},{8,14},{10,12},{12,2},{14,0},{1,7},{3,5},... | collective-permute-start | bytes 1572872 | tf_op jit(solution)/shard_map/ppermute | solution.py:78
  117.1 68.2 %collective-permute-start.4 = (bf16[64,2,16,128]{3,2,1,0:T(8,128)(2,1)S(1)}, bf16[64,2,16,128]{3,2,1,0:T(8,128)(2,1)S(1)}, u32[]{:S(2)}, u32[]{:S(2)}) collective-permute-start(bf16[64,2,16,128]{3,2,1,0:T(8,128)(2,1)S(1)} %get-tuple-element.10), channel_id=1, source_target_pairs={{0,8},{2,10},{4,12},{6,14},{8,0},{10,2},{12,4},{14,6},{1,9},{3,11}... | collective-permute-start | bytes 1572872 | tf_op jit(solution)/shard_map/ppermute | solution.py:78
  128.8 68.8 %collective-permute-start.5 = (bf16[64,2,16,128]{3,2,1,0:T(8,128)(2,1)S(1)}, bf16[64,2,16,128]{3,2,1,0:T(8,128)(2,1)S(1)}, u32[]{:S(2)}, u32[]{:S(2)}) collective-permute-start(bf16[64,2,16,128]{3,2,1,0:T(8,128)(2,1)S(1)} %get-tuple-element.9), channel_id=1, source_target_pairs={{0,10},{2,8},{4,14},{6,12},{8,2},{10,0},{12,6},{14,4},{1,11},{3,9}... | collective-permute-start | bytes 1572872 | tf_op jit(solution)/shard_map/ppermute | solution.py:78
  200.3 7.5 %collective-permute-start.8 = (bf16[64,2,2,16,512]{4,3,2,1,0:T(8,128)(2,1)}, bf16[64,2,2,16,512]{4,3,2,1,0:T(8,128)(2,1)}, u32[]{:S(2)}, u32[]{:S(2)}) collective-permute-start(bf16[64,2,2,16,512]{4,3,2,1,0:T(8,128)(2,1)} %bitcast_dynamic-update-slice_fusion), channel_id=1, source_target_pairs={{0,1},{1,0},{2,3},{3,2},{4,5},{5,4},{6,7},{7,6},{8,9},{9,8},{10,11... | collective-permute-start | bytes 12582920 | tf_op jit(solution)/shard_map/ppermute | solution.py:84
  218.0 2.6 copy-start

commit v3 on v2

--- a/solution.py
+++ b/solution.py
@@ -1,8 +1,10 @@
+import functools
 import math
 
 import jax
 import jax.numpy as jnp
 from jax import lax
+from jax.experimental import pallas as pl
 from jax.sharding import PartitionSpec as P
 
 CH = 512
@@ -65,7 +67,67 @@
     inp_at = lax.axis_index("inp")
     tm_at = lax.axis_index("tm")
     cols = inp_size * inputs_here
-    half = jnp.zeros((own_channels, 2, tm_size, spectra_here, cols), jnp.bfloat16)
+    chunks = 2 if own_channels % 2 == 0 else 1
+    per_chunk = own_channels // chunks
+    parts = [blocks[:, chunk * per_chunk : (chunk + 1) * per_chunk] for chunk in range(chunks)]
+    out = None
+    half = None
+    for chunk in range(chunks):
+        if chunk:
+            half, parts[chunk] = lax.optimization_barrier((half, parts[chunk]))
+        pieces = send_chunk(parts[chunk], inp_at, tm_at, inp_size, tm_size)
+        if chunk:
+            lhs, rhs = finish_chunk(half, pol_size, cols)
+            out = correlate(lhs, rhs, out, (chunk - 1) * per_chunk, own_channels)
+            out, pieces = lax.optimization_barrier((out, pieces))
+        half = assemble_chunk(pieces, inp_at, inp_size, tm_size, cols)
+    lhs, rhs = finish_chunk(half, pol_size, cols)
+    return correlate(lhs, rhs, out, (chunks - 1) * per_chunk, own_channels)
+
+
+def correlate_kernel(scale, lhs_ref, rhs_ref, *rest):
+    out_ref = rest[-1]
+    rows = out_ref.shape[2]
+    for k in range(lhs_ref.shape[0]):
+        acc = jnp.dot(lhs_ref[k], rhs_ref[k], preferred_element_type=jnp.float32) * scale
+        out_ref[k, 0] = acc[:rows]
+        out_ref[k, 1] = acc[rows:]
+
+
+def correlate(lhs, rhs, prev, first_channel, own_channels):
+    count, two_rows, depth = lhs.shape
+    cols = rhs.shape[2]
+    rows = two_rows // 2
+    step = 2 if count % 2 == 0 else 1
+    offset = first_channel // step
+    in_specs = [
+        pl.BlockSpec((step, two_rows, depth), lambda c: (c, 0, 0)),
+        pl.BlockSpec((step, depth, cols), lambda c: (c, 0, 0)),
+    ]
+    args = [lhs, rhs]
+    aliases = {}
+    if prev is not None:
+        in_specs.append(pl.BlockSpec(memory_space=pl.ANY))
+        args.append(prev)
+        aliases = {2: 0}
+    flops = 2 * count * two_rows * depth * cols
+    out_bytes = count * two_rows * cols * 4
+    return pl.pallas_call(
+        functools.partial(correlate_kernel, 1.0 / (depth // 2)),
+        grid=(count // step,),
+        in_specs=in_specs,
+        out_specs=pl.BlockSpec((step, 2, rows, cols), lambda c: (c + offset, 0, 0, 0)),
+        out_shape=jax.ShapeDtypeStruct((own_channels, 2, rows, cols), jnp.float32),
+        input_output_aliases=aliases,
+        cost_estimate=pl.CostEstimate(
+            flops=flops, bytes_accessed=out_bytes + lhs.size * 2 + rhs.size * 2, transcendentals=0
+        ),
+    )(*args)
+
+
+def send_chunk(blocks, inp_at, tm_at, inp_size, tm_size):
+    group_size = blocks.shape[0]
+    pieces = []
     for inp_step in range(inp_size):
         for tm_step in range(tm_size):
             target = ((inp_at + inp_step) % inp_size) * tm_size + (tm_at + tm_step) % tm_size
@@ -76,10 +138,25 @@
                     for g in range(group_size)
                 ]
                 block = lax.ppermute(block, ("inp", "tm"), route)
+            pieces.append(block)
+    return pieces
+
+
+def assemble_chunk(pieces, inp_at, inp_size, tm_size, cols):
+    own_channels, _, spectra_here, inputs_here = pieces[0].shape
+    half = jnp.zeros((own_channels, 2, tm_size, spectra_here, cols), jnp.bfloat16)
+    for inp_step in range(inp_size):
+        for tm_step in range(tm_size):
+            block = pieces[inp_step * tm_size + tm_step]
             source_inp = (inp_at + inp_size - inp_step) % inp_size
             half = lax.dynamic_update_slice(
                 half, block[:, :, None], (0, 0, tm_step, 0, source_inp * inputs_here)
             )
+    return half
+
+
+def finish_chunk(half, pol_size, cols):
+    own_channels, _, tm_size, spectra_here, _ = half.shape
     if pol_size == 2:
         partner = lax.ppermute(half, "pol", [(0, 1), (1, 0)])
         both = jnp.stack([half, partner], axis=1)
@@ -92,13 +169,8 @@
     own_rows = lax.dynamic_slice_in_dim(both, row_start, rows_here, 5)
     swapped = jnp.stack([own_rows[:, :, 1], -own_rows[:, :, 0]], axis=2)
     lhs = jnp.stack([own_rows, swapped], axis=1).reshape(own_channels, 2, depth, rows_here)
-    summed = lax.dot_general(
-        lhs,
-        left_all,
-        (((2,), (1,)), ((0,), (0,))),
-        preferred_element_type=jnp.float32,
-    )
-    return summed * (1.0 / (depth // 2))
+    lhs = lhs.transpose(0, 1, 3, 2).reshape(own_channels, 2 * rows_here, depth)
+    return lhs, left_all
 
 
 def solution(mesh):

time: 267 us -> 247 us (0.925)
  Pallas kernels: 0 us -> 36.6 us
  matrix products: 35.6 us -> 6.95 us
  waiting for transfers between devices: 58.9 us -> 40.4 us
  starting transfers between devices: 66.5 us -> 60.7 us
  other arithmetic: 51.3 us -> 47.4 us
    pallas_call x0 -> x2, Pallas kernels: none -> 36.6 us  [correlate(): pl.pallas_call(functools.partial(correlate_kernel, 1.0 / (depth // 2)), g...]
    dot_general x1 -> x0, matrix products: 28.6 us -> none  [per_device(): lax.dot_general(lhs, left_all, (((2,), (1,)), ((0,), (0,))), preferred_el...]
    ppermute x8 -> x16, waiting for transfers between devices: 58.9 us -> 40.4 us  [the longest x14 36.3 us: send_chunk(): block = lax.ppermute(block, ('inp', 'tm'), route)]
    transpose x0 -> x2, local copies, waits for them, and re-layouts: none -> 12.9 us  [finish_chunk(): lhs = lhs.transpose(0, 1, 3, 2).reshape(own_channels, 2 * rows_here, depth)]
    another operation x2 -> x4, local copies, waits for them, and re-layouts: 12.7 us -> 3.14 us  [the longest x1 2.45 us: finish_chunk(): both = jnp.stack([half, partner], axis=1)]
    another operation x4 -> x7, other arithmetic: 22.7 us -> 15 us  [the longest x2 10.2 us: per_device(): both = jnp.stack([half, partner], axis=1)]
    ppermute x8 -> x16, starting transfers between devices: 62.3 us -> 56.4 us  [the longest x14 56.3 us: send_chunk(): block = lax.ppermute(block, ('inp', 'tm'), route)]
    dynamic_update_slice x8 -> x16, local copies, waits for them, and re-layouts: 10.2 us -> 4.89 us  [assemble_chunk(): lax.dynamic_update_slice(half, block[:, :, None], (0, 0, tm_step, 0, sour...]
  transfers between devices with their start and end apart: 9 -> 17, of which waited for: 5 -> 6; matrix products, arithmetic and copies ran while one was open for 10% -> 14% of each run, Pallas kernels for 0% -> 7%
where the time goes in v3:
time: 247 us; the launch traced here: 244 us
  starting transfers between devices  60.7 us (25%)
  local copies, waits for them, and re-layouts  51.6 us (21%)
  other arithmetic  47.4 us (19%)
  waiting for transfers between devices  40.4 us (16%)
  Pallas kernels  36.6 us (15%)
  matrix products  6.95 us (3%)
    ppermute x14, starting transfers between devices, send_chunk(): block = lax.ppermute(block, ('inp', 'tm'), route)  56.3 us
    pallas_call x2, Pallas kernels, correlate(): pl.pallas_call(functools.partial(correlate_kernel, 1.0 / (depth // 2)), g...  36.6 us
    ppermute x14, waiting for transfers between devices, send_chunk(): block = lax.ppermute(block, ('inp', 'tm'), route)  36.3 us
    convert_element_type x1, other arithmetic, per_device(): filtered = filtered.astype(jnp.bfloat16)  25.7 us
    transpose x2, local copies, waits for them, and re-layouts, finish_chunk(): lhs = lhs.transpose(0, 1, 3, 2).reshape(own_channels, 2 * rows_here, depth)  12.9 us
    unnamed x14, local copies, waits for them, and re-layouts  9.11 us
    another operation x1, other arithmetic  8.5 us
    dot_general x1, matrix products, per_device(): lax.dot_general(dft_table_t(frame_len), filtered.reshape(spectra_here * i...  6.95 us
  transfers between devices with their start and end apart: 17, of which 6 were waited for; matrix products, arithmetic and copies ran while one was open for 14% of the time, Pallas kernels for 7%

profile of v3, /device:TPU:0, one launch (start us, length us, event | category | flops | bytes accessed | tf_op | source)
XLA Modules:
  0.0 244.5 jit_solution(7997511522275217932)
XLA Ops:
  0.0 6.4 %copy.28 = bf16[128,16384]{0,1:T(8,128)(2,1)} copy(bf16[128,16384]{1,0:T(8,128)(2,1)} %param.1) | data formatting | bytes 8388608 | tf_op args[0]
  6.4 4.3 %slice.169 = bf16[15,128,1024]{1,2,0:T(8,128)(2,1)} slice(bf16[16,128,1024]{1,2,0:T(8,128)(2,1)} %bitcast.90), slice={[1:16], [0:128], [0:1024]} | slice | bytes 7864320 | tf_op jit(solution)/shard_map/slice | solution.py:44
  10.7 4.2 %collective-permute-start = (bf16[15,128,1024]{1,2,0:T(8,128)(2,1)}, bf16[15,128,1024]{1,2,0:T(8,128)(2,1)}, u32[]{:S(2)}, u32[]{:S(2)}) collective-permute-start(bf16[15,128,1024]{1,2,0:T(8,128)(2,1)} %slice.169), channel_id=1, source_target_pairs={{0,1},{1,2},{2,3},{4,5},{5,6},{6,7},{8,9},{9,10},{10,11},{12,13},{... | collective-permute-start | bytes 11796488 | tf_op jit(solution)/shard_map/ppermute | solution.py:17
  14.9 1.1 multiply_reduce_fusion
  16.6 8.5 %negate_convert_fusion = (bf16[512,1,1024]{2,0,1:T(8,128)(2,1)S(1)}, bf16[512,1,1024]{2,0,1:T(8,128)(2,1)S(1)}) fusion(), kind=kLoop, calls=%fused_computation.64 | loop fusion | flops 8912896 | bytes 2097152 | tf_op jit(solution)/shard_map/convert.1
  25.1 0.2 pad_maximum_fusion.3
  25.3 2.2 copy.27
  27.5 2.3 convert_element_type.86
  29.8 0.5 broadcast_divide_fusion
  30.3 25.7 %add_convert_fusion = bf16[16,128,1024]{1,2,0:T(8,128)(2,1)} fusion(bf16[16,128,1024]{1,2,0:T(8,128)(2,1)} %bitcast.91, bf16[15,128,1024]{1,2,0:T(8,128)(2,1)} %collective-permute-done, f32[1024]{0:T(1024)S(1)} %get-tuple-element.49, f32[1024]{0:T(1024)S(1)} %get-tuple-element.50, f32[1024]{0:T(1024)S(1)} %get-tuple-element.51, ...), kind=kLoop, calls=%fused_computation.28 | loop fusion | flops 132120576 | bytes 12386304 | tf_op jit(solution)/shard_map/convert_element_type | solution.py:53
  56.0 6.5 %copy.29 = bf16[16,128,1024]{2,1,0:T(8,128)(2,1)} copy(bf16[16,128,1024]{1,2,0:T(8,128)(2,1)} %add_convert_fusion) | data formatting | bytes 8388608 | tf_op jit(solution)/shard_map/convert_element_type | solution.py:53
  62.5 6.9 %convert_bitcast_fusion = bf16[128,8,16,128]{3,1,2,0:T(8,128)(2,1)S(1)} fusion(bf16[1024,1024]{1,0:T(8,128)(2,1)S(1)} %copy-done.1, bf16[2048,1024]{1,0:T(8,128)(2,1)} %bitcast.107), kind=kOutput, calls=%fused_computation.52 | convolution fusion | flops 4297064448 | bytes 10485760 | tf_op jit(solution)/shard_map/dot_general | solution.py:54
  69.5 1.4 copy.36
  70.9 2.0 fusion.23
  72.9 1.3 copy-done
  74.3 1.1 dynamic-slice_bitcast_fusion.8
  75.4 30.7 %collective-permute-start.1 = (bf16[32,2,16,128]{3,2,1,0:T(8,128)(2,1)}, bf16[32,2,16,128]{3,2,1,0:T(8,128)(2,1)S(1)}, u32[]{:S(2)}, u32[]{:S(2)}) collective-permute-start(bf16[32,2,16,128]{3,2,1,0:T(8,128)(2,1)} %get-tuple-element.47), channel_id=1, source_target_pairs={{0,2},{2,0},{4,6},{6,4},{8,10},{10,8},{12,14},{14,12},{1,3},{3,1},... | collective-permute-start | bytes 786440 | tf_op jit(solution)/shard_map/ppermute | solution.py:140
  106.0 3.0 %collective-permute-start.7 = (bf16[32,2,16,128]{3,2,1,0:T(8,128)(2,1)S(1)}, bf16[32,2,16,128]{3,2,1,0:T(8,128)(2,1)S(1)}, u32[]{:S(2)}, u32[]{:S(2)}) collective-permute-start(bf16[32,2,16,128]{3,2,1,0:T(8,128)(2,1)S(1)} %get-tuple-element.41), channel_id=1, source_target_pairs={{0,14},{2,12},{4,2},{6,0},{8,6},{10,4},{12,10},{14,8},{1,15},{3,13... | collective-permute-start | bytes 786440 | tf_op jit(solution)/shard_map/ppermute | solution.py:140
  109.1 0.6 collective-permute-start.6
  109.6 0.8 collective-permute-start.5
  110.4 1.6 collective-permute-start.2
  112.0 0.3 broadcast.109.clone
  112.2 1.0 bitcast_dynamic-update-slice_fusion.15
  113.3 5.2 %collective-permute-done.1 = bf16[32,2,16,128]{3,2,1,0:T(8,128)(2,1)S(1)} collective-permute-done((bf16[32,2,16,128]{3,2,1,0:T(8,128)(2,1)}, bf16[32,2,16,128]{3,2,1,0:T(8,128)(2,1)S(1)}, u32[]{:S(2)}, u32[]{:S(2)}) %collective-permute-start.1) | collective-permute-done | bytes 262176 | tf_op jit(solution)/shard_map/ppermute | solution.py:140
  118.5 1.1 collective-permute-start.3
  119.6 14.2 %collective-permute-done.2 = bf16[32,2,16,128]{3,2,1,0:T(8,128)(2,1)S(1)} collective-permute-done((bf16[32,2,16,128]{3,2,1,0:T(8,128)(2,1)}, bf16[32,2,16,128]{3,2,1,0:T(8,128)(2,1)S(1)}, u32[]{:S(2)}, u32[]{:S(2)}) %collective-permute-start.2) | collective-permute-done | bytes 262176 | tf_op jit(solution)/shard_map/ppermute | solution.py:140
  133.8 6.5 %collective-permute-start.4 = (bf16[32,2,16,128]{3,2,1,0:T(8,128)(2,1)S(1)}, bf16[32,2,16,128]{3,2,1,0:T(8,128)(2,1)S(1)}, u32[]{:S(2)}, u32[]{:S(2)}) collective-permute-start(bf16[32,2,16,128]{3,2,1,0:T(8,128)(2,1)S(1)} %get-tuple-element.44), channel_id=1, source_target_pairs={{0,8},{2,10},{4,12},{6,14},{8,0},{10,2},{12,4},{14,6},{1,9},{3,11}... | collective-permute-start | bytes 786440 | tf_op jit(solution)/shard_map/ppermute | solution.py:140
  140.3 0.1 bitcast_dynamic-update-slice_fusion.12
  140.4 13.0 %collective-permute-done.4 = bf16[32,2,16,128]{3,2,1,0:T(8,128)(2,1)S(1)} collective-permute-done((bf16[32,2,16,128]{3,2,1,0:T(8,128)(2,1)S(1)}, bf16[32,2,16,128]{3,2,1,0:T(8,128)(2,1)S(1)}, u32[]{:S(2)}, u32[]{:S(2)}) %collective-permute-start.4) | collective-permute-done | bytes 262176 | tf_op jit(solution)/shard_map/ppermute | solution.py:140
  153.8 0.1 collective-permute-start.8
  153.8 2.8 %dynamic-slice_bitcast_fusion = (bf16[32,2,16,128]{3,2,1,0:T(8,128)(2,1)S(1)}, bf16[32,2,16,128]{3,2,1,0:T(8,128)(2,1)S(1)}, bf16[32,2,16,128]{3,2,1,0:T(8,128)(...) fusion(bf16[8,32,2,16,128]{4,3,2,1,0:T(8,128)(2,1)} %get-tuple-, ...), kind=kLoop, calls=%fused_computation.87 | loop fusion | bytes 4194336 | tf_op jit(solution)/shard_map/jit(dynamic_index_in_dim)/squeeze | solution.py:134
  156.6 4.2 %collective-permute-start.15 = (bf16[32,2,16,128]{3,2,1,0:T(8,128)(2,1)S(1)}, bf16[32,2,16,128]{3,2,1,0:T(8,128)(2,1)S(1)}, u32[]{:S(2)}, u32[]{:S(2)}) collective-permute-start(bf16[32,2,16,128]{3,2,1,0:T(8,128)(2,1)S(1)} %get-tuple-element.31), channel_id=1, source_target_pairs={{0,14},{2,12},{4,2},{6,0},{8,6},{10,4},{12,10},{14,8},{1,15},{3,13... | collective-permute-start | bytes 786440 | tf_op jit(solution)/shard_map/ppermute | solution.py:140
  160.8 0.3 collective-permute-start.14
  161.1 3.8 %collective-permute-start.12 = (bf16[32,2,16,128]{3,2,1,0:T(8,128)(2,1)S(1)}, bf16[32,2,16,128]{3,2,1,0:T(8,128)(2,1)}, u32[]{:S(2)}, u32[]{:S(2)}) collective-permute-start(bf16[32,2,16,128]{3,2,1,0:T(8,128)(2,1)S(1)} %get-tuple-element.34), channel_id=1, source_target_pairs={{0,8},{2,10},{4,12},{6,14},{8,0},{10,2},{12,4},{14,6},{1,9},{3,11}... | collective-permute-start | bytes 786440 | tf_op jit(solution)/shard_map/ppermute | solution.py:140
  164.9 1.7 collective-permute-start.11
  166.6 1.5 fusion.18
  168.1 0.1 fusion.25
  168.3 0.2 pad_maximum_fusion.4
  168.5 3.9 %pad_maximum_fusion = bf16[32,2,2,2,16,512]{5,4,3,2,1,0:T(8,128)(2,1)} fusion(bf16[32,1,2,2,16,512]{5,4,3,2,1,0:T(8,128)(2,1)} %bitcast.21, bf16[32,1,2,2,16,512]{5,4,3,2,1,0:T(8,128)(2,1)S(1)} %bitcast.96), kind=kLoop, calls=%fused_computation.30 | loop fusion | flops 2097152 | bytes 8388608 | tf_op jit(solution)/shard_map/stack | solution.py:162
  172.4 0.3 collective-permute-start.10
  172.7 0.3 collective-permute-done.14
  173.1 1.8 collective-permute-start.9
  174.9 2.4 maximum_bitcast_fusion
  177.3 6.5 %copy.31 = bf16[32,2,256,128]{3,2,1,0:T(8,128)(2,1)} copy(bf16[32,2,256,128]{2,3,0,1:T(8,128)(2,1)} %maximum_bitcast_fusion) | data formatting | bytes 8388608 | tf_op jit(solution)/shard_map/transpose | solution.py:172
  183.7 18.3 %shard_map.17.rest_0_ = f32[64,2,256,512]{3,2,1,0:T(8,128)} custom-call(bf16[32,512,128]{2,1,0:T(8,128)(2,1)} %bitcast.100, bf16[32,128,512]{2,1,0:T(8,128)(2,1)} %bitcast.97), custom_call_target="tpu_custom_call" | custom-call | flops 2147483648 | bytes 41943040 | tf_op jit(solution)/shard_map/pallas_call | solution.py:115
  202.0 3.5 %collective-permute-done.12 = bf16[32,2,16,128]{3,2,1,0:T(8,128)(2,1)} collective-permute-done((bf16[32,2,16,128]{3,2,1,0:T(8,128)(2,1)S(1)}, bf16[32,2,16,128]{3,2,1,0:T(8,128)(2,1)}, u32[]{:S(2)}, u32[]{:S(2)}) %collective-permute-start.12) | collective-permute-done | bytes 262176 | tf_op jit(solution)/shard_map/ppermute | solution.py:140
  205.5 0.3 broadcast.109
  205.8 0.1 bitcast_dynamic-update-slice_fusion.7
  205.8 0.1 bitcast_dynamic-update-slice_fusion.6
  206.0 1.0 bitcast_dynamic-update-slice_fusion.4
  207.0 1.0 bitcast_dynamic-update-slice_fusion.3
  208.0 1.0 bitcast_dynamic-update-slice_fusion.2
  209.2 0.1 collective-permute-start.16
  209.3 4.1 %collective-permute-done.16 = bf16[32,2,2,16,512]{4,3,2,1,0:T(8,128)(2,1)S(1)} collective-permute-done((bf16[32,2,2,16,512]{4,3,2,1,0:T(8,128)(2,1)S(1)}, bf16[32,2,2,16,512]{4,3,2,1,0:T(8,128)(2,1)S(1)}, u32[]{:S(2)}, u32[]{:S(2)}) %collective-permute-start.16) | collective-permute-done | bytes 2097184 | tf_op jit(solution)/shard_map/ppermute | solution.py:161
  213.5 0.3 fusion.17
  213.7 0.4 pad_maximum_fusion.1
  214.1 0.3 copy.32
  214.4 0.1 fusion.24
  214.6 2.4 %copy.35 = bf16[32,2,2,2,16,512]{5,4,3,2,1,0:T(8,128)(2,1)} copy(bf16[32,2,2,2,16,512]{5,4,3,2,0,1:T(8,128)(2,1)S(1)} %pad_maximum_fusion.1) | data formatting | bytes 8388608 | tf_op jit(solution)/shard_map/stack | solution.py:162
  217.0 0.2 pad_maximum_fusion.5
  217.2 0.2 copy.33
  217.4 2.3 maximum_bitcast_fusion.1
  219.8 6.5 %copy.34 = bf16[32,2,256,128]{3,2,1,0:T(8,128)(2,1)} copy(bf16[32,2,256,128]{2,3,0,1:T(8,128)(2,1)} %maximum_bitcast_fusion.1) | data formatting | bytes 8388608 | tf_op jit(solution)/shard_map/transpose | solution.py:172
  226.2 18.3 %shard_map.18 = f32[64,2,256,512]{3,2,1,0:T(8,128)} custom-call(bf16[32,512,128]{2,1,0:T(8,128)(2,1)} %bitcast.99, bf16[32,128,512]{2,1,0:T(8,128)(2,1)} %bitcast.98, f32[64,2,256,512]{3,2,1,0:T(8,128)} %shard_map.17.rest_0_), custom_call_target="tpu_custom_call", output_to_operand_aliasing={{}: (2, {})} | custom-call | flops 2147483648 | bytes 41943040 | tf_op jit(solution)/shard_map/pallas_call | solution.py:115
  (33 shorter events, 0.7 us)
Async XLA Ops:
  10.7 19.6 %collective-permute-start = (bf16[15,128,1024]{1,2,0:T(8,128)(2,1)}, bf16[15,128,1024]{1,2,0:T(8,128)(2,1)}, u32[]{:S(2)}, u32[]{:S(2)}) collective-permute-start(bf16[15,128,1024]{1,2,0:T(8,128)(2,1)} %slice.169), channel_id=1, source_target_pairs={{0,1},{1,2},{2,3},{4,5},{5,6},{6,7},{8,9},{9,10},{10,11},{12,13},{... | collective-permute-start | bytes 11796488 | tf_op jit(solution)/shard_map/ppermute | solution.py:17
  55.9 6.6 %copy-start.1 = (bf16[1024,1024]{1,0:T(8,128)(2,1)S(1)}, bf16[1024,1024]{1,0:T(8,128)(2,1)}, u32[]{:S(2)}) copy-start(bf16[1024,1024]{1,0:T(8,128)(2,1)} %convert_element_type.86) | copy-start | bytes 6291460
  72.9 1.3 copy-start
  75.4 43.1 %collective-permute-start.1 = (bf16[32,2,16,128]{3,2,1,0:T(8,128)(2,1)}, bf16[32,2,16,128]{3,2,1,0:T(8,128)(2,1)S(1)}, u32[]{:S(2)}, u32[]{:S(2)}) collective-permute-start(bf16[32,2,16,128]{3,2,1,0:T(8,128)(2,1)} %get-tuple-element.47), channel_id=1, source_target_pairs={{0,2},{2,0},{4,6},{6,4},{8,10},{10,8},{12,14},{14,12},{1,3},{3,1},... | collective-permute-start | bytes 786440 | tf_op jit(solution)/shard_map/ppermute | solution.py:140
  106.0 47.7 %collective-permute-start.7 = (bf16[32,2,16,128]{3,2,1,0:T(8,128)(2,1)S(1)}, bf16[32,2,16,128]{3,2,1,0:T(8,128)(2,1)S(1)}, u32[]{:S(2)}, u32[]{:S(2)}) collective-permute-start(bf16[32,2,16,128]{3,2,1,0:T(8,128)(2,1)S(1)} %get-tuple-element.41), channel_id=1, source_target_pairs={{0,14},{2,12},{4,2},{6,0},{8,6},{10,4},{12,10},{14,8},{1,15},{3,13... | collective-permute-start | bytes 786440 | tf_op jit(solution)/shard_map/ppermute | solution.py:140
  109.1 44.5 %collective-permute-start.6 = (bf16[32,2,16,128]{3,2,1,0:T(8,128)(2,1)S(1)}, bf16[32,2,16,128]{3,2,1,0:T(8,128)(2,1)S(1)}, u32[]{:S(2)}, u32[]{:S(2)}) collective-permute-start(bf16[32,2,16,128]{3,2,1,0:T(8,128)(2,1)S(1)} %get-tuple-element.42), channel_id=1, source_target_pairs={{0,12},{2,14},{4,0},{6,2},{8,4},{10,6},{12,8},{14,10},{1,13},{3,15... | collective-permute-start | bytes 786440 | tf_op jit(solution)/shard_map/ppermute | solution.py:140
  109.6 43.9 %collective-permute-start.5 = (bf16[32,2,16,128]{3,2,1,0:T(8,128)(2,1)S(1)}, bf16[32,2,16,128]{3,2,1,0:T(8,128)(2,1)S(1)}, u32[]{:S(2)}, u32[]{:S(2)}) collective-permute-start(bf16[32,2,16,128]{3,2,1,0:T(8,128)(2,1)S(1)} %get-tuple-element.43), channel_id=1, source_target_pairs={{0,10},{2,8},{4,14},{6,12},{8,2},{10,0},{12,6},{14,4},{1,11},{3,9}... | collective-permute-start | bytes 786440 | tf_op jit(solution)/shard_map/ppermute | solution.py:140
  110.4 23.4 %collective-permute-start.2 = (bf16[32,2,16,128]{3,2,1,0:T(8,128)(2,1)}, bf16[32,2,16,128]{3,2,1,0:T(8,128)(2,1)S(1)}, u32[]{:S(2)}, u32[]{:S(2)}) collective-permute-start(bf16[32,2,16,128]{3,2,1,0:T(8,128)(2,1)} %get-tuple-element.46), channel_id=1, source_target_pairs={{0,4},{2,6},{4,8},{6,10},{8,12},{10,14},{12,0},{14,2},{1,5},{3,7},... | collective-permute-start | bytes 786440 | tf_op jit(solution)/shard_map/ppermute | solution.py:140
  118.5 21.8 %collective-permute-start.3 = (bf16[32,2,16,128]{3,2,1,0:T(8,128)(2,1)}, bf16[32,2,16,128]{3,2,1,0:T(8,128)(2,1)S(1)}, u32[]{:S(2)}, u32[]{:S(2)}) collective-permute-start(bf16[32,2,16,128]{3,2,1,0:T(8,128)(2,1)} %get-tuple-element.45), channel_id=1, source_target_pairs={{0,6},{2,4},{4,10},{6,8},{8,14},{10,12},{12,2},{14,0},{1,7},{3,5},... | collective-permute-start | bytes 786440 | tf_op jit(solution)/shard_map/ppermute | solution.py:140
  133.8 19.6 %collective-permute-start.4 = (bf16[32,2,16,128]{3,2,1,0:T(8,128)(2,1)S(1)}, bf16[32,2,16,128]{3,2,1,0:T(8,128)(2,1)S(1)}, u32[]{:S(2)}, u32[]{:S(2)}) collective-permute-start(bf16[32,2,16,128]{3,2,1,0:T(8,128)(2,1)S(1)} %get-tuple-element.44), channel_id=1, source_target_pairs={{0,8},{2,10},{4,12},{6,14},{8,0},{10,2},{12,4},{14,6},{1,9},{3,11}... | collective-permute-start | bytes 786440 | tf_op jit(solution)/shard_map/ppermute | solution.py:140
  153.8 11.1 %collective-permute-start.8 = (bf16[32,2,2,16,512]{4,3,2,1,0:T(8,128)(2,1)S(1)}, bf16[32,2,2,16,512]{4,3,2,1,0:T(8,128)(2,1)}, u32[]{:S(2)}, u32[]{:S(2)}) collective-permute-start(bf16[32,2,2,16,512]{4,3,2,1,0:T(8,128)(2,1)S(1)} %bitcast_dynamic-update-slice_fusion.8), channel_id=1, source_target_pairs={{0,1},{1,0},{2,3},{3,2},{4,5},{5,4},{6,7},{7,6},{8,9},{9,8},{10,11... | collective-permute-start | bytes 6291464 | tf_op jit(solution)/shard_map/ppermute | solution.py:161
  156.6 15.8 %collective-permute-start.15 = (bf16[32,2,16,128]{3,2,1,0:T(8,128)(2,1)S(1)}, bf16[32,2,16,128]{3,2,1,0:T(8,128)(2,1)S(1)}, u32[]{:S(2)}, u32[]{:S(2)}) collective-permute-start(bf16[32,2,16,128]{3,2,1,0:T(8,128)(2,1)S(1)} %get-tuple-element.31), channel_id=1, source_target_pairs={{0,14},{2,12},{4,2},{6,0},{8,6},{10,4},{12,10},{14,8},{1,15},{3,13... | collective-permute-start | bytes 786440 | tf_op jit(solution)/shard_map/ppermute | solution.py:140
  160.8 12.3 %collective-permute-start.14 = (bf16[32,2,16,128]{3,2,1,0:T(8,128)(2,1)S(1)}, bf16[32,2,16,128]{3,2,1,0:T(8,128)(2,1)S(1)}, u32[]{:S(2)}, u32[]{:S(2)}) collective-permute-start(bf16[32,2,16,128]{3,2,1,0:T(8,128)(2,1)S(1)} %get-tuple-element.32), channel_id=1, source_target_pairs={{0,12},{2,14},{4,0},{6,2},{8,4},{10,6},{12,8},{14,10},{1,13},{3,15... | collective-permute-start | bytes 786440 | tf_op jit(solution)/shard_map/ppermute | solution.py:140
  161.1 40.9 %collective-permute-start.13 = (bf16[32,2,16,128]{3,2,1,0:T(8,128)(2,1)}, bf16[32,2,16,128]{3,2,1,0:T(8,128)(2,1)}, u32[]{:S(2)}, u32[]{:S(2)}) collective-permute-start(bf16[32,2,16,128]{3,2,1,0:T(8,128)(2,1)} %get-tuple-element.33), channel_id=1, source_target_pairs={{0,10},{2,8},{4,14},{6,12},{8,2},{10,0},{12,6},{14,4},{1,11},{3,9}... | collective-permute-start | bytes 786440 | tf_op jit(solution)/shard_map/ppermute | solution.py:140
  161.1 44.4 %collective-permute-start.12 = (bf16[32,2,16,128]{3,2,1,0:T(8,128)(2,1)S(1)}, bf16[32,2,16,128]{3,2,1,0:T(8,128)(2,1)}, u32[]{:S(2)}, u32[]{:S(2)}) collective-permute-start(bf16[32,2,16,128]{3,2,1,0:T(8,128)(2,1)S(1)} %get-tuple-element.34), channel_id=1, source_target_pairs={{0,8},{2,10},{4,12},{6,14},{8,0},{10,2},{12,4},{14,6},{1,9},{3,11}... | collective-permute-start | bytes 786440 | tf_op jit(solution)/shard_map/ppermute | solution.py:140
  164.9 40.6 %collective-permute-start.11 = (bf16[32,2,16,128]{3,2,1,0:T(8,128)(2,1)S(1)}, bf16[32,2,16,128]{3,2,1,0:T(8,128)(2,1)}, u32[]{:S(2)}, u32[]{:S(2)}) collective-permute-start(bf16[32,2,16,128]{3,2,1,0:T(8,128)(2,1)S(1)} %get-tuple-element.35), channel_id=1, source_target_pairs={{0,6},{2,4},{4,10},{6,8},{8,14},{10,12},{12,2},{14,0},{1,7},{3,5},... | collective-permute-start | bytes 786440 | tf_op jit(solution)/shard_map/ppermute | solution.py:140
  172.4 2.5 %copy-start.2 = (bf16[32,2,16,128]{3,2,1,0:T(8,128)(2,1)}, bf16[32,2,16,128]{3,2,1,0:T(8,128)(2,1)S(1)}, u32[]{:S(2)}) copy-start(bf16[32,2,16,128]{3,2,1,0:T(8,128)(2,1)S(1)} %collective-permute-done.15) | copy-start | bytes 786436
  172.4 33.1 %collective-permute-start.10 = (bf16[32,2,16,128]{3,2,1,0:T(8,128)(2,1)S(1)}, bf16[32,2,16,128]{3,2,1,0:T(8,128)(2,1)S(1)}, u32[]{:S(2)}, u32[]{:S(2)}) collective-permute-start(bf16[32,2,16,128]{3,2,1,0:T(8,128)(2,1)S(1)} %get-tuple-element.36), channel_id=1, source_target_pairs={{0,4},{2,6},{4,8},{6,10},{8,12},{10,14},{12,0},{14,2},{1,5},{3,7},... | collective-permute-start | bytes 786440 | tf_op jit(solution)/shard_map/ppermute | solution.py:140
  173.1 1.8 copy-start.4
  173.1 32.4 %collective-permute-start.9 = (bf16[32,2,16,128]{3,2,1,0:T(8,128)(2,1)S(1)}, bf16[32,2,16,128]{3,2,1,0:T(8,128)(2,1)S(1)}, u32[]{:S(2)}, u32[]{:S(2)}) collective-permute-start(bf16[32,2,16,128]{3,2,1,0:T(8,128)(2,1)S(1)} %get-tuple-element.37), channel_id=1, source_target_pairs={{0,2},{2,0},{4,6},{6,4},{8,10},{10,8},{12,14},{14,12},{1,3},{3,1},... | collective-permute-start | bytes 786440 | tf_op jit(solution)/shard_map/ppermute | solution.py:140
  202.0 7.1 %copy-start.5 = (bf16[32,2,16,128]{3,2,1,0:T(8,128)(2,1)S(1)}, bf16[32,2,16,128]{3,2,1,0:T(8,128)(2,1)}, u32[]{:S(2)}) copy-start(bf16[32,2,16,128]{3,2,1,0:T(8,128)(2,1)} %copy-done.4) | copy-start | bytes 786436
  202.0 7.1 %copy-start.3 = (bf16[32,2,16,128]{3,2,1,0:T(8,128)(2,1)S(1)}, bf16[32,2,16,128]{3,2,1,0:T(8,128)(2,1)}, u32[]{:S(2)}) copy-start(bf16[32,2,16,128]{3,2,1,0:T(8,128)(2,1)} %copy-done.2) | copy-start | bytes 786436
  209.2 4.2 %collective-permute-start.16 = (bf16[32,2,2,16,512]{4,3,2,1,0:T(8,128)(2,1)S(1)}, bf16[32,2,2,16,512]{4,3,2,1,0:T(8,128)(2,1)S(1)}, u32[]{:S(2)}, u32[]{:S(2)}) collective-permute-start(bf16[32,2,2,16,512]{4,3,2,1,0:T(8,128)(2,1)S(1)} %bitcast_dynamic-update-slice_fusion), channel_id=1, source_target_pairs={{0,1},{1,0},{2,3},{3,2},{4,5},{5,4},{6,7},{7,6},{8,9},{9,8},{10,11... | collective-permute-start | bytes 6291464 | tf_op jit(solution)/shard_map/ppermute | solution.py:161

commit v4 on v3

--- a/solution.py
+++ b/solution.py
@@ -67,7 +67,7 @@
     inp_at = lax.axis_index("inp")
     tm_at = lax.axis_index("tm")
     cols = inp_size * inputs_here
-    chunks = 2 if own_channels % 2 == 0 else 1
+    chunks = 4 if own_channels % 8 == 0 else 1
     per_chunk = own_channels // chunks
     parts = [blocks[:, chunk * per_chunk : (chunk + 1) * per_chunk] for chunk in range(chunks)]
     out = None

time: 247 us -> 242 us (0.980)
  waiting for transfers between devices: 40.4 us -> 12.3 us
  starting transfers between devices: 60.7 us -> 83.6 us
  other arithmetic: 47.4 us -> 39.9 us
  local copies, waits for them, and re-layouts: 51.6 us -> 56.6 us
  Pallas kernels: 36.6 us -> 39.3 us
    ppermute x14 -> x28, waiting for transfers between devices: 36.3 us -> 9.6 us  [send_chunk(): block = lax.ppermute(block, ('inp', 'tm'), route)]
    ppermute x14 -> x28, starting transfers between devices: 56.3 us -> 79 us  [send_chunk(): block = lax.ppermute(block, ('inp', 'tm'), route)]
    dynamic_update_slice x16 -> x32, local copies, waits for them, and re-layouts: 4.89 us -> 11.1 us  [assemble_chunk(): lax.dynamic_update_slice(half, block[:, :, None], (0, 0, tm_step, 0, sour...]
    transpose x2 -> x4, other arithmetic: 4.71 us -> 0.77 us  [finish_chunk(): lhs = lhs.transpose(0, 1, 3, 2).reshape(own_channels, 2 * rows_here, depth)]
    another operation x4 -> x8, other arithmetic: 6.09 us -> 2.57 us  [finish_chunk(): both = jnp.stack([half, partner], axis=1)]
    transpose x2 -> x4, local copies, waits for them, and re-layouts: 12.9 us -> 9.52 us  [finish_chunk(): lhs = lhs.transpose(0, 1, 3, 2).reshape(own_channels, 2 * rows_here, depth)]
    pallas_call x2 -> x4, Pallas kernels: 36.6 us -> 39.3 us  [correlate(): pl.pallas_call(functools.partial(correlate_kernel, 1.0 / (depth // 2)), g...]
    unnamed x14 -> x22, local copies, waits for them, and re-layouts: 9.11 us -> 7.8 us
  transfers between devices with their start and end apart: 17 -> 33, of which waited for: 6 -> 4; matrix products, arithmetic and copies ran while one was open for 14% -> 14% of each run, Pallas kernels for 7% -> 12%
where the time goes in v4:
time: 242 us; the launch traced here: 240 us
  starting transfers between devices  83.6 us (35%)
  local copies, waits for them, and re-layouts  56.6 us (23%)
  other arithmetic  39.9 us (16%)
  Pallas kernels  39.3 us (16%)
  waiting for transfers between devices  12.3 us (5%)
  matrix products  6.95 us (3%)
    ppermute x28, starting transfers between devices, send_chunk(): block = lax.ppermute(block, ('inp', 'tm'), route)  79 us
    pallas_call x4, Pallas kernels, correlate(): pl.pallas_call(functools.partial(correlate_kernel, 1.0 / (depth // 2)), g...  39.3 us
    convert_element_type x1, other arithmetic, per_device(): filtered = filtered.astype(jnp.bfloat16)  25.6 us
    dynamic_update_slice x32, local copies, waits for them, and re-layouts, assemble_chunk(): lax.dynamic_update_slice(half, block[:, :, None], (0, 0, tm_step, 0, sour...  11.1 us
    ppermute x28, waiting for transfers between devices, send_chunk(): block = lax.ppermute(block, ('inp', 'tm'), route)  9.6 us
    transpose x4, local copies, waits for them, and re-layouts, finish_chunk(): lhs = lhs.transpose(0, 1, 3, 2).reshape(own_channels, 2 * rows_here, depth)  9.52 us
    another operation x1, other arithmetic  8.5 us
    unnamed x22, local copies, waits for them, and re-layouts  7.8 us
  transfers between devices with their start and end apart: 33, of which 4 were waited for; matrix products, arithmetic and copies ran while one was open for 14% of the time, Pallas kernels for 12%

profile of v4, /device:TPU:0, one launch (start us, length us, event | category | flops | bytes accessed | tf_op | source)
XLA Modules:
  0.0 240.0 jit_solution(6422030341252400246)
XLA Ops:
  0.0 6.4 %copy.56 = bf16[128,16384]{0,1:T(8,128)(2,1)} copy(bf16[128,16384]{1,0:T(8,128)(2,1)} %param.1) | data formatting | bytes 8388608 | tf_op args[0]
  6.4 4.3 %slice.193 = bf16[15,128,1024]{1,2,0:T(8,128)(2,1)} slice(bf16[16,128,1024]{1,2,0:T(8,128)(2,1)} %bitcast.170), slice={[1:16], [0:128], [0:1024]} | slice | bytes 7864320 | tf_op jit(solution)/shard_map/slice | solution.py:44
  10.7 4.3 %collective-permute-start = (bf16[15,128,1024]{1,2,0:T(8,128)(2,1)}, bf16[15,128,1024]{1,2,0:T(8,128)(2,1)}, u32[]{:S(2)}, u32[]{:S(2)}) collective-permute-start(bf16[15,128,1024]{1,2,0:T(8,128)(2,1)} %slice.193), channel_id=1, source_target_pairs={{0,1},{1,2},{2,3},{4,5},{5,6},{6,7},{8,9},{9,10},{10,11},{12,13},{... | collective-permute-start | bytes 11796488 | tf_op jit(solution)/shard_map/ppermute | solution.py:17
  15.0 1.1 multiply_reduce_fusion
  16.8 8.5 %negate_convert_fusion = (bf16[512,1,1024]{2,0,1:T(8,128)(2,1)S(1)}, bf16[512,1,1024]{2,0,1:T(8,128)(2,1)S(1)}) fusion(), kind=kLoop, calls=%fused_computation.68 | loop fusion | flops 8912896 | bytes 2097152 | tf_op jit(solution)/shard_map/convert.1
  25.5 2.2 copy.55
  27.7 2.3 convert_element_type.86
  30.4 25.6 %add_convert_fusion = bf16[16,128,1024]{1,2,0:T(8,128)(2,1)} fusion(bf16[16,128,1024]{1,2,0:T(8,128)(2,1)} %bitcast.171, bf16[15,128,1024]{1,2,0:T(8,128)(2,1)} %collective-permute-done, f32[1024]{0:T(1024)S(1)} %get-tuple-element.115, f32[1024]{0:T(1024)S(1)} %get-tuple-element.116, f32[1024]{0:T(1024)S(1)} %get-tuple-element.117, ...), kind=kLoop, calls=%fused_computation.28 | loop fusion | flops 132120576 | bytes 12386304 | tf_op jit(solution)/shard_map/convert_element_type | solution.py:53
  56.1 6.5 %copy.57 = bf16[16,128,1024]{2,1,0:T(8,128)(2,1)} copy(bf16[16,128,1024]{1,2,0:T(8,128)(2,1)} %add_convert_fusion) | data formatting | bytes 8388608 | tf_op jit(solution)/shard_map/convert_element_type | solution.py:53
  62.6 7.0 %convert_bitcast_fusion = bf16[128,8,16,128]{3,1,2,0:T(8,128)(2,1)S(1)} fusion(bf16[1024,1024]{1,0:T(8,128)(2,1)S(1)} %copy-done.1, bf16[2048,1024]{1,0:T(8,128)(2,1)} %bitcast.190), kind=kOutput, calls=%fused_computation.44 | convolution fusion | flops 4297064448 | bytes 10485760 | tf_op jit(solution)/shard_map/dot_general | solution.py:54
  69.6 1.4 copy.72
  71.0 2.2 fusion.25
  73.3 0.9 dynamic-slice_bitcast_fusion.24
  74.1 30.5 %collective-permute-start.1 = (bf16[16,2,16,128]{3,2,1,0:T(8,128)(2,1)}, bf16[16,2,16,128]{3,2,1,0:T(8,128)(2,1)}, u32[]{:S(2)}, u32[]{:S(2)}) collective-permute-start(bf16[16,2,16,128]{3,2,1,0:T(8,128)(2,1)} %get-tuple-element.113), channel_id=1, source_target_pairs={{0,2},{2,0},{4,6},{6,4},{8,10},{10,8},{12,14},{14,12},{1,3},{3,1},... | collective-permute-start | bytes 393224 | tf_op jit(solution)/shard_map/ppermute | solution.py:140
  104.6 1.6 collective-permute-start.2
  106.2 1.0 collective-permute-start.3
  107.2 1.6 collective-permute-start.4
  108.8 2.8 %collective-permute-start.5 = (bf16[16,2,16,128]{3,2,1,0:T(8,128)(2,1)S(1)}, bf16[16,2,16,128]{3,2,1,0:T(8,128)(2,1)S(1)}, u32[]{:S(2)}, u32[]{:S(2)}) collective-permute-start(bf16[16,2,16,128]{3,2,1,0:T(8,128)(2,1)S(1)} %get-tuple-element.109), channel_id=1, source_target_pairs={{0,10},{2,8},{4,14},{6,12},{8,2},{10,0},{12,6},{14,4},{1,11},{3,9}... | collective-permute-start | bytes 393224 | tf_op jit(solution)/shard_map/ppermute | solution.py:140
  111.8 2.3 collective-permute-start.6
  114.1 0.9 bitcast_dynamic-update-slice_fusion.30
  115.9 6.3 %collective-permute-done.4 = bf16[16,2,16,128]{3,2,1,0:T(8,128)(2,1)S(1)} collective-permute-done((bf16[16,2,16,128]{3,2,1,0:T(8,128)(2,1)}, bf16[16,2,16,128]{3,2,1,0:T(8,128)(2,1)S(1)}, u32[]{:S(2)}, u32[]{:S(2)}) %collective-permute-start.4) | collective-permute-done | bytes 131104 | tf_op jit(solution)/shard_map/ppermute | solution.py:140
  122.2 2.9 %collective-permute-done.5 = bf16[16,2,16,128]{3,2,1,0:T(8,128)(2,1)S(1)} collective-permute-done((bf16[16,2,16,128]{3,2,1,0:T(8,128)(2,1)S(1)}, bf16[16,2,16,128]{3,2,1,0:T(8,128)(2,1)S(1)}, u32[]{:S(2)}, u32[]{:S(2)}) %collective-permute-start.5) | collective-permute-done | bytes 131104 | tf_op jit(solution)/shard_map/ppermute | solution.py:140
  125.7 2.1 dynamic-slice_bitcast_fusion.16
  127.8 5.6 %collective-permute-start.10 = (bf16[16,2,16,128]{3,2,1,0:T(8,128)(2,1)S(1)}, bf16[16,2,16,128]{3,2,1,0:T(8,128)(2,1)S(1)}, u32[]{:S(2)}, u32[]{:S(2)}) collective-permute-start(bf16[16,2,16,128]{3,2,1,0:T(8,128)(2,1)S(1)} %get-tuple-element.102), channel_id=1, source_target_pairs={{0,4},{2,6},{4,8},{6,10},{8,12},{10,14},{12,0},{14,2},{1,5},{3,7},... | collective-permute-start | bytes 393224 | tf_op jit(solution)/shard_map/ppermute | solution.py:140
  134.2 1.8 collective-permute-start.12
  135.9 1.3 collective-permute-start.13
  137.3 3.8 %collective-permute-start.14 = (bf16[16,2,16,128]{3,2,1,0:T(8,128)(2,1)}, bf16[16,2,16,128]{3,2,1,0:T(8,128)(2,1)}, u32[]{:S(2)}, u32[]{:S(2)}) collective-permute-start(bf16[16,2,16,128]{3,2,1,0:T(8,128)(2,1)} %get-tuple-element.98), channel_id=1, source_target_pairs={{0,12},{2,14},{4,0},{6,2},{8,4},{10,6},{12,8},{14,10},{1,13},{3,15... | collective-permute-start | bytes 393224 | tf_op jit(solution)/shard_map/ppermute | solution.py:140
  141.1 1.5 pad_maximum_fusion.1
  144.7 2.4 copy.59
  147.1 9.9 %shard_map.17.rest_0_ = f32[64,2,256,512]{3,2,1,0:T(8,128)} custom-call(bf16[16,512,128]{2,1,0:T(8,128)(2,1)} %bitcast.189, bf16[16,128,512]{2,1,0:T(8,128)(2,1)} %bitcast.188), custom_call_target="tpu_custom_call" | custom-call | flops 1073741824 | bytes 20971520 | tf_op jit(solution)/shard_map/pallas_call | solution.py:115
  157.2 0.9 bitcast_dynamic-update-slice_fusion.22
  158.2 0.9 bitcast_dynamic-update-slice_fusion.19
  159.2 0.9 bitcast_dynamic-update-slice_fusion.18
  160.1 0.9 bitcast_dynamic-update-slice_fusion.17
  161.1 0.9 bitcast_dynamic-update-slice_fusion.16
  162.1 0.9 dynamic-slice_bitcast_fusion.8
  163.0 1.3 collective-permute-start.17
  164.3 2.3 collective-permute-start.18
  166.6 0.8 collective-permute-start.19
  167.3 1.5 collective-permute-start.20
  168.8 1.5 collective-permute-start.21
  171.1 3.9 %collective-permute-start.22 = (bf16[16,2,16,128]{3,2,1,0:T(8,128)(2,1)S(1)}, bf16[16,2,16,128]{3,2,1,0:T(8,128)(2,1)}, u32[]{:S(2)}, u32[]{:S(2)}) collective-permute-start(bf16[16,2,16,128]{3,2,1,0:T(8,128)(2,1)S(1)} %get-tuple-element.88), channel_id=1, source_target_pairs={{0,12},{2,14},{4,0},{6,2},{8,4},{10,6},{12,8},{14,10},{1,13},{3,15... | collective-permute-start | bytes 393224 | tf_op jit(solution)/shard_map/ppermute | solution.py:140
  175.0 0.9 collective-permute-start.23
  176.1 1.6 copy.63
  177.7 2.4 copy.62
  180.0 9.8 %shard_map.18.rest_0_ = f32[64,2,256,512]{3,2,1,0:T(8,128)} custom-call(bf16[16,512,128]{2,1,0:T(8,128)(2,1)} %bitcast.185, bf16[16,128,512]{2,1,0:T(8,128)(2,1)} %bitcast.183, f32[64,2,256,512]{3,2,1,0:T(8,128)} %shard_map.17.rest_0_), custom_call_target="tpu_custom_call", output_to_operand_aliasing={{}: (2, {})} | custom-call | flops 1073741824 | bytes 20971520 | tf_op jit(solution)/shard_map/pallas_call | solution.py:115
  190.2 0.9 bitcast_dynamic-update-slice_fusion.12
  191.1 0.9 bitcast_dynamic-update-slice_fusion.11
  192.1 0.9 bitcast_dynamic-update-slice_fusion.10
  193.0 0.9 bitcast_dynamic-update-slice_fusion.9
  194.0 0.9 bitcast_dynamic-update-slice_fusion.8
  195.0 0.9 dynamic-slice_bitcast_fusion
  195.9 1.1 collective-permute-start.25
  197.0 2.5 %collective-permute-start.26 = (bf16[16,2,16,128]{3,2,1,0:T(8,128)(2,1)S(1)}, bf16[16,2,16,128]{3,2,1,0:T(8,128)(2,1)S(1)}, u32[]{:S(2)}, u32[]{:S(2)}) collective-permute-start(bf16[16,2,16,128]{3,2,1,0:T(8,128)(2,1)S(1)} %get-tuple-element.82), channel_id=1, source_target_pairs={{0,4},{2,6},{4,8},{6,10},{8,12},{10,14},{12,0},{14,2},{1,5},{3,7},... | collective-permute-start | bytes 393224 | tf_op jit(solution)/shard_map/ppermute | solution.py:140
  199.6 2.1 collective-permute-start.28
  201.7 1.6 collective-permute-start.29
  204.0 3.9 %collective-permute-start.30 = (bf16[16,2,16,128]{3,2,1,0:T(8,128)(2,1)S(1)}, bf16[16,2,16,128]{3,2,1,0:T(8,128)(2,1)S(1)}, u32[]{:S(2)}, u32[]{:S(2)}) collective-permute-start(bf16[16,2,16,128]{3,2,1,0:T(8,128)(2,1)S(1)} %get-tuple-element.78), channel_id=1, source_target_pairs={{0,12},{2,14},{4,0},{6,2},{8,4},{10,6},{12,8},{14,10},{1,13},{3,15... | collective-permute-start | bytes 393224 | tf_op jit(solution)/shard_map/ppermute | solution.py:140
  208.4 1.6 copy.67
  209.9 2.4 copy.66
  212.3 9.8 %shard_map.19.rest_0_ = f32[64,2,256,512]{3,2,1,0:T(8,128)} custom-call(bf16[16,512,128]{2,1,0:T(8,128)(2,1)} %bitcast.186, bf16[16,128,512]{2,1,0:T(8,128)(2,1)} %bitcast.184, f32[64,2,256,512]{3,2,1,0:T(8,128)} %shard_map.18.rest_0_), custom_call_target="tpu_custom_call", output_to_operand_aliasing={{}: (2, {})} | custom-call | flops 1073741824 | bytes 20971520 | tf_op jit(solution)/shard_map/pallas_call | solution.py:115
  222.7 2.6 %collective-permute-done.32 = bf16[16,2,2,16,512]{4,3,2,1,0:T(8,128)(2,1)S(1)} collective-permute-done((bf16[16,2,2,16,512]{4,3,2,1,0:T(8,128)(2,1)S(1)}, bf16[16,2,2,16,512]{4,3,2,1,0:T(8,128)(2,1)S(1)}, u32[]{:S(2)}, u32[]{:S(2)}) %collective-permute-start.32) | collective-permute-done | bytes 1048608 | tf_op jit(solution)/shard_map/ppermute | solution.py:161
  225.9 1.6 copy.71
  227.8 2.4 copy.70
  230.2 9.8 %shard_map.20 = f32[64,2,256,512]{3,2,1,0:T(8,128)} custom-call(bf16[16,512,128]{2,1,0:T(8,128)(2,1)} %bitcast.187, bf16[16,128,512]{2,1,0:T(8,128)(2,1)} %bitcast.182, f32[64,2,256,512]{3,2,1,0:T(8,128)} %shard_map.19.rest_0_), custom_call_target="tpu_custom_call", output_to_operand_aliasing={{}: (2, {})} | custom-call | flops 1073741824 | bytes 20971520 | tf_op jit(solution)/shard_map/pallas_call | solution.py:115
  (113 shorter events, 9.2 us)
Async XLA Ops:
  10.7 19.7 %collective-permute-start = (bf16[15,128,1024]{1,2,0:T(8,128)(2,1)}, bf16[15,128,1024]{1,2,0:T(8,128)(2,1)}, u32[]{:S(2)}, u32[]{:S(2)}) collective-permute-start(bf16[15,128,1024]{1,2,0:T(8,128)(2,1)} %slice.193), channel_id=1, source_target_pairs={{0,1},{1,2},{2,3},{4,5},{5,6},{6,7},{8,9},{9,10},{10,11},{12,13},{... | collective-permute-start | bytes 11796488 | tf_op jit(solution)/shard_map/ppermute | solution.py:17
  56.1 6.6 %copy-start.1 = (bf16[1024,1024]{1,0:T(8,128)(2,1)S(1)}, bf16[1024,1024]{1,0:T(8,128)(2,1)}, u32[]{:S(2)}) copy-start(bf16[1024,1024]{1,0:T(8,128)(2,1)} %convert_element_type.86) | copy-start | bytes 6291460
  74.1 37.7 %collective-permute-start.1 = (bf16[16,2,16,128]{3,2,1,0:T(8,128)(2,1)}, bf16[16,2,16,128]{3,2,1,0:T(8,128)(2,1)}, u32[]{:S(2)}, u32[]{:S(2)}) collective-permute-start(bf16[16,2,16,128]{3,2,1,0:T(8,128)(2,1)} %get-tuple-element.113), channel_id=1, source_target_pairs={{0,2},{2,0},{4,6},{6,4},{8,10},{10,8},{12,14},{14,12},{1,3},{3,1},... | collective-permute-start | bytes 393224 | tf_op jit(solution)/shard_map/ppermute | solution.py:140
  104.6 10.4 %collective-permute-start.2 = (bf16[16,2,16,128]{3,2,1,0:T(8,128)(2,1)}, bf16[16,2,16,128]{3,2,1,0:T(8,128)(2,1)S(1)}, u32[]{:S(2)}, u32[]{:S(2)}) collective-permute-start(bf16[16,2,16,128]{3,2,1,0:T(8,128)(2,1)} %get-tuple-element.112), channel_id=1, source_target_pairs={{0,4},{2,6},{4,8},{6,10},{8,12},{10,14},{12,0},{14,2},{1,5},{3,7},... | collective-permute-start | bytes 393224 | tf_op jit(solution)/shard_map/ppermute | solution.py:140
  106.2 9.6 %collective-permute-start.3 = (bf16[16,2,16,128]{3,2,1,0:T(8,128)(2,1)}, bf16[16,2,16,128]{3,2,1,0:T(8,128)(2,1)S(1)}, u32[]{:S(2)}, u32[]{:S(2)}) collective-permute-start(bf16[16,2,16,128]{3,2,1,0:T(8,128)(2,1)} %get-tuple-element.111), channel_id=1, source_target_pairs={{0,6},{2,4},{4,10},{6,8},{8,14},{10,12},{12,2},{14,0},{1,7},{3,5},... | collective-permute-start | bytes 393224 | tf_op jit(solution)/shard_map/ppermute | solution.py:140
  107.2 15.0 %collective-permute-start.4 = (bf16[16,2,16,128]{3,2,1,0:T(8,128)(2,1)}, bf16[16,2,16,128]{3,2,1,0:T(8,128)(2,1)S(1)}, u32[]{:S(2)}, u32[]{:S(2)}) collective-permute-start(bf16[16,2,16,128]{3,2,1,0:T(8,128)(2,1)} %get-tuple-element.110), channel_id=1, source_target_pairs={{0,8},{2,10},{4,12},{6,14},{8,0},{10,2},{12,4},{14,6},{1,9},{3,11}... | collective-permute-start | bytes 393224 | tf_op jit(solution)/shard_map/ppermute | solution.py:140
  108.8 16.3 %collective-permute-start.5 = (bf16[16,2,16,128]{3,2,1,0:T(8,128)(2,1)S(1)}, bf16[16,2,16,128]{3,2,1,0:T(8,128)(2,1)S(1)}, u32[]{:S(2)}, u32[]{:S(2)}) collective-permute-start(bf16[16,2,16,128]{3,2,1,0:T(8,128)(2,1)S(1)} %get-tuple-element.109), channel_id=1, source_target_pairs={{0,10},{2,8},{4,14},{6,12},{8,2},{10,0},{12,6},{14,4},{1,11},{3,9}... | collective-permute-start | bytes 393224 | tf_op jit(solution)/shard_map/ppermute | solution.py:140
  111.8 13.4 %collective-permute-start.6 = (bf16[16,2,16,128]{3,2,1,0:T(8,128)(2,1)S(1)}, bf16[16,2,16,128]{3,2,1,0:T(8,128)(2,1)S(1)}, u32[]{:S(2)}, u32[]{:S(2)}) collective-permute-start(bf16[16,2,16,128]{3,2,1,0:T(8,128)(2,1)S(1)} %get-tuple-element.108), channel_id=1, source_target_pairs={{0,12},{2,14},{4,0},{6,2},{8,4},{10,6},{12,8},{14,10},{1,13},{3,15... | collective-permute-start | bytes 393224 | tf_op jit(solution)/shard_map/ppermute | solution.py:140
  115.0 10.5 %collective-permute-start.7 = (bf16[16,2,16,128]{3,2,1,0:T(8,128)(2,1)S(1)}, bf16[16,2,16,128]{3,2,1,0:T(8,128)(2,1)S(1)}, u32[]{:S(2)}, u32[]{:S(2)}) collective-permute-start(bf16[16,2,16,128]{3,2,1,0:T(8,128)(2,1)S(1)} %get-tuple-element.107), channel_id=1, source_target_pairs={{0,14},{2,12},{4,2},{6,0},{8,6},{10,4},{12,10},{14,8},{1,15},{3,13... | collective-permute-start | bytes 393224 | tf_op jit(solution)/shard_map/ppermute | solution.py:140
  125.6 11.7 %collective-permute-start.8 = (bf16[16,2,2,16,512]{4,3,2,1,0:T(8,128)(2,1)S(1)}, bf16[16,2,2,16,512]{4,3,2,1,0:T(8,128)(2,1)S(1)}, u32[]{:S(2)}, u32[]{:S(2)}) collective-permute-start(bf16[16,2,2,16,512]{4,3,2,1,0:T(8,128)(2,1)S(1)} %bitcast_dynamic-update-slice_fusion.24), channel_id=1, source_target_pairs={{0,1},{1,0},{2,3},{3,2},{4,5},{5,4},{6,7},{7,6},{8,9},{9,8},{10,11... | collective-permute-start | bytes 3145736 | tf_op jit(solution)/shard_map/ppermute | solution.py:161
  127.8 15.1 %collective-permute-start.10 = (bf16[16,2,16,128]{3,2,1,0:T(8,128)(2,1)S(1)}, bf16[16,2,16,128]{3,2,1,0:T(8,128)(2,1)S(1)}, u32[]{:S(2)}, u32[]{:S(2)}) collective-permute-start(bf16[16,2,16,128]{3,2,1,0:T(8,128)(2,1)S(1)} %get-tuple-element.102), channel_id=1, source_target_pairs={{0,4},{2,6},{4,8},{6,10},{8,12},{10,14},{12,0},{14,2},{1,5},{3,7},... | collective-permute-start | bytes 393224 | tf_op jit(solution)/shard_map/ppermute | solution.py:140
  133.5 10.3 %collective-permute-start.11 = (bf16[16,2,16,128]{3,2,1,0:T(8,128)(2,1)S(1)}, bf16[16,2,16,128]{3,2,1,0:T(8,128)(2,1)S(1)}, u32[]{:S(2)}, u32[]{:S(2)}) collective-permute-start(bf16[16,2,16,128]{3,2,1,0:T(8,128)(2,1)S(1)} %get-tuple-element.101), channel_id=1, source_target_pairs={{0,6},{2,4},{4,10},{6,8},{8,14},{10,12},{12,2},{14,0},{1,7},{3,5},... | collective-permute-start | bytes 393224 | tf_op jit(solution)/shard_map/ppermute | solution.py:140
  134.2 22.8 %collective-permute-start.12 = (bf16[16,2,16,128]{3,2,1,0:T(8,128)(2,1)}, bf16[16,2,16,128]{3,2,1,0:T(8,128)(2,1)}, u32[]{:S(2)}, u32[]{:S(2)}) collective-permute-start(bf16[16,2,16,128]{3,2,1,0:T(8,128)(2,1)} %get-tuple-element.100), channel_id=1, source_target_pairs={{0,8},{2,10},{4,12},{6,14},{8,0},{10,2},{12,4},{14,6},{1,9},{3,11}... | collective-permute-start | bytes 393224 | tf_op jit(solution)/shard_map/ppermute | solution.py:140
  135.9 21.0 %collective-permute-start.13 = (bf16[16,2,16,128]{3,2,1,0:T(8,128)(2,1)}, bf16[16,2,16,128]{3,2,1,0:T(8,128)(2,1)}, u32[]{:S(2)}, u32[]{:S(2)}) collective-permute-start(bf16[16,2,16,128]{3,2,1,0:T(8,128)(2,1)} %get-tuple-element.99), channel_id=1, source_target_pairs={{0,10},{2,8},{4,14},{6,12},{8,2},{10,0},{12,6},{14,4},{1,11},{3,9}... | collective-permute-start | bytes 393224 | tf_op jit(solution)/shard_map/ppermute | solution.py:140
  137.3 19.7 %collective-permute-start.14 = (bf16[16,2,16,128]{3,2,1,0:T(8,128)(2,1)}, bf16[16,2,16,128]{3,2,1,0:T(8,128)(2,1)}, u32[]{:S(2)}, u32[]{:S(2)}) collective-permute-start(bf16[16,2,16,128]{3,2,1,0:T(8,128)(2,1)} %get-tuple-element.98), channel_id=1, source_target_pairs={{0,12},{2,14},{4,0},{6,2},{8,4},{10,6},{12,8},{14,10},{1,13},{3,15... | collective-permute-start | bytes 393224 | tf_op jit(solution)/shard_map/ppermute | solution.py:140
  142.9 1.5 copy-start.6
  142.9 14.0 %collective-permute-start.15 = (bf16[16,2,16,128]{3,2,1,0:T(8,128)(2,1)S(1)}, bf16[16,2,16,128]{3,2,1,0:T(8,128)(2,1)}, u32[]{:S(2)}, u32[]{:S(2)}) collective-permute-start(bf16[16,2,16,128]{3,2,1,0:T(8,128)(2,1)S(1)} %get-tuple-element.97), channel_id=1, source_target_pairs={{0,14},{2,12},{4,2},{6,0},{8,6},{10,4},{12,10},{14,8},{1,15},{3,13... | collective-permute-start | bytes 393224 | tf_op jit(solution)/shard_map/ppermute | solution.py:140
  143.7 0.7 copy-start.8
  143.7 13.3 %collective-permute-start.9 = (bf16[16,2,16,128]{3,2,1,0:T(8,128)(2,1)S(1)}, bf16[16,2,16,128]{3,2,1,0:T(8,128)(2,1)}, u32[]{:S(2)}, u32[]{:S(2)}) collective-permute-start(bf16[16,2,16,128]{3,2,1,0:T(8,128)(2,1)S(1)} %get-tuple-element.103), channel_id=1, source_target_pairs={{0,2},{2,0},{4,6},{6,4},{8,10},{10,8},{12,14},{14,12},{1,3},{3,1},... | collective-permute-start | bytes 393224 | tf_op jit(solution)/shard_map/ppermute | solution.py:140
  147.1 11.1 %copy-start.7 = (bf16[16,2,16,128]{3,2,1,0:T(8,128)(2,1)S(1)}, bf16[16,2,16,128]{3,2,1,0:T(8,128)(2,1)}, u32[]{:S(2)}) copy-start(bf16[16,2,16,128]{3,2,1,0:T(8,128)(2,1)} %copy-done.6) | copy-start | bytes 393220
  147.1 11.1 %copy-start.9 = (bf16[16,2,16,128]{3,2,1,0:T(8,128)(2,1)S(1)}, bf16[16,2,16,128]{3,2,1,0:T(8,128)(2,1)}, u32[]{:S(2)}) copy-start(bf16[16,2,16,128]{3,2,1,0:T(8,128)(2,1)} %copy-done.8) | copy-start | bytes 393220
  147.1 15.0 %copy-start = (bf16[8,16,2,16,128]{4,3,2,1,0:T(8,128)(2,1)S(1)}, bf16[8,16,2,16,128]{4,3,2,1,0:T(8,128)(2,1)}, u32[]{:S(2)}) copy-start(bf16[8,16,2,16,128]{4,3,2,1,0:T(8,128)(2,1)} %get-tuple-element.50) | copy-start | bytes 3145732
  162.0 6.8 %collective-permute-start.16 = (bf16[16,2,2,16,512]{4,3,2,1,0:T(8,128)(2,1)S(1)}, bf16[16,2,2,16,512]{4,3,2,1,0:T(8,128)(2,1)S(1)}, u32[]{:S(2)}, u32[]{:S(2)}) collective-permute-start(bf16[16,2,2,16,512]{4,3,2,1,0:T(8,128)(2,1)S(1)} %bitcast_dynamic-update-slice_fusion.16), channel_id=1, source_target_pairs={{0,1},{1,0},{2,3},{3,2},{4,5},{5,4},{6,7},{7,6},{8,9},{9,8},{10,11... | collective-permute-start | bytes 3145736 | tf_op jit(solution)/shard_map/ppermute | solution.py:161
  163.0 8.1 %collective-permute-start.17 = (bf16[16,2,16,128]{3,2,1,0:T(8,128)(2,1)S(1)}, bf16[16,2,16,128]{3,2,1,0:T(8,128)(2,1)S(1)}, u32[]{:S(2)}, u32[]{:S(2)}) collective-permute-start(bf16[16,2,16,128]{3,2,1,0:T(8,128)(2,1)S(1)} %get-tuple-element.93), channel_id=1, source_target_pairs={{0,2},{2,0},{4,6},{6,4},{8,10},{10,8},{12,14},{14,12},{1,3},{3,1},... | collective-permute-start | bytes 393224 | tf_op jit(solution)/shard_map/ppermute | solution.py:140
  164.3 10.7 %collective-permute-start.18 = (bf16[16,2,16,128]{3,2,1,0:T(8,128)(2,1)S(1)}, bf16[16,2,16,128]{3,2,1,0:T(8,128)(2,1)S(1)}, u32[]{:S(2)}, u32[]{:S(2)}) collective-permute-start(bf16[16,2,16,128]{3,2,1,0:T(8,128)(2,1)S(1)} %get-tuple-element.92), channel_id=1, source_target_pairs={{0,4},{2,6},{4,8},{6,10},{8,12},{10,14},{12,0},{14,2},{1,5},{3,7},... | collective-permute-start | bytes 393224 | tf_op jit(solution)/shard_map/ppermute | solution.py:140
  166.6 23.3 %collective-permute-start.19 = (bf16[16,2,16,128]{3,2,1,0:T(8,128)(2,1)}, bf16[16,2,16,128]{3,2,1,0:T(8,128)(2,1)}, u32[]{:S(2)}, u32[]{:S(2)}) collective-permute-start(bf16[16,2,16,128]{3,2,1,0:T(8,128)(2,1)} %get-tuple-element.91), channel_id=1, source_target_pairs={{0,6},{2,4},{4,10},{6,8},{8,14},{10,12},{12,2},{14,0},{1,7},{3,5},... | collective-permute-start | bytes 393224 | tf_op jit(solution)/shard_map/ppermute | solution.py:140
  167.3 22.5 %collective-permute-start.20 = (bf16[16,2,16,128]{3,2,1,0:T(8,128)(2,1)}, bf16[16,2,16,128]{3,2,1,0:T(8,128)(2,1)}, u32[]{:S(2)}, u32[]{:S(2)}) collective-permute-start(bf16[16,2,16,128]{3,2,1,0:T(8,128)(2,1)} %get-tuple-element.90), channel_id=1, source_target_pairs={{0,8},{2,10},{4,12},{6,14},{8,0},{10,2},{12,4},{14,6},{1,9},{3,11}... | collective-permute-start | bytes 393224 | tf_op jit(solution)/shard_map/ppermute | solution.py:140
  168.8 21.0 %collective-permute-start.21 = (bf16[16,2,16,128]{3,2,1,0:T(8,128)(2,1)}, bf16[16,2,16,128]{3,2,1,0:T(8,128)(2,1)}, u32[]{:S(2)}, u32[]{:S(2)}) collective-permute-start(bf16[16,2,16,128]{3,2,1,0:T(8,128)(2,1)} %get-tuple-element.89), channel_id=1, source_target_pairs={{0,10},{2,8},{4,14},{6,12},{8,2},{10,0},{12,6},{14,4},{1,11},{3,9}... | collective-permute-start | bytes 393224 | tf_op jit(solution)/shard_map/ppermute | solution.py:140
  171.1 4.8 %copy-start.2 = (bf16[16,2,16,128]{3,2,1,0:T(8,128)(2,1)}, bf16[16,2,16,128]{3,2,1,0:T(8,128)(2,1)S(1)}, u32[]{:S(2)}) copy-start(bf16[16,2,16,128]{3,2,1,0:T(8,128)(2,1)S(1)} %collective-permute-done.17) | copy-start | bytes 393220
  171.1 18.8 %collective-permute-start.22 = (bf16[16,2,16,128]{3,2,1,0:T(8,128)(2,1)S(1)}, bf16[16,2,16,128]{3,2,1,0:T(8,128)(2,1)}, u32[]{:S(2)}, u32[]{:S(2)}) collective-permute-start(bf16[16,2,16,128]{3,2,1,0:T(8,128)(2,1)S(1)} %get-tuple-element.88), channel_id=1, source_target_pairs={{0,12},{2,14},{4,0},{6,2},{8,4},{10,6},{12,8},{14,10},{1,13},{3,15... | collective-permute-start | bytes 393224 | tf_op jit(solution)/shard_map/ppermute | solution.py:140
  175.0 0.9 copy-start.4
  175.0 14.9 %collective-permute-start.23 = (bf16[16,2,16,128]{3,2,1,0:T(8,128)(2,1)S(1)}, bf16[16,2,16,128]{3,2,1,0:T(8,128)(2,1)}, u32[]{:S(2)}, u32[]{:S(2)}) collective-permute-start(bf16[16,2,16,128]{3,2,1,0:T(8,128)(2,1)S(1)} %get-tuple-element.87), channel_id=1, source_target_pairs={{0,14},{2,12},{4,2},{6,0},{8,6},{10,4},{12,10},{14,8},{1,15},{3,13... | collective-permute-start | bytes 393224 | tf_op jit(solution)/shard_map/ppermute | solution.py:140
  180.0 10.1 %copy-start.3 = (bf16[16,2,16,128]{3,2,1,0:T(8,128)(2,1)S(1)}, bf16[16,2,16,128]{3,2,1,0:T(8,128)(2,1)}, u32[]{:S(2)}) copy-start(bf16[16,2,16,128]{3,2,1,0:T(8,128)(2,1)} %copy-done.2) | copy-start | bytes 393220
  180.0 10.1 %copy-start.5 = (bf16[16,2,16,128]{3,2,1,0:T(8,128)(2,1)S(1)}, bf16[16,2,16,128]{3,2,1,0:T(8,128)(2,1)}, u32[]{:S(2)}) copy-start(bf16[16,2,16,128]{3,2,1,0:T(8,128)(2,1)} %copy-done.4) | copy-start | bytes 393220
  194.9 6.8 %collective-permute-start.24 = (bf16[16,2,2,16,512]{4,3,2,1,0:T(8,128)(2,1)S(1)}, bf16[16,2,2,16,512]{4,3,2,1,0:T(8,128)(2,1)S(1)}, u32[]{:S(2)}, u32[]{:S(2)}) collective-permute-start(bf16[16,2,2,16,512]{4,3,2,1,0:T(8,128)(2,1)S(1)} %bitcast_dynamic-update-slice_fusion.8), channel_id=1, source_target_pairs={{0,1},{1,0},{2,3},{3,2},{4,5},{5,4},{6,7},{7,6},{8,9},{9,8},{10,11... | collective-permute-start | bytes 3145736 | tf_op jit(solution)/shard_map/ppermute | solution.py:161
  195.9 8.2 %collective-permute-start.25 = (bf16[16,2,16,128]{3,2,1,0:T(8,128)(2,1)S(1)}, bf16[16,2,16,128]{3,2,1,0:T(8,128)(2,1)S(1)}, u32[]{:S(2)}, u32[]{:S(2)}) collective-permute-start(bf16[16,2,16,128]{3,2,1,0:T(8,128)(2,1)S(1)} %get-tuple-element.83), channel_id=1, source_target_pairs={{0,2},{2,0},{4,6},{6,4},{8,10},{10,8},{12,14},{14,12},{1,3},{3,1},... | collective-permute-start | bytes 393224 | tf_op jit(solution)/shard_map/ppermute | solution.py:140
  197.0 10.9 %collective-permute-start.26 = (bf16[16,2,16,128]{3,2,1,0:T(8,128)(2,1)S(1)}, bf16[16,2,16,128]{3,2,1,0:T(8,128)(2,1)S(1)}, u32[]{:S(2)}, u32[]{:S(2)}) collective-permute-start(bf16[16,2,16,128]{3,2,1,0:T(8,128)(2,1)S(1)} %get-tuple-element.82), channel_id=1, source_target_pairs={{0,4},{2,6},{4,8},{6,10},{8,12},{10,14},{12,0},{14,2},{1,5},{3,7},... | collective-permute-start | bytes 393224 | tf_op jit(solution)/shard_map/ppermute | solution.py:140
  199.5 22.6 %collective-permute-start.27 = (bf16[16,2,16,128]{3,2,1,0:T(8,128)(2,1)}, bf16[16,2,16,128]{3,2,1,0:T(8,128)(2,1)S(1)}, u32[]{:S(2)}, u32[]{:S(2)}) collective-permute-start(bf16[16,2,16,128]{3,2,1,0:T(8,128)(2,1)} %get-tuple-element.81), channel_id=1, source_target_pairs={{0,6},{2,4},{4,10},{6,8},{8,14},{10,12},{12,2},{14,0},{1,7},{3,5},... | collective-permute-start | bytes 393224 | tf_op jit(solution)/shard_map/ppermute | solution.py:140
  199.6 22.4 %collective-permute-start.28 = (bf16[16,2,16,128]{3,2,1,0:T(8,128)(2,1)}, bf16[16,2,16,128]{3,2,1,0:T(8,128)(2,1)S(1)}, u32[]{:S(2)}, u32[]{:S(2)}) collective-permute-start(bf16[16,2,16,128]{3,2,1,0:T(8,128)(2,1)} %get-tuple-element.80), channel_id=1, source_target_pairs={{0,8},{2,10},{4,12},{6,14},{8,0},{10,2},{12,4},{14,6},{1,9},{3,11}... | collective-permute-start | bytes 393224 | tf_op jit(solution)/shard_map/ppermute | solution.py:140
  201.7 20.4 %collective-permute-start.29 = (bf16[16,2,16,128]{3,2,1,0:T(8,128)(2,1)}, bf16[16,2,16,128]{3,2,1,0:T(8,128)(2,1)S(1)}, u32[]{:S(2)}, u32[]{:S(2)}) collective-permute-start(bf16[16,2,16,128]{3,2,1,0:T(8,128)(2,1)} %get-tuple-element.79), channel_id=1, source_target_pairs={{0,10},{2,8},{4,14},{6,12},{8,2},{10,0},{12,6},{14,4},{1,11},{3,9}... | collective-permute-start | bytes 393224 | tf_op jit(solution)/shard_map/ppermute | solution.py:140
  204.0 18.1 %collective-permute-start.30 = (bf16[16,2,16,128]{3,2,1,0:T(8,128)(2,1)S(1)}, bf16[16,2,16,128]{3,2,1,0:T(8,128)(2,1)S(1)}, u32[]{:S(2)}, u32[]{:S(2)}) collective-permute-start(bf16[16,2,16,128]{3,2,1,0:T(8,128)(2,1)S(1)} %get-tuple-element.78), channel_id=1, source_target_pairs={{0,12},{2,14},{4,0},{6,2},{8,4},{10,6},{12,8},{14,10},{1,13},{3,15... | collective-permute-start | bytes 393224 | tf_op jit(solution)/shard_map/ppermute | solution.py:140
  207.9 14.2 %collective-permute-start.31 = (bf16[16,2,16,128]{3,2,1,0:T(8,128)(2,1)S(1)}, bf16[16,2,16,128]{3,2,1,0:T(8,128)(2,1)S(1)}, u32[]{:S(2)}, u32[]{:S(2)}) collective-permute-start(bf16[16,2,16,128]{3,2,1,0:T(8,128)(2,1)S(1)} %get-tuple-element.77), channel_id=1, source_target_pairs={{0,14},{2,12},{4,2},{6,0},{8,6},{10,4},{12,10},{14,8},{1,15},{3,13... | collective-permute-start | bytes 393224 | tf_op jit(solution)/shard_map/ppermute | solution.py:140
  222.6 2.7 %collective-permute-start.32 = (bf16[16,2,2,16,512]{4,3,2,1,0:T(8,128)(2,1)S(1)}, bf16[16,2,2,16,512]{4,3,2,1,0:T(8,128)(2,1)S(1)}, u32[]{:S(2)}, u32[]{:S(2)}) collective-permute-start(bf16[16,2,2,16,512]{4,3,2,1,0:T(8,128)(2,1)S(1)} %bitcast_dynamic-update-slice_fusion), channel_id=1, source_target_pairs={{0,1},{1,0},{2,3},{3,2},{4,5},{5,4},{6,7},{7,6},{8,9},{9,8},{10,11... | collective-permute-start | bytes 3145736 | tf_op jit(solution)/shard_map/ppermute | solution.py:161

commit v5 on v4

--- a/solution.py
+++ b/solution.py
@@ -42,21 +42,33 @@
     spectra_here = voltages.shape[1] // frame_len
     frames = voltages.reshape(inputs_here, spectra_here, frame_len).transpose(1, 0, 2)
     last_frames = frames[spectra_here - (TAPS - 1) :]
-    history = shifted(last_frames, ("tm", "pol"), 1)
-    extended = jnp.concatenate([history, frames], axis=0)
     filter_taps = prototype(TAPS, frame_len)
-    filtered = jnp.zeros((spectra_here, inputs_here, frame_len), jnp.float32)
-    for tap_index in range(TAPS):
-        filtered = filtered + filter_taps[tap_index] * extended[
-            tap_index : tap_index + spectra_here
-        ].astype(jnp.float32)
-    filtered = filtered.astype(jnp.bfloat16)
-    spectra = lax.dot_general(
-        dft_table_t(frame_len),
-        filtered.reshape(spectra_here * inputs_here, frame_len),
-        (((1,), (1,)), ((), ())),
-        preferred_element_type=jnp.float32,
-    )
+    table = dft_table_t(frame_len)
+    quarters = 4
+    width = frame_len // quarters
+    spectra = None
+    history = None
+    for quarter in range(quarters):
+        cut = slice(quarter * width, (quarter + 1) * width)
+        last_part = last_frames[:, :, cut]
+        if quarter:
+            history, last_part = lax.optimization_barrier((history, last_part))
+        history = shifted(last_part, ("tm", "pol"), 1)
+        extended = jnp.concatenate([history, frames[:, :, cut]], axis=0)
+        taps = filter_taps[:, cut]
+        filtered = jnp.zeros((spectra_here, inputs_here, width), jnp.float32)
+        for tap_index in range(TAPS):
+            filtered = filtered + taps[tap_index] * extended[
+                tap_index : tap_index + spectra_here
+            ].astype(jnp.float32)
+        filtered = filtered.astype(jnp.bfloat16)
+        partial = lax.dot_general(
+            table[:, cut],
+            filtered.reshape(spectra_here * inputs_here, width),
+            (((1,), (1,)), ((), ())),
+            preferred_element_type=jnp.float32,
+        )
+        spectra = partial if spectra is None else spectra + partial
     spectra = spectra.astype(jnp.bfloat16).reshape(CH, 2, spectra_here, inputs_here)
     inp_size = lax.axis_size("inp")
     tm_size = lax.axis_size("tm")

time: 242 us -> 256 us (1.058)
  starting transfers between devices: 83.6 us -> 62.7 us
  matrix products: 6.95 us -> 27.8 us
  other arithmetic: 39.9 us -> 49.2 us
  local copies, waits for them, and re-layouts: 56.6 us -> 61.7 us
    ppermute x28, starting transfers between devices: 79 us -> 50.1 us  [send_chunk(): block = lax.ppermute(block, ('inp', 'tm'), route)]
    dot_general x1 -> x4, matrix products: 6.95 us -> 27.8 us  [per_device(): lax.dot_general(table[:, cut], filtered.reshape(spectra_here * inputs_her...]
    convert_element_type x1 -> x4, other arithmetic: 25.6 us -> 34.9 us  [per_device(): filtered = filtered.astype(jnp.bfloat16)]
    ppermute x1 -> x4, starting transfers between devices: 4.29 us -> 12.3 us  [shifted(): return lax.ppermute(block, axis, route)]
    slice x2 -> x6, local copies, waits for them, and re-layouts: 4.35 us -> 8.29 us  [the longest x1 4.24 us: per_device(): last_part = last_frames[:, :, cut]]
    convert_element_type x1 -> x4, local copies, waits for them, and re-layouts: 6.55 us -> 5.31 us  [per_device(): filtered = filtered.astype(jnp.bfloat16)]
    unnamed x22 -> x28, local copies, waits for them, and re-layouts: 7.8 us -> 8.01 us
  transfers between devices with their start and end apart: 33 -> 36, of which waited for: 4 -> 5; matrix products, arithmetic and copies ran while one was open for 14% -> 35% of each run, Pallas kernels for 12% -> 12%
where the time goes in v5:
time: 256 us; the launch traced here: 254 us
  starting transfers between devices  62.7 us (24%)
  local copies, waits for them, and re-layouts  61.7 us (24%)
  other arithmetic  49.2 us (19%)
  Pallas kernels  39.2 us (15%)
  matrix products  27.8 us (11%)
  waiting for transfers between devices  11.8 us (5%)
    ppermute x28, starting transfers between devices, send_chunk(): block = lax.ppermute(block, ('inp', 'tm'), route)  50.1 us
    pallas_call x4, Pallas kernels, correlate(): pl.pallas_call(functools.partial(correlate_kernel, 1.0 / (depth // 2)), g...  39.2 us
    convert_element_type x4, other arithmetic, per_device(): filtered = filtered.astype(jnp.bfloat16)  34.9 us
    dot_general x4, matrix products, per_device(): lax.dot_general(table[:, cut], filtered.reshape(spectra_here * inputs_her...  27.8 us
    ppermute x4, starting transfers between devices, shifted(): return lax.ppermute(block, axis, route)  12.3 us
    dynamic_update_slice x32, local copies, waits for them, and re-layouts, assemble_chunk(): lax.dynamic_update_slice(half, block[:, :, None], (0, 0, tm_step, 0, sour...  11.1 us
    transpose x4, local copies, waits for them, and re-layouts, finish_chunk(): lhs = lhs.transpose(0, 1, 3, 2).reshape(own_channels, 2 * rows_here, depth)  9.73 us
    ppermute x28, waiting for transfers between devices, send_chunk(): block = lax.ppermute(block, ('inp', 'tm'), route)  9.15 us
  transfers between devices with their start and end apart: 36, of which 5 were waited for; matrix products, arithmetic and copies ran while one was open for 35% of the time, Pallas kernels for 12%

profile of v5, /device:TPU:0, one launch (start us, length us, event | category | flops | bytes accessed | tf_op | source)
XLA Modules:
  0.0 254.1 jit_solution(2730007355810145038)
XLA Ops:
  0.0 6.4 %copy.62 = bf16[128,16384]{0,1:T(8,128)(2,1)} copy(bf16[128,16384]{1,0:T(8,128)(2,1)} %param.1) | data formatting | bytes 8388608 | tf_op args[0]
  6.4 4.2 %fusion.81 = (bf16[15,128,256]{1,2,0:T(8,128)(2,1)}, bf16[15,128,256]{1,2,0:T(8,128)(2,1)}, bf16[15,128,256]{1,2,0:T(8,128)(2,1)}, bf16[15,128,256]{1,2,0:T(8,128)(2,1)}) fusion(bf16[16,128,1024]{1,2,0:T(8,128)(2,1)} %bitcast.239), kind=kLoop, calls=%fused_computation.297 | loop fusion | bytes 7864320 | tf_op jit(solution)/shard_map/slice | solution.py:53
  10.6 2.4 collective-permute-start
  13.0 1.1 fusion.78
  14.2 8.5 %negate_convert_fusion = (bf16[512,1,1024]{2,0,1:T(8,128)(2,1)S(1)}, bf16[512,1,1024]{2,0,1:T(8,128)(2,1)S(1)}) fusion(), kind=kLoop, calls=%fused_computation.141 | loop fusion | flops 8912896 | bytes 2097152 | tf_op jit(solution)/shard_map/convert.1
  24.2 3.5 %copy.61 = bf16[512,2,1024]{2,1,0:T(2,128)(2,1)} copy(bf16[512,2,1024]{2,0,1:T(8,128)(2,1)S(1)} %pad_maximum_fusion.4) | data formatting | bytes 4194304 | tf_op jit(solution)/shard_map/stack | solution.py:35
  27.7 2.7 %convert_element_type.234 = bf16[1024,1024]{1,0:T(8,128)(2,1)S(1)} reshape(bf16[512,2,1024]{2,1,0:T(2,128)(2,1)} %copy.61) | data formatting | bytes 4194304 | tf_op jit(solution)/shard_map/convert_element_type | solution.py:36
  30.5 4.0 %fusion.80 = (bf16[16,128,256]{1,2,0:T(8,128)(2,1)}, bf16[16,128,256]{1,2,0:T(8,128)(2,1)}, bf16[16,128,256]{1,2,0:T(8,128)(2,1)}, bf16[16,128,256]{1,2,0:T(8,128)(2,1)S(1)}) fusion(bf16[16,128,1024]{1,2,0:T(8,128)(2,1)} %bitcast.240), kind=kLoop, calls=%fused_computation.296 | loop fusion | bytes 8388608 | tf_op jit(solution)/shard_map/slice | solution.py:57
  34.5 5.4 %collective-permute-start.1 = (bf16[15,128,256]{1,2,0:T(8,128)(2,1)}, bf16[15,128,256]{1,2,0:T(8,128)(2,1)}, u32[]{:S(2)}, u32[]{:S(2)}) collective-permute-start(bf16[15,128,256]{1,2,0:T(8,128)(2,1)} %get-tuple-element.41), channel_id=1, source_target_pairs={{0,1},{1,2},{2,3},{4,5},{5,6},{6,7},{8,9},{9,10},{10,11},{12,13},{... | collective-permute-start | bytes 2949128 | tf_op jit(solution)/shard_map/ppermute | solution.py:17
  39.9 8.7 %add_convert_fusion.4 = bf16[16,128,256]{1,2,0:T(8,128)(2,1)S(1)} fusion(bf16[16,128,256]{1,2,0:T(8,128)(2,1)S(1)} %get-tuple-element.84, bf16[15,128,256]{1,2,0:T(8,128)(2,1)} %copy-done.4, f32[256]{0:T(256)S(1)} %bitcast.333, f32[256]{0:T(256)S(1)} %bitcast.334, f32[256]{0:T(256)S(1)} %bitcast.335, f32[256]{0:T(256)S(1)} %bitcast.336, ...), kind=kLoop, calls=%fused_computation.140 | loop fusion | flops 33030144 | bytes 3096576 | tf_op jit(solution)/shard_map/convert_element_type | solution.py:64
  48.6 1.3 copy.63
  49.9 5.9 %fusion.72 = f32[1024,2048]{1,0:T(8,128)} fusion(bf16[2048,256]{1,0:T(8,128)(2,1)} %bitcast.259, bf16[1024,1024]{1,0:T(8,128)(2,1)S(1)} %convert_element_type.234), kind=kOutput, calls=%fused_computation.223 | convolution fusion | flops 1073741824 | bytes 9961472 | tf_op jit(solution)/shard_map/dot_general | solution.py:65
  55.9 2.3 collective-permute-start.2
  58.1 8.5 %add_convert_fusion.3 = bf16[16,128,256]{1,2,0:T(8,128)(2,1)S(1)} fusion(bf16[16,128,256]{1,2,0:T(8,128)(2,1)S(1)} %copy-done.2, bf16[15,128,256]{1,2,0:T(8,128)(2,1)} %collective-permute-done.1, f32[256]{0:T(256)S(1)} %bitcast.300, f32[256]{0:T(256)S(1)} %bitcast.301, f32[256]{0:T(256)S(1)} %bitcast.302, f32[256]{0:T(256)S(1)} %bitcast.303, ...), kind=kLoop, calls=%fused_computation.139 | loop fusion | flops 33030144 | bytes 3096576 | tf_op jit(solution)/shard_map/convert_element_type | solution.py:64
  66.6 1.3 copy.64
  67.9 5.9 %fusion.70 = f32[1024,2048]{1,0:T(8,128)} fusion(bf16[2048,256]{1,0:T(8,128)(2,1)} %bitcast.260, bf16[1024,1024]{1,0:T(8,128)(2,1)S(1)} %convert_element_type.234), kind=kOutput, calls=%fused_computation.221 | convolution fusion | flops 1073741824 | bytes 9961472 | tf_op jit(solution)/shard_map/dot_general | solution.py:65
  73.8 2.2 collective-permute-start.3
  76.1 8.9 %add_convert_fusion.2 = bf16[16,128,256]{1,2,0:T(8,128)(2,1)S(1)} fusion(bf16[16,128,256]{1,2,0:T(8,128)(2,1)S(1)} %copy-done.1, bf16[15,128,256]{1,2,0:T(8,128)(2,1)} %collective-permute-done.2, f32[256]{0:T(256)S(1)} %bitcast.320, f32[256]{0:T(256)S(1)} %bitcast.321, f32[256]{0:T(256)S(1)} %bitcast.285, f32[256]{0:T(256)S(1)} %bitcast.286, ...), kind=kLoop, calls=%fused_computation.138 | loop fusion | flops 33030144 | bytes 3096576 | tf_op jit(solution)/shard_map/convert_element_type | solution.py:64
  84.9 1.3 copy.65
  86.3 6.0 %fusion.68 = f32[1024,2048]{1,0:T(8,128)} fusion(bf16[2048,256]{1,0:T(8,128)(2,1)} %bitcast.261, bf16[1024,1024]{1,0:T(8,128)(2,1)S(1)} %convert_element_type.234), kind=kOutput, calls=%fused_computation.219 | convolution fusion | flops 1073741824 | bytes 9961472 | tf_op jit(solution)/shard_map/dot_general | solution.py:65
  92.3 8.9 %add_convert_fusion.1 = bf16[16,128,256]{1,2,0:T(8,128)(2,1)S(1)} fusion(bf16[16,128,256]{1,2,0:T(8,128)(2,1)S(1)} %copy-done, bf16[15,128,256]{1,2,0:T(8,128)(2,1)} %collective-permute-done.3, f32[256]{0:T(256)S(1)} %bitcast.304, f32[256]{0:T(256)S(1)} %bitcast.305, f32[256]{0:T(256)S(1)} %bitcast.306, f32[256]{0:T(256)S(1)} %bitcast.307, ...), kind=kLoop, calls=%fused_computation.137 | loop fusion | flops 33030144 | bytes 3096576 | tf_op jit(solution)/shard_map/convert_element_type | solution.py:64
  101.2 1.3 copy.66
  102.5 10.0 %fusion = bf16[128,8,16,128]{3,1,2,0:T(8,128)(2,1)S(1)} fusion(bf16[2048,256]{1,0:T(8,128)(2,1)} %bitcast.277, f32[1024,2048]{1,0:T(8,128)} %fusion.68, f32[1024,2048]{1,0:T(8,128)} %fusion.72, f32[1024,2048]{1,0:T(8,128)} %fusion.70, bf16[1024,1024]{1,0:T(8,128)(2,1)S(1)} %convert_element_type.234), kind=kOutput, calls=%fused_computation.128 | convolution fusion | flops 1082130432 | bytes 30932992 | tf_op jit(solution)/shard_map/dot_general | solution.py:65
  112.5 1.4 copy.81
  113.9 2.2 fusion.79
  117.1 1.6 collective-permute-start.5
  118.7 3.0 %collective-permute-start.6 = (bf16[16,2,16,128]{3,2,1,0:T(8,128)(2,1)}, bf16[16,2,16,128]{3,2,1,0:T(8,128)(2,1)S(1)}, u32[]{:S(2)}, u32[]{:S(2)}) collective-permute-start(bf16[16,2,16,128]{3,2,1,0:T(8,128)(2,1)} %get-tuple-element.125), channel_id=1, source_target_pairs={{0,6},{2,4},{4,10},{6,8},{8,14},{10,12},{12,2},{14,0},{1,7},{3,5},... | collective-permute-start | bytes 393224 | tf_op jit(solution)/shard_map/ppermute | solution.py:152
  121.7 1.2 collective-permute-start.7
  122.9 1.1 collective-permute-start.8
  124.2 3.1 %collective-permute-start.9 = (bf16[16,2,16,128]{3,2,1,0:T(8,128)(2,1)S(1)}, bf16[16,2,16,128]{3,2,1,0:T(8,128)(2,1)S(1)}, u32[]{:S(2)}, u32[]{:S(2)}) collective-permute-start(bf16[16,2,16,128]{3,2,1,0:T(8,128)(2,1)S(1)} %get-tuple-element.122), channel_id=1, source_target_pairs={{0,12},{2,14},{4,0},{6,2},{8,4},{10,6},{12,8},{14,10},{1,13},{3,15... | collective-permute-start | bytes 393224 | tf_op jit(solution)/shard_map/ppermute | solution.py:152
  128.3 1.4 collective-permute-start.10
  129.9 5.6 %collective-permute-done.7 = bf16[16,2,16,128]{3,2,1,0:T(8,128)(2,1)S(1)} collective-permute-done((bf16[16,2,16,128]{3,2,1,0:T(8,128)(2,1)}, bf16[16,2,16,128]{3,2,1,0:T(8,128)(2,1)S(1)}, u32[]{:S(2)}, u32[]{:S(2)}) %collective-permute-start.7) | collective-permute-done | bytes 131104 | tf_op jit(solution)/shard_map/ppermute | solution.py:152
  135.5 3.1 %collective-permute-done.8 = bf16[16,2,16,128]{3,2,1,0:T(8,128)(2,1)S(1)} collective-permute-done((bf16[16,2,16,128]{3,2,1,0:T(8,128)(2,1)S(1)}, bf16[16,2,16,128]{3,2,1,0:T(8,128)(2,1)S(1)}, u32[]{:S(2)}, u32[]{:S(2)}) %collective-permute-start.8) | collective-permute-done | bytes 131104 | tf_op jit(solution)/shard_map/ppermute | solution.py:152
  139.1 2.2 dynamic-slice_bitcast_fusion.16
  141.2 1.3 collective-permute-start.12
  142.5 5.5 %collective-permute-start.13 = (bf16[16,2,16,128]{3,2,1,0:T(8,128)(2,1)S(1)}, bf16[16,2,16,128]{3,2,1,0:T(8,128)(2,1)S(1)}, u32[]{:S(2)}, u32[]{:S(2)}) collective-permute-start(bf16[16,2,16,128]{3,2,1,0:T(8,128)(2,1)S(1)} %get-tuple-element.116), channel_id=1, source_target_pairs={{0,4},{2,6},{4,8},{6,10},{8,12},{10,14},{12,0},{14,2},{1,5},{3,7},... | collective-permute-start | bytes 393224 | tf_op jit(solution)/shard_map/ppermute | solution.py:152
  148.4 1.7 collective-permute-start.15
  150.2 1.7 collective-permute-start.16
  151.9 1.5 pad_maximum_fusion
  153.7 3.9 %collective-permute-start.17 = (bf16[16,2,16,128]{3,2,1,0:T(8,128)(2,1)S(1)}, bf16[16,2,16,128]{3,2,1,0:T(8,128)(2,1)}, u32[]{:S(2)}, u32[]{:S(2)}) collective-permute-start(bf16[16,2,16,128]{3,2,1,0:T(8,128)(2,1)S(1)} %get-tuple-element.112), channel_id=1, source_target_pairs={{0,12},{2,14},{4,0},{6,2},{8,4},{10,6},{12,8},{14,10},{1,13},{3,15... | collective-permute-start | bytes 393224 | tf_op jit(solution)/shard_map/ppermute | solution.py:152
  158.5 2.4 copy.68
  160.9 9.8 %shard_map.17.rest_0_ = f32[64,2,256,512]{3,2,1,0:T(8,128)} custom-call(bf16[16,512,128]{2,1,0:T(8,128)(2,1)} %bitcast.258, bf16[16,128,512]{2,1,0:T(8,128)(2,1)} %bitcast.257), custom_call_target="tpu_custom_call" | custom-call | flops 1073741824 | bytes 20971520 | tf_op jit(solution)/shard_map/pallas_call | solution.py:127
  172.0 0.9 bitcast_dynamic-update-slice_fusion.19
  172.9 0.9 bitcast_dynamic-update-slice_fusion.18
  176.7 0.9 collective-permute-start.20
  177.7 3.2 %collective-permute-start.21 = (bf16[16,2,16,128]{3,2,1,0:T(8,128)(2,1)S(1)}, bf16[16,2,16,128]{3,2,1,0:T(8,128)(2,1)S(1)}, u32[]{:S(2)}, u32[]{:S(2)}) collective-permute-start(bf16[16,2,16,128]{3,2,1,0:T(8,128)(2,1)S(1)} %get-tuple-element.106), channel_id=1, source_target_pairs={{0,4},{2,6},{4,8},{6,10},{8,12},{10,14},{12,0},{14,2},{1,5},{3,7},... | collective-permute-start | bytes 393224 | tf_op jit(solution)/shard_map/ppermute | solution.py:152
  181.3 1.3 collective-permute-start.23
  182.6 2.2 collective-permute-start.24
  185.5 3.9 %collective-permute-start.25 = (bf16[16,2,16,128]{3,2,1,0:T(8,128)(2,1)S(1)}, bf16[16,2,16,128]{3,2,1,0:T(8,128)(2,1)}, u32[]{:S(2)}, u32[]{:S(2)}) collective-permute-start(bf16[16,2,16,128]{3,2,1,0:T(8,128)(2,1)S(1)} %get-tuple-element.102), channel_id=1, source_target_pairs={{0,12},{2,14},{4,0},{6,2},{8,4},{10,6},{12,8},{14,10},{1,13},{3,15... | collective-permute-start | bytes 393224 | tf_op jit(solution)/shard_map/ppermute | solution.py:152
  190.1 1.6 copy.72
  191.7 2.4 copy.71
  194.1 9.8 %shard_map.18.rest_0_ = f32[64,2,256,512]{3,2,1,0:T(8,128)} custom-call(bf16[16,512,128]{2,1,0:T(8,128)(2,1)} %bitcast.254, bf16[16,128,512]{2,1,0:T(8,128)(2,1)} %bitcast.252, f32[64,2,256,512]{3,2,1,0:T(8,128)} %shard_map.17.rest_0_), custom_call_target="tpu_custom_call", output_to_operand_aliasing={{}: (2, {})} | custom-call | flops 1073741824 | bytes 20971520 | tf_op jit(solution)/shard_map/pallas_call | solution.py:127
  209.9 1.1 collective-permute-start.28
  211.0 2.1 collective-permute-start.29
  213.5 2.3 collective-permute-start.31
  215.8 1.2 collective-permute-start.32
  217.7 3.9 %collective-permute-start.33 = (bf16[16,2,16,128]{3,2,1,0:T(8,128)(2,1)S(1)}, bf16[16,2,16,128]{3,2,1,0:T(8,128)(2,1)S(1)}, u32[]{:S(2)}, u32[]{:S(2)}) collective-permute-start(bf16[16,2,16,128]{3,2,1,0:T(8,128)(2,1)S(1)} %get-tuple-element.92), channel_id=1, source_target_pairs={{0,12},{2,14},{4,0},{6,2},{8,4},{10,6},{12,8},{14,10},{1,13},{3,15... | collective-permute-start | bytes 393224 | tf_op jit(solution)/shard_map/ppermute | solution.py:152
  222.2 1.6 copy.76
  223.8 2.4 copy.75
  226.3 9.8 %shard_map.19.rest_0_ = f32[64,2,256,512]{3,2,1,0:T(8,128)} custom-call(bf16[16,512,128]{2,1,0:T(8,128)(2,1)} %bitcast.255, bf16[16,128,512]{2,1,0:T(8,128)(2,1)} %bitcast.253, f32[64,2,256,512]{3,2,1,0:T(8,128)} %shard_map.18.rest_0_), custom_call_target="tpu_custom_call", output_to_operand_aliasing={{}: (2, {})} | custom-call | flops 1073741824 | bytes 20971520 | tf_op jit(solution)/shard_map/pallas_call | solution.py:127
  236.7 2.6 %collective-permute-done.35 = bf16[16,2,2,16,512]{4,3,2,1,0:T(8,128)(2,1)S(1)} collective-permute-done((bf16[16,2,2,16,512]{4,3,2,1,0:T(8,128)(2,1)S(1)}, bf16[16,2,2,16,512]{4,3,2,1,0:T(8,128)(2,1)S(1)}, u32[]{:S(2)}, u32[]{:S(2)}) %collective-permute-start.35) | collective-permute-done | bytes 1048608 | tf_op jit(solution)/shard_map/ppermute | solution.py:173
  239.8 1.6 copy.80
  241.9 2.4 copy.79
  244.3 9.8 %shard_map.20 = f32[64,2,256,512]{3,2,1,0:T(8,128)} custom-call(bf16[16,512,128]{2,1,0:T(8,128)(2,1)} %bitcast.256, bf16[16,128,512]{2,1,0:T(8,128)(2,1)} %bitcast.251, f32[64,2,256,512]{3,2,1,0:T(8,128)} %shard_map.19.rest_0_), custom_call_target="tpu_custom_call", output_to_operand_aliasing={{}: (2, {})} | custom-call | flops 1073741824 | bytes 20971520 | tf_op jit(solution)/shard_map/pallas_call | solution.py:127
  (138 shorter events, 19.7 us)
Async XLA Ops:
  10.6 23.9 %collective-permute-start = (bf16[15,128,256]{1,2,0:T(8,128)(2,1)}, bf16[15,128,256]{1,2,0:T(8,128)(2,1)S(1)}, u32[]{:S(2)}, u32[]{:S(2)}) collective-permute-start(bf16[15,128,256]{1,2,0:T(8,128)(2,1)} %get-tuple-element.88), channel_id=1, source_target_pairs={{0,1},{1,2},{2,3},{4,5},{5,6},{6,7},{8,9},{9,10},{10,11},{12,13},{... | collective-permute-start | bytes 2949128 | tf_op jit(solution)/shard_map/ppermute | solution.py:17
  34.5 5.4 %copy-start.4 = (bf16[15,128,256]{1,2,0:T(8,128)(2,1)}, bf16[15,128,256]{1,2,0:T(8,128)(2,1)S(1)}, u32[]{:S(2)}) copy-start(bf16[15,128,256]{1,2,0:T(8,128)(2,1)S(1)} %collective-permute-done) | copy-start | bytes 2949124
  34.5 21.3 %collective-permute-start.1 = (bf16[15,128,256]{1,2,0:T(8,128)(2,1)}, bf16[15,128,256]{1,2,0:T(8,128)(2,1)}, u32[]{:S(2)}, u32[]{:S(2)}) collective-permute-start(bf16[15,128,256]{1,2,0:T(8,128)(2,1)} %get-tuple-element.41), channel_id=1, source_target_pairs={{0,1},{1,2},{2,3},{4,5},{5,6},{6,7},{8,9},{9,10},{10,11},{12,13},{... | collective-permute-start | bytes 2949128 | tf_op jit(solution)/shard_map/ppermute | solution.py:17
  49.9 8.2 %copy-start.2 = (bf16[16,128,256]{1,2,0:T(8,128)(2,1)S(1)}, bf16[16,128,256]{1,2,0:T(8,128)(2,1)}, u32[]{:S(2)}) copy-start(bf16[16,128,256]{1,2,0:T(8,128)(2,1)} %get-tuple-element.81) | copy-start | bytes 3145732
  55.9 18.0 %collective-permute-start.2 = (bf16[15,128,256]{1,2,0:T(8,128)(2,1)}, bf16[15,128,256]{1,2,0:T(8,128)(2,1)}, u32[]{:S(2)}, u32[]{:S(2)}) collective-permute-start(bf16[15,128,256]{1,2,0:T(8,128)(2,1)} %get-tuple-element.42), channel_id=1, source_target_pairs={{0,1},{1,2},{2,3},{4,5},{5,6},{6,7},{8,9},{9,10},{10,11},{12,13},{... | collective-permute-start | bytes 2949128 | tf_op jit(solution)/shard_map/ppermute | solution.py:17
  67.9 8.2 %copy-start.1 = (bf16[16,128,256]{1,2,0:T(8,128)(2,1)S(1)}, bf16[16,128,256]{1,2,0:T(8,128)(2,1)}, u32[]{:S(2)}) copy-start(bf16[16,128,256]{1,2,0:T(8,128)(2,1)} %get-tuple-element.83) | copy-start | bytes 3145732
  73.8 18.4 %collective-permute-start.3 = (bf16[15,128,256]{1,2,0:T(8,128)(2,1)}, bf16[15,128,256]{1,2,0:T(8,128)(2,1)}, u32[]{:S(2)}, u32[]{:S(2)}) collective-permute-start(bf16[15,128,256]{1,2,0:T(8,128)(2,1)} %get-tuple-element.43), channel_id=1, source_target_pairs={{0,1},{1,2},{2,3},{4,5},{5,6},{6,7},{8,9},{9,10},{10,11},{12,13},{... | collective-permute-start | bytes 2949128 | tf_op jit(solution)/shard_map/ppermute | solution.py:17
  86.3 6.0 %copy-start = (bf16[16,128,256]{1,2,0:T(8,128)(2,1)S(1)}, bf16[16,128,256]{1,2,0:T(8,128)(2,1)}, u32[]{:S(2)}) copy-start(bf16[16,128,256]{1,2,0:T(8,128)(2,1)} %get-tuple-element.82) | copy-start | bytes 3145732
  117.1 7.2 %collective-permute-start.4 = (bf16[16,2,16,128]{3,2,1,0:T(8,128)(2,1)}, bf16[16,2,16,128]{3,2,1,0:T(8,128)(2,1)}, u32[]{:S(2)}, u32[]{:S(2)}) collective-permute-start(bf16[16,2,16,128]{3,2,1,0:T(8,128)(2,1)} %get-tuple-element.127), channel_id=1, source_target_pairs={{0,2},{2,0},{4,6},{6,4},{8,10},{10,8},{12,14},{14,12},{1,3},{3,1},... | collective-permute-start | bytes 393224 | tf_op jit(solution)/shard_map/ppermute | solution.py:152
  117.1 11.2 %collective-permute-start.5 = (bf16[16,2,16,128]{3,2,1,0:T(8,128)(2,1)}, bf16[16,2,16,128]{3,2,1,0:T(8,128)(2,1)S(1)}, u32[]{:S(2)}, u32[]{:S(2)}) collective-permute-start(bf16[16,2,16,128]{3,2,1,0:T(8,128)(2,1)} %get-tuple-element.126), channel_id=1, source_target_pairs={{0,4},{2,6},{4,8},{6,10},{8,12},{10,14},{12,0},{14,2},{1,5},{3,7},... | collective-permute-start | bytes 393224 | tf_op jit(solution)/shard_map/ppermute | solution.py:152
  118.7 11.2 %collective-permute-start.6 = (bf16[16,2,16,128]{3,2,1,0:T(8,128)(2,1)}, bf16[16,2,16,128]{3,2,1,0:T(8,128)(2,1)S(1)}, u32[]{:S(2)}, u32[]{:S(2)}) collective-permute-start(bf16[16,2,16,128]{3,2,1,0:T(8,128)(2,1)} %get-tuple-element.125), channel_id=1, source_target_pairs={{0,6},{2,4},{4,10},{6,8},{8,14},{10,12},{12,2},{14,0},{1,7},{3,5},... | collective-permute-start | bytes 393224 | tf_op jit(solution)/shard_map/ppermute | solution.py:152
  121.7 13.8 %collective-permute-start.7 = (bf16[16,2,16,128]{3,2,1,0:T(8,128)(2,1)}, bf16[16,2,16,128]{3,2,1,0:T(8,128)(2,1)S(1)}, u32[]{:S(2)}, u32[]{:S(2)}) collective-permute-start(bf16[16,2,16,128]{3,2,1,0:T(8,128)(2,1)} %get-tuple-element.124), channel_id=1, source_target_pairs={{0,8},{2,10},{4,12},{6,14},{8,0},{10,2},{12,4},{14,6},{1,9},{3,11}... | collective-permute-start | bytes 393224 | tf_op jit(solution)/shard_map/ppermute | solution.py:152
  122.9 15.7 %collective-permute-start.8 = (bf16[16,2,16,128]{3,2,1,0:T(8,128)(2,1)S(1)}, bf16[16,2,16,128]{3,2,1,0:T(8,128)(2,1)S(1)}, u32[]{:S(2)}, u32[]{:S(2)}) collective-permute-start(bf16[16,2,16,128]{3,2,1,0:T(8,128)(2,1)S(1)} %get-tuple-element.123), channel_id=1, source_target_pairs={{0,10},{2,8},{4,14},{6,12},{8,2},{10,0},{12,6},{14,4},{1,11},{3,9}... | collective-permute-start | bytes 393224 | tf_op jit(solution)/shard_map/ppermute | solution.py:152
  124.2 14.4 %collective-permute-start.9 = (bf16[16,2,16,128]{3,2,1,0:T(8,128)(2,1)S(1)}, bf16[16,2,16,128]{3,2,1,0:T(8,128)(2,1)S(1)}, u32[]{:S(2)}, u32[]{:S(2)}) collective-permute-start(bf16[16,2,16,128]{3,2,1,0:T(8,128)(2,1)S(1)} %get-tuple-element.122), channel_id=1, source_target_pairs={{0,12},{2,14},{4,0},{6,2},{8,4},{10,6},{12,8},{14,10},{1,13},{3,15... | collective-permute-start | bytes 393224 | tf_op jit(solution)/shard_map/ppermute | solution.py:152
  128.3 10.6 %collective-permute-start.10 = (bf16[16,2,16,128]{3,2,1,0:T(8,128)(2,1)S(1)}, bf16[16,2,16,128]{3,2,1,0:T(8,128)(2,1)S(1)}, u32[]{:S(2)}, u32[]{:S(2)}) collective-permute-start(bf16[16,2,16,128]{3,2,1,0:T(8,128)(2,1)S(1)} %get-tuple-element.121), channel_id=1, source_target_pairs={{0,14},{2,12},{4,2},{6,0},{8,6},{10,4},{12,10},{14,8},{1,15},{3,13... | collective-permute-start | bytes 393224 | tf_op jit(solution)/shard_map/ppermute | solution.py:152
  139.0 11.2 %collective-permute-start.11 = (bf16[16,2,2,16,512]{4,3,2,1,0:T(8,128)(2,1)S(1)}, bf16[16,2,2,16,512]{4,3,2,1,0:T(8,128)(2,1)S(1)}, u32[]{:S(2)}, u32[]{:S(2)}) collective-permute-start(bf16[16,2,2,16,512]{4,3,2,1,0:T(8,128)(2,1)S(1)} %bitcast_dynamic-update-slice_fusion.24), channel_id=1, source_target_pairs={{0,1},{1,0},{2,3},{3,2},{4,5},{5,4},{6,7},{7,6},{8,9},{9,8},{10,11... | collective-permute-start | bytes 3145736 | tf_op jit(solution)/shard_map/ppermute | solution.py:173
  141.2 12.5 %collective-permute-start.12 = (bf16[16,2,16,128]{3,2,1,0:T(8,128)(2,1)S(1)}, bf16[16,2,16,128]{3,2,1,0:T(8,128)(2,1)S(1)}, u32[]{:S(2)}, u32[]{:S(2)}) collective-permute-start(bf16[16,2,16,128]{3,2,1,0:T(8,128)(2,1)S(1)} %get-tuple-element.117), channel_id=1, source_target_pairs={{0,2},{2,0},{4,6},{6,4},{8,10},{10,8},{12,14},{14,12},{1,3},{3,1},... | collective-permute-start | bytes 393224 | tf_op jit(solution)/shard_map/ppermute | solution.py:152
  142.5 15.1 %collective-permute-start.13 = (bf16[16,2,16,128]{3,2,1,0:T(8,128)(2,1)S(1)}, bf16[16,2,16,128]{3,2,1,0:T(8,128)(2,1)S(1)}, u32[]{:S(2)}, u32[]{:S(2)}) collective-permute-start(bf16[16,2,16,128]{3,2,1,0:T(8,128)(2,1)S(1)} %get-tuple-element.116), channel_id=1, source_target_pairs={{0,4},{2,6},{4,8},{6,10},{8,12},{10,14},{12,0},{14,2},{1,5},{3,7},... | collective-permute-start | bytes 393224 | tf_op jit(solution)/shard_map/ppermute | solution.py:152
  148.0 22.7 %collective-permute-start.14 = (bf16[16,2,16,128]{3,2,1,0:T(8,128)(2,1)}, bf16[16,2,16,128]{3,2,1,0:T(8,128)(2,1)}, u32[]{:S(2)}, u32[]{:S(2)}) collective-permute-start(bf16[16,2,16,128]{3,2,1,0:T(8,128)(2,1)} %get-tuple-element.115), channel_id=1, source_target_pairs={{0,6},{2,4},{4,10},{6,8},{8,14},{10,12},{12,2},{14,0},{1,7},{3,5},... | collective-permute-start | bytes 393224 | tf_op jit(solution)/shard_map/ppermute | solution.py:152
  148.4 22.3 %collective-permute-start.15 = (bf16[16,2,16,128]{3,2,1,0:T(8,128)(2,1)}, bf16[16,2,16,128]{3,2,1,0:T(8,128)(2,1)}, u32[]{:S(2)}, u32[]{:S(2)}) collective-permute-start(bf16[16,2,16,128]{3,2,1,0:T(8,128)(2,1)} %get-tuple-element.114), channel_id=1, source_target_pairs={{0,8},{2,10},{4,12},{6,14},{8,0},{10,2},{12,4},{14,6},{1,9},{3,11}... | collective-permute-start | bytes 393224 | tf_op jit(solution)/shard_map/ppermute | solution.py:152
  150.2 20.6 %collective-permute-start.16 = (bf16[16,2,16,128]{3,2,1,0:T(8,128)(2,1)}, bf16[16,2,16,128]{3,2,1,0:T(8,128)(2,1)}, u32[]{:S(2)}, u32[]{:S(2)}) collective-permute-start(bf16[16,2,16,128]{3,2,1,0:T(8,128)(2,1)} %get-tuple-element.113), channel_id=1, source_target_pairs={{0,10},{2,8},{4,14},{6,12},{8,2},{10,0},{12,6},{14,4},{1,11},{3,9}... | collective-permute-start | bytes 393224 | tf_op jit(solution)/shard_map/ppermute | solution.py:152
  153.7 4.3 %copy-start.9 = (bf16[16,2,16,128]{3,2,1,0:T(8,128)(2,1)}, bf16[16,2,16,128]{3,2,1,0:T(8,128)(2,1)S(1)}, u32[]{:S(2)}) copy-start(bf16[16,2,16,128]{3,2,1,0:T(8,128)(2,1)S(1)} %collective-permute-done.12) | copy-start | bytes 393220
  153.7 17.0 %collective-permute-start.17 = (bf16[16,2,16,128]{3,2,1,0:T(8,128)(2,1)S(1)}, bf16[16,2,16,128]{3,2,1,0:T(8,128)(2,1)}, u32[]{:S(2)}, u32[]{:S(2)}) collective-permute-start(bf16[16,2,16,128]{3,2,1,0:T(8,128)(2,1)S(1)} %get-tuple-element.112), channel_id=1, source_target_pairs={{0,12},{2,14},{4,0},{6,2},{8,4},{10,6},{12,8},{14,10},{1,13},{3,15... | collective-permute-start | bytes 393224 | tf_op jit(solution)/shard_map/ppermute | solution.py:152
  157.6 0.6 copy-start.11
  157.6 13.1 %collective-permute-start.18 = (bf16[16,2,16,128]{3,2,1,0:T(8,128)(2,1)S(1)}, bf16[16,2,16,128]{3,2,1,0:T(8,128)(2,1)}, u32[]{:S(2)}, u32[]{:S(2)}) collective-permute-start(bf16[16,2,16,128]{3,2,1,0:T(8,128)(2,1)S(1)} %get-tuple-element.111), channel_id=1, source_target_pairs={{0,14},{2,12},{4,2},{6,0},{8,6},{10,4},{12,10},{14,8},{1,15},{3,13... | collective-permute-start | bytes 393224 | tf_op jit(solution)/shard_map/ppermute | solution.py:152
  160.9 10.0 %copy-start.10 = (bf16[16,2,16,128]{3,2,1,0:T(8,128)(2,1)S(1)}, bf16[16,2,16,128]{3,2,1,0:T(8,128)(2,1)}, u32[]{:S(2)}) copy-start(bf16[16,2,16,128]{3,2,1,0:T(8,128)(2,1)} %copy-done.9) | copy-start | bytes 393220
  160.9 10.1 %copy-start.12 = (bf16[16,2,16,128]{3,2,1,0:T(8,128)(2,1)S(1)}, bf16[16,2,16,128]{3,2,1,0:T(8,128)(2,1)}, u32[]{:S(2)}) copy-start(bf16[16,2,16,128]{3,2,1,0:T(8,128)(2,1)} %copy-done.11) | copy-start | bytes 393220
  170.7 5.1 %copy-start.3 = (bf16[8,16,2,16,128]{4,3,2,1,0:T(8,128)(2,1)S(1)}, bf16[8,16,2,16,128]{4,3,2,1,0:T(8,128)(2,1)}, u32[]{:S(2)}) copy-start(bf16[8,16,2,16,128]{4,3,2,1,0:T(8,128)(2,1)} %get-tuple-element.56) | copy-start | bytes 3145732
  175.8 6.8 %collective-permute-start.19 = (bf16[16,2,2,16,512]{4,3,2,1,0:T(8,128)(2,1)S(1)}, bf16[16,2,2,16,512]{4,3,2,1,0:T(8,128)(2,1)S(1)}, u32[]{:S(2)}, u32[]{:S(2)}) collective-permute-start(bf16[16,2,2,16,512]{4,3,2,1,0:T(8,128)(2,1)S(1)} %bitcast_dynamic-update-slice_fusion.16), channel_id=1, source_target_pairs={{0,1},{1,0},{2,3},{3,2},{4,5},{5,4},{6,7},{7,6},{8,9},{9,8},{10,11... | collective-permute-start | bytes 3145736 | tf_op jit(solution)/shard_map/ppermute | solution.py:173
  176.7 8.7 %collective-permute-start.20 = (bf16[16,2,16,128]{3,2,1,0:T(8,128)(2,1)S(1)}, bf16[16,2,16,128]{3,2,1,0:T(8,128)(2,1)S(1)}, u32[]{:S(2)}, u32[]{:S(2)}) collective-permute-start(bf16[16,2,16,128]{3,2,1,0:T(8,128)(2,1)S(1)} %get-tuple-element.107), channel_id=1, source_target_pairs={{0,2},{2,0},{4,6},{6,4},{8,10},{10,8},{12,14},{14,12},{1,3},{3,1},... | collective-permute-start | bytes 393224 | tf_op jit(solution)/shard_map/ppermute | solution.py:152
  177.7 11.7 %collective-permute-start.21 = (bf16[16,2,16,128]{3,2,1,0:T(8,128)(2,1)S(1)}, bf16[16,2,16,128]{3,2,1,0:T(8,128)(2,1)S(1)}, u32[]{:S(2)}, u32[]{:S(2)}) collective-permute-start(bf16[16,2,16,128]{3,2,1,0:T(8,128)(2,1)S(1)} %get-tuple-element.106), channel_id=1, source_target_pairs={{0,4},{2,6},{4,8},{6,10},{8,12},{10,14},{12,0},{14,2},{1,5},{3,7},... | collective-permute-start | bytes 393224 | tf_op jit(solution)/shard_map/ppermute | solution.py:152
  180.9 23.0 %collective-permute-start.22 = (bf16[16,2,16,128]{3,2,1,0:T(8,128)(2,1)}, bf16[16,2,16,128]{3,2,1,0:T(8,128)(2,1)}, u32[]{:S(2)}, u32[]{:S(2)}) collective-permute-start(bf16[16,2,16,128]{3,2,1,0:T(8,128)(2,1)} %get-tuple-element.105), channel_id=1, source_target_pairs={{0,6},{2,4},{4,10},{6,8},{8,14},{10,12},{12,2},{14,0},{1,7},{3,5},... | collective-permute-start | bytes 393224 | tf_op jit(solution)/shard_map/ppermute | solution.py:152
  181.3 22.7 %collective-permute-start.23 = (bf16[16,2,16,128]{3,2,1,0:T(8,128)(2,1)}, bf16[16,2,16,128]{3,2,1,0:T(8,128)(2,1)}, u32[]{:S(2)}, u32[]{:S(2)}) collective-permute-start(bf16[16,2,16,128]{3,2,1,0:T(8,128)(2,1)} %get-tuple-element.104), channel_id=1, source_target_pairs={{0,8},{2,10},{4,12},{6,14},{8,0},{10,2},{12,4},{14,6},{1,9},{3,11}... | collective-permute-start | bytes 393224 | tf_op jit(solution)/shard_map/ppermute | solution.py:152
  182.6 21.3 %collective-permute-start.24 = (bf16[16,2,16,128]{3,2,1,0:T(8,128)(2,1)}, bf16[16,2,16,128]{3,2,1,0:T(8,128)(2,1)}, u32[]{:S(2)}, u32[]{:S(2)}) collective-permute-start(bf16[16,2,16,128]{3,2,1,0:T(8,128)(2,1)} %get-tuple-element.103), channel_id=1, source_target_pairs={{0,10},{2,8},{4,14},{6,12},{8,2},{10,0},{12,6},{14,4},{1,11},{3,9}... | collective-permute-start | bytes 393224 | tf_op jit(solution)/shard_map/ppermute | solution.py:152
  185.5 4.5 %copy-start.5 = (bf16[16,2,16,128]{3,2,1,0:T(8,128)(2,1)}, bf16[16,2,16,128]{3,2,1,0:T(8,128)(2,1)S(1)}, u32[]{:S(2)}) copy-start(bf16[16,2,16,128]{3,2,1,0:T(8,128)(2,1)S(1)} %collective-permute-done.20) | copy-start | bytes 393220
  185.5 18.4 %collective-permute-start.25 = (bf16[16,2,16,128]{3,2,1,0:T(8,128)(2,1)S(1)}, bf16[16,2,16,128]{3,2,1,0:T(8,128)(2,1)}, u32[]{:S(2)}, u32[]{:S(2)}) collective-permute-start(bf16[16,2,16,128]{3,2,1,0:T(8,128)(2,1)S(1)} %get-tuple-element.102), channel_id=1, source_target_pairs={{0,12},{2,14},{4,0},{6,2},{8,4},{10,6},{12,8},{14,10},{1,13},{3,15... | collective-permute-start | bytes 393224 | tf_op jit(solution)/shard_map/ppermute | solution.py:152
  189.4 0.7 copy-start.7
  189.4 14.6 %collective-permute-start.26 = (bf16[16,2,16,128]{3,2,1,0:T(8,128)(2,1)S(1)}, bf16[16,2,16,128]{3,2,1,0:T(8,128)(2,1)}, u32[]{:S(2)}, u32[]{:S(2)}) collective-permute-start(bf16[16,2,16,128]{3,2,1,0:T(8,128)(2,1)S(1)} %get-tuple-element.101), channel_id=1, source_target_pairs={{0,14},{2,12},{4,2},{6,0},{8,6},{10,4},{12,10},{14,8},{1,15},{3,13... | collective-permute-start | bytes 393224 | tf_op jit(solution)/shard_map/ppermute | solution.py:152
  194.1 10.1 %copy-start.6 = (bf16[16,2,16,128]{3,2,1,0:T(8,128)(2,1)S(1)}, bf16[16,2,16,128]{3,2,1,0:T(8,128)(2,1)}, u32[]{:S(2)}) copy-start(bf16[16,2,16,128]{3,2,1,0:T(8,128)(2,1)} %copy-done.5) | copy-start | bytes 393220
  194.1 10.1 %copy-start.8 = (bf16[16,2,16,128]{3,2,1,0:T(8,128)(2,1)S(1)}, bf16[16,2,16,128]{3,2,1,0:T(8,128)(2,1)}, u32[]{:S(2)}) copy-start(bf16[16,2,16,128]{3,2,1,0:T(8,128)(2,1)} %copy-done.7) | copy-start | bytes 393220
  209.0 6.8 %collective-permute-start.27 = (bf16[16,2,2,16,512]{4,3,2,1,0:T(8,128)(2,1)S(1)}, bf16[16,2,2,16,512]{4,3,2,1,0:T(8,128)(2,1)S(1)}, u32[]{:S(2)}, u32[]{:S(2)}) collective-permute-start(bf16[16,2,2,16,512]{4,3,2,1,0:T(8,128)(2,1)S(1)} %bitcast_dynamic-update-slice_fusion.8), channel_id=1, source_target_pairs={{0,1},{1,0},{2,3},{3,2},{4,5},{5,4},{6,7},{7,6},{8,9},{9,8},{10,11... | collective-permute-start | bytes 3145736 | tf_op jit(solution)/shard_map/ppermute | solution.py:173
  209.9 7.8 %collective-permute-start.28 = (bf16[16,2,16,128]{3,2,1,0:T(8,128)(2,1)S(1)}, bf16[16,2,16,128]{3,2,1,0:T(8,128)(2,1)S(1)}, u32[]{:S(2)}, u32[]{:S(2)}) collective-permute-start(bf16[16,2,16,128]{3,2,1,0:T(8,128)(2,1)S(1)} %get-tuple-element.97), channel_id=1, source_target_pairs={{0,2},{2,0},{4,6},{6,4},{8,10},{10,8},{12,14},{14,12},{1,3},{3,1},... | collective-permute-start | bytes 393224 | tf_op jit(solution)/shard_map/ppermute | solution.py:152
  211.0 10.6 %collective-permute-start.29 = (bf16[16,2,16,128]{3,2,1,0:T(8,128)(2,1)S(1)}, bf16[16,2,16,128]{3,2,1,0:T(8,128)(2,1)S(1)}, u32[]{:S(2)}, u32[]{:S(2)}) collective-permute-start(bf16[16,2,16,128]{3,2,1,0:T(8,128)(2,1)S(1)} %get-tuple-element.96), channel_id=1, source_target_pairs={{0,4},{2,6},{4,8},{6,10},{8,12},{10,14},{12,0},{14,2},{1,5},{3,7},... | collective-permute-start | bytes 393224 | tf_op jit(solution)/shard_map/ppermute | solution.py:152
  213.2 22.9 %collective-permute-start.30 = (bf16[16,2,16,128]{3,2,1,0:T(8,128)(2,1)}, bf16[16,2,16,128]{3,2,1,0:T(8,128)(2,1)S(1)}, u32[]{:S(2)}, u32[]{:S(2)}) collective-permute-start(bf16[16,2,16,128]{3,2,1,0:T(8,128)(2,1)} %get-tuple-element.95), channel_id=1, source_target_pairs={{0,6},{2,4},{4,10},{6,8},{8,14},{10,12},{12,2},{14,0},{1,7},{3,5},... | collective-permute-start | bytes 393224 | tf_op jit(solution)/shard_map/ppermute | solution.py:152
  213.5 22.5 %collective-permute-start.31 = (bf16[16,2,16,128]{3,2,1,0:T(8,128)(2,1)}, bf16[16,2,16,128]{3,2,1,0:T(8,128)(2,1)S(1)}, u32[]{:S(2)}, u32[]{:S(2)}) collective-permute-start(bf16[16,2,16,128]{3,2,1,0:T(8,128)(2,1)} %get-tuple-element.94), channel_id=1, source_target_pairs={{0,8},{2,10},{4,12},{6,14},{8,0},{10,2},{12,4},{14,6},{1,9},{3,11}... | collective-permute-start | bytes 393224 | tf_op jit(solution)/shard_map/ppermute | solution.py:152
  215.8 20.3 %collective-permute-start.32 = (bf16[16,2,16,128]{3,2,1,0:T(8,128)(2,1)}, bf16[16,2,16,128]{3,2,1,0:T(8,128)(2,1)S(1)}, u32[]{:S(2)}, u32[]{:S(2)}) collective-permute-start(bf16[16,2,16,128]{3,2,1,0:T(8,128)(2,1)} %get-tuple-element.93), channel_id=1, source_target_pairs={{0,10},{2,8},{4,14},{6,12},{8,2},{10,0},{12,6},{14,4},{1,11},{3,9}... | collective-permute-start | bytes 393224 | tf_op jit(solution)/shard_map/ppermute | solution.py:152
  217.7 18.4 %collective-permute-start.33 = (bf16[16,2,16,128]{3,2,1,0:T(8,128)(2,1)S(1)}, bf16[16,2,16,128]{3,2,1,0:T(8,128)(2,1)S(1)}, u32[]{:S(2)}, u32[]{:S(2)}) collective-permute-start(bf16[16,2,16,128]{3,2,1,0:T(8,128)(2,1)S(1)} %get-tuple-element.92), channel_id=1, source_target_pairs={{0,12},{2,14},{4,0},{6,2},{8,4},{10,6},{12,8},{14,10},{1,13},{3,15... | collective-permute-start | bytes 393224 | tf_op jit(solution)/shard_map/ppermute | solution.py:152
  221.6 14.5 %collective-permute-start.34 = (bf16[16,2,16,128]{3,2,1,0:T(8,128)(2,1)S(1)}, bf16[16,2,16,128]{3,2,1,0:T(8,128)(2,1)S(1)}, u32[]{:S(2)}, u32[]{:S(2)}) collective-permute-start(bf16[16,2,16,128]{3,2,1,0:T(8,128)(2,1)S(1)} %get-tuple-element.91), channel_id=1, source_target_pairs={{0,14},{2,12},{4,2},{6,0},{8,6},{10,4},{12,10},{14,8},{1,15},{3,13... | collective-permute-start | bytes 393224 | tf_op jit(solution)/shard_map/ppermute | solution.py:152
  236.6 2.7 %collective-permute-start.35 = (bf16[16,2,2,16,512]{4,3,2,1,0:T(8,128)(2,1)S(1)}, bf16[16,2,2,16,512]{4,3,2,1,0:T(8,128)(2,1)S(1)}, u32[]{:S(2)}, u32[]{:S(2)}) collective-permute-start(bf16[16,2,2,16,512]{4,3,2,1,0:T(8,128)(2,1)S(1)} %bitcast_dynamic-update-slice_fusion), channel_id=1, source_target_pairs={{0,1},{1,0},{2,3},{3,2},{4,5},{5,4},{6,7},{7,6},{8,9},{9,8},{10,11... | collective-permute-start | bytes 3145736 | tf_op jit(solution)/shard_map/ppermute | solution.py:173

commit v6 on v5

--- a/solution.py
+++ b/solution.py
@@ -46,8 +46,8 @@
     table = dft_table_t(frame_len)
     quarters = 4
     width = frame_len // quarters
-    spectra = None
     history = None
+    filtered_all = jnp.zeros((spectra_here, inputs_here, frame_len), jnp.bfloat16)
     for quarter in range(quarters):
         cut = slice(quarter * width, (quarter + 1) * width)
         last_part = last_frames[:, :, cut]
@@ -61,14 +61,15 @@
             filtered = filtered + taps[tap_index] * extended[
                 tap_index : tap_index + spectra_here
             ].astype(jnp.float32)
-        filtered = filtered.astype(jnp.bfloat16)
-        partial = lax.dot_general(
-            table[:, cut],
-            filtered.reshape(spectra_here * inputs_here, width),
-            (((1,), (1,)), ((), ())),
-            preferred_element_type=jnp.float32,
+        filtered_all = lax.dynamic_update_slice(
+            filtered_all, filtered.astype(jnp.bfloat16), (0, 0, quarter * width)
         )
-        spectra = partial if spectra is None else spectra + partial
+    spectra = lax.dot_general(
+        table,
+        filtered_all.reshape(spectra_here * inputs_here, frame_len),
+        (((1,), (1,)), ((), ())),
+        preferred_element_type=jnp.float32,
+    )
     spectra = spectra.astype(jnp.bfloat16).reshape(CH, 2, spectra_here, inputs_here)
     inp_size = lax.axis_size("inp")
     tm_size = lax.axis_size("tm")

time: 256 us -> 242 us (0.945)
  matrix products: 27.8 us -> 6.95 us
  starting transfers between devices: 62.7 us -> 77.7 us
  other arithmetic: 49.2 us -> 39.1 us
    convert_element_type x4 -> x1, other arithmetic: 34.9 us -> 8.41 us  [per_device(): filtered.astype(jnp.bfloat16)]
    dot_general x4 -> x1, matrix products: 27.8 us -> 6.95 us  [per_device(): lax.dot_general(table, filtered_all.reshape(spectra_here * inputs_here, f...]
    dynamic_update_slice x0 -> x3, other arithmetic: none -> 16.4 us  [per_device(): lax.dynamic_update_slice(filtered_all, filtered.astype(jnp.bfloat16), (0,...]
    dynamic_update_slice x0 -> x2, local copies, waits for them, and re-layouts: none -> 9.29 us  [per_device(): lax.dynamic_update_slice(filtered_all, filtered.astype(jnp.bfloat16), (0,...]
    ppermute x28, starting transfers between devices: 50.1 us -> 58.6 us  [send_chunk(): block = lax.ppermute(block, ('inp', 'tm'), route)]
    ppermute x4, starting transfers between devices: 12.3 us -> 18.8 us  [shifted(): return lax.ppermute(block, axis, route)]
    convert_element_type x4 -> x0, local copies, waits for them, and re-layouts: 5.31 us -> none  [per_device(): filtered = filtered.astype(jnp.bfloat16)]
    unnamed x28 -> x26, local copies, waits for them, and re-layouts: 8.01 us -> 8.43 us
  transfers between devices with their start and end apart: 36 -> 36, of which waited for: 5 -> 4; matrix products, arithmetic and copies ran while one was open for 35% -> 24% of each run, Pallas kernels for 12% -> 12%
where the time goes in v6:
time: 242 us; the launch traced here: 240 us
  starting transfers between devices  77.7 us (32%)
  local copies, waits for them, and re-layouts  63.4 us (26%)
  Pallas kernels  39.2 us (16%)
  other arithmetic  39.1 us (16%)
  waiting for transfers between devices  12.3 us (5%)
  matrix products  6.95 us (3%)
    ppermute x28, starting transfers between devices, send_chunk(): block = lax.ppermute(block, ('inp', 'tm'), route)  58.6 us
    pallas_call x4, Pallas kernels, correlate(): pl.pallas_call(functools.partial(correlate_kernel, 1.0 / (depth // 2)), g...  39.2 us
    ppermute x4, starting transfers between devices, shifted(): return lax.ppermute(block, axis, route)  18.8 us
    dynamic_update_slice x3, other arithmetic, per_device(): lax.dynamic_update_slice(filtered_all, filtered.astype(jnp.bfloat16), (0,...  16.4 us
    dynamic_update_slice x32, local copies, waits for them, and re-layouts, assemble_chunk(): lax.dynamic_update_slice(half, block[:, :, None], (0, 0, tm_step, 0, sour...  12.9 us
    transpose x4, local copies, waits for them, and re-layouts, finish_chunk(): lhs = lhs.transpose(0, 1, 3, 2).reshape(own_channels, 2 * rows_here, depth)  9.66 us
    ppermute x28, waiting for transfers between devices, send_chunk(): block = lax.ppermute(block, ('inp', 'tm'), route)  9.6 us
    dynamic_update_slice x2, local copies, waits for them, and re-layouts, per_device(): lax.dynamic_update_slice(filtered_all, filtered.astype(jnp.bfloat16), (0,...  9.29 us
  transfers between devices with their start and end apart: 36, of which 4 were waited for; matrix products, arithmetic and copies ran while one was open for 24% of the time, Pallas kernels for 12%

profile of v6, /device:TPU:0, one launch (start us, length us, event | category | flops | bytes accessed | tf_op | source)
XLA Modules:
  0.0 240.2 jit_solution(1091816786335303814)
XLA Ops:
  0.0 6.4 %copy.56 = bf16[128,16384]{0,1:T(8,128)(2,1)} copy(bf16[128,16384]{1,0:T(8,128)(2,1)} %param.1) | data formatting | bytes 8388608 | tf_op args[0]
  6.4 3.7 %fusion.75 = (bf16[15,128,256]{1,2,0:T(8,128)(2,1)S(1)}, bf16[15,128,256]{1,2,0:T(8,128)(2,1)}, bf16[15,128,256]{1,2,0:T(8,128)(2,1)}, bf16[15,128,256]{1,2,0:T(8,128)(2,1)}) fusion(bf16[16,128,1024]{1,2,0:T(8,128)(2,1)} %bitcast.234), kind=kLoop, calls=%fused_computation.291 | loop fusion | bytes 7864320 | tf_op jit(solution)/shard_map/slice | solution.py:53
  10.1 3.3 %collective-permute-start = (bf16[15,128,256]{1,2,0:T(8,128)(2,1)}, bf16[15,128,256]{1,2,0:T(8,128)(2,1)}, u32[]{:S(2)}, u32[]{:S(2)}) collective-permute-start(bf16[15,128,256]{1,2,0:T(8,128)(2,1)} %get-tuple-element.84), channel_id=1, source_target_pairs={{0,1},{1,2},{2,3},{4,5},{5,6},{6,7},{8,9},{9,10},{10,11},{12,13},{... | collective-permute-start | bytes 2949128 | tf_op jit(solution)/shard_map/ppermute | solution.py:17
  13.4 1.1 fusion.73
  14.5 8.5 %negate_convert_fusion = (bf16[512,1,1024]{2,0,1:T(8,128)(2,1)S(1)}, bf16[512,1,1024]{2,0,1:T(8,128)(2,1)S(1)}) fusion(), kind=kLoop, calls=%fused_computation.140 | loop fusion | flops 8912896 | bytes 2097152 | tf_op jit(solution)/shard_map/convert.1
  24.4 2.2 copy.55
  26.6 2.2 convert_element_type.240
  28.9 2.8 %fusion.76 = (bf16[16,128,256]{1,2,0:T(8,128)(2,1)S(1)}, bf16[16,128,256]{1,2,0:T(8,128)(2,1)S(1)}, bf16[16,128,256]{1,2,0:T(8,128)(2,1)S(1)}, bf16[16,128,256]{1,2,0:T(8,128)(2,1)S(1)}) fusion(bf16[16,128,1024]{1,2,0:T(8,128)(2,1)} %bitcast.235), kind=kLoop, calls=%fused_computation.292 | loop fusion | bytes 8388608 | tf_op jit(solution)/shard_map/slice | solution.py:57
  31.7 3.6 %collective-permute-start.1 = (bf16[15,128,256]{1,2,0:T(8,128)(2,1)S(1)}, bf16[15,128,256]{1,2,0:T(8,128)(2,1)S(1)}, u32[]{:S(2)}, u32[]{:S(2)}) collective-permute-start(bf16[15,128,256]{1,2,0:T(8,128)(2,1)S(1)} %copy-done.3), channel_id=1, source_target_pairs={{0,1},{1,2},{2,3},{4,5},{5,6},{6,7},{8,9},{9,10},{10,11},{12,13},{... | collective-permute-start | bytes 2949128 | tf_op jit(solution)/shard_map/ppermute | solution.py:17
  35.3 8.4 %add_convert_fusion.3 = bf16[16,128,256]{1,2,0:T(8,128)(2,1)S(1)} fusion(bf16[16,128,256]{1,2,0:T(8,128)(2,1)S(1)} %get-tuple-element.88, bf16[15,128,256]{1,2,0:T(8,128)(2,1)} %collective-permute-done, f32[256]{0:T(256)S(1)} %bitcast.287, f32[256]{0:T(256)S(1)} %bitcast.288, f32[256]{0:T(256)S(1)} %bitcast.289, f32[256]{0:T(256)S(1)} %bitcast.290, ...), kind=kLoop, calls=%fused_computation.139 | loop fusion | flops 33030144 | bytes 3096576 | tf_op jit(solution)/shard_map/convert_element_type | solution.py:65
  43.7 2.7 %dynamic_update_slice.108 = bf16[16,128,1024]{1,2,0:T(8,128)(2,1)} pad(bf16[16,128,256]{1,2,0:T(8,128)(2,1)S(1)} %add_convert_fusion.3, bf16[]{:T(256)} %constant.338.clone.1), padding=0_0x0_0x0_768 | pad | bytes 5242882 | tf_op jit(solution)/shard_map/dynamic_update_slice | solution.py:64
  46.5 1.9 collective-permute-start.2
  48.4 5.5 %fusion.66 = bf16[16,128,1024]{1,2,0:T(8,128)(2,1)} fusion(bf16[16,128,1024]{1,2,0:T(8,128)(2,1)} %dynamic_update_slice.108, bf16[16,128,256]{1,2,0:T(8,128)(2,1)S(1)} %get-tuple-element.87, f32[256]{0:T(256)S(1)} %bitcast.328, bf16[15,128,256]{1,2,0:T(8,128)(2,1)S(1)} %collective-permute-done.1, f32[256]{0:T(256)S(1)} %bitcast.329, f32[256]{0:T(256)S(1)} %bitcast.330, ...), kind=kLoop, calls=%fused_computation.213 | loop fusion | flops 48758784 | bytes 3096576 | tf_op jit(solution)/shard_map/dynamic_update_slice | solution.py:64
  53.9 9.9 %collective-permute-start.3 = (bf16[15,128,256]{1,2,0:T(8,128)(2,1)S(1)}, bf16[15,128,256]{1,2,0:T(8,128)(2,1)S(1)}, u32[]{:S(2)}, u32[]{:S(2)}) collective-permute-start(bf16[15,128,256]{1,2,0:T(8,128)(2,1)S(1)} %get-tuple-element.43), channel_id=1, source_target_pairs={{0,1},{1,2},{2,3},{4,5},{5,6},{6,7},{8,9},{9,10},{10,11},{12,13},{... | collective-permute-start | bytes 2949128 | tf_op jit(solution)/shard_map/ppermute | solution.py:17
  63.8 5.5 %fusion.67 = bf16[16,128,1024]{1,2,0:T(8,128)(2,1)} fusion(bf16[16,128,1024]{1,2,0:T(8,128)(2,1)} %fusion.66, bf16[16,128,256]{1,2,0:T(8,128)(2,1)S(1)} %get-tuple-element.86, f32[256]{0:T(256)S(1)} %bitcast.325, bf16[15,128,256]{1,2,0:T(8,128)(2,1)S(1)} %collective-permute-done.2, f32[256]{0:T(256)S(1)} %bitcast.326, f32[256]{0:T(256)S(1)} %bitcast.327, ...), kind=kLoop, calls=%fused_computation.214 | loop fusion | flops 48758784 | bytes 3096576 | tf_op jit(solution)/shard_map/dynamic_update_slice | solution.py:64
  69.3 5.4 %fusion.68 = bf16[16,128,1024]{1,2,0:T(8,128)(2,1)} fusion(bf16[16,128,1024]{1,2,0:T(8,128)(2,1)} %fusion.67, bf16[16,128,256]{1,2,0:T(8,128)(2,1)S(1)} %get-tuple-element.85, f32[256]{0:T(256)S(1)} %bitcast.297, bf16[15,128,256]{1,2,0:T(8,128)(2,1)S(1)} %collective-permute-done.3, f32[256]{0:T(256)S(1)} %bitcast.298, f32[256]{0:T(256)S(1)} %bitcast.299, ...), kind=kLoop, calls=%fused_computation.215 | loop fusion | flops 48758784 | bytes 3096576 | tf_op jit(solution)/shard_map/dynamic_update_slice | solution.py:64
  74.8 6.6 %copy.57 = bf16[16,128,1024]{2,1,0:T(8,128)(2,1)} copy(bf16[16,128,1024]{1,2,0:T(8,128)(2,1)} %fusion.68) | data formatting | bytes 8388608 | tf_op jit(solution)/shard_map/dynamic_update_slice | solution.py:64
  81.3 7.0 %convert_bitcast_fusion = bf16[128,8,16,128]{3,1,2,0:T(8,128)(2,1)S(1)} fusion(bf16[1024,1024]{1,0:T(8,128)(2,1)S(1)} %copy-done.1, bf16[2048,1024]{1,0:T(8,128)(2,1)} %bitcast.254), kind=kOutput, calls=%fused_computation.112 | convolution fusion | flops 4297064448 | bytes 10485760 | tf_op jit(solution)/shard_map/dot_general | solution.py:67
  88.3 1.4 copy.72
  89.7 2.2 fusion.74
  92.8 10.1 %collective-permute-start.4 = (bf16[16,2,16,128]{3,2,1,0:T(8,128)(2,1)}, bf16[16,2,16,128]{3,2,1,0:T(8,128)(2,1)}, u32[]{:S(2)}, u32[]{:S(2)}) collective-permute-start(bf16[16,2,16,128]{3,2,1,0:T(8,128)(2,1)} %get-tuple-element.127), channel_id=1, source_target_pairs={{0,2},{2,0},{4,6},{6,4},{8,10},{10,8},{12,14},{14,12},{1,3},{3,1},... | collective-permute-start | bytes 393224 | tf_op jit(solution)/shard_map/ppermute | solution.py:153
  103.0 1.6 collective-permute-start.5
  104.6 1.0 collective-permute-start.6
  105.6 1.6 collective-permute-start.7
  107.1 2.8 %collective-permute-start.8 = (bf16[16,2,16,128]{3,2,1,0:T(8,128)(2,1)S(1)}, bf16[16,2,16,128]{3,2,1,0:T(8,128)(2,1)S(1)}, u32[]{:S(2)}, u32[]{:S(2)}) collective-permute-start(bf16[16,2,16,128]{3,2,1,0:T(8,128)(2,1)S(1)} %get-tuple-element.123), channel_id=1, source_target_pairs={{0,10},{2,8},{4,14},{6,12},{8,2},{10,0},{12,6},{14,4},{1,11},{3,9}... | collective-permute-start | bytes 393224 | tf_op jit(solution)/shard_map/ppermute | solution.py:153
  110.1 2.3 collective-permute-start.9
  114.2 6.3 %collective-permute-done.7 = bf16[16,2,16,128]{3,2,1,0:T(8,128)(2,1)S(1)} collective-permute-done((bf16[16,2,16,128]{3,2,1,0:T(8,128)(2,1)}, bf16[16,2,16,128]{3,2,1,0:T(8,128)(2,1)S(1)}, u32[]{:S(2)}, u32[]{:S(2)}) %collective-permute-start.7) | collective-permute-done | bytes 131104 | tf_op jit(solution)/shard_map/ppermute | solution.py:153
  120.6 2.9 %collective-permute-done.8 = bf16[16,2,16,128]{3,2,1,0:T(8,128)(2,1)S(1)} collective-permute-done((bf16[16,2,16,128]{3,2,1,0:T(8,128)(2,1)S(1)}, bf16[16,2,16,128]{3,2,1,0:T(8,128)(2,1)S(1)}, u32[]{:S(2)}, u32[]{:S(2)}) %collective-permute-start.8) | collective-permute-done | bytes 131104 | tf_op jit(solution)/shard_map/ppermute | solution.py:153
  124.0 2.2 dynamic-slice_bitcast_fusion.16
  126.2 1.1 collective-permute-start.12
  127.3 5.8 %collective-permute-start.13 = (bf16[16,2,16,128]{3,2,1,0:T(8,128)(2,1)S(1)}, bf16[16,2,16,128]{3,2,1,0:T(8,128)(2,1)S(1)}, u32[]{:S(2)}, u32[]{:S(2)}) collective-permute-start(bf16[16,2,16,128]{3,2,1,0:T(8,128)(2,1)S(1)} %get-tuple-element.116), channel_id=1, source_target_pairs={{0,4},{2,6},{4,8},{6,10},{8,12},{10,14},{12,0},{14,2},{1,5},{3,7},... | collective-permute-start | bytes 393224 | tf_op jit(solution)/shard_map/ppermute | solution.py:153
  133.3 1.7 collective-permute-start.15
  135.0 2.0 collective-permute-start.16
  136.9 1.5 pad_maximum_fusion
  138.8 3.9 %collective-permute-start.17 = (bf16[16,2,16,128]{3,2,1,0:T(8,128)(2,1)S(1)}, bf16[16,2,16,128]{3,2,1,0:T(8,128)(2,1)}, u32[]{:S(2)}, u32[]{:S(2)}) collective-permute-start(bf16[16,2,16,128]{3,2,1,0:T(8,128)(2,1)S(1)} %get-tuple-element.112), channel_id=1, source_target_pairs={{0,12},{2,14},{4,0},{6,2},{8,4},{10,6},{12,8},{14,10},{1,13},{3,15... | collective-permute-start | bytes 393224 | tf_op jit(solution)/shard_map/ppermute | solution.py:153
  143.5 2.4 %copy.59 = bf16[16,2,256,128]{3,2,1,0:T(8,128)(2,1)} copy(bf16[16,2,256,128]{2,3,0,1:T(8,128)(2,1)S(1)} %maximum_bitcast_fusion) | data formatting | bytes 4194304 | tf_op jit(solution)/shard_map/transpose | solution.py:185
  145.9 9.8 %shard_map.17.rest_0_ = f32[64,2,256,512]{3,2,1,0:T(8,128)} custom-call(bf16[16,512,128]{2,1,0:T(8,128)(2,1)} %bitcast.253, bf16[16,128,512]{2,1,0:T(8,128)(2,1)} %bitcast.252), custom_call_target="tpu_custom_call" | custom-call | flops 1073741824 | bytes 20971520 | tf_op jit(solution)/shard_map/pallas_call | solution.py:128
  156.1 0.9 bitcast_dynamic-update-slice_fusion.20
  157.0 0.9 bitcast_dynamic-update-slice_fusion.19
  159.9 0.9 bitcast_dynamic-update-slice_fusion.16
  162.7 3.3 %collective-permute-start.21 = (bf16[16,2,16,128]{3,2,1,0:T(8,128)(2,1)S(1)}, bf16[16,2,16,128]{3,2,1,0:T(8,128)(2,1)S(1)}, u32[]{:S(2)}, u32[]{:S(2)}) collective-permute-start(bf16[16,2,16,128]{3,2,1,0:T(8,128)(2,1)S(1)} %get-tuple-element.106), channel_id=1, source_target_pairs={{0,4},{2,6},{4,8},{6,10},{8,12},{10,14},{12,0},{14,2},{1,5},{3,7},... | collective-permute-start | bytes 393224 | tf_op jit(solution)/shard_map/ppermute | solution.py:153
  166.1 1.6 collective-permute-start.23
  167.6 2.2 collective-permute-start.24
  170.6 3.9 %collective-permute-start.25 = (bf16[16,2,16,128]{3,2,1,0:T(8,128)(2,1)S(1)}, bf16[16,2,16,128]{3,2,1,0:T(8,128)(2,1)}, u32[]{:S(2)}, u32[]{:S(2)}) collective-permute-start(bf16[16,2,16,128]{3,2,1,0:T(8,128)(2,1)S(1)} %get-tuple-element.102), channel_id=1, source_target_pairs={{0,12},{2,14},{4,0},{6,2},{8,4},{10,6},{12,8},{14,10},{1,13},{3,15... | collective-permute-start | bytes 393224 | tf_op jit(solution)/shard_map/ppermute | solution.py:153
  175.3 1.6 copy.63
  176.9 2.4 %copy.62 = bf16[16,2,256,128]{3,2,1,0:T(8,128)(2,1)} copy(bf16[16,2,256,128]{2,3,0,1:T(8,128)(2,1)S(1)} %maximum_bitcast_fusion.1) | data formatting | bytes 4194304 | tf_op jit(solution)/shard_map/transpose | solution.py:185
  179.3 9.8 %shard_map.18.rest_0_ = f32[64,2,256,512]{3,2,1,0:T(8,128)} custom-call(bf16[16,512,128]{2,1,0:T(8,128)(2,1)} %bitcast.249, bf16[16,128,512]{2,1,0:T(8,128)(2,1)} %bitcast.247, f32[64,2,256,512]{3,2,1,0:T(8,128)} %shard_map.17.rest_0_), custom_call_target="tpu_custom_call", output_to_operand_aliasing={{}: (2, {})} | custom-call | flops 1073741824 | bytes 20971520 | tf_op jit(solution)/shard_map/pallas_call | solution.py:128
  190.4 0.9 bitcast_dynamic-update-slice_fusion.11
  191.3 0.9 bitcast_dynamic-update-slice_fusion.10
  193.2 0.9 bitcast_dynamic-update-slice_fusion.8
  194.4 1.2 collective-permute-start.28
  195.6 1.9 collective-permute-start.29
  197.8 2.5 %collective-permute-start.31 = (bf16[16,2,16,128]{3,2,1,0:T(8,128)(2,1)S(1)}, bf16[16,2,16,128]{3,2,1,0:T(8,128)(2,1)S(1)}, u32[]{:S(2)}, u32[]{:S(2)}) collective-permute-start(bf16[16,2,16,128]{3,2,1,0:T(8,128)(2,1)S(1)} %get-tuple-element.94), channel_id=1, source_target_pairs={{0,8},{2,10},{4,12},{6,14},{8,0},{10,2},{12,4},{14,6},{1,9},{3,11}... | collective-permute-start | bytes 393224 | tf_op jit(solution)/shard_map/ppermute | solution.py:153
  200.3 1.0 collective-permute-start.32
  202.1 3.9 %collective-permute-start.33 = (bf16[16,2,16,128]{3,2,1,0:T(8,128)(2,1)S(1)}, bf16[16,2,16,128]{3,2,1,0:T(8,128)(2,1)}, u32[]{:S(2)}, u32[]{:S(2)}) collective-permute-start(bf16[16,2,16,128]{3,2,1,0:T(8,128)(2,1)S(1)} %get-tuple-element.92), channel_id=1, source_target_pairs={{0,12},{2,14},{4,0},{6,2},{8,4},{10,6},{12,8},{14,10},{1,13},{3,15... | collective-permute-start | bytes 393224 | tf_op jit(solution)/shard_map/ppermute | solution.py:153
  206.6 1.6 copy.67
  208.2 2.4 %copy.66 = bf16[16,2,256,128]{3,2,1,0:T(8,128)(2,1)} copy(bf16[16,2,256,128]{2,3,0,1:T(8,128)(2,1)S(1)} %maximum_bitcast_fusion.2) | data formatting | bytes 4194304 | tf_op jit(solution)/shard_map/transpose | solution.py:185
  210.6 9.8 %shard_map.19.rest_0_ = f32[64,2,256,512]{3,2,1,0:T(8,128)} custom-call(bf16[16,512,128]{2,1,0:T(8,128)(2,1)} %bitcast.250, bf16[16,128,512]{2,1,0:T(8,128)(2,1)} %bitcast.248, f32[64,2,256,512]{3,2,1,0:T(8,128)} %shard_map.18.rest_0_), custom_call_target="tpu_custom_call", output_to_operand_aliasing={{}: (2, {})} | custom-call | flops 1073741824 | bytes 20971520 | tf_op jit(solution)/shard_map/pallas_call | solution.py:128
  220.8 0.9 bitcast_dynamic-update-slice_fusion.1
  221.8 0.9 bitcast_dynamic-update-slice_fusion
  222.8 2.6 %collective-permute-done.35 = bf16[16,2,2,16,512]{4,3,2,1,0:T(8,128)(2,1)S(1)} collective-permute-done((bf16[16,2,2,16,512]{4,3,2,1,0:T(8,128)(2,1)S(1)}, bf16[16,2,2,16,512]{4,3,2,1,0:T(8,128)(2,1)S(1)}, u32[]{:S(2)}, u32[]{:S(2)}) %collective-permute-start.35) | collective-permute-done | bytes 1048608 | tf_op jit(solution)/shard_map/ppermute | solution.py:174
  226.0 1.6 copy.71
  228.0 2.4 %copy.70 = bf16[16,2,256,128]{3,2,1,0:T(8,128)(2,1)} copy(bf16[16,2,256,128]{2,3,0,1:T(8,128)(2,1)S(1)} %maximum_bitcast_fusion.3) | data formatting | bytes 4194304 | tf_op jit(solution)/shard_map/transpose | solution.py:185
  230.4 9.8 %shard_map.20 = f32[64,2,256,512]{3,2,1,0:T(8,128)} custom-call(bf16[16,512,128]{2,1,0:T(8,128)(2,1)} %bitcast.251, bf16[16,128,512]{2,1,0:T(8,128)(2,1)} %bitcast.246, f32[64,2,256,512]{3,2,1,0:T(8,128)} %shard_map.19.rest_0_), custom_call_target="tpu_custom_call", output_to_operand_aliasing={{}: (2, {})} | custom-call | flops 1073741824 | bytes 20971520 | tf_op jit(solution)/shard_map/pallas_call | solution.py:128
  (131 shorter events, 16.3 us)
Async XLA Ops:
  10.1 21.6 %collective-permute-start = (bf16[15,128,256]{1,2,0:T(8,128)(2,1)}, bf16[15,128,256]{1,2,0:T(8,128)(2,1)}, u32[]{:S(2)}, u32[]{:S(2)}) collective-permute-start(bf16[15,128,256]{1,2,0:T(8,128)(2,1)} %get-tuple-element.84), channel_id=1, source_target_pairs={{0,1},{1,2},{2,3},{4,5},{5,6},{6,7},{8,9},{9,10},{10,11},{12,13},{... | collective-permute-start | bytes 2949128 | tf_op jit(solution)/shard_map/ppermute | solution.py:17
  28.9 2.8 %copy-start.3 = (bf16[15,128,256]{1,2,0:T(8,128)(2,1)S(1)}, bf16[15,128,256]{1,2,0:T(8,128)(2,1)}, u32[]{:S(2)}) copy-start(bf16[15,128,256]{1,2,0:T(8,128)(2,1)} %get-tuple-element.41) | copy-start | bytes 2949124
  31.7 14.8 %collective-permute-start.1 = (bf16[15,128,256]{1,2,0:T(8,128)(2,1)S(1)}, bf16[15,128,256]{1,2,0:T(8,128)(2,1)S(1)}, u32[]{:S(2)}, u32[]{:S(2)}) collective-permute-start(bf16[15,128,256]{1,2,0:T(8,128)(2,1)S(1)} %copy-done.3), channel_id=1, source_target_pairs={{0,1},{1,2},{2,3},{4,5},{5,6},{6,7},{8,9},{9,10},{10,11},{12,13},{... | collective-permute-start | bytes 2949128 | tf_op jit(solution)/shard_map/ppermute | solution.py:17
  43.7 2.7 %copy-start.2 = (bf16[15,128,256]{1,2,0:T(8,128)(2,1)S(1)}, bf16[15,128,256]{1,2,0:T(8,128)(2,1)}, u32[]{:S(2)}) copy-start(bf16[15,128,256]{1,2,0:T(8,128)(2,1)} %get-tuple-element.42) | copy-start | bytes 2949124
  46.5 7.5 %collective-permute-start.2 = (bf16[15,128,256]{1,2,0:T(8,128)(2,1)S(1)}, bf16[15,128,256]{1,2,0:T(8,128)(2,1)S(1)}, u32[]{:S(2)}, u32[]{:S(2)}) collective-permute-start(bf16[15,128,256]{1,2,0:T(8,128)(2,1)S(1)} %copy-done.2), channel_id=1, source_target_pairs={{0,1},{1,2},{2,3},{4,5},{5,6},{6,7},{8,9},{9,10},{10,11},{12,13},{... | collective-permute-start | bytes 2949128 | tf_op jit(solution)/shard_map/ppermute | solution.py:17
  53.9 15.4 %collective-permute-start.3 = (bf16[15,128,256]{1,2,0:T(8,128)(2,1)S(1)}, bf16[15,128,256]{1,2,0:T(8,128)(2,1)S(1)}, u32[]{:S(2)}, u32[]{:S(2)}) collective-permute-start(bf16[15,128,256]{1,2,0:T(8,128)(2,1)S(1)} %get-tuple-element.43), channel_id=1, source_target_pairs={{0,1},{1,2},{2,3},{4,5},{5,6},{6,7},{8,9},{9,10},{10,11},{12,13},{... | collective-permute-start | bytes 2949128 | tf_op jit(solution)/shard_map/ppermute | solution.py:17
  74.8 6.6 %copy-start.1 = (bf16[1024,1024]{1,0:T(8,128)(2,1)S(1)}, bf16[1024,1024]{1,0:T(8,128)(2,1)}, u32[]{:S(2)}) copy-start(bf16[1024,1024]{1,0:T(8,128)(2,1)} %convert_element_type.240) | copy-start | bytes 6291460
  92.8 17.3 %collective-permute-start.4 = (bf16[16,2,16,128]{3,2,1,0:T(8,128)(2,1)}, bf16[16,2,16,128]{3,2,1,0:T(8,128)(2,1)}, u32[]{:S(2)}, u32[]{:S(2)}) collective-permute-start(bf16[16,2,16,128]{3,2,1,0:T(8,128)(2,1)} %get-tuple-element.127), channel_id=1, source_target_pairs={{0,2},{2,0},{4,6},{6,4},{8,10},{10,8},{12,14},{14,12},{1,3},{3,1},... | collective-permute-start | bytes 393224 | tf_op jit(solution)/shard_map/ppermute | solution.py:153
  103.0 10.4 %collective-permute-start.5 = (bf16[16,2,16,128]{3,2,1,0:T(8,128)(2,1)}, bf16[16,2,16,128]{3,2,1,0:T(8,128)(2,1)S(1)}, u32[]{:S(2)}, u32[]{:S(2)}) collective-permute-start(bf16[16,2,16,128]{3,2,1,0:T(8,128)(2,1)} %get-tuple-element.126), channel_id=1, source_target_pairs={{0,4},{2,6},{4,8},{6,10},{8,12},{10,14},{12,0},{14,2},{1,5},{3,7},... | collective-permute-start | bytes 393224 | tf_op jit(solution)/shard_map/ppermute | solution.py:153
  104.6 9.6 %collective-permute-start.6 = (bf16[16,2,16,128]{3,2,1,0:T(8,128)(2,1)}, bf16[16,2,16,128]{3,2,1,0:T(8,128)(2,1)S(1)}, u32[]{:S(2)}, u32[]{:S(2)}) collective-permute-start(bf16[16,2,16,128]{3,2,1,0:T(8,128)(2,1)} %get-tuple-element.125), channel_id=1, source_target_pairs={{0,6},{2,4},{4,10},{6,8},{8,14},{10,12},{12,2},{14,0},{1,7},{3,5},... | collective-permute-start | bytes 393224 | tf_op jit(solution)/shard_map/ppermute | solution.py:153
  105.6 15.0 %collective-permute-start.7 = (bf16[16,2,16,128]{3,2,1,0:T(8,128)(2,1)}, bf16[16,2,16,128]{3,2,1,0:T(8,128)(2,1)S(1)}, u32[]{:S(2)}, u32[]{:S(2)}) collective-permute-start(bf16[16,2,16,128]{3,2,1,0:T(8,128)(2,1)} %get-tuple-element.124), channel_id=1, source_target_pairs={{0,8},{2,10},{4,12},{6,14},{8,0},{10,2},{12,4},{14,6},{1,9},{3,11}... | collective-permute-start | bytes 393224 | tf_op jit(solution)/shard_map/ppermute | solution.py:153
  107.1 16.3 %collective-permute-start.8 = (bf16[16,2,16,128]{3,2,1,0:T(8,128)(2,1)S(1)}, bf16[16,2,16,128]{3,2,1,0:T(8,128)(2,1)S(1)}, u32[]{:S(2)}, u32[]{:S(2)}) collective-permute-start(bf16[16,2,16,128]{3,2,1,0:T(8,128)(2,1)S(1)} %get-tuple-element.123), channel_id=1, source_target_pairs={{0,10},{2,8},{4,14},{6,12},{8,2},{10,0},{12,6},{14,4},{1,11},{3,9}... | collective-permute-start | bytes 393224 | tf_op jit(solution)/shard_map/ppermute | solution.py:153
  110.1 13.3 %collective-permute-start.9 = (bf16[16,2,16,128]{3,2,1,0:T(8,128)(2,1)S(1)}, bf16[16,2,16,128]{3,2,1,0:T(8,128)(2,1)S(1)}, u32[]{:S(2)}, u32[]{:S(2)}) collective-permute-start(bf16[16,2,16,128]{3,2,1,0:T(8,128)(2,1)S(1)} %get-tuple-element.122), channel_id=1, source_target_pairs={{0,12},{2,14},{4,0},{6,2},{8,4},{10,6},{12,8},{14,10},{1,13},{3,15... | collective-permute-start | bytes 393224 | tf_op jit(solution)/shard_map/ppermute | solution.py:153
  113.4 10.5 %collective-permute-start.10 = (bf16[16,2,16,128]{3,2,1,0:T(8,128)(2,1)S(1)}, bf16[16,2,16,128]{3,2,1,0:T(8,128)(2,1)S(1)}, u32[]{:S(2)}, u32[]{:S(2)}) collective-permute-start(bf16[16,2,16,128]{3,2,1,0:T(8,128)(2,1)S(1)} %get-tuple-element.121), channel_id=1, source_target_pairs={{0,14},{2,12},{4,2},{6,0},{8,6},{10,4},{12,10},{14,8},{1,15},{3,13... | collective-permute-start | bytes 393224 | tf_op jit(solution)/shard_map/ppermute | solution.py:153
  123.9 11.0 %collective-permute-start.11 = (bf16[16,2,2,16,512]{4,3,2,1,0:T(8,128)(2,1)S(1)}, bf16[16,2,2,16,512]{4,3,2,1,0:T(8,128)(2,1)S(1)}, u32[]{:S(2)}, u32[]{:S(2)}) collective-permute-start(bf16[16,2,2,16,512]{4,3,2,1,0:T(8,128)(2,1)S(1)} %bitcast_dynamic-update-slice_fusion.24), channel_id=1, source_target_pairs={{0,1},{1,0},{2,3},{3,2},{4,5},{5,4},{6,7},{7,6},{8,9},{9,8},{10,11... | collective-permute-start | bytes 3145736 | tf_op jit(solution)/shard_map/ppermute | solution.py:174
  126.2 12.6 %collective-permute-start.12 = (bf16[16,2,16,128]{3,2,1,0:T(8,128)(2,1)S(1)}, bf16[16,2,16,128]{3,2,1,0:T(8,128)(2,1)S(1)}, u32[]{:S(2)}, u32[]{:S(2)}) collective-permute-start(bf16[16,2,16,128]{3,2,1,0:T(8,128)(2,1)S(1)} %get-tuple-element.117), channel_id=1, source_target_pairs={{0,2},{2,0},{4,6},{6,4},{8,10},{10,8},{12,14},{14,12},{1,3},{3,1},... | collective-permute-start | bytes 393224 | tf_op jit(solution)/shard_map/ppermute | solution.py:153
  127.3 15.4 %collective-permute-start.13 = (bf16[16,2,16,128]{3,2,1,0:T(8,128)(2,1)S(1)}, bf16[16,2,16,128]{3,2,1,0:T(8,128)(2,1)S(1)}, u32[]{:S(2)}, u32[]{:S(2)}) collective-permute-start(bf16[16,2,16,128]{3,2,1,0:T(8,128)(2,1)S(1)} %get-tuple-element.116), channel_id=1, source_target_pairs={{0,4},{2,6},{4,8},{6,10},{8,12},{10,14},{12,0},{14,2},{1,5},{3,7},... | collective-permute-start | bytes 393224 | tf_op jit(solution)/shard_map/ppermute | solution.py:153
  133.1 22.7 %collective-permute-start.14 = (bf16[16,2,16,128]{3,2,1,0:T(8,128)(2,1)}, bf16[16,2,16,128]{3,2,1,0:T(8,128)(2,1)}, u32[]{:S(2)}, u32[]{:S(2)}) collective-permute-start(bf16[16,2,16,128]{3,2,1,0:T(8,128)(2,1)} %get-tuple-element.115), channel_id=1, source_target_pairs={{0,6},{2,4},{4,10},{6,8},{8,14},{10,12},{12,2},{14,0},{1,7},{3,5},... | collective-permute-start | bytes 393224 | tf_op jit(solution)/shard_map/ppermute | solution.py:153
  133.3 22.5 %collective-permute-start.15 = (bf16[16,2,16,128]{3,2,1,0:T(8,128)(2,1)}, bf16[16,2,16,128]{3,2,1,0:T(8,128)(2,1)}, u32[]{:S(2)}, u32[]{:S(2)}) collective-permute-start(bf16[16,2,16,128]{3,2,1,0:T(8,128)(2,1)} %get-tuple-element.114), channel_id=1, source_target_pairs={{0,8},{2,10},{4,12},{6,14},{8,0},{10,2},{12,4},{14,6},{1,9},{3,11}... | collective-permute-start | bytes 393224 | tf_op jit(solution)/shard_map/ppermute | solution.py:153
  135.0 20.8 %collective-permute-start.16 = (bf16[16,2,16,128]{3,2,1,0:T(8,128)(2,1)}, bf16[16,2,16,128]{3,2,1,0:T(8,128)(2,1)}, u32[]{:S(2)}, u32[]{:S(2)}) collective-permute-start(bf16[16,2,16,128]{3,2,1,0:T(8,128)(2,1)} %get-tuple-element.113), channel_id=1, source_target_pairs={{0,10},{2,8},{4,14},{6,12},{8,2},{10,0},{12,6},{14,4},{1,11},{3,9}... | collective-permute-start | bytes 393224 | tf_op jit(solution)/shard_map/ppermute | solution.py:153
  138.8 4.1 %copy-start.8 = (bf16[16,2,16,128]{3,2,1,0:T(8,128)(2,1)}, bf16[16,2,16,128]{3,2,1,0:T(8,128)(2,1)S(1)}, u32[]{:S(2)}) copy-start(bf16[16,2,16,128]{3,2,1,0:T(8,128)(2,1)S(1)} %collective-permute-done.12) | copy-start | bytes 393220
  138.8 17.0 %collective-permute-start.17 = (bf16[16,2,16,128]{3,2,1,0:T(8,128)(2,1)S(1)}, bf16[16,2,16,128]{3,2,1,0:T(8,128)(2,1)}, u32[]{:S(2)}, u32[]{:S(2)}) collective-permute-start(bf16[16,2,16,128]{3,2,1,0:T(8,128)(2,1)S(1)} %get-tuple-element.112), channel_id=1, source_target_pairs={{0,12},{2,14},{4,0},{6,2},{8,4},{10,6},{12,8},{14,10},{1,13},{3,15... | collective-permute-start | bytes 393224 | tf_op jit(solution)/shard_map/ppermute | solution.py:153
  142.7 0.6 copy-start.10
  142.7 13.1 %collective-permute-start.18 = (bf16[16,2,16,128]{3,2,1,0:T(8,128)(2,1)S(1)}, bf16[16,2,16,128]{3,2,1,0:T(8,128)(2,1)}, u32[]{:S(2)}, u32[]{:S(2)}) collective-permute-start(bf16[16,2,16,128]{3,2,1,0:T(8,128)(2,1)S(1)} %get-tuple-element.111), channel_id=1, source_target_pairs={{0,14},{2,12},{4,2},{6,0},{8,6},{10,4},{12,10},{14,8},{1,15},{3,13... | collective-permute-start | bytes 393224 | tf_op jit(solution)/shard_map/ppermute | solution.py:153
  145.9 10.1 %copy-start.9 = (bf16[16,2,16,128]{3,2,1,0:T(8,128)(2,1)S(1)}, bf16[16,2,16,128]{3,2,1,0:T(8,128)(2,1)}, u32[]{:S(2)}) copy-start(bf16[16,2,16,128]{3,2,1,0:T(8,128)(2,1)} %copy-done.8) | copy-start | bytes 393220
  145.9 10.1 %copy-start.11 = (bf16[16,2,16,128]{3,2,1,0:T(8,128)(2,1)S(1)}, bf16[16,2,16,128]{3,2,1,0:T(8,128)(2,1)}, u32[]{:S(2)}) copy-start(bf16[16,2,16,128]{3,2,1,0:T(8,128)(2,1)} %copy-done.10) | copy-start | bytes 393220
  155.8 5.1 %copy-start = (bf16[8,16,2,16,128]{4,3,2,1,0:T(8,128)(2,1)S(1)}, bf16[8,16,2,16,128]{4,3,2,1,0:T(8,128)(2,1)}, u32[]{:S(2)}) copy-start(bf16[8,16,2,16,128]{4,3,2,1,0:T(8,128)(2,1)} %get-tuple-element.56) | copy-start | bytes 3145732
  160.8 6.8 %collective-permute-start.19 = (bf16[16,2,2,16,512]{4,3,2,1,0:T(8,128)(2,1)S(1)}, bf16[16,2,2,16,512]{4,3,2,1,0:T(8,128)(2,1)S(1)}, u32[]{:S(2)}, u32[]{:S(2)}) collective-permute-start(bf16[16,2,2,16,512]{4,3,2,1,0:T(8,128)(2,1)S(1)} %bitcast_dynamic-update-slice_fusion.16), channel_id=1, source_target_pairs={{0,1},{1,0},{2,3},{3,2},{4,5},{5,4},{6,7},{7,6},{8,9},{9,8},{10,11... | collective-permute-start | bytes 3145736 | tf_op jit(solution)/shard_map/ppermute | solution.py:174
  161.8 8.7 %collective-permute-start.20 = (bf16[16,2,16,128]{3,2,1,0:T(8,128)(2,1)S(1)}, bf16[16,2,16,128]{3,2,1,0:T(8,128)(2,1)S(1)}, u32[]{:S(2)}, u32[]{:S(2)}) collective-permute-start(bf16[16,2,16,128]{3,2,1,0:T(8,128)(2,1)S(1)} %get-tuple-element.107), channel_id=1, source_target_pairs={{0,2},{2,0},{4,6},{6,4},{8,10},{10,8},{12,14},{14,12},{1,3},{3,1},... | collective-permute-start | bytes 393224 | tf_op jit(solution)/shard_map/ppermute | solution.py:153
  162.7 11.7 %collective-permute-start.21 = (bf16[16,2,16,128]{3,2,1,0:T(8,128)(2,1)S(1)}, bf16[16,2,16,128]{3,2,1,0:T(8,128)(2,1)S(1)}, u32[]{:S(2)}, u32[]{:S(2)}) collective-permute-start(bf16[16,2,16,128]{3,2,1,0:T(8,128)(2,1)S(1)} %get-tuple-element.106), channel_id=1, source_target_pairs={{0,4},{2,6},{4,8},{6,10},{8,12},{10,14},{12,0},{14,2},{1,5},{3,7},... | collective-permute-start | bytes 393224 | tf_op jit(solution)/shard_map/ppermute | solution.py:153
  166.0 23.2 %collective-permute-start.22 = (bf16[16,2,16,128]{3,2,1,0:T(8,128)(2,1)}, bf16[16,2,16,128]{3,2,1,0:T(8,128)(2,1)}, u32[]{:S(2)}, u32[]{:S(2)}) collective-permute-start(bf16[16,2,16,128]{3,2,1,0:T(8,128)(2,1)} %get-tuple-element.105), channel_id=1, source_target_pairs={{0,6},{2,4},{4,10},{6,8},{8,14},{10,12},{12,2},{14,0},{1,7},{3,5},... | collective-permute-start | bytes 393224 | tf_op jit(solution)/shard_map/ppermute | solution.py:153
  166.1 23.0 %collective-permute-start.23 = (bf16[16,2,16,128]{3,2,1,0:T(8,128)(2,1)}, bf16[16,2,16,128]{3,2,1,0:T(8,128)(2,1)}, u32[]{:S(2)}, u32[]{:S(2)}) collective-permute-start(bf16[16,2,16,128]{3,2,1,0:T(8,128)(2,1)} %get-tuple-element.104), channel_id=1, source_target_pairs={{0,8},{2,10},{4,12},{6,14},{8,0},{10,2},{12,4},{14,6},{1,9},{3,11}... | collective-permute-start | bytes 393224 | tf_op jit(solution)/shard_map/ppermute | solution.py:153
  167.6 21.5 %collective-permute-start.24 = (bf16[16,2,16,128]{3,2,1,0:T(8,128)(2,1)}, bf16[16,2,16,128]{3,2,1,0:T(8,128)(2,1)}, u32[]{:S(2)}, u32[]{:S(2)}) collective-permute-start(bf16[16,2,16,128]{3,2,1,0:T(8,128)(2,1)} %get-tuple-element.103), channel_id=1, source_target_pairs={{0,10},{2,8},{4,14},{6,12},{8,2},{10,0},{12,6},{14,4},{1,11},{3,9}... | collective-permute-start | bytes 393224 | tf_op jit(solution)/shard_map/ppermute | solution.py:153
  170.5 4.3 %copy-start.4 = (bf16[16,2,16,128]{3,2,1,0:T(8,128)(2,1)}, bf16[16,2,16,128]{3,2,1,0:T(8,128)(2,1)S(1)}, u32[]{:S(2)}) copy-start(bf16[16,2,16,128]{3,2,1,0:T(8,128)(2,1)S(1)} %collective-permute-done.20) | copy-start | bytes 393220
  170.6 18.6 %collective-permute-start.25 = (bf16[16,2,16,128]{3,2,1,0:T(8,128)(2,1)S(1)}, bf16[16,2,16,128]{3,2,1,0:T(8,128)(2,1)}, u32[]{:S(2)}, u32[]{:S(2)}) collective-permute-start(bf16[16,2,16,128]{3,2,1,0:T(8,128)(2,1)S(1)} %get-tuple-element.102), channel_id=1, source_target_pairs={{0,12},{2,14},{4,0},{6,2},{8,4},{10,6},{12,8},{14,10},{1,13},{3,15... | collective-permute-start | bytes 393224 | tf_op jit(solution)/shard_map/ppermute | solution.py:153
  174.4 0.7 copy-start.6
  174.4 14.7 %collective-permute-start.26 = (bf16[16,2,16,128]{3,2,1,0:T(8,128)(2,1)S(1)}, bf16[16,2,16,128]{3,2,1,0:T(8,128)(2,1)}, u32[]{:S(2)}, u32[]{:S(2)}) collective-permute-start(bf16[16,2,16,128]{3,2,1,0:T(8,128)(2,1)S(1)} %get-tuple-element.101), channel_id=1, source_target_pairs={{0,14},{2,12},{4,2},{6,0},{8,6},{10,4},{12,10},{14,8},{1,15},{3,13... | collective-permute-start | bytes 393224 | tf_op jit(solution)/shard_map/ppermute | solution.py:153
  179.3 10.1 %copy-start.5 = (bf16[16,2,16,128]{3,2,1,0:T(8,128)(2,1)S(1)}, bf16[16,2,16,128]{3,2,1,0:T(8,128)(2,1)}, u32[]{:S(2)}) copy-start(bf16[16,2,16,128]{3,2,1,0:T(8,128)(2,1)} %copy-done.4) | copy-start | bytes 393220
  179.3 10.1 %copy-start.7 = (bf16[16,2,16,128]{3,2,1,0:T(8,128)(2,1)S(1)}, bf16[16,2,16,128]{3,2,1,0:T(8,128)(2,1)}, u32[]{:S(2)}) copy-start(bf16[16,2,16,128]{3,2,1,0:T(8,128)(2,1)} %copy-done.6) | copy-start | bytes 393220
  194.2 6.2 %collective-permute-start.27 = (bf16[16,2,2,16,512]{4,3,2,1,0:T(8,128)(2,1)S(1)}, bf16[16,2,2,16,512]{4,3,2,1,0:T(8,128)(2,1)S(1)}, u32[]{:S(2)}, u32[]{:S(2)}) collective-permute-start(bf16[16,2,2,16,512]{4,3,2,1,0:T(8,128)(2,1)S(1)} %bitcast_dynamic-update-slice_fusion.8), channel_id=1, source_target_pairs={{0,1},{1,0},{2,3},{3,2},{4,5},{5,4},{6,7},{7,6},{8,9},{9,8},{10,11... | collective-permute-start | bytes 3145736 | tf_op jit(solution)/shard_map/ppermute | solution.py:174
  194.4 7.7 %collective-permute-start.28 = (bf16[16,2,16,128]{3,2,1,0:T(8,128)(2,1)S(1)}, bf16[16,2,16,128]{3,2,1,0:T(8,128)(2,1)S(1)}, u32[]{:S(2)}, u32[]{:S(2)}) collective-permute-start(bf16[16,2,16,128]{3,2,1,0:T(8,128)(2,1)S(1)} %get-tuple-element.97), channel_id=1, source_target_pairs={{0,2},{2,0},{4,6},{6,4},{8,10},{10,8},{12,14},{14,12},{1,3},{3,1},... | collective-permute-start | bytes 393224 | tf_op jit(solution)/shard_map/ppermute | solution.py:153
  195.6 10.4 %collective-permute-start.29 = (bf16[16,2,16,128]{3,2,1,0:T(8,128)(2,1)S(1)}, bf16[16,2,16,128]{3,2,1,0:T(8,128)(2,1)S(1)}, u32[]{:S(2)}, u32[]{:S(2)}) collective-permute-start(bf16[16,2,16,128]{3,2,1,0:T(8,128)(2,1)S(1)} %get-tuple-element.96), channel_id=1, source_target_pairs={{0,4},{2,6},{4,8},{6,10},{8,12},{10,14},{12,0},{14,2},{1,5},{3,7},... | collective-permute-start | bytes 393224 | tf_op jit(solution)/shard_map/ppermute | solution.py:153
  197.5 22.9 %collective-permute-start.30 = (bf16[16,2,16,128]{3,2,1,0:T(8,128)(2,1)S(1)}, bf16[16,2,16,128]{3,2,1,0:T(8,128)(2,1)S(1)}, u32[]{:S(2)}, u32[]{:S(2)}) collective-permute-start(bf16[16,2,16,128]{3,2,1,0:T(8,128)(2,1)S(1)} %get-tuple-element.95), channel_id=1, source_target_pairs={{0,6},{2,4},{4,10},{6,8},{8,14},{10,12},{12,2},{14,0},{1,7},{3,5},... | collective-permute-start | bytes 393224 | tf_op jit(solution)/shard_map/ppermute | solution.py:153
  197.8 22.6 %collective-permute-start.31 = (bf16[16,2,16,128]{3,2,1,0:T(8,128)(2,1)S(1)}, bf16[16,2,16,128]{3,2,1,0:T(8,128)(2,1)S(1)}, u32[]{:S(2)}, u32[]{:S(2)}) collective-permute-start(bf16[16,2,16,128]{3,2,1,0:T(8,128)(2,1)S(1)} %get-tuple-element.94), channel_id=1, source_target_pairs={{0,8},{2,10},{4,12},{6,14},{8,0},{10,2},{12,4},{14,6},{1,9},{3,11}... | collective-permute-start | bytes 393224 | tf_op jit(solution)/shard_map/ppermute | solution.py:153
  200.3 20.1 %collective-permute-start.32 = (bf16[16,2,16,128]{3,2,1,0:T(8,128)(2,1)S(1)}, bf16[16,2,16,128]{3,2,1,0:T(8,128)(2,1)S(1)}, u32[]{:S(2)}, u32[]{:S(2)}) collective-permute-start(bf16[16,2,16,128]{3,2,1,0:T(8,128)(2,1)S(1)} %get-tuple-element.93), channel_id=1, source_target_pairs={{0,10},{2,8},{4,14},{6,12},{8,2},{10,0},{12,6},{14,4},{1,11},{3,9}... | collective-permute-start | bytes 393224 | tf_op jit(solution)/shard_map/ppermute | solution.py:153
  202.1 18.3 %collective-permute-start.33 = (bf16[16,2,16,128]{3,2,1,0:T(8,128)(2,1)S(1)}, bf16[16,2,16,128]{3,2,1,0:T(8,128)(2,1)}, u32[]{:S(2)}, u32[]{:S(2)}) collective-permute-start(bf16[16,2,16,128]{3,2,1,0:T(8,128)(2,1)S(1)} %get-tuple-element.92), channel_id=1, source_target_pairs={{0,12},{2,14},{4,0},{6,2},{8,4},{10,6},{12,8},{14,10},{1,13},{3,15... | collective-permute-start | bytes 393224 | tf_op jit(solution)/shard_map/ppermute | solution.py:153
  206.0 14.5 %collective-permute-start.34 = (bf16[16,2,16,128]{3,2,1,0:T(8,128)(2,1)S(1)}, bf16[16,2,16,128]{3,2,1,0:T(8,128)(2,1)}, u32[]{:S(2)}, u32[]{:S(2)}) collective-permute-start(bf16[16,2,16,128]{3,2,1,0:T(8,128)(2,1)S(1)} %get-tuple-element.91), channel_id=1, source_target_pairs={{0,14},{2,12},{4,2},{6,0},{8,6},{10,4},{12,10},{14,8},{1,15},{3,13... | collective-permute-start | bytes 393224 | tf_op jit(solution)/shard_map/ppermute | solution.py:153
  222.7 2.7 %collective-permute-start.35 = (bf16[16,2,2,16,512]{4,3,2,1,0:T(8,128)(2,1)S(1)}, bf16[16,2,2,16,512]{4,3,2,1,0:T(8,128)(2,1)S(1)}, u32[]{:S(2)}, u32[]{:S(2)}) collective-permute-start(bf16[16,2,2,16,512]{4,3,2,1,0:T(8,128)(2,1)S(1)} %bitcast_dynamic-update-slice_fusion), channel_id=1, source_target_pairs={{0,1},{1,0},{2,3},{3,2},{4,5},{5,4},{6,7},{7,6},{8,9},{9,8},{10,11... | collective-permute-start | bytes 3145736 | tf_op jit(solution)/shard_map/ppermute | solution.py:174

commit v7 on v4

--- a/solution.py
+++ b/solution.py
@@ -67,9 +67,14 @@
     inp_at = lax.axis_index("inp")
     tm_at = lax.axis_index("tm")
     cols = inp_size * inputs_here
-    chunks = 4 if own_channels % 8 == 0 else 1
-    per_chunk = own_channels // chunks
-    parts = [blocks[:, chunk * per_chunk : (chunk + 1) * per_chunk] for chunk in range(chunks)]
+    if own_channels % 8 == 0:
+        eighth = own_channels // 8
+        sizes = [3 * eighth, 2 * eighth, 2 * eighth, eighth]
+    else:
+        sizes = [own_channels]
+    chunks = len(sizes)
+    firsts = [sum(sizes[:chunk]) for chunk in range(chunks)]
+    parts = [blocks[:, first : first + size] for first, size in zip(firsts, sizes)]
     out = None
     half = None
     for chunk in range(chunks):
@@ -78,11 +83,11 @@
         pieces = send_chunk(parts[chunk], inp_at, tm_at, inp_size, tm_size)
         if chunk:
             lhs, rhs = finish_chunk(half, pol_size, cols)
-            out = correlate(lhs, rhs, out, (chunk - 1) * per_chunk, own_channels)
+            out = correlate(lhs, rhs, out, firsts[chunk - 1], own_channels)
             out, pieces = lax.optimization_barrier((out, pieces))
         half = assemble_chunk(pieces, inp_at, inp_size, tm_size, cols)
     lhs, rhs = finish_chunk(half, pol_size, cols)
-    return correlate(lhs, rhs, out, (chunks - 1) * per_chunk, own_channels)
+    return correlate(lhs, rhs, out, firsts[-1], own_channels)
 
 
 def correlate_kernel(scale, lhs_ref, rhs_ref, *rest):

time: 242 us -> 257 us (1.062)
  waiting for transfers between devices: 12.3 us -> 23.4 us
  other arithmetic: 39.9 us -> 44.4 us
  local copies, waits for them, and re-layouts: 56.6 us -> 52.3 us
  starting transfers between devices: 83.6 us -> 87.3 us
    ppermute x28, waiting for transfers between devices: 9.6 us -> 21.4 us  [send_chunk(): block = lax.ppermute(block, ('inp', 'tm'), route)]
    ppermute x28, starting transfers between devices: 79 us -> 82.7 us  [send_chunk(): block = lax.ppermute(block, ('inp', 'tm'), route)]
    another operation x3 -> x1, local copies, waits for them, and re-layouts: 4.71 us -> 1.56 us  [finish_chunk(): both = jnp.stack([half, partner], axis=1)]
    another operation x8, other arithmetic: 2.57 us -> 5.33 us  [finish_chunk(): both = jnp.stack([half, partner], axis=1)]
    unnamed x22 -> x12, local copies, waits for them, and re-layouts: 7.8 us -> 7.78 us
  transfers between devices with their start and end apart: 33 -> 33, of which waited for: 4 -> 4; matrix products, arithmetic and copies ran while one was open for 14% -> 15% of each run, Pallas kernels for 12% -> 13%
where the time goes in v7:
time: 257 us; the launch traced here: 255 us
  starting transfers between devices  87.3 us (34%)
  local copies, waits for them, and re-layouts  52.3 us (20%)
  other arithmetic  44.4 us (17%)
  Pallas kernels  39.5 us (15%)
  waiting for transfers between devices  23.4 us (9%)
  matrix products  6.95 us (3%)
    ppermute x28, starting transfers between devices, send_chunk(): block = lax.ppermute(block, ('inp', 'tm'), route)  82.7 us
    pallas_call x4, Pallas kernels, correlate(): pl.pallas_call(functools.partial(correlate_kernel, 1.0 / (depth // 2)), g...  39.5 us
    convert_element_type x1, other arithmetic, per_device(): filtered = filtered.astype(jnp.bfloat16)  25.8 us
    ppermute x28, waiting for transfers between devices, send_chunk(): block = lax.ppermute(block, ('inp', 'tm'), route)  21.4 us
    transpose x4, local copies, waits for them, and re-layouts, finish_chunk(): lhs = lhs.transpose(0, 1, 3, 2).reshape(own_channels, 2 * rows_here, depth)  10.8 us
    dynamic_update_slice x32, local copies, waits for them, and re-layouts, assemble_chunk(): lax.dynamic_update_slice(half, block[:, :, None], (0, 0, tm_step, 0, sour...  10.3 us
    another operation x1, other arithmetic  8.5 us
    unnamed x12, local copies, waits for them, and re-layouts  7.78 us
  transfers between devices with their start and end apart: 33, of which 4 were waited for; matrix products, arithmetic and copies ran while one was open for 15% of the time, Pallas kernels for 13%

profile of v7, /device:TPU:0, one launch (start us, length us, event | category | flops | bytes accessed | tf_op | source)
XLA Modules:
  0.0 255.1 jit_solution(3458974632705629735)
XLA Ops:
  0.0 6.4 %copy.46 = bf16[128,16384]{0,1:T(8,128)(2,1)} copy(bf16[128,16384]{1,0:T(8,128)(2,1)} %param.1) | data formatting | bytes 8388608 | tf_op args[0]
  6.4 4.3 %slice.193 = bf16[15,128,1024]{1,2,0:T(8,128)(2,1)} slice(bf16[16,128,1024]{1,2,0:T(8,128)(2,1)} %bitcast.174), slice={[1:16], [0:128], [0:1024]} | slice | bytes 7864320 | tf_op jit(solution)/shard_map/slice | solution.py:44
  10.7 4.3 %collective-permute-start = (bf16[15,128,1024]{1,2,0:T(8,128)(2,1)}, bf16[15,128,1024]{1,2,0:T(8,128)(2,1)}, u32[]{:S(2)}, u32[]{:S(2)}) collective-permute-start(bf16[15,128,1024]{1,2,0:T(8,128)(2,1)} %slice.193), channel_id=1, source_target_pairs={{0,1},{1,2},{2,3},{4,5},{5,6},{6,7},{8,9},{9,10},{10,11},{12,13},{... | collective-permute-start | bytes 11796488 | tf_op jit(solution)/shard_map/ppermute | solution.py:17
  15.0 1.1 multiply_reduce_fusion
  16.6 8.5 %negate_convert_fusion = (bf16[512,1,1024]{2,0,1:T(8,128)(2,1)S(1)}, bf16[512,1,1024]{2,0,1:T(8,128)(2,1)S(1)}) fusion(), kind=kLoop, calls=%fused_computation.64 | loop fusion | flops 8912896 | bytes 2097152 | tf_op jit(solution)/shard_map/convert.1
  25.4 2.2 copy.45
  27.5 2.3 convert_element_type.86
  29.9 0.5 broadcast_divide_fusion
  30.3 25.8 %add_convert_fusion = bf16[16,128,1024]{1,2,0:T(8,128)(2,1)} fusion(bf16[16,128,1024]{1,2,0:T(8,128)(2,1)} %bitcast.175, bf16[15,128,1024]{1,2,0:T(8,128)(2,1)} %collective-permute-done, f32[1024]{0:T(1024)S(1)} %get-tuple-element.113, f32[1024]{0:T(1024)S(1)} %get-tuple-element.114, f32[1024]{0:T(1024)S(1)} %get-tuple-element.115, ...), kind=kLoop, calls=%fused_computation.28 | loop fusion | flops 132120576 | bytes 12386304 | tf_op jit(solution)/shard_map/convert_element_type | solution.py:53
  56.1 6.5 %copy.47 = bf16[16,128,1024]{2,1,0:T(8,128)(2,1)} copy(bf16[16,128,1024]{1,2,0:T(8,128)(2,1)} %add_convert_fusion) | data formatting | bytes 8388608 | tf_op jit(solution)/shard_map/convert_element_type | solution.py:53
  62.7 7.0 %convert_bitcast_fusion = bf16[128,8,16,128]{3,1,2,0:T(8,128)(2,1)S(1)} fusion(bf16[1024,1024]{1,0:T(8,128)(2,1)S(1)} %copy-done.2, bf16[2048,1024]{1,0:T(8,128)(2,1)} %bitcast.201), kind=kOutput, calls=%fused_computation.44 | convolution fusion | flops 4297064448 | bytes 10485760 | tf_op jit(solution)/shard_map/dot_general | solution.py:54
  69.6 1.4 copy.58
  71.6 30.6 %collective-permute-start.1 = (bf16[24,2,16,128]{3,2,1,0:T(8,128)(2,1)S(1)}, bf16[24,2,16,128]{3,2,1,0:T(8,128)(2,1)S(1)}, u32[]{:S(2)}, u32[]{:S(2)}) collective-permute-start(bf16[24,2,16,128]{3,2,1,0:T(8,128)(2,1)S(1)} %get-tuple-element.81), channel_id=1, source_target_pairs={{0,2},{2,0},{4,6},{6,4},{8,10},{10,8},{12,14},{14,12},{1,3},{3,1},... | collective-permute-start | bytes 589832 | tf_op jit(solution)/shard_map/ppermute | solution.py:145
  102.3 1.8 fusion.25
  104.1 3.3 %collective-permute-start.7 = (bf16[24,2,16,128]{3,2,1,0:T(8,128)(2,1)S(1)}, bf16[24,2,16,128]{3,2,1,0:T(8,128)(2,1)S(1)}, u32[]{:S(2)}, u32[]{:S(2)}) collective-permute-start(bf16[24,2,16,128]{3,2,1,0:T(8,128)(2,1)S(1)} %get-tuple-element.75), channel_id=1, source_target_pairs={{0,14},{2,12},{4,2},{6,0},{8,6},{10,4},{12,10},{14,8},{1,15},{3,13... | collective-permute-start | bytes 589832 | tf_op jit(solution)/shard_map/ppermute | solution.py:145
  107.4 0.5 collective-permute-start.6
  107.8 0.7 collective-permute-start.5
  108.5 3.5 %collective-permute-start.4 = (bf16[24,2,16,128]{3,2,1,0:T(8,128)(2,1)S(1)}, bf16[24,2,16,128]{3,2,1,0:T(8,128)(2,1)S(1)}, u32[]{:S(2)}, u32[]{:S(2)}) collective-permute-start(bf16[24,2,16,128]{3,2,1,0:T(8,128)(2,1)S(1)} %get-tuple-element.78), channel_id=1, source_target_pairs={{0,8},{2,10},{4,12},{6,14},{8,0},{10,2},{12,4},{14,6},{1,9},{3,11}... | collective-permute-start | bytes 589832 | tf_op jit(solution)/shard_map/ppermute | solution.py:145
  112.2 1.6 collective-permute-start.2
  113.9 14.8 %collective-permute-done.2 = bf16[24,2,16,128]{3,2,1,0:T(8,128)(2,1)S(1)} collective-permute-done((bf16[24,2,16,128]{3,2,1,0:T(8,128)(2,1)S(1)}, bf16[24,2,16,128]{3,2,1,0:T(8,128)(2,1)S(1)}, u32[]{:S(2)}, u32[]{:S(2)}) %collective-permute-start.2) | collective-permute-done | bytes 196640 | tf_op jit(solution)/shard_map/ppermute | solution.py:145
  128.7 8.8 %collective-permute-start.3 = (bf16[24,2,16,128]{3,2,1,0:T(8,128)(2,1)S(1)}, bf16[24,2,16,128]{3,2,1,0:T(8,128)(2,1)S(1)}, u32[]{:S(2)}, u32[]{:S(2)}) collective-permute-start(bf16[24,2,16,128]{3,2,1,0:T(8,128)(2,1)S(1)} %get-tuple-element.79), channel_id=1, source_target_pairs={{0,6},{2,4},{4,10},{6,8},{8,14},{10,12},{12,2},{14,0},{1,7},{3,5},... | collective-permute-start | bytes 589832 | tf_op jit(solution)/shard_map/ppermute | solution.py:145
  137.6 4.3 %collective-permute-done.3 = bf16[24,2,16,128]{3,2,1,0:T(8,128)(2,1)S(1)} collective-permute-done((bf16[24,2,16,128]{3,2,1,0:T(8,128)(2,1)S(1)}, bf16[24,2,16,128]{3,2,1,0:T(8,128)(2,1)S(1)}, u32[]{:S(2)}, u32[]{:S(2)}) %collective-permute-start.3) | collective-permute-done | bytes 196640 | tf_op jit(solution)/shard_map/ppermute | solution.py:145
  142.3 2.2 dynamic-slice_bitcast_fusion.15
  144.5 5.1 %collective-permute-start.15 = (bf16[16,2,16,128]{3,2,1,0:T(8,128)(2,1)}, bf16[16,2,16,128]{3,2,1,0:T(8,128)(2,1)}, u32[]{:S(2)}, u32[]{:S(2)}) collective-permute-start(bf16[16,2,16,128]{3,2,1,0:T(8,128)(2,1)} %get-tuple-element.94), channel_id=1, source_target_pairs={{0,14},{2,12},{4,2},{6,0},{8,6},{10,4},{12,10},{14,8},{1,15},{3,13... | collective-permute-start | bytes 393224 | tf_op jit(solution)/shard_map/ppermute | solution.py:145
  149.6 1.7 collective-permute-start.14
  151.3 3.9 %collective-permute-start.12 = (bf16[16,2,16,128]{3,2,1,0:T(8,128)(2,1)}, bf16[16,2,16,128]{3,2,1,0:T(8,128)(2,1)}, u32[]{:S(2)}, u32[]{:S(2)}) collective-permute-start(bf16[16,2,16,128]{3,2,1,0:T(8,128)(2,1)} %get-tuple-element.97), channel_id=1, source_target_pairs={{0,8},{2,10},{4,12},{6,14},{8,0},{10,2},{12,4},{14,6},{1,9},{3,11}... | collective-permute-start | bytes 393224 | tf_op jit(solution)/shard_map/ppermute | solution.py:145
  155.9 1.9 maximum_bitcast_fusion
  157.9 4.7 %copy.49 = bf16[24,2,256,128]{3,2,1,0:T(8,128)(2,1)} copy(bf16[24,2,256,128]{2,3,0,1:T(8,128)(2,1)} %maximum_bitcast_fusion) | data formatting | bytes 6291456 | tf_op jit(solution)/shard_map/transpose | solution.py:177
  162.5 2.0 pad_maximum_fusion.1
  164.8 1.5 collective-permute-start.9
  166.3 14.1 %shard_map.17.rest_0_ = f32[64,2,256,512]{3,2,1,0:T(8,128)} custom-call(bf16[24,512,128]{2,1,0:T(8,128)(2,1)} %bitcast.182, bf16[24,128,512]{2,1,0:T(8,128)(2,1)} %bitcast.183), custom_call_target="tpu_custom_call" | custom-call | flops 1610612736 | bytes 31457280 | tf_op jit(solution)/shard_map/pallas_call | solution.py:120
  180.7 1.0 bitcast_dynamic-update-slice_fusion.20
  181.6 0.9 bitcast_dynamic-update-slice_fusion.19
  182.6 0.9 bitcast_dynamic-update-slice_fusion.18
  183.5 0.9 bitcast_dynamic-update-slice_fusion.17
  184.5 0.9 bitcast_dynamic-update-slice_fusion.16
  185.5 1.1 slice.244
  186.8 3.6 %collective-permute-start.23 = (bf16[16,2,16,128]{3,2,1,0:T(8,128)(2,1)S(1)}, bf16[16,2,16,128]{3,2,1,0:T(8,128)(2,1)S(1)}, u32[]{:S(2)}, u32[]{:S(2)}) collective-permute-start(bf16[16,2,16,128]{3,2,1,0:T(8,128)(2,1)S(1)} %get-tuple-element.84), channel_id=1, source_target_pairs={{0,14},{2,12},{4,2},{6,0},{8,6},{10,4},{12,10},{14,8},{1,15},{3,13... | collective-permute-start | bytes 393224 | tf_op jit(solution)/shard_map/ppermute | solution.py:145
  190.4 1.7 collective-permute-start.22
  192.1 3.9 %collective-permute-start.20 = (bf16[16,2,16,128]{3,2,1,0:T(8,128)(2,1)S(1)}, bf16[16,2,16,128]{3,2,1,0:T(8,128)(2,1)}, u32[]{:S(2)}, u32[]{:S(2)}) collective-permute-start(bf16[16,2,16,128]{3,2,1,0:T(8,128)(2,1)S(1)} %get-tuple-element.87), channel_id=1, source_target_pairs={{0,8},{2,10},{4,12},{6,14},{8,0},{10,2},{12,4},{14,6},{1,9},{3,11}... | collective-permute-start | bytes 393224 | tf_op jit(solution)/shard_map/ppermute | solution.py:145
  196.0 0.3 collective-permute-start.19
  196.4 1.5 pad_maximum_fusion.2
  198.1 0.3 collective-permute-start.18
  198.5 1.5 collective-permute-start.17
  200.1 2.4 copy.51
  202.5 9.8 %shard_map.18.rest_0_ = f32[64,2,256,512]{3,2,1,0:T(8,128)} custom-call(bf16[16,512,128]{2,1,0:T(8,128)(2,1)} %bitcast.192, bf16[16,128,512]{2,1,0:T(8,128)(2,1)} %bitcast.189, f32[64,2,256,512]{3,2,1,0:T(8,128)} %shard_map.17.rest_0_), custom_call_target="tpu_custom_call", output_to_operand_aliasing={{}: (2, {})} | custom-call | flops 1073741824 | bytes 20971520 | tf_op jit(solution)/shard_map/pallas_call | solution.py:120
  212.3 2.3 collective-permute-done.20
  214.8 0.9 bitcast_dynamic-update-slice_fusion.14
  215.7 0.9 bitcast_dynamic-update-slice_fusion.13
  216.7 0.9 bitcast_dynamic-update-slice_fusion.12
  217.6 0.9 bitcast_dynamic-update-slice_fusion.11
  218.6 0.9 bitcast_dynamic-update-slice_fusion.10
  219.7 1.4 collective-permute-start.31
  221.1 3.3 %collective-permute-start.30 = (bf16[8,2,16,128]{3,2,1,0:T(8,128)(2,1)S(1)}, bf16[8,2,16,128]{3,2,1,0:T(8,128)(2,1)S(1)}, u32[]{:S(2)}, u32[]{:S(2)}) collective-permute-start(bf16[8,2,16,128]{3,2,1,0:T(8,128)(2,1)S(1)} %get-tuple-element.105), channel_id=1, source_target_pairs={{0,12},{2,14},{4,0},{6,2},{8,4},{10,6},{12,8},{14,10},{1,13},{3,15... | collective-permute-start | bytes 196616 | tf_op jit(solution)/shard_map/ppermute | solution.py:145
  224.4 3.1 %collective-permute-start.28 = (bf16[8,2,16,128]{3,2,1,0:T(8,128)(2,1)S(1)}, bf16[8,2,16,128]{3,2,1,0:T(8,128)(2,1)S(1)}, u32[]{:S(2)}, u32[]{:S(2)}) collective-permute-start(bf16[8,2,16,128]{3,2,1,0:T(8,128)(2,1)S(1)} %get-tuple-element.107), channel_id=1, source_target_pairs={{0,8},{2,10},{4,12},{6,14},{8,0},{10,2},{12,4},{14,6},{1,9},{3,11}... | collective-permute-start | bytes 196616 | tf_op jit(solution)/shard_map/ppermute | solution.py:145
  228.5 1.6 copy.55
  230.0 2.4 copy.54
  232.4 1.3 collective-permute-start.26
  233.7 0.8 collective-permute-start.25
  234.4 9.8 %shard_map.19.rest_0_ = f32[64,2,256,512]{3,2,1,0:T(8,128)} custom-call(bf16[16,512,128]{2,1,0:T(8,128)(2,1)} %bitcast.191, bf16[16,128,512]{2,1,0:T(8,128)(2,1)} %bitcast.190, f32[64,2,256,512]{3,2,1,0:T(8,128)} %shard_map.18.rest_0_), custom_call_target="tpu_custom_call", output_to_operand_aliasing={{}: (2, {})} | custom-call | flops 1073741824 | bytes 20971520 | tf_op jit(solution)/shard_map/pallas_call | solution.py:120
  244.6 1.9 collective-permute-done.32
  246.6 1.1 pad_maximum_fusion.6
  247.9 1.4 copy.57
  249.2 5.8 %shard_map.20 = f32[64,2,256,512]{3,2,1,0:T(8,128)} custom-call(bf16[8,512,128]{2,1,0:T(8,128)(2,1)} %bitcast.200, bf16[8,128,512]{2,1,0:T(8,128)(2,1)} %bitcast.199, f32[64,2,256,512]{3,2,1,0:T(8,128)} %shard_map.19.rest_0_), custom_call_target="tpu_custom_call", output_to_operand_aliasing={{}: (2, {})} | custom-call | flops 536870912 | bytes 10485760 | tf_op jit(solution)/shard_map/pallas_call | solution.py:120
  (99 shorter events, 5.3 us)
Async XLA Ops:
  10.7 19.6 %collective-permute-start = (bf16[15,128,1024]{1,2,0:T(8,128)(2,1)}, bf16[15,128,1024]{1,2,0:T(8,128)(2,1)}, u32[]{:S(2)}, u32[]{:S(2)}) collective-permute-start(bf16[15,128,1024]{1,2,0:T(8,128)(2,1)} %slice.193), channel_id=1, source_target_pairs={{0,1},{1,2},{2,3},{4,5},{5,6},{6,7},{8,9},{9,10},{10,11},{12,13},{... | collective-permute-start | bytes 11796488 | tf_op jit(solution)/shard_map/ppermute | solution.py:17
  56.1 6.6 %copy-start.2 = (bf16[1024,1024]{1,0:T(8,128)(2,1)S(1)}, bf16[1024,1024]{1,0:T(8,128)(2,1)}, u32[]{:S(2)}) copy-start(bf16[1024,1024]{1,0:T(8,128)(2,1)} %convert_element_type.86) | copy-start | bytes 6291460
  71.1 33.0 %copy-start = (bf16[128,8,16,128]{3,2,1,0:T(8,128)(2,1)}, bf16[128,8,16,128]{3,2,1,0:T(8,128)(2,1)S(1)}, u32[]{:S(2)}) copy-start(bf16[128,8,16,128]{3,2,1,0:T(8,128)(2,1)S(1)} %copy.58) | copy-start | bytes 12582916
  71.6 40.6 %collective-permute-start.1 = (bf16[24,2,16,128]{3,2,1,0:T(8,128)(2,1)S(1)}, bf16[24,2,16,128]{3,2,1,0:T(8,128)(2,1)S(1)}, u32[]{:S(2)}, u32[]{:S(2)}) collective-permute-start(bf16[24,2,16,128]{3,2,1,0:T(8,128)(2,1)S(1)} %get-tuple-element.81), channel_id=1, source_target_pairs={{0,2},{2,0},{4,6},{6,4},{8,10},{10,8},{12,14},{14,12},{1,3},{3,1},... | collective-permute-start | bytes 589832 | tf_op jit(solution)/shard_map/ppermute | solution.py:145
  104.1 38.1 %collective-permute-start.7 = (bf16[24,2,16,128]{3,2,1,0:T(8,128)(2,1)S(1)}, bf16[24,2,16,128]{3,2,1,0:T(8,128)(2,1)S(1)}, u32[]{:S(2)}, u32[]{:S(2)}) collective-permute-start(bf16[24,2,16,128]{3,2,1,0:T(8,128)(2,1)S(1)} %get-tuple-element.75), channel_id=1, source_target_pairs={{0,14},{2,12},{4,2},{6,0},{8,6},{10,4},{12,10},{14,8},{1,15},{3,13... | collective-permute-start | bytes 589832 | tf_op jit(solution)/shard_map/ppermute | solution.py:145
  107.4 34.7 %collective-permute-start.6 = (bf16[24,2,16,128]{3,2,1,0:T(8,128)(2,1)S(1)}, bf16[24,2,16,128]{3,2,1,0:T(8,128)(2,1)S(1)}, u32[]{:S(2)}, u32[]{:S(2)}) collective-permute-start(bf16[24,2,16,128]{3,2,1,0:T(8,128)(2,1)S(1)} %get-tuple-element.76), channel_id=1, source_target_pairs={{0,12},{2,14},{4,0},{6,2},{8,4},{10,6},{12,8},{14,10},{1,13},{3,15... | collective-permute-start | bytes 589832 | tf_op jit(solution)/shard_map/ppermute | solution.py:145
  107.8 34.2 %collective-permute-start.5 = (bf16[24,2,16,128]{3,2,1,0:T(8,128)(2,1)S(1)}, bf16[24,2,16,128]{3,2,1,0:T(8,128)(2,1)S(1)}, u32[]{:S(2)}, u32[]{:S(2)}) collective-permute-start(bf16[24,2,16,128]{3,2,1,0:T(8,128)(2,1)S(1)} %get-tuple-element.77), channel_id=1, source_target_pairs={{0,10},{2,8},{4,14},{6,12},{8,2},{10,0},{12,6},{14,4},{1,11},{3,9}... | collective-permute-start | bytes 589832 | tf_op jit(solution)/shard_map/ppermute | solution.py:145
  108.5 33.5 %collective-permute-start.4 = (bf16[24,2,16,128]{3,2,1,0:T(8,128)(2,1)S(1)}, bf16[24,2,16,128]{3,2,1,0:T(8,128)(2,1)S(1)}, u32[]{:S(2)}, u32[]{:S(2)}) collective-permute-start(bf16[24,2,16,128]{3,2,1,0:T(8,128)(2,1)S(1)} %get-tuple-element.78), channel_id=1, source_target_pairs={{0,8},{2,10},{4,12},{6,14},{8,0},{10,2},{12,4},{14,6},{1,9},{3,11}... | collective-permute-start | bytes 589832 | tf_op jit(solution)/shard_map/ppermute | solution.py:145
  112.2 16.5 %collective-permute-start.2 = (bf16[24,2,16,128]{3,2,1,0:T(8,128)(2,1)S(1)}, bf16[24,2,16,128]{3,2,1,0:T(8,128)(2,1)S(1)}, u32[]{:S(2)}, u32[]{:S(2)}) collective-permute-start(bf16[24,2,16,128]{3,2,1,0:T(8,128)(2,1)S(1)} %get-tuple-element.80), channel_id=1, source_target_pairs={{0,4},{2,6},{4,8},{6,10},{8,12},{10,14},{12,0},{14,2},{1,5},{3,7},... | collective-permute-start | bytes 589832 | tf_op jit(solution)/shard_map/ppermute | solution.py:145
  128.7 13.2 %collective-permute-start.3 = (bf16[24,2,16,128]{3,2,1,0:T(8,128)(2,1)S(1)}, bf16[24,2,16,128]{3,2,1,0:T(8,128)(2,1)S(1)}, u32[]{:S(2)}, u32[]{:S(2)}) collective-permute-start(bf16[24,2,16,128]{3,2,1,0:T(8,128)(2,1)S(1)} %get-tuple-element.79), channel_id=1, source_target_pairs={{0,6},{2,4},{4,10},{6,8},{8,14},{10,12},{12,2},{14,0},{1,7},{3,5},... | collective-permute-start | bytes 589832 | tf_op jit(solution)/shard_map/ppermute | solution.py:145
  142.2 12.9 %collective-permute-start.8 = (bf16[24,2,2,16,512]{4,3,2,1,0:T(8,128)(2,1)S(1)}, bf16[24,2,2,16,512]{4,3,2,1,0:T(8,128)(2,1)S(1)}, u32[]{:S(2)}, u32[]{:S(2)}) collective-permute-start(bf16[24,2,2,16,512]{4,3,2,1,0:T(8,128)(2,1)S(1)} %bitcast_dynamic-update-slice_fusion), channel_id=1, source_target_pairs={{0,1},{1,0},{2,3},{3,2},{4,5},{5,4},{6,7},{7,6},{8,9},{9,8},{10,11... | collective-permute-start | bytes 4718600 | tf_op jit(solution)/shard_map/ppermute | solution.py:166
  144.5 20.0 %collective-permute-start.15 = (bf16[16,2,16,128]{3,2,1,0:T(8,128)(2,1)}, bf16[16,2,16,128]{3,2,1,0:T(8,128)(2,1)}, u32[]{:S(2)}, u32[]{:S(2)}) collective-permute-start(bf16[16,2,16,128]{3,2,1,0:T(8,128)(2,1)} %get-tuple-element.94), channel_id=1, source_target_pairs={{0,14},{2,12},{4,2},{6,0},{8,6},{10,4},{12,10},{14,8},{1,15},{3,13... | collective-permute-start | bytes 393224 | tf_op jit(solution)/shard_map/ppermute | solution.py:145
  149.6 15.2 %collective-permute-start.14 = (bf16[16,2,16,128]{3,2,1,0:T(8,128)(2,1)}, bf16[16,2,16,128]{3,2,1,0:T(8,128)(2,1)}, u32[]{:S(2)}, u32[]{:S(2)}) collective-permute-start(bf16[16,2,16,128]{3,2,1,0:T(8,128)(2,1)} %get-tuple-element.95), channel_id=1, source_target_pairs={{0,12},{2,14},{4,0},{6,2},{8,4},{10,6},{12,8},{14,10},{1,13},{3,15... | collective-permute-start | bytes 393224 | tf_op jit(solution)/shard_map/ppermute | solution.py:145
  151.3 29.1 %collective-permute-start.13 = (bf16[16,2,16,128]{3,2,1,0:T(8,128)(2,1)}, bf16[16,2,16,128]{3,2,1,0:T(8,128)(2,1)}, u32[]{:S(2)}, u32[]{:S(2)}) collective-permute-start(bf16[16,2,16,128]{3,2,1,0:T(8,128)(2,1)} %get-tuple-element.96), channel_id=1, source_target_pairs={{0,10},{2,8},{4,14},{6,12},{8,2},{10,0},{12,6},{14,4},{1,11},{3,9}... | collective-permute-start | bytes 393224 | tf_op jit(solution)/shard_map/ppermute | solution.py:145
  151.3 29.1 %collective-permute-start.12 = (bf16[16,2,16,128]{3,2,1,0:T(8,128)(2,1)}, bf16[16,2,16,128]{3,2,1,0:T(8,128)(2,1)}, u32[]{:S(2)}, u32[]{:S(2)}) collective-permute-start(bf16[16,2,16,128]{3,2,1,0:T(8,128)(2,1)} %get-tuple-element.97), channel_id=1, source_target_pairs={{0,8},{2,10},{4,12},{6,14},{8,0},{10,2},{12,4},{14,6},{1,9},{3,11}... | collective-permute-start | bytes 393224 | tf_op jit(solution)/shard_map/ppermute | solution.py:145
  155.2 25.2 %collective-permute-start.11 = (bf16[16,2,16,128]{3,2,1,0:T(8,128)(2,1)}, bf16[16,2,16,128]{3,2,1,0:T(8,128)(2,1)}, u32[]{:S(2)}, u32[]{:S(2)}) collective-permute-start(bf16[16,2,16,128]{3,2,1,0:T(8,128)(2,1)} %get-tuple-element.98), channel_id=1, source_target_pairs={{0,6},{2,4},{4,10},{6,8},{8,14},{10,12},{12,2},{14,0},{1,7},{3,5},... | collective-permute-start | bytes 393224 | tf_op jit(solution)/shard_map/ppermute | solution.py:145
  164.5 15.8 %collective-permute-start.10 = (bf16[16,2,16,128]{3,2,1,0:T(8,128)(2,1)S(1)}, bf16[16,2,16,128]{3,2,1,0:T(8,128)(2,1)S(1)}, u32[]{:S(2)}, u32[]{:S(2)}) collective-permute-start(bf16[16,2,16,128]{3,2,1,0:T(8,128)(2,1)S(1)} %get-tuple-element.99), channel_id=1, source_target_pairs={{0,4},{2,6},{4,8},{6,10},{8,12},{10,14},{12,0},{14,2},{1,5},{3,7},... | collective-permute-start | bytes 393224 | tf_op jit(solution)/shard_map/ppermute | solution.py:145
  164.8 15.6 %collective-permute-start.9 = (bf16[16,2,16,128]{3,2,1,0:T(8,128)(2,1)S(1)}, bf16[16,2,16,128]{3,2,1,0:T(8,128)(2,1)S(1)}, u32[]{:S(2)}, u32[]{:S(2)}) collective-permute-start(bf16[16,2,16,128]{3,2,1,0:T(8,128)(2,1)S(1)} %get-tuple-element.100), channel_id=1, source_target_pairs={{0,2},{2,0},{4,6},{6,4},{8,10},{10,8},{12,14},{14,12},{1,3},{3,1},... | collective-permute-start | bytes 393224 | tf_op jit(solution)/shard_map/ppermute | solution.py:145
  180.3 6.2 %copy-start.1 = (bf16[8,16,2,16,128]{4,3,2,1,0:T(8,128)(2,1)S(1)}, bf16[8,16,2,16,128]{4,3,2,1,0:T(8,128)(2,1)}, u32[]{:S(2)}) copy-start(bf16[8,16,2,16,128]{4,3,2,1,0:T(8,128)(2,1)} %get-tuple-element.50) | copy-start | bytes 3145732
  185.4 10.5 %collective-permute-start.16 = (bf16[16,2,2,16,512]{4,3,2,1,0:T(8,128)(2,1)S(1)}, bf16[16,2,2,16,512]{4,3,2,1,0:T(8,128)(2,1)S(1)}, u32[]{:S(2)}, u32[]{:S(2)}) collective-permute-start(bf16[16,2,2,16,512]{4,3,2,1,0:T(8,128)(2,1)S(1)} %bitcast_dynamic-update-slice_fusion.16), channel_id=1, source_target_pairs={{0,1},{1,0},{2,3},{3,2},{4,5},{5,4},{6,7},{7,6},{8,9},{9,8},{10,11... | collective-permute-start | bytes 3145736 | tf_op jit(solution)/shard_map/ppermute | solution.py:166
  186.8 11.3 %collective-permute-start.23 = (bf16[16,2,16,128]{3,2,1,0:T(8,128)(2,1)S(1)}, bf16[16,2,16,128]{3,2,1,0:T(8,128)(2,1)S(1)}, u32[]{:S(2)}, u32[]{:S(2)}) collective-permute-start(bf16[16,2,16,128]{3,2,1,0:T(8,128)(2,1)S(1)} %get-tuple-element.84), channel_id=1, source_target_pairs={{0,14},{2,12},{4,2},{6,0},{8,6},{10,4},{12,10},{14,8},{1,15},{3,13... | collective-permute-start | bytes 393224 | tf_op jit(solution)/shard_map/ppermute | solution.py:145
  190.4 8.0 %collective-permute-start.22 = (bf16[16,2,16,128]{3,2,1,0:T(8,128)(2,1)S(1)}, bf16[16,2,16,128]{3,2,1,0:T(8,128)(2,1)S(1)}, u32[]{:S(2)}, u32[]{:S(2)}) collective-permute-start(bf16[16,2,16,128]{3,2,1,0:T(8,128)(2,1)S(1)} %get-tuple-element.85), channel_id=1, source_target_pairs={{0,12},{2,14},{4,0},{6,2},{8,4},{10,6},{12,8},{14,10},{1,13},{3,15... | collective-permute-start | bytes 393224 | tf_op jit(solution)/shard_map/ppermute | solution.py:145
  192.1 20.3 %collective-permute-start.21 = (bf16[16,2,16,128]{3,2,1,0:T(8,128)(2,1)S(1)}, bf16[16,2,16,128]{3,2,1,0:T(8,128)(2,1)}, u32[]{:S(2)}, u32[]{:S(2)}) collective-permute-start(bf16[16,2,16,128]{3,2,1,0:T(8,128)(2,1)S(1)} %get-tuple-element.86), channel_id=1, source_target_pairs={{0,10},{2,8},{4,14},{6,12},{8,2},{10,0},{12,6},{14,4},{1,11},{3,9}... | collective-permute-start | bytes 393224 | tf_op jit(solution)/shard_map/ppermute | solution.py:145
  192.1 22.5 %collective-permute-start.20 = (bf16[16,2,16,128]{3,2,1,0:T(8,128)(2,1)S(1)}, bf16[16,2,16,128]{3,2,1,0:T(8,128)(2,1)}, u32[]{:S(2)}, u32[]{:S(2)}) collective-permute-start(bf16[16,2,16,128]{3,2,1,0:T(8,128)(2,1)S(1)} %get-tuple-element.87), channel_id=1, source_target_pairs={{0,8},{2,10},{4,12},{6,14},{8,0},{10,2},{12,4},{14,6},{1,9},{3,11}... | collective-permute-start | bytes 393224 | tf_op jit(solution)/shard_map/ppermute | solution.py:145
  196.0 18.6 %collective-permute-start.19 = (bf16[16,2,16,128]{3,2,1,0:T(8,128)(2,1)S(1)}, bf16[16,2,16,128]{3,2,1,0:T(8,128)(2,1)}, u32[]{:S(2)}, u32[]{:S(2)}) collective-permute-start(bf16[16,2,16,128]{3,2,1,0:T(8,128)(2,1)S(1)} %get-tuple-element.88), channel_id=1, source_target_pairs={{0,6},{2,4},{4,10},{6,8},{8,14},{10,12},{12,2},{14,0},{1,7},{3,5},... | collective-permute-start | bytes 393224 | tf_op jit(solution)/shard_map/ppermute | solution.py:145
  198.1 16.5 %collective-permute-start.18 = (bf16[16,2,16,128]{3,2,1,0:T(8,128)(2,1)S(1)}, bf16[16,2,16,128]{3,2,1,0:T(8,128)(2,1)}, u32[]{:S(2)}, u32[]{:S(2)}) collective-permute-start(bf16[16,2,16,128]{3,2,1,0:T(8,128)(2,1)S(1)} %get-tuple-element.89), channel_id=1, source_target_pairs={{0,4},{2,6},{4,8},{6,10},{8,12},{10,14},{12,0},{14,2},{1,5},{3,7},... | collective-permute-start | bytes 393224 | tf_op jit(solution)/shard_map/ppermute | solution.py:145
  198.5 1.5 copy-start.3
  198.5 16.1 %collective-permute-start.17 = (bf16[16,2,16,128]{3,2,1,0:T(8,128)(2,1)S(1)}, bf16[16,2,16,128]{3,2,1,0:T(8,128)(2,1)}, u32[]{:S(2)}, u32[]{:S(2)}) collective-permute-start(bf16[16,2,16,128]{3,2,1,0:T(8,128)(2,1)S(1)} %get-tuple-element.90), channel_id=1, source_target_pairs={{0,2},{2,0},{4,6},{6,4},{8,10},{10,8},{12,14},{14,12},{1,3},{3,1},... | collective-permute-start | bytes 393224 | tf_op jit(solution)/shard_map/ppermute | solution.py:145
  202.5 17.0 %copy-start.4 = (bf16[16,2,16,128]{3,2,1,0:T(8,128)(2,1)S(1)}, bf16[16,2,16,128]{3,2,1,0:T(8,128)(2,1)}, u32[]{:S(2)}) copy-start(bf16[16,2,16,128]{3,2,1,0:T(8,128)(2,1)} %copy-done.3) | copy-start | bytes 393220
  219.6 7.9 %collective-permute-start.24 = (bf16[16,2,2,16,512]{4,3,2,1,0:T(8,128)(2,1)S(1)}, bf16[16,2,2,16,512]{4,3,2,1,0:T(8,128)(2,1)S(1)}, u32[]{:S(2)}, u32[]{:S(2)}) collective-permute-start(bf16[16,2,2,16,512]{4,3,2,1,0:T(8,128)(2,1)S(1)} %bitcast_dynamic-update-slice_fusion.8), channel_id=1, source_target_pairs={{0,1},{1,0},{2,3},{3,2},{4,5},{5,4},{6,7},{7,6},{8,9},{9,8},{10,11... | collective-permute-start | bytes 3145736 | tf_op jit(solution)/shard_map/ppermute | solution.py:166
  219.7 12.7 %collective-permute-start.31 = (bf16[8,2,16,128]{3,2,1,0:T(8,128)(2,1)S(1)}, bf16[8,2,16,128]{3,2,1,0:T(8,128)(2,1)S(1)}, u32[]{:S(2)}, u32[]{:S(2)}) collective-permute-start(bf16[8,2,16,128]{3,2,1,0:T(8,128)(2,1)S(1)} %get-tuple-element.104), channel_id=1, source_target_pairs={{0,14},{2,12},{4,2},{6,0},{8,6},{10,4},{12,10},{14,8},{1,15},{3,13... | collective-permute-start | bytes 196616 | tf_op jit(solution)/shard_map/ppermute | solution.py:145
  221.1 12.6 %collective-permute-start.30 = (bf16[8,2,16,128]{3,2,1,0:T(8,128)(2,1)S(1)}, bf16[8,2,16,128]{3,2,1,0:T(8,128)(2,1)S(1)}, u32[]{:S(2)}, u32[]{:S(2)}) collective-permute-start(bf16[8,2,16,128]{3,2,1,0:T(8,128)(2,1)S(1)} %get-tuple-element.105), channel_id=1, source_target_pairs={{0,12},{2,14},{4,0},{6,2},{8,4},{10,6},{12,8},{14,10},{1,13},{3,15... | collective-permute-start | bytes 196616 | tf_op jit(solution)/shard_map/ppermute | solution.py:145
  224.4 19.8 %collective-permute-start.29 = (bf16[8,2,16,128]{3,2,1,0:T(8,128)(2,1)S(1)}, bf16[8,2,16,128]{3,2,1,0:T(8,128)(2,1)S(1)}, u32[]{:S(2)}, u32[]{:S(2)}) collective-permute-start(bf16[8,2,16,128]{3,2,1,0:T(8,128)(2,1)S(1)} %get-tuple-element.106), channel_id=1, source_target_pairs={{0,10},{2,8},{4,14},{6,12},{8,2},{10,0},{12,6},{14,4},{1,11},{3,9}... | collective-permute-start | bytes 196616 | tf_op jit(solution)/shard_map/ppermute | solution.py:145
  224.4 19.8 %collective-permute-start.28 = (bf16[8,2,16,128]{3,2,1,0:T(8,128)(2,1)S(1)}, bf16[8,2,16,128]{3,2,1,0:T(8,128)(2,1)S(1)}, u32[]{:S(2)}, u32[]{:S(2)}) collective-permute-start(bf16[8,2,16,128]{3,2,1,0:T(8,128)(2,1)S(1)} %get-tuple-element.107), channel_id=1, source_target_pairs={{0,8},{2,10},{4,12},{6,14},{8,0},{10,2},{12,4},{14,6},{1,9},{3,11}... | collective-permute-start | bytes 196616 | tf_op jit(solution)/shard_map/ppermute | solution.py:145
  227.5 16.7 %collective-permute-start.27 = (bf16[8,2,16,128]{3,2,1,0:T(8,128)(2,1)S(1)}, bf16[8,2,16,128]{3,2,1,0:T(8,128)(2,1)S(1)}, u32[]{:S(2)}, u32[]{:S(2)}) collective-permute-start(bf16[8,2,16,128]{3,2,1,0:T(8,128)(2,1)S(1)} %get-tuple-element.108), channel_id=1, source_target_pairs={{0,6},{2,4},{4,10},{6,8},{8,14},{10,12},{12,2},{14,0},{1,7},{3,5},... | collective-permute-start | bytes 196616 | tf_op jit(solution)/shard_map/ppermute | solution.py:145
  232.4 11.8 %collective-permute-start.26 = (bf16[8,2,16,128]{3,2,1,0:T(8,128)(2,1)S(1)}, bf16[8,2,16,128]{3,2,1,0:T(8,128)(2,1)S(1)}, u32[]{:S(2)}, u32[]{:S(2)}) collective-permute-start(bf16[8,2,16,128]{3,2,1,0:T(8,128)(2,1)S(1)} %get-tuple-element.109), channel_id=1, source_target_pairs={{0,4},{2,6},{4,8},{6,10},{8,12},{10,14},{12,0},{14,2},{1,5},{3,7},... | collective-permute-start | bytes 196616 | tf_op jit(solution)/shard_map/ppermute | solution.py:145
  233.7 10.6 %collective-permute-start.25 = (bf16[8,2,16,128]{3,2,1,0:T(8,128)(2,1)S(1)}, bf16[8,2,16,128]{3,2,1,0:T(8,128)(2,1)S(1)}, u32[]{:S(2)}, u32[]{:S(2)}) collective-permute-start(bf16[8,2,16,128]{3,2,1,0:T(8,128)(2,1)S(1)} %get-tuple-element.110), channel_id=1, source_target_pairs={{0,2},{2,0},{4,6},{6,4},{8,10},{10,8},{12,14},{14,12},{1,3},{3,1},... | collective-permute-start | bytes 196616 | tf_op jit(solution)/shard_map/ppermute | solution.py:145
  244.6 2.0 collective-permute-start.32

commit v8 on v4

--- a/solution.py
+++ b/solution.py
@@ -36,11 +36,28 @@
     return table.reshape(frame_len, frame_len).astype(jnp.bfloat16)
 
 
+def copy_kernel(in_ref, out_ref):
+    out_ref[0] = in_ref[...]
+
+
+def split_frames(voltages, frame_len):
+    inputs_here = voltages.shape[0]
+    spectra_here = voltages.shape[1] // frame_len
+    return pl.pallas_call(
+        copy_kernel,
+        grid=(spectra_here,),
+        in_specs=[pl.BlockSpec((inputs_here, frame_len), lambda s: (0, s))],
+        out_specs=pl.BlockSpec((1, inputs_here, frame_len), lambda s: (s, 0, 0)),
+        out_shape=jax.ShapeDtypeStruct((spectra_here, inputs_here, frame_len), voltages.dtype),
+        cost_estimate=pl.CostEstimate(flops=0, bytes_accessed=2 * voltages.size * 2, transcendentals=0),
+    )(voltages)
+
+
 def per_device(voltages):
     inputs_here = voltages.shape[0]
     frame_len = 2 * CH
     spectra_here = voltages.shape[1] // frame_len
-    frames = voltages.reshape(inputs_here, spectra_here, frame_len).transpose(1, 0, 2)
+    frames = split_frames(voltages, frame_len)
     last_frames = frames[spectra_here - (TAPS - 1) :]
     history = shifted(last_frames, ("tm", "pol"), 1)
     extended = jnp.concatenate([history, frames], axis=0)

time: 242 us -> 242 us (level)
  local copies, waits for them, and re-layouts: 56.6 us -> 45 us
  Pallas kernels: 39.3 us -> 49.4 us
    pallas_call x0 -> x1, Pallas kernels: none -> 10.1 us  [split_frames(): pl.pallas_call(copy_kernel, grid=(spectra_here,), in_specs=[pl.BlockSpec(...]
    convert_element_type x1 -> x0, local copies, waits for them, and re-layouts: 6.55 us -> none  [per_device(): filtered = filtered.astype(jnp.bfloat16)]
    unnamed x22 -> x21, local copies, waits for them, and re-layouts: 7.8 us -> 1.45 us
where the time goes in v8:
time: 242 us; the launch traced here: 241 us
  starting transfers between devices  83.6 us (35%)
  Pallas kernels  49.4 us (20%)
  local copies, waits for them, and re-layouts  45 us (19%)
  other arithmetic  41.9 us (17%)
  waiting for transfers between devices  12.3 us (5%)
  matrix products  6.97 us (3%)
    ppermute x28, starting transfers between devices, send_chunk(): block = lax.ppermute(block, ('inp', 'tm'), route)  79.1 us
    pallas_call x4, Pallas kernels, correlate(): pl.pallas_call(functools.partial(correlate_kernel, 1.0 / (depth // 2)), g...  39.3 us
    convert_element_type x1, other arithmetic, per_device(): filtered = filtered.astype(jnp.bfloat16)  27.6 us
    dynamic_update_slice x32, local copies, waits for them, and re-layouts, assemble_chunk(): lax.dynamic_update_slice(half, block[:, :, None], (0, 0, tm_step, 0, sour...  12.9 us
    pallas_call x1, Pallas kernels, split_frames(): pl.pallas_call(copy_kernel, grid=(spectra_here,), in_specs=[pl.BlockSpec(...  10.1 us
    ppermute x28, waiting for transfers between devices, send_chunk(): block = lax.ppermute(block, ('inp', 'tm'), route)  9.6 us
    transpose x4, local copies, waits for them, and re-layouts, finish_chunk(): lhs = lhs.transpose(0, 1, 3, 2).reshape(own_channels, 2 * rows_here, depth)  9.52 us
    another operation x1, other arithmetic  8.5 us
  transfers between devices with their start and end apart: 33, of which 4 were waited for; matrix products, arithmetic and copies ran while one was open for 14% of the time, Pallas kernels for 12%

profile of v8, /device:TPU:0, one launch (start us, length us, event | category | flops | bytes accessed | tf_op | source)
XLA Modules:
  0.0 240.6 jit_solution(10654285997936714318)
XLA Ops:
  0.0 10.1 %shard_map.17 = bf16[16,128,1024]{2,1,0:T(8,128)(2,1)} custom-call(bf16[128,16384]{1,0:T(8,128)(2,1)} %in_ref.1), custom_call_target="tpu_custom_call" | custom-call | bytes 8388608 | tf_op jit(solution)/shard_map/pallas_call | solution.py:46
  10.1 4.6 %slice.193 = bf16[15,128,1024]{2,1,0:T(8,128)(2,1)} slice(bf16[16,128,1024]{2,1,0:T(8,128)(2,1)} %shard_map.17), slice={[1:16], [0:128], [0:1024]} | slice | bytes 7864320 | tf_op jit(solution)/shard_map/slice | solution.py:61
  14.7 4.3 %collective-permute-start = (bf16[15,128,1024]{2,1,0:T(8,128)(2,1)}, bf16[15,128,1024]{2,1,0:T(8,128)(2,1)}, u32[]{:S(2)}, u32[]{:S(2)}) collective-permute-start(bf16[15,128,1024]{2,1,0:T(8,128)(2,1)} %slice.193), channel_id=1, source_target_pairs={{0,1},{1,2},{2,3},{4,5},{5,6},{6,7},{8,9},{9,10},{10,11},{12,13},{... | collective-permute-start | bytes 11796488 | tf_op jit(solution)/shard_map/ppermute | solution.py:17
  18.9 1.1 multiply_reduce_fusion
  20.7 8.5 %negate_convert_fusion = (bf16[512,1,1024]{2,0,1:T(8,128)(2,1)S(1)}, bf16[512,1,1024]{2,0,1:T(8,128)(2,1)S(1)}) fusion(), kind=kLoop, calls=%fused_computation.68 | loop fusion | flops 8912896 | bytes 2097152 | tf_op jit(solution)/shard_map/convert.1
  29.5 2.2 copy.51
  31.6 2.3 convert_element_type.86
  34.4 27.6 %add_convert_fusion = bf16[16,128,1024]{2,1,0:T(8,128)(2,1)} fusion(bf16[16,128,1024]{2,1,0:T(8,128)(2,1)} %shard_map.17, bf16[15,128,1024]{2,1,0:T(8,128)(2,1)} %collective-permute-done, f32[1024]{0:T(1024)S(1)} %get-tuple-element.115, f32[1024]{0:T(1024)S(1)} %get-tuple-element.116, f32[1024]{0:T(1024)S(1)} %get-tuple-element.117, ...), kind=kLoop, calls=%fused_computation.28 | loop fusion | flops 132120576 | bytes 12386304 | tf_op jit(solution)/shard_map/convert_element_type | solution.py:70
  62.0 7.0 %convert_bitcast_fusion = bf16[128,8,16,128]{3,1,2,0:T(8,128)(2,1)S(1)} fusion(bf16[1024,1024]{1,0:T(8,128)(2,1)S(1)} %copy-done.1, bf16[2048,1024]{1,0:T(8,128)(2,1)} %bitcast.185), kind=kOutput, calls=%fused_computation.44 | convolution fusion | flops 4297064448 | bytes 10485760 | tf_op jit(solution)/shard_map/dot_general | solution.py:71
  69.0 1.4 copy.66
  70.4 2.2 fusion.25
  72.6 0.9 dynamic-slice_bitcast_fusion.24
  73.5 30.5 %collective-permute-start.1 = (bf16[16,2,16,128]{3,2,1,0:T(8,128)(2,1)}, bf16[16,2,16,128]{3,2,1,0:T(8,128)(2,1)}, u32[]{:S(2)}, u32[]{:S(2)}) collective-permute-start(bf16[16,2,16,128]{3,2,1,0:T(8,128)(2,1)} %get-tuple-element.113), channel_id=1, source_target_pairs={{0,2},{2,0},{4,6},{6,4},{8,10},{10,8},{12,14},{14,12},{1,3},{3,1},... | collective-permute-start | bytes 393224 | tf_op jit(solution)/shard_map/ppermute | solution.py:157
  104.0 1.6 collective-permute-start.2
  105.6 1.0 collective-permute-start.3
  106.6 1.6 collective-permute-start.4
  108.2 2.8 %collective-permute-start.5 = (bf16[16,2,16,128]{3,2,1,0:T(8,128)(2,1)S(1)}, bf16[16,2,16,128]{3,2,1,0:T(8,128)(2,1)S(1)}, u32[]{:S(2)}, u32[]{:S(2)}) collective-permute-start(bf16[16,2,16,128]{3,2,1,0:T(8,128)(2,1)S(1)} %get-tuple-element.109), channel_id=1, source_target_pairs={{0,10},{2,8},{4,14},{6,12},{8,2},{10,0},{12,6},{14,4},{1,11},{3,9}... | collective-permute-start | bytes 393224 | tf_op jit(solution)/shard_map/ppermute | solution.py:157
  111.1 2.3 collective-permute-start.6
  113.4 0.9 bitcast_dynamic-update-slice_fusion.30
  115.3 6.3 %collective-permute-done.4 = bf16[16,2,16,128]{3,2,1,0:T(8,128)(2,1)S(1)} collective-permute-done((bf16[16,2,16,128]{3,2,1,0:T(8,128)(2,1)}, bf16[16,2,16,128]{3,2,1,0:T(8,128)(2,1)S(1)}, u32[]{:S(2)}, u32[]{:S(2)}) %collective-permute-start.4) | collective-permute-done | bytes 131104 | tf_op jit(solution)/shard_map/ppermute | solution.py:157
  121.6 2.9 %collective-permute-done.5 = bf16[16,2,16,128]{3,2,1,0:T(8,128)(2,1)S(1)} collective-permute-done((bf16[16,2,16,128]{3,2,1,0:T(8,128)(2,1)S(1)}, bf16[16,2,16,128]{3,2,1,0:T(8,128)(2,1)S(1)}, u32[]{:S(2)}, u32[]{:S(2)}) %collective-permute-start.5) | collective-permute-done | bytes 131104 | tf_op jit(solution)/shard_map/ppermute | solution.py:157
  125.0 2.1 dynamic-slice_bitcast_fusion.16
  127.2 5.6 %collective-permute-start.10 = (bf16[16,2,16,128]{3,2,1,0:T(8,128)(2,1)S(1)}, bf16[16,2,16,128]{3,2,1,0:T(8,128)(2,1)S(1)}, u32[]{:S(2)}, u32[]{:S(2)}) collective-permute-start(bf16[16,2,16,128]{3,2,1,0:T(8,128)(2,1)S(1)} %get-tuple-element.102), channel_id=1, source_target_pairs={{0,4},{2,6},{4,8},{6,10},{8,12},{10,14},{12,0},{14,2},{1,5},{3,7},... | collective-permute-start | bytes 393224 | tf_op jit(solution)/shard_map/ppermute | solution.py:157
  133.5 1.8 collective-permute-start.12
  135.3 1.3 collective-permute-start.13
  136.6 3.8 %collective-permute-start.14 = (bf16[16,2,16,128]{3,2,1,0:T(8,128)(2,1)}, bf16[16,2,16,128]{3,2,1,0:T(8,128)(2,1)}, u32[]{:S(2)}, u32[]{:S(2)}) collective-permute-start(bf16[16,2,16,128]{3,2,1,0:T(8,128)(2,1)} %get-tuple-element.98), channel_id=1, source_target_pairs={{0,12},{2,14},{4,0},{6,2},{8,4},{10,6},{12,8},{14,10},{1,13},{3,15... | collective-permute-start | bytes 393224 | tf_op jit(solution)/shard_map/ppermute | solution.py:157
  140.5 1.5 pad_maximum_fusion.1
  144.0 2.4 copy.53
  146.4 9.9 %shard_map.18.rest_0_ = f32[64,2,256,512]{3,2,1,0:T(8,128)} custom-call(bf16[16,512,128]{2,1,0:T(8,128)(2,1)} %bitcast.184, bf16[16,128,512]{2,1,0:T(8,128)(2,1)} %bitcast.183), custom_call_target="tpu_custom_call" | custom-call | flops 1073741824 | bytes 20971520 | tf_op jit(solution)/shard_map/pallas_call | solution.py:132
  156.5 0.9 bitcast_dynamic-update-slice_fusion.22
  157.6 0.9 bitcast_dynamic-update-slice_fusion.19
  158.5 0.9 bitcast_dynamic-update-slice_fusion.18
  159.5 0.9 bitcast_dynamic-update-slice_fusion.17
  160.4 0.9 bitcast_dynamic-update-slice_fusion.16
  161.5 0.9 dynamic-slice_bitcast_fusion.8
  162.4 1.3 collective-permute-start.17
  163.6 2.3 collective-permute-start.18
  165.9 0.8 collective-permute-start.19
  166.7 1.5 collective-permute-start.20
  168.2 1.5 collective-permute-start.21
  170.5 3.9 %collective-permute-start.22 = (bf16[16,2,16,128]{3,2,1,0:T(8,128)(2,1)S(1)}, bf16[16,2,16,128]{3,2,1,0:T(8,128)(2,1)}, u32[]{:S(2)}, u32[]{:S(2)}) collective-permute-start(bf16[16,2,16,128]{3,2,1,0:T(8,128)(2,1)S(1)} %get-tuple-element.88), channel_id=1, source_target_pairs={{0,12},{2,14},{4,0},{6,2},{8,4},{10,6},{12,8},{14,10},{1,13},{3,15... | collective-permute-start | bytes 393224 | tf_op jit(solution)/shard_map/ppermute | solution.py:157
  174.4 0.9 collective-permute-start.23
  175.4 1.6 copy.57
  177.0 2.4 copy.56
  179.4 9.8 %shard_map.19.rest_0_ = f32[64,2,256,512]{3,2,1,0:T(8,128)} custom-call(bf16[16,512,128]{2,1,0:T(8,128)(2,1)} %bitcast.180, bf16[16,128,512]{2,1,0:T(8,128)(2,1)} %bitcast.178, f32[64,2,256,512]{3,2,1,0:T(8,128)} %shard_map.18.rest_0_), custom_call_target="tpu_custom_call", output_to_operand_aliasing={{}: (2, {})} | custom-call | flops 1073741824 | bytes 20971520 | tf_op jit(solution)/shard_map/pallas_call | solution.py:132
  189.6 0.9 bitcast_dynamic-update-slice_fusion.12
  190.5 0.9 bitcast_dynamic-update-slice_fusion.11
  191.4 0.9 bitcast_dynamic-update-slice_fusion.10
  192.4 0.9 bitcast_dynamic-update-slice_fusion.9
  193.3 0.9 bitcast_dynamic-update-slice_fusion.8
  194.5 1.2 collective-permute-start.25
  195.7 2.5 %collective-permute-start.26 = (bf16[16,2,16,128]{3,2,1,0:T(8,128)(2,1)S(1)}, bf16[16,2,16,128]{3,2,1,0:T(8,128)(2,1)S(1)}, u32[]{:S(2)}, u32[]{:S(2)}) collective-permute-start(bf16[16,2,16,128]{3,2,1,0:T(8,128)(2,1)S(1)} %get-tuple-element.82), channel_id=1, source_target_pairs={{0,4},{2,6},{4,8},{6,10},{8,12},{10,14},{12,0},{14,2},{1,5},{3,7},... | collective-permute-start | bytes 393224 | tf_op jit(solution)/shard_map/ppermute | solution.py:157
  198.4 2.1 collective-permute-start.28
  200.4 1.6 collective-permute-start.29
  202.8 3.9 %collective-permute-start.30 = (bf16[16,2,16,128]{3,2,1,0:T(8,128)(2,1)S(1)}, bf16[16,2,16,128]{3,2,1,0:T(8,128)(2,1)}, u32[]{:S(2)}, u32[]{:S(2)}) collective-permute-start(bf16[16,2,16,128]{3,2,1,0:T(8,128)(2,1)S(1)} %get-tuple-element.78), channel_id=1, source_target_pairs={{0,12},{2,14},{4,0},{6,2},{8,4},{10,6},{12,8},{14,10},{1,13},{3,15... | collective-permute-start | bytes 393224 | tf_op jit(solution)/shard_map/ppermute | solution.py:157
  207.1 1.6 copy.61
  208.7 2.4 copy.60
  211.0 9.8 %shard_map.20.rest_0_ = f32[64,2,256,512]{3,2,1,0:T(8,128)} custom-call(bf16[16,512,128]{2,1,0:T(8,128)(2,1)} %bitcast.181, bf16[16,128,512]{2,1,0:T(8,128)(2,1)} %bitcast.179, f32[64,2,256,512]{3,2,1,0:T(8,128)} %shard_map.19.rest_0_), custom_call_target="tpu_custom_call", output_to_operand_aliasing={{}: (2, {})} | custom-call | flops 1073741824 | bytes 20971520 | tf_op jit(solution)/shard_map/pallas_call | solution.py:132
  221.3 0.9 bitcast_dynamic-update-slice_fusion.1
  222.2 0.9 bitcast_dynamic-update-slice_fusion
  223.2 2.6 %collective-permute-done.32 = bf16[16,2,2,16,512]{4,3,2,1,0:T(8,128)(2,1)S(1)} collective-permute-done((bf16[16,2,2,16,512]{4,3,2,1,0:T(8,128)(2,1)S(1)}, bf16[16,2,2,16,512]{4,3,2,1,0:T(8,128)(2,1)S(1)}, u32[]{:S(2)}, u32[]{:S(2)}) %collective-permute-start.32) | collective-permute-done | bytes 1048608 | tf_op jit(solution)/shard_map/ppermute | solution.py:178
  226.4 1.6 copy.65
  228.4 2.4 copy.64
  230.8 9.8 %shard_map.21 = f32[64,2,256,512]{3,2,1,0:T(8,128)} custom-call(bf16[16,512,128]{2,1,0:T(8,128)(2,1)} %bitcast.182, bf16[16,128,512]{2,1,0:T(8,128)(2,1)} %bitcast.177, f32[64,2,256,512]{3,2,1,0:T(8,128)} %shard_map.20.rest_0_), custom_call_target="tpu_custom_call", output_to_operand_aliasing={{}: (2, {})} | custom-call | flops 1073741824 | bytes 20971520 | tf_op jit(solution)/shard_map/pallas_call | solution.py:132
  (112 shorter events, 9.3 us)
Async XLA Ops:
  14.7 19.7 %collective-permute-start = (bf16[15,128,1024]{2,1,0:T(8,128)(2,1)}, bf16[15,128,1024]{2,1,0:T(8,128)(2,1)}, u32[]{:S(2)}, u32[]{:S(2)}) collective-permute-start(bf16[15,128,1024]{2,1,0:T(8,128)(2,1)} %slice.193), channel_id=1, source_target_pairs={{0,1},{1,2},{2,3},{4,5},{5,6},{6,7},{8,9},{9,10},{10,11},{12,13},{... | collective-permute-start | bytes 11796488 | tf_op jit(solution)/shard_map/ppermute | solution.py:17
  34.4 27.6 %copy-start.1 = (bf16[1024,1024]{1,0:T(8,128)(2,1)S(1)}, bf16[1024,1024]{1,0:T(8,128)(2,1)}, u32[]{:S(2)}) copy-start(bf16[1024,1024]{1,0:T(8,128)(2,1)} %convert_element_type.86) | copy-start | bytes 6291460
  73.5 37.7 %collective-permute-start.1 = (bf16[16,2,16,128]{3,2,1,0:T(8,128)(2,1)}, bf16[16,2,16,128]{3,2,1,0:T(8,128)(2,1)}, u32[]{:S(2)}, u32[]{:S(2)}) collective-permute-start(bf16[16,2,16,128]{3,2,1,0:T(8,128)(2,1)} %get-tuple-element.113), channel_id=1, source_target_pairs={{0,2},{2,0},{4,6},{6,4},{8,10},{10,8},{12,14},{14,12},{1,3},{3,1},... | collective-permute-start | bytes 393224 | tf_op jit(solution)/shard_map/ppermute | solution.py:157
  104.0 10.4 %collective-permute-start.2 = (bf16[16,2,16,128]{3,2,1,0:T(8,128)(2,1)}, bf16[16,2,16,128]{3,2,1,0:T(8,128)(2,1)S(1)}, u32[]{:S(2)}, u32[]{:S(2)}) collective-permute-start(bf16[16,2,16,128]{3,2,1,0:T(8,128)(2,1)} %get-tuple-element.112), channel_id=1, source_target_pairs={{0,4},{2,6},{4,8},{6,10},{8,12},{10,14},{12,0},{14,2},{1,5},{3,7},... | collective-permute-start | bytes 393224 | tf_op jit(solution)/shard_map/ppermute | solution.py:157
  105.6 9.6 %collective-permute-start.3 = (bf16[16,2,16,128]{3,2,1,0:T(8,128)(2,1)}, bf16[16,2,16,128]{3,2,1,0:T(8,128)(2,1)S(1)}, u32[]{:S(2)}, u32[]{:S(2)}) collective-permute-start(bf16[16,2,16,128]{3,2,1,0:T(8,128)(2,1)} %get-tuple-element.111), channel_id=1, source_target_pairs={{0,6},{2,4},{4,10},{6,8},{8,14},{10,12},{12,2},{14,0},{1,7},{3,5},... | collective-permute-start | bytes 393224 | tf_op jit(solution)/shard_map/ppermute | solution.py:157
  106.6 15.0 %collective-permute-start.4 = (bf16[16,2,16,128]{3,2,1,0:T(8,128)(2,1)}, bf16[16,2,16,128]{3,2,1,0:T(8,128)(2,1)S(1)}, u32[]{:S(2)}, u32[]{:S(2)}) collective-permute-start(bf16[16,2,16,128]{3,2,1,0:T(8,128)(2,1)} %get-tuple-element.110), channel_id=1, source_target_pairs={{0,8},{2,10},{4,12},{6,14},{8,0},{10,2},{12,4},{14,6},{1,9},{3,11}... | collective-permute-start | bytes 393224 | tf_op jit(solution)/shard_map/ppermute | solution.py:157
  108.2 16.3 %collective-permute-start.5 = (bf16[16,2,16,128]{3,2,1,0:T(8,128)(2,1)S(1)}, bf16[16,2,16,128]{3,2,1,0:T(8,128)(2,1)S(1)}, u32[]{:S(2)}, u32[]{:S(2)}) collective-permute-start(bf16[16,2,16,128]{3,2,1,0:T(8,128)(2,1)S(1)} %get-tuple-element.109), channel_id=1, source_target_pairs={{0,10},{2,8},{4,14},{6,12},{8,2},{10,0},{12,6},{14,4},{1,11},{3,9}... | collective-permute-start | bytes 393224 | tf_op jit(solution)/shard_map/ppermute | solution.py:157
  111.1 13.3 %collective-permute-start.6 = (bf16[16,2,16,128]{3,2,1,0:T(8,128)(2,1)S(1)}, bf16[16,2,16,128]{3,2,1,0:T(8,128)(2,1)S(1)}, u32[]{:S(2)}, u32[]{:S(2)}) collective-permute-start(bf16[16,2,16,128]{3,2,1,0:T(8,128)(2,1)S(1)} %get-tuple-element.108), channel_id=1, source_target_pairs={{0,12},{2,14},{4,0},{6,2},{8,4},{10,6},{12,8},{14,10},{1,13},{3,15... | collective-permute-start | bytes 393224 | tf_op jit(solution)/shard_map/ppermute | solution.py:157
  114.4 10.5 %collective-permute-start.7 = (bf16[16,2,16,128]{3,2,1,0:T(8,128)(2,1)S(1)}, bf16[16,2,16,128]{3,2,1,0:T(8,128)(2,1)S(1)}, u32[]{:S(2)}, u32[]{:S(2)}) collective-permute-start(bf16[16,2,16,128]{3,2,1,0:T(8,128)(2,1)S(1)} %get-tuple-element.107), channel_id=1, source_target_pairs={{0,14},{2,12},{4,2},{6,0},{8,6},{10,4},{12,10},{14,8},{1,15},{3,13... | collective-permute-start | bytes 393224 | tf_op jit(solution)/shard_map/ppermute | solution.py:157
  125.0 11.7 %collective-permute-start.8 = (bf16[16,2,2,16,512]{4,3,2,1,0:T(8,128)(2,1)S(1)}, bf16[16,2,2,16,512]{4,3,2,1,0:T(8,128)(2,1)S(1)}, u32[]{:S(2)}, u32[]{:S(2)}) collective-permute-start(bf16[16,2,2,16,512]{4,3,2,1,0:T(8,128)(2,1)S(1)} %bitcast_dynamic-update-slice_fusion.24), channel_id=1, source_target_pairs={{0,1},{1,0},{2,3},{3,2},{4,5},{5,4},{6,7},{7,6},{8,9},{9,8},{10,11... | collective-permute-start | bytes 3145736 | tf_op jit(solution)/shard_map/ppermute | solution.py:178
  127.2 15.1 %collective-permute-start.10 = (bf16[16,2,16,128]{3,2,1,0:T(8,128)(2,1)S(1)}, bf16[16,2,16,128]{3,2,1,0:T(8,128)(2,1)S(1)}, u32[]{:S(2)}, u32[]{:S(2)}) collective-permute-start(bf16[16,2,16,128]{3,2,1,0:T(8,128)(2,1)S(1)} %get-tuple-element.102), channel_id=1, source_target_pairs={{0,4},{2,6},{4,8},{6,10},{8,12},{10,14},{12,0},{14,2},{1,5},{3,7},... | collective-permute-start | bytes 393224 | tf_op jit(solution)/shard_map/ppermute | solution.py:157
  132.8 10.3 %collective-permute-start.11 = (bf16[16,2,16,128]{3,2,1,0:T(8,128)(2,1)S(1)}, bf16[16,2,16,128]{3,2,1,0:T(8,128)(2,1)S(1)}, u32[]{:S(2)}, u32[]{:S(2)}) collective-permute-start(bf16[16,2,16,128]{3,2,1,0:T(8,128)(2,1)S(1)} %get-tuple-element.101), channel_id=1, source_target_pairs={{0,6},{2,4},{4,10},{6,8},{8,14},{10,12},{12,2},{14,0},{1,7},{3,5},... | collective-permute-start | bytes 393224 | tf_op jit(solution)/shard_map/ppermute | solution.py:157
  133.5 22.8 %collective-permute-start.12 = (bf16[16,2,16,128]{3,2,1,0:T(8,128)(2,1)}, bf16[16,2,16,128]{3,2,1,0:T(8,128)(2,1)}, u32[]{:S(2)}, u32[]{:S(2)}) collective-permute-start(bf16[16,2,16,128]{3,2,1,0:T(8,128)(2,1)} %get-tuple-element.100), channel_id=1, source_target_pairs={{0,8},{2,10},{4,12},{6,14},{8,0},{10,2},{12,4},{14,6},{1,9},{3,11}... | collective-permute-start | bytes 393224 | tf_op jit(solution)/shard_map/ppermute | solution.py:157
  135.3 21.0 %collective-permute-start.13 = (bf16[16,2,16,128]{3,2,1,0:T(8,128)(2,1)}, bf16[16,2,16,128]{3,2,1,0:T(8,128)(2,1)}, u32[]{:S(2)}, u32[]{:S(2)}) collective-permute-start(bf16[16,2,16,128]{3,2,1,0:T(8,128)(2,1)} %get-tuple-element.99), channel_id=1, source_target_pairs={{0,10},{2,8},{4,14},{6,12},{8,2},{10,0},{12,6},{14,4},{1,11},{3,9}... | collective-permute-start | bytes 393224 | tf_op jit(solution)/shard_map/ppermute | solution.py:157
  136.6 19.7 %collective-permute-start.14 = (bf16[16,2,16,128]{3,2,1,0:T(8,128)(2,1)}, bf16[16,2,16,128]{3,2,1,0:T(8,128)(2,1)}, u32[]{:S(2)}, u32[]{:S(2)}) collective-permute-start(bf16[16,2,16,128]{3,2,1,0:T(8,128)(2,1)} %get-tuple-element.98), channel_id=1, source_target_pairs={{0,12},{2,14},{4,0},{6,2},{8,4},{10,6},{12,8},{14,10},{1,13},{3,15... | collective-permute-start | bytes 393224 | tf_op jit(solution)/shard_map/ppermute | solution.py:157
  142.3 1.5 copy-start.6
  142.3 14.0 %collective-permute-start.15 = (bf16[16,2,16,128]{3,2,1,0:T(8,128)(2,1)S(1)}, bf16[16,2,16,128]{3,2,1,0:T(8,128)(2,1)}, u32[]{:S(2)}, u32[]{:S(2)}) collective-permute-start(bf16[16,2,16,128]{3,2,1,0:T(8,128)(2,1)S(1)} %get-tuple-element.97), channel_id=1, source_target_pairs={{0,14},{2,12},{4,2},{6,0},{8,6},{10,4},{12,10},{14,8},{1,15},{3,13... | collective-permute-start | bytes 393224 | tf_op jit(solution)/shard_map/ppermute | solution.py:157
  143.1 0.7 copy-start.8
  143.1 13.3 %collective-permute-start.9 = (bf16[16,2,16,128]{3,2,1,0:T(8,128)(2,1)S(1)}, bf16[16,2,16,128]{3,2,1,0:T(8,128)(2,1)}, u32[]{:S(2)}, u32[]{:S(2)}) collective-permute-start(bf16[16,2,16,128]{3,2,1,0:T(8,128)(2,1)S(1)} %get-tuple-element.103), channel_id=1, source_target_pairs={{0,2},{2,0},{4,6},{6,4},{8,10},{10,8},{12,14},{14,12},{1,3},{3,1},... | collective-permute-start | bytes 393224 | tf_op jit(solution)/shard_map/ppermute | solution.py:157
  146.4 11.1 %copy-start.7 = (bf16[16,2,16,128]{3,2,1,0:T(8,128)(2,1)S(1)}, bf16[16,2,16,128]{3,2,1,0:T(8,128)(2,1)}, u32[]{:S(2)}) copy-start(bf16[16,2,16,128]{3,2,1,0:T(8,128)(2,1)} %copy-done.6) | copy-start | bytes 393220
  146.4 11.1 %copy-start.9 = (bf16[16,2,16,128]{3,2,1,0:T(8,128)(2,1)S(1)}, bf16[16,2,16,128]{3,2,1,0:T(8,128)(2,1)}, u32[]{:S(2)}) copy-start(bf16[16,2,16,128]{3,2,1,0:T(8,128)(2,1)} %copy-done.8) | copy-start | bytes 393220
  146.4 15.0 %copy-start = (bf16[8,16,2,16,128]{4,3,2,1,0:T(8,128)(2,1)S(1)}, bf16[8,16,2,16,128]{4,3,2,1,0:T(8,128)(2,1)}, u32[]{:S(2)}) copy-start(bf16[8,16,2,16,128]{4,3,2,1,0:T(8,128)(2,1)} %get-tuple-element.50) | copy-start | bytes 3145732
  161.4 6.8 %collective-permute-start.16 = (bf16[16,2,2,16,512]{4,3,2,1,0:T(8,128)(2,1)S(1)}, bf16[16,2,2,16,512]{4,3,2,1,0:T(8,128)(2,1)S(1)}, u32[]{:S(2)}, u32[]{:S(2)}) collective-permute-start(bf16[16,2,2,16,512]{4,3,2,1,0:T(8,128)(2,1)S(1)} %bitcast_dynamic-update-slice_fusion.16), channel_id=1, source_target_pairs={{0,1},{1,0},{2,3},{3,2},{4,5},{5,4},{6,7},{7,6},{8,9},{9,8},{10,11... | collective-permute-start | bytes 3145736 | tf_op jit(solution)/shard_map/ppermute | solution.py:178
  162.4 8.1 %collective-permute-start.17 = (bf16[16,2,16,128]{3,2,1,0:T(8,128)(2,1)S(1)}, bf16[16,2,16,128]{3,2,1,0:T(8,128)(2,1)S(1)}, u32[]{:S(2)}, u32[]{:S(2)}) collective-permute-start(bf16[16,2,16,128]{3,2,1,0:T(8,128)(2,1)S(1)} %get-tuple-element.93), channel_id=1, source_target_pairs={{0,2},{2,0},{4,6},{6,4},{8,10},{10,8},{12,14},{14,12},{1,3},{3,1},... | collective-permute-start | bytes 393224 | tf_op jit(solution)/shard_map/ppermute | solution.py:157
  163.6 10.7 %collective-permute-start.18 = (bf16[16,2,16,128]{3,2,1,0:T(8,128)(2,1)S(1)}, bf16[16,2,16,128]{3,2,1,0:T(8,128)(2,1)S(1)}, u32[]{:S(2)}, u32[]{:S(2)}) collective-permute-start(bf16[16,2,16,128]{3,2,1,0:T(8,128)(2,1)S(1)} %get-tuple-element.92), channel_id=1, source_target_pairs={{0,4},{2,6},{4,8},{6,10},{8,12},{10,14},{12,0},{14,2},{1,5},{3,7},... | collective-permute-start | bytes 393224 | tf_op jit(solution)/shard_map/ppermute | solution.py:157
  165.9 23.3 %collective-permute-start.19 = (bf16[16,2,16,128]{3,2,1,0:T(8,128)(2,1)}, bf16[16,2,16,128]{3,2,1,0:T(8,128)(2,1)}, u32[]{:S(2)}, u32[]{:S(2)}) collective-permute-start(bf16[16,2,16,128]{3,2,1,0:T(8,128)(2,1)} %get-tuple-element.91), channel_id=1, source_target_pairs={{0,6},{2,4},{4,10},{6,8},{8,14},{10,12},{12,2},{14,0},{1,7},{3,5},... | collective-permute-start | bytes 393224 | tf_op jit(solution)/shard_map/ppermute | solution.py:157
  166.7 22.5 %collective-permute-start.20 = (bf16[16,2,16,128]{3,2,1,0:T(8,128)(2,1)}, bf16[16,2,16,128]{3,2,1,0:T(8,128)(2,1)}, u32[]{:S(2)}, u32[]{:S(2)}) collective-permute-start(bf16[16,2,16,128]{3,2,1,0:T(8,128)(2,1)} %get-tuple-element.90), channel_id=1, source_target_pairs={{0,8},{2,10},{4,12},{6,14},{8,0},{10,2},{12,4},{14,6},{1,9},{3,11}... | collective-permute-start | bytes 393224 | tf_op jit(solution)/shard_map/ppermute | solution.py:157
  168.2 21.0 %collective-permute-start.21 = (bf16[16,2,16,128]{3,2,1,0:T(8,128)(2,1)}, bf16[16,2,16,128]{3,2,1,0:T(8,128)(2,1)}, u32[]{:S(2)}, u32[]{:S(2)}) collective-permute-start(bf16[16,2,16,128]{3,2,1,0:T(8,128)(2,1)} %get-tuple-element.89), channel_id=1, source_target_pairs={{0,10},{2,8},{4,14},{6,12},{8,2},{10,0},{12,6},{14,4},{1,11},{3,9}... | collective-permute-start | bytes 393224 | tf_op jit(solution)/shard_map/ppermute | solution.py:157
  170.5 4.8 %copy-start.2 = (bf16[16,2,16,128]{3,2,1,0:T(8,128)(2,1)}, bf16[16,2,16,128]{3,2,1,0:T(8,128)(2,1)S(1)}, u32[]{:S(2)}) copy-start(bf16[16,2,16,128]{3,2,1,0:T(8,128)(2,1)S(1)} %collective-permute-done.17) | copy-start | bytes 393220
  170.5 18.8 %collective-permute-start.22 = (bf16[16,2,16,128]{3,2,1,0:T(8,128)(2,1)S(1)}, bf16[16,2,16,128]{3,2,1,0:T(8,128)(2,1)}, u32[]{:S(2)}, u32[]{:S(2)}) collective-permute-start(bf16[16,2,16,128]{3,2,1,0:T(8,128)(2,1)S(1)} %get-tuple-element.88), channel_id=1, source_target_pairs={{0,12},{2,14},{4,0},{6,2},{8,4},{10,6},{12,8},{14,10},{1,13},{3,15... | collective-permute-start | bytes 393224 | tf_op jit(solution)/shard_map/ppermute | solution.py:157
  174.4 0.9 copy-start.4
  174.4 14.9 %collective-permute-start.23 = (bf16[16,2,16,128]{3,2,1,0:T(8,128)(2,1)S(1)}, bf16[16,2,16,128]{3,2,1,0:T(8,128)(2,1)}, u32[]{:S(2)}, u32[]{:S(2)}) collective-permute-start(bf16[16,2,16,128]{3,2,1,0:T(8,128)(2,1)S(1)} %get-tuple-element.87), channel_id=1, source_target_pairs={{0,14},{2,12},{4,2},{6,0},{8,6},{10,4},{12,10},{14,8},{1,15},{3,13... | collective-permute-start | bytes 393224 | tf_op jit(solution)/shard_map/ppermute | solution.py:157
  179.4 10.1 %copy-start.3 = (bf16[16,2,16,128]{3,2,1,0:T(8,128)(2,1)S(1)}, bf16[16,2,16,128]{3,2,1,0:T(8,128)(2,1)}, u32[]{:S(2)}) copy-start(bf16[16,2,16,128]{3,2,1,0:T(8,128)(2,1)} %copy-done.2) | copy-start | bytes 393220
  179.4 10.1 %copy-start.5 = (bf16[16,2,16,128]{3,2,1,0:T(8,128)(2,1)S(1)}, bf16[16,2,16,128]{3,2,1,0:T(8,128)(2,1)}, u32[]{:S(2)}) copy-start(bf16[16,2,16,128]{3,2,1,0:T(8,128)(2,1)} %copy-done.4) | copy-start | bytes 393220
  194.3 6.2 %collective-permute-start.24 = (bf16[16,2,2,16,512]{4,3,2,1,0:T(8,128)(2,1)S(1)}, bf16[16,2,2,16,512]{4,3,2,1,0:T(8,128)(2,1)S(1)}, u32[]{:S(2)}, u32[]{:S(2)}) collective-permute-start(bf16[16,2,2,16,512]{4,3,2,1,0:T(8,128)(2,1)S(1)} %bitcast_dynamic-update-slice_fusion.8), channel_id=1, source_target_pairs={{0,1},{1,0},{2,3},{3,2},{4,5},{5,4},{6,7},{7,6},{8,9},{9,8},{10,11... | collective-permute-start | bytes 3145736 | tf_op jit(solution)/shard_map/ppermute | solution.py:178
  194.5 8.2 %collective-permute-start.25 = (bf16[16,2,16,128]{3,2,1,0:T(8,128)(2,1)S(1)}, bf16[16,2,16,128]{3,2,1,0:T(8,128)(2,1)S(1)}, u32[]{:S(2)}, u32[]{:S(2)}) collective-permute-start(bf16[16,2,16,128]{3,2,1,0:T(8,128)(2,1)S(1)} %get-tuple-element.83), channel_id=1, source_target_pairs={{0,2},{2,0},{4,6},{6,4},{8,10},{10,8},{12,14},{14,12},{1,3},{3,1},... | collective-permute-start | bytes 393224 | tf_op jit(solution)/shard_map/ppermute | solution.py:157
  195.7 10.9 %collective-permute-start.26 = (bf16[16,2,16,128]{3,2,1,0:T(8,128)(2,1)S(1)}, bf16[16,2,16,128]{3,2,1,0:T(8,128)(2,1)S(1)}, u32[]{:S(2)}, u32[]{:S(2)}) collective-permute-start(bf16[16,2,16,128]{3,2,1,0:T(8,128)(2,1)S(1)} %get-tuple-element.82), channel_id=1, source_target_pairs={{0,4},{2,6},{4,8},{6,10},{8,12},{10,14},{12,0},{14,2},{1,5},{3,7},... | collective-permute-start | bytes 393224 | tf_op jit(solution)/shard_map/ppermute | solution.py:157
  198.2 22.6 %collective-permute-start.27 = (bf16[16,2,16,128]{3,2,1,0:T(8,128)(2,1)S(1)}, bf16[16,2,16,128]{3,2,1,0:T(8,128)(2,1)S(1)}, u32[]{:S(2)}, u32[]{:S(2)}) collective-permute-start(bf16[16,2,16,128]{3,2,1,0:T(8,128)(2,1)S(1)} %get-tuple-element.81), channel_id=1, source_target_pairs={{0,6},{2,4},{4,10},{6,8},{8,14},{10,12},{12,2},{14,0},{1,7},{3,5},... | collective-permute-start | bytes 393224 | tf_op jit(solution)/shard_map/ppermute | solution.py:157
  198.4 22.5 %collective-permute-start.28 = (bf16[16,2,16,128]{3,2,1,0:T(8,128)(2,1)S(1)}, bf16[16,2,16,128]{3,2,1,0:T(8,128)(2,1)S(1)}, u32[]{:S(2)}, u32[]{:S(2)}) collective-permute-start(bf16[16,2,16,128]{3,2,1,0:T(8,128)(2,1)S(1)} %get-tuple-element.80), channel_id=1, source_target_pairs={{0,8},{2,10},{4,12},{6,14},{8,0},{10,2},{12,4},{14,6},{1,9},{3,11}... | collective-permute-start | bytes 393224 | tf_op jit(solution)/shard_map/ppermute | solution.py:157
  200.4 20.4 %collective-permute-start.29 = (bf16[16,2,16,128]{3,2,1,0:T(8,128)(2,1)S(1)}, bf16[16,2,16,128]{3,2,1,0:T(8,128)(2,1)S(1)}, u32[]{:S(2)}, u32[]{:S(2)}) collective-permute-start(bf16[16,2,16,128]{3,2,1,0:T(8,128)(2,1)S(1)} %get-tuple-element.79), channel_id=1, source_target_pairs={{0,10},{2,8},{4,14},{6,12},{8,2},{10,0},{12,6},{14,4},{1,11},{3,9}... | collective-permute-start | bytes 393224 | tf_op jit(solution)/shard_map/ppermute | solution.py:157
  202.8 18.1 %collective-permute-start.30 = (bf16[16,2,16,128]{3,2,1,0:T(8,128)(2,1)S(1)}, bf16[16,2,16,128]{3,2,1,0:T(8,128)(2,1)}, u32[]{:S(2)}, u32[]{:S(2)}) collective-permute-start(bf16[16,2,16,128]{3,2,1,0:T(8,128)(2,1)S(1)} %get-tuple-element.78), channel_id=1, source_target_pairs={{0,12},{2,14},{4,0},{6,2},{8,4},{10,6},{12,8},{14,10},{1,13},{3,15... | collective-permute-start | bytes 393224 | tf_op jit(solution)/shard_map/ppermute | solution.py:157
  206.6 14.2 %collective-permute-start.31 = (bf16[16,2,16,128]{3,2,1,0:T(8,128)(2,1)S(1)}, bf16[16,2,16,128]{3,2,1,0:T(8,128)(2,1)}, u32[]{:S(2)}, u32[]{:S(2)}) collective-permute-start(bf16[16,2,16,128]{3,2,1,0:T(8,128)(2,1)S(1)} %get-tuple-element.77), channel_id=1, source_target_pairs={{0,14},{2,12},{4,2},{6,0},{8,6},{10,4},{12,10},{14,8},{1,15},{3,13... | collective-permute-start | bytes 393224 | tf_op jit(solution)/shard_map/ppermute | solution.py:157
  223.2 2.7 %collective-permute-start.32 = (bf16[16,2,2,16,512]{4,3,2,1,0:T(8,128)(2,1)S(1)}, bf16[16,2,2,16,512]{4,3,2,1,0:T(8,128)(2,1)S(1)}, u32[]{:S(2)}, u32[]{:S(2)}) collective-permute-start(bf16[16,2,2,16,512]{4,3,2,1,0:T(8,128)(2,1)S(1)} %bitcast_dynamic-update-slice_fusion), channel_id=1, source_target_pairs={{0,1},{1,0},{2,3},{3,2},{4,5},{5,4},{6,7},{7,6},{8,9},{9,8},{10,11... | collective-permute-start | bytes 3145736 | tf_op jit(solution)/shard_map/ppermute | solution.py:178

commit v9 on v4

--- a/solution.py
+++ b/solution.py
@@ -36,21 +36,52 @@
     return table.reshape(frame_len, frame_len).astype(jnp.bfloat16)
 
 
+def filter_kernel(taps_ref, own_ref, history_ref, out_ref):
+    spectra_here, inputs_here, frame_len = out_ref.shape
+    tile_rows, tile_cols = 16, 128
+    col_tiles = frame_len // tile_cols
+
+    def body(tile, carry):
+        r0 = pl.multiple_of((tile // col_tiles) * tile_rows, tile_rows)
+        c0 = pl.multiple_of((tile % col_tiles) * tile_cols, tile_cols)
+        taps = [taps_ref[k : k + 1, pl.ds(c0, tile_cols)] for k in range(TAPS)]
+        sums = [None] * spectra_here
+        for j in range(spectra_here + TAPS - 1):
+            if j < TAPS - 1:
+                col = (spectra_here - (TAPS - 1) + j) * frame_len
+                block = history_ref[pl.ds(r0, tile_rows), pl.ds(col + c0, tile_cols)]
+            else:
+                col = (j - (TAPS - 1)) * frame_len
+                block = own_ref[pl.ds(r0, tile_rows), pl.ds(col + c0, tile_cols)]
+            block = block.astype(jnp.float32)
+            for s in range(max(0, j - (TAPS - 1)), min(spectra_here - 1, j) + 1):
+                term = taps[j - s] * block
+                sums[s] = term if sums[s] is None else sums[s] + term
+        for s in range(spectra_here):
+            out_ref[s, pl.ds(r0, tile_rows), pl.ds(c0, tile_cols)] = sums[s].astype(out_ref.dtype)
+        return carry
+
+    lax.fori_loop(0, (inputs_here // tile_rows) * col_tiles, body, 0)
+
+
+def polyphase_filter(filter_taps, own, history, frame_len):
+    inputs_here = own.shape[0]
+    spectra_here = own.shape[1] // frame_len
+    return pl.pallas_call(
+        filter_kernel,
+        out_shape=jax.ShapeDtypeStruct((spectra_here, inputs_here, frame_len), jnp.bfloat16),
+        cost_estimate=pl.CostEstimate(
+            flops=2 * TAPS * own.size, bytes_accessed=3 * own.size * 2, transcendentals=0
+        ),
+    )(filter_taps, own, history)
+
+
 def per_device(voltages):
     inputs_here = voltages.shape[0]
     frame_len = 2 * CH
     spectra_here = voltages.shape[1] // frame_len
-    frames = voltages.reshape(inputs_here, spectra_here, frame_len).transpose(1, 0, 2)
-    last_frames = frames[spectra_here - (TAPS - 1) :]
-    history = shifted(last_frames, ("tm", "pol"), 1)
-    extended = jnp.concatenate([history, frames], axis=0)
-    filter_taps = prototype(TAPS, frame_len)
-    filtered = jnp.zeros((spectra_here, inputs_here, frame_len), jnp.float32)
-    for tap_index in range(TAPS):
-        filtered = filtered + filter_taps[tap_index] * extended[
-            tap_index : tap_index + spectra_here
-        ].astype(jnp.float32)
-    filtered = filtered.astype(jnp.bfloat16)
+    history = shifted(voltages, ("tm", "pol"), 1)
+    filtered = polyphase_filter(prototype(TAPS, frame_len), voltages, history, frame_len)
     spectra = lax.dot_general(
         dft_table_t(frame_len),
         filtered.reshape(spectra_here * inputs_here, frame_len),

time: 242 us -> 219 us (0.905)
  other arithmetic: 39.9 us -> 14.9 us
  Pallas kernels: 39.3 us -> 55.5 us
  local copies, waits for them, and re-layouts: 56.6 us -> 40.6 us
    convert_element_type x1 -> x0, other arithmetic: 25.6 us -> none  [per_device(): filtered = filtered.astype(jnp.bfloat16)]
    pallas_call x0 -> x1, Pallas kernels: none -> 16.2 us  [polyphase_filter(): pl.pallas_call(filter_kernel, out_shape=jax.ShapeDtypeStruct((spectra_her...]
    convert_element_type x1 -> x0, local copies, waits for them, and re-layouts: 6.55 us -> none  [per_device(): filtered = filtered.astype(jnp.bfloat16)]
    unnamed x22 -> x21, local copies, waits for them, and re-layouts: 7.8 us -> 1.45 us
    slice x2 -> x0, local copies, waits for them, and re-layouts: 4.35 us -> none  [the longest x1 4.34 us: per_device(): last_frames = frames[spectra_here - (TAPS - 1):]]
  transfers between devices with their start and end apart: 33 -> 33, of which waited for: 4 -> 4; matrix products, arithmetic and copies ran while one was open for 14% -> 16% of each run, Pallas kernels for 12% -> 14%
where the time goes in v9:
time: 219 us; the launch traced here: 218 us
  starting transfers between devices  86 us (39%)
  Pallas kernels  55.5 us (25%)
  local copies, waits for them, and re-layouts  40.6 us (19%)
  other arithmetic  14.9 us (7%)
  waiting for transfers between devices  12.3 us (6%)
  matrix products  6.95 us (3%)
    ppermute x28, starting transfers between devices, send_chunk(): block = lax.ppermute(block, ('inp', 'tm'), route)  81.4 us
    pallas_call x4, Pallas kernels, correlate(): pl.pallas_call(functools.partial(correlate_kernel, 1.0 / (depth // 2)), g...  39.2 us
    pallas_call x1, Pallas kernels, polyphase_filter(): pl.pallas_call(filter_kernel, out_shape=jax.ShapeDtypeStruct((spectra_her...  16.2 us
    dynamic_update_slice x32, local copies, waits for them, and re-layouts, assemble_chunk(): lax.dynamic_update_slice(half, block[:, :, None], (0, 0, tm_step, 0, sour...  13 us
    ppermute x28, waiting for transfers between devices, send_chunk(): block = lax.ppermute(block, ('inp', 'tm'), route)  9.6 us
    transpose x4, local copies, waits for them, and re-layouts, finish_chunk(): lhs = lhs.transpose(0, 1, 3, 2).reshape(own_channels, 2 * rows_here, depth)  9.58 us
    another operation x1, other arithmetic  8.49 us
    dot_general x1, matrix products, per_device(): lax.dot_general(dft_table_t(frame_len), filtered.reshape(spectra_here * i...  6.95 us
  transfers between devices with their start and end apart: 33, of which 4 were waited for; matrix products, arithmetic and copies ran while one was open for 16% of the time, Pallas kernels for 14%

profile of v9, /device:TPU:0, one launch (start us, length us, event | category | flops | bytes accessed | tf_op | source)
XLA Modules:
  0.0 217.5 jit_solution(989553894714742239)
XLA Ops:
  0.0 4.3 %collective-permute-start = (bf16[128,16384]{1,0:T(8,128)(2,1)}, bf16[128,16384]{1,0:T(8,128)(2,1)}, u32[]{:S(2)}, u32[]{:S(2)}) collective-permute-start(bf16[128,16384]{1,0:T(8,128)(2,1)} %own_ref.1), channel_id=1, source_target_pairs={{0,1},{1,2},{2,3},{4,5},{5,6},{6,7},{8,9},{9,10},{10,11},{12,13},{... | collective-permute-start | bytes 12582920 | tf_op jit(solution)/shard_map/ppermute | solution.py:17
  4.3 8.5 %negate_convert_fusion = (bf16[512,1,1024]{2,0,1:T(8,128)(2,1)S(1)}, bf16[512,1,1024]{2,0,1:T(8,128)(2,1)S(1)}) fusion(), kind=kLoop, calls=%fused_computation.24 | loop fusion | flops 8912896 | bytes 2097152 | tf_op jit(solution)/shard_map/convert.1
  13.0 2.2 copy.51
  15.2 2.3 %convert_element_type.36 = bf16[1024,1024]{1,0:T(8,128)(2,1)} reshape(bf16[512,2,1024]{2,1,0:T(2,128)(2,1)S(1)} %copy.51) | data formatting | bytes 4194304 | tf_op jit(solution)/shard_map/convert_element_type | solution.py:36
  17.4 1.1 fusion.14
  19.2 1.1 fusion.11.taps_ref
  20.3 16.2 %shard_map.17 = bf16[16,128,1024]{2,1,0:T(8,128)(2,1)} custom-call(f32[16,1024]{1,0:T(8,128)} %fusion.11.taps_ref, bf16[128,16384]{1,0:T(8,128)(2,1)} %own_ref.1, bf16[128,16384]{1,0:T(8,128)(2,1)} %collective-permute-done.history_ref), custom_call_target="tpu_custom_call" | custom-call | flops 67108864 | bytes 12582912 | tf_op jit(solution)/shard_map/pallas_call | solution.py:70
  36.6 7.0 %convert_bitcast_fusion = bf16[128,8,16,128]{3,1,2,0:T(8,128)(2,1)S(1)} fusion(bf16[1024,1024]{1,0:T(8,128)(2,1)S(1)} %copy-done.1, bf16[2048,1024]{1,0:T(8,128)(2,1)} %bitcast.185), kind=kOutput, calls=%fused_computation | convolution fusion | flops 4297064448 | bytes 10485760 | tf_op jit(solution)/shard_map/dot_general | solution.py:85
  43.5 1.4 copy.66
  44.9 2.2 %fusion.15 = (bf16[8,16,2,16,128]{4,3,2,1,0:T(8,128)(2,1)S(1)}, bf16[8,16,2,16,128]{4,3,2,1,0:T(8,128)(2,1)}, bf16[8,16,2,16,128]{4,3,2,1,0:T(8,128)(2,1)}, bf16[8,16,2,16,128]{4,3,2,1,0:T(8,128)(2,1)S(1)}) fusion(bf16[8,64,2,16,128]{4,3,2,1,0:T(8,128)(2,1)S(1)} %bitcast.167), kind=kLoop, calls=%fused_computation.111 | loop fusion | bytes 8388608 | tf_op jit(solution)/shard_map/slice | solution.py:103
  47.2 0.9 dynamic-slice_bitcast_fusion.24
  48.1 32.6 %collective-permute-start.1 = (bf16[16,2,16,128]{3,2,1,0:T(8,128)(2,1)}, bf16[16,2,16,128]{3,2,1,0:T(8,128)(2,1)}, u32[]{:S(2)}, u32[]{:S(2)}) collective-permute-start(bf16[16,2,16,128]{3,2,1,0:T(8,128)(2,1)} %get-tuple-element.113), channel_id=1, source_target_pairs={{0,2},{2,0},{4,6},{6,4},{8,10},{10,8},{12,14},{14,12},{1,3},{3,1},... | collective-permute-start | bytes 393224 | tf_op jit(solution)/shard_map/ppermute | solution.py:171
  80.7 1.6 collective-permute-start.2
  82.3 1.0 collective-permute-start.3
  83.3 1.6 collective-permute-start.4
  84.8 2.8 %collective-permute-start.5 = (bf16[16,2,16,128]{3,2,1,0:T(8,128)(2,1)S(1)}, bf16[16,2,16,128]{3,2,1,0:T(8,128)(2,1)S(1)}, u32[]{:S(2)}, u32[]{:S(2)}) collective-permute-start(bf16[16,2,16,128]{3,2,1,0:T(8,128)(2,1)S(1)} %get-tuple-element.109), channel_id=1, source_target_pairs={{0,10},{2,8},{4,14},{6,12},{8,2},{10,0},{12,6},{14,4},{1,11},{3,9}... | collective-permute-start | bytes 393224 | tf_op jit(solution)/shard_map/ppermute | solution.py:171
  87.8 2.3 %collective-permute-start.6 = (bf16[16,2,16,128]{3,2,1,0:T(8,128)(2,1)S(1)}, bf16[16,2,16,128]{3,2,1,0:T(8,128)(2,1)S(1)}, u32[]{:S(2)}, u32[]{:S(2)}) collective-permute-start(bf16[16,2,16,128]{3,2,1,0:T(8,128)(2,1)S(1)} %get-tuple-element.108), channel_id=1, source_target_pairs={{0,12},{2,14},{4,0},{6,2},{8,4},{10,6},{12,8},{14,10},{1,13},{3,15... | collective-permute-start | bytes 393224 | tf_op jit(solution)/shard_map/ppermute | solution.py:171
  90.1 0.9 bitcast_dynamic-update-slice_fusion.30
  91.9 6.3 %collective-permute-done.4 = bf16[16,2,16,128]{3,2,1,0:T(8,128)(2,1)S(1)} collective-permute-done((bf16[16,2,16,128]{3,2,1,0:T(8,128)(2,1)}, bf16[16,2,16,128]{3,2,1,0:T(8,128)(2,1)S(1)}, u32[]{:S(2)}, u32[]{:S(2)}) %collective-permute-start.4) | collective-permute-done | bytes 131104 | tf_op jit(solution)/shard_map/ppermute | solution.py:171
  98.3 2.9 %collective-permute-done.5 = bf16[16,2,16,128]{3,2,1,0:T(8,128)(2,1)S(1)} collective-permute-done((bf16[16,2,16,128]{3,2,1,0:T(8,128)(2,1)S(1)}, bf16[16,2,16,128]{3,2,1,0:T(8,128)(2,1)S(1)}, u32[]{:S(2)}, u32[]{:S(2)}) %collective-permute-start.5) | collective-permute-done | bytes 131104 | tf_op jit(solution)/shard_map/ppermute | solution.py:171
  101.7 2.1 dynamic-slice_bitcast_fusion.16
  103.9 5.6 %collective-permute-start.10 = (bf16[16,2,16,128]{3,2,1,0:T(8,128)(2,1)S(1)}, bf16[16,2,16,128]{3,2,1,0:T(8,128)(2,1)S(1)}, u32[]{:S(2)}, u32[]{:S(2)}) collective-permute-start(bf16[16,2,16,128]{3,2,1,0:T(8,128)(2,1)S(1)} %get-tuple-element.102), channel_id=1, source_target_pairs={{0,4},{2,6},{4,8},{6,10},{8,12},{10,14},{12,0},{14,2},{1,5},{3,7},... | collective-permute-start | bytes 393224 | tf_op jit(solution)/shard_map/ppermute | solution.py:171
  110.2 1.8 collective-permute-start.12
  112.0 1.3 collective-permute-start.13
  113.3 3.8 %collective-permute-start.14 = (bf16[16,2,16,128]{3,2,1,0:T(8,128)(2,1)}, bf16[16,2,16,128]{3,2,1,0:T(8,128)(2,1)}, u32[]{:S(2)}, u32[]{:S(2)}) collective-permute-start(bf16[16,2,16,128]{3,2,1,0:T(8,128)(2,1)} %get-tuple-element.98), channel_id=1, source_target_pairs={{0,12},{2,14},{4,0},{6,2},{8,4},{10,6},{12,8},{14,10},{1,13},{3,15... | collective-permute-start | bytes 393224 | tf_op jit(solution)/shard_map/ppermute | solution.py:171
  117.2 1.5 pad_maximum_fusion
  119.0 1.0 collective-permute-start.15
  120.9 2.4 %copy.53 = bf16[16,2,256,128]{3,2,1,0:T(8,128)(2,1)} copy(bf16[16,2,256,128]{2,3,0,1:T(8,128)(2,1)S(1)} %maximum_bitcast_fusion) | data formatting | bytes 4194304 | tf_op jit(solution)/shard_map/transpose | solution.py:203
  123.3 9.8 %shard_map.18.rest_0_ = f32[64,2,256,512]{3,2,1,0:T(8,128)} custom-call(bf16[16,512,128]{2,1,0:T(8,128)(2,1)} %bitcast.184, bf16[16,128,512]{2,1,0:T(8,128)(2,1)} %bitcast.183), custom_call_target="tpu_custom_call" | custom-call | flops 1073741824 | bytes 20971520 | tf_op jit(solution)/shard_map/pallas_call | solution.py:146
  133.3 1.0 bitcast_dynamic-update-slice_fusion.22
  134.5 0.9 bitcast_dynamic-update-slice_fusion.19
  135.4 0.9 bitcast_dynamic-update-slice_fusion.18
  136.4 0.9 bitcast_dynamic-update-slice_fusion.17
  137.3 0.9 bitcast_dynamic-update-slice_fusion.16
  138.4 0.9 dynamic-slice_bitcast_fusion.8
  139.3 1.3 collective-permute-start.17
  140.6 2.0 collective-permute-start.18
  142.6 0.8 collective-permute-start.19
  143.4 1.7 collective-permute-start.20
  145.2 1.3 collective-permute-start.21
  147.2 3.9 %collective-permute-start.22 = (bf16[16,2,16,128]{3,2,1,0:T(8,128)(2,1)S(1)}, bf16[16,2,16,128]{3,2,1,0:T(8,128)(2,1)}, u32[]{:S(2)}, u32[]{:S(2)}) collective-permute-start(bf16[16,2,16,128]{3,2,1,0:T(8,128)(2,1)S(1)} %get-tuple-element.88), channel_id=1, source_target_pairs={{0,12},{2,14},{4,0},{6,2},{8,4},{10,6},{12,8},{14,10},{1,13},{3,15... | collective-permute-start | bytes 393224 | tf_op jit(solution)/shard_map/ppermute | solution.py:171
  151.1 0.9 collective-permute-start.23
  152.2 1.6 copy.57
  153.7 2.4 %copy.56 = bf16[16,2,256,128]{3,2,1,0:T(8,128)(2,1)} copy(bf16[16,2,256,128]{2,3,0,1:T(8,128)(2,1)S(1)} %maximum_bitcast_fusion.1) | data formatting | bytes 4194304 | tf_op jit(solution)/shard_map/transpose | solution.py:203
  156.1 9.8 %shard_map.19.rest_0_ = f32[64,2,256,512]{3,2,1,0:T(8,128)} custom-call(bf16[16,512,128]{2,1,0:T(8,128)(2,1)} %bitcast.180, bf16[16,128,512]{2,1,0:T(8,128)(2,1)} %bitcast.178, f32[64,2,256,512]{3,2,1,0:T(8,128)} %shard_map.18.rest_0_), custom_call_target="tpu_custom_call", output_to_operand_aliasing={{}: (2, {})} | custom-call | flops 1073741824 | bytes 20971520 | tf_op jit(solution)/shard_map/pallas_call | solution.py:146
  166.3 0.9 bitcast_dynamic-update-slice_fusion.12
  167.2 0.9 bitcast_dynamic-update-slice_fusion.11
  168.2 0.9 bitcast_dynamic-update-slice_fusion.10
  169.1 0.9 bitcast_dynamic-update-slice_fusion.9
  170.1 0.9 bitcast_dynamic-update-slice_fusion.8
  171.3 1.2 collective-permute-start.25
  172.5 2.7 %collective-permute-start.26 = (bf16[16,2,16,128]{3,2,1,0:T(8,128)(2,1)S(1)}, bf16[16,2,16,128]{3,2,1,0:T(8,128)(2,1)S(1)}, u32[]{:S(2)}, u32[]{:S(2)}) collective-permute-start(bf16[16,2,16,128]{3,2,1,0:T(8,128)(2,1)S(1)} %get-tuple-element.82), channel_id=1, source_target_pairs={{0,4},{2,6},{4,8},{6,10},{8,12},{10,14},{12,0},{14,2},{1,5},{3,7},... | collective-permute-start | bytes 393224 | tf_op jit(solution)/shard_map/ppermute | solution.py:171
  175.3 1.9 collective-permute-start.28
  177.2 1.8 collective-permute-start.29
  179.7 3.9 %collective-permute-start.30 = (bf16[16,2,16,128]{3,2,1,0:T(8,128)(2,1)S(1)}, bf16[16,2,16,128]{3,2,1,0:T(8,128)(2,1)}, u32[]{:S(2)}, u32[]{:S(2)}) collective-permute-start(bf16[16,2,16,128]{3,2,1,0:T(8,128)(2,1)S(1)} %get-tuple-element.78), channel_id=1, source_target_pairs={{0,12},{2,14},{4,0},{6,2},{8,4},{10,6},{12,8},{14,10},{1,13},{3,15... | collective-permute-start | bytes 393224 | tf_op jit(solution)/shard_map/ppermute | solution.py:171
  184.0 1.6 copy.61
  185.6 2.4 %copy.60 = bf16[16,2,256,128]{3,2,1,0:T(8,128)(2,1)} copy(bf16[16,2,256,128]{2,3,0,1:T(8,128)(2,1)S(1)} %maximum_bitcast_fusion.2) | data formatting | bytes 4194304 | tf_op jit(solution)/shard_map/transpose | solution.py:203
  188.0 9.8 %shard_map.20.rest_0_ = f32[64,2,256,512]{3,2,1,0:T(8,128)} custom-call(bf16[16,512,128]{2,1,0:T(8,128)(2,1)} %bitcast.181, bf16[16,128,512]{2,1,0:T(8,128)(2,1)} %bitcast.179, f32[64,2,256,512]{3,2,1,0:T(8,128)} %shard_map.19.rest_0_), custom_call_target="tpu_custom_call", output_to_operand_aliasing={{}: (2, {})} | custom-call | flops 1073741824 | bytes 20971520 | tf_op jit(solution)/shard_map/pallas_call | solution.py:146
  198.2 0.9 bitcast_dynamic-update-slice_fusion.1
  199.2 0.9 bitcast_dynamic-update-slice_fusion
  200.2 2.6 %collective-permute-done.32 = bf16[16,2,2,16,512]{4,3,2,1,0:T(8,128)(2,1)S(1)} collective-permute-done((bf16[16,2,2,16,512]{4,3,2,1,0:T(8,128)(2,1)S(1)}, bf16[16,2,2,16,512]{4,3,2,1,0:T(8,128)(2,1)S(1)}, u32[]{:S(2)}, u32[]{:S(2)}) %collective-permute-start.32) | collective-permute-done | bytes 1048608 | tf_op jit(solution)/shard_map/ppermute | solution.py:192
  203.3 1.6 copy.65
  205.3 2.4 %copy.64 = bf16[16,2,256,128]{3,2,1,0:T(8,128)(2,1)} copy(bf16[16,2,256,128]{2,3,0,1:T(8,128)(2,1)S(1)} %maximum_bitcast_fusion.3) | data formatting | bytes 4194304 | tf_op jit(solution)/shard_map/transpose | solution.py:203
  207.7 9.8 %shard_map.21 = f32[64,2,256,512]{3,2,1,0:T(8,128)} custom-call(bf16[16,512,128]{2,1,0:T(8,128)(2,1)} %bitcast.182, bf16[16,128,512]{2,1,0:T(8,128)(2,1)} %bitcast.177, f32[64,2,256,512]{3,2,1,0:T(8,128)} %shard_map.20.rest_0_), custom_call_target="tpu_custom_call", output_to_operand_aliasing={{}: (2, {})} | custom-call | flops 1073741824 | bytes 20971520 | tf_op jit(solution)/shard_map/pallas_call | solution.py:146
  (109 shorter events, 8.0 us)
Async XLA Ops:
  0.0 20.3 %collective-permute-start = (bf16[128,16384]{1,0:T(8,128)(2,1)}, bf16[128,16384]{1,0:T(8,128)(2,1)}, u32[]{:S(2)}, u32[]{:S(2)}) collective-permute-start(bf16[128,16384]{1,0:T(8,128)(2,1)} %own_ref.1), channel_id=1, source_target_pairs={{0,1},{1,2},{2,3},{4,5},{5,6},{6,7},{8,9},{9,10},{10,11},{12,13},{... | collective-permute-start | bytes 12582920 | tf_op jit(solution)/shard_map/ppermute | solution.py:17
  20.3 16.2 %copy-start.1 = (bf16[1024,1024]{1,0:T(8,128)(2,1)S(1)}, bf16[1024,1024]{1,0:T(8,128)(2,1)}, u32[]{:S(2)}) copy-start(bf16[1024,1024]{1,0:T(8,128)(2,1)} %convert_element_type.36) | copy-start | bytes 6291460
  48.1 39.8 %collective-permute-start.1 = (bf16[16,2,16,128]{3,2,1,0:T(8,128)(2,1)}, bf16[16,2,16,128]{3,2,1,0:T(8,128)(2,1)}, u32[]{:S(2)}, u32[]{:S(2)}) collective-permute-start(bf16[16,2,16,128]{3,2,1,0:T(8,128)(2,1)} %get-tuple-element.113), channel_id=1, source_target_pairs={{0,2},{2,0},{4,6},{6,4},{8,10},{10,8},{12,14},{14,12},{1,3},{3,1},... | collective-permute-start | bytes 393224 | tf_op jit(solution)/shard_map/ppermute | solution.py:171
  80.7 10.4 %collective-permute-start.2 = (bf16[16,2,16,128]{3,2,1,0:T(8,128)(2,1)}, bf16[16,2,16,128]{3,2,1,0:T(8,128)(2,1)S(1)}, u32[]{:S(2)}, u32[]{:S(2)}) collective-permute-start(bf16[16,2,16,128]{3,2,1,0:T(8,128)(2,1)} %get-tuple-element.112), channel_id=1, source_target_pairs={{0,4},{2,6},{4,8},{6,10},{8,12},{10,14},{12,0},{14,2},{1,5},{3,7},... | collective-permute-start | bytes 393224 | tf_op jit(solution)/shard_map/ppermute | solution.py:171
  82.3 9.6 %collective-permute-start.3 = (bf16[16,2,16,128]{3,2,1,0:T(8,128)(2,1)}, bf16[16,2,16,128]{3,2,1,0:T(8,128)(2,1)S(1)}, u32[]{:S(2)}, u32[]{:S(2)}) collective-permute-start(bf16[16,2,16,128]{3,2,1,0:T(8,128)(2,1)} %get-tuple-element.111), channel_id=1, source_target_pairs={{0,6},{2,4},{4,10},{6,8},{8,14},{10,12},{12,2},{14,0},{1,7},{3,5},... | collective-permute-start | bytes 393224 | tf_op jit(solution)/shard_map/ppermute | solution.py:171
  83.3 15.0 %collective-permute-start.4 = (bf16[16,2,16,128]{3,2,1,0:T(8,128)(2,1)}, bf16[16,2,16,128]{3,2,1,0:T(8,128)(2,1)S(1)}, u32[]{:S(2)}, u32[]{:S(2)}) collective-permute-start(bf16[16,2,16,128]{3,2,1,0:T(8,128)(2,1)} %get-tuple-element.110), channel_id=1, source_target_pairs={{0,8},{2,10},{4,12},{6,14},{8,0},{10,2},{12,4},{14,6},{1,9},{3,11}... | collective-permute-start | bytes 393224 | tf_op jit(solution)/shard_map/ppermute | solution.py:171
  84.8 16.3 %collective-permute-start.5 = (bf16[16,2,16,128]{3,2,1,0:T(8,128)(2,1)S(1)}, bf16[16,2,16,128]{3,2,1,0:T(8,128)(2,1)S(1)}, u32[]{:S(2)}, u32[]{:S(2)}) collective-permute-start(bf16[16,2,16,128]{3,2,1,0:T(8,128)(2,1)S(1)} %get-tuple-element.109), channel_id=1, source_target_pairs={{0,10},{2,8},{4,14},{6,12},{8,2},{10,0},{12,6},{14,4},{1,11},{3,9}... | collective-permute-start | bytes 393224 | tf_op jit(solution)/shard_map/ppermute | solution.py:171
  87.8 13.4 %collective-permute-start.6 = (bf16[16,2,16,128]{3,2,1,0:T(8,128)(2,1)S(1)}, bf16[16,2,16,128]{3,2,1,0:T(8,128)(2,1)S(1)}, u32[]{:S(2)}, u32[]{:S(2)}) collective-permute-start(bf16[16,2,16,128]{3,2,1,0:T(8,128)(2,1)S(1)} %get-tuple-element.108), channel_id=1, source_target_pairs={{0,12},{2,14},{4,0},{6,2},{8,4},{10,6},{12,8},{14,10},{1,13},{3,15... | collective-permute-start | bytes 393224 | tf_op jit(solution)/shard_map/ppermute | solution.py:171
  91.1 10.5 %collective-permute-start.7 = (bf16[16,2,16,128]{3,2,1,0:T(8,128)(2,1)S(1)}, bf16[16,2,16,128]{3,2,1,0:T(8,128)(2,1)S(1)}, u32[]{:S(2)}, u32[]{:S(2)}) collective-permute-start(bf16[16,2,16,128]{3,2,1,0:T(8,128)(2,1)S(1)} %get-tuple-element.107), channel_id=1, source_target_pairs={{0,14},{2,12},{4,2},{6,0},{8,6},{10,4},{12,10},{14,8},{1,15},{3,13... | collective-permute-start | bytes 393224 | tf_op jit(solution)/shard_map/ppermute | solution.py:171
  101.6 11.7 %collective-permute-start.8 = (bf16[16,2,2,16,512]{4,3,2,1,0:T(8,128)(2,1)S(1)}, bf16[16,2,2,16,512]{4,3,2,1,0:T(8,128)(2,1)S(1)}, u32[]{:S(2)}, u32[]{:S(2)}) collective-permute-start(bf16[16,2,2,16,512]{4,3,2,1,0:T(8,128)(2,1)S(1)} %bitcast_dynamic-update-slice_fusion.24), channel_id=1, source_target_pairs={{0,1},{1,0},{2,3},{3,2},{4,5},{5,4},{6,7},{7,6},{8,9},{9,8},{10,11... | collective-permute-start | bytes 3145736 | tf_op jit(solution)/shard_map/ppermute | solution.py:192
  103.9 15.1 %collective-permute-start.10 = (bf16[16,2,16,128]{3,2,1,0:T(8,128)(2,1)S(1)}, bf16[16,2,16,128]{3,2,1,0:T(8,128)(2,1)S(1)}, u32[]{:S(2)}, u32[]{:S(2)}) collective-permute-start(bf16[16,2,16,128]{3,2,1,0:T(8,128)(2,1)S(1)} %get-tuple-element.102), channel_id=1, source_target_pairs={{0,4},{2,6},{4,8},{6,10},{8,12},{10,14},{12,0},{14,2},{1,5},{3,7},... | collective-permute-start | bytes 393224 | tf_op jit(solution)/shard_map/ppermute | solution.py:171
  109.5 10.5 %collective-permute-start.11 = (bf16[16,2,16,128]{3,2,1,0:T(8,128)(2,1)S(1)}, bf16[16,2,16,128]{3,2,1,0:T(8,128)(2,1)S(1)}, u32[]{:S(2)}, u32[]{:S(2)}) collective-permute-start(bf16[16,2,16,128]{3,2,1,0:T(8,128)(2,1)S(1)} %get-tuple-element.101), channel_id=1, source_target_pairs={{0,6},{2,4},{4,10},{6,8},{8,14},{10,12},{12,2},{14,0},{1,7},{3,5},... | collective-permute-start | bytes 393224 | tf_op jit(solution)/shard_map/ppermute | solution.py:171
  110.2 22.9 %collective-permute-start.12 = (bf16[16,2,16,128]{3,2,1,0:T(8,128)(2,1)}, bf16[16,2,16,128]{3,2,1,0:T(8,128)(2,1)}, u32[]{:S(2)}, u32[]{:S(2)}) collective-permute-start(bf16[16,2,16,128]{3,2,1,0:T(8,128)(2,1)} %get-tuple-element.100), channel_id=1, source_target_pairs={{0,8},{2,10},{4,12},{6,14},{8,0},{10,2},{12,4},{14,6},{1,9},{3,11}... | collective-permute-start | bytes 393224 | tf_op jit(solution)/shard_map/ppermute | solution.py:171
  112.0 21.1 %collective-permute-start.13 = (bf16[16,2,16,128]{3,2,1,0:T(8,128)(2,1)}, bf16[16,2,16,128]{3,2,1,0:T(8,128)(2,1)}, u32[]{:S(2)}, u32[]{:S(2)}) collective-permute-start(bf16[16,2,16,128]{3,2,1,0:T(8,128)(2,1)} %get-tuple-element.99), channel_id=1, source_target_pairs={{0,10},{2,8},{4,14},{6,12},{8,2},{10,0},{12,6},{14,4},{1,11},{3,9}... | collective-permute-start | bytes 393224 | tf_op jit(solution)/shard_map/ppermute | solution.py:171
  113.3 19.8 %collective-permute-start.14 = (bf16[16,2,16,128]{3,2,1,0:T(8,128)(2,1)}, bf16[16,2,16,128]{3,2,1,0:T(8,128)(2,1)}, u32[]{:S(2)}, u32[]{:S(2)}) collective-permute-start(bf16[16,2,16,128]{3,2,1,0:T(8,128)(2,1)} %get-tuple-element.98), channel_id=1, source_target_pairs={{0,12},{2,14},{4,0},{6,2},{8,4},{10,6},{12,8},{14,10},{1,13},{3,15... | collective-permute-start | bytes 393224 | tf_op jit(solution)/shard_map/ppermute | solution.py:171
  119.0 1.7 copy-start.6
  119.0 14.2 %collective-permute-start.15 = (bf16[16,2,16,128]{3,2,1,0:T(8,128)(2,1)S(1)}, bf16[16,2,16,128]{3,2,1,0:T(8,128)(2,1)}, u32[]{:S(2)}, u32[]{:S(2)}) collective-permute-start(bf16[16,2,16,128]{3,2,1,0:T(8,128)(2,1)S(1)} %get-tuple-element.97), channel_id=1, source_target_pairs={{0,14},{2,12},{4,2},{6,0},{8,6},{10,4},{12,10},{14,8},{1,15},{3,13... | collective-permute-start | bytes 393224 | tf_op jit(solution)/shard_map/ppermute | solution.py:171
  120.0 0.7 copy-start.8
  120.0 13.2 %collective-permute-start.9 = (bf16[16,2,16,128]{3,2,1,0:T(8,128)(2,1)S(1)}, bf16[16,2,16,128]{3,2,1,0:T(8,128)(2,1)}, u32[]{:S(2)}, u32[]{:S(2)}) collective-permute-start(bf16[16,2,16,128]{3,2,1,0:T(8,128)(2,1)S(1)} %get-tuple-element.103), channel_id=1, source_target_pairs={{0,2},{2,0},{4,6},{6,4},{8,10},{10,8},{12,14},{14,12},{1,3},{3,1},... | collective-permute-start | bytes 393224 | tf_op jit(solution)/shard_map/ppermute | solution.py:171
  123.3 11.1 %copy-start.7 = (bf16[16,2,16,128]{3,2,1,0:T(8,128)(2,1)S(1)}, bf16[16,2,16,128]{3,2,1,0:T(8,128)(2,1)}, u32[]{:S(2)}) copy-start(bf16[16,2,16,128]{3,2,1,0:T(8,128)(2,1)} %copy-done.6) | copy-start | bytes 393220
  123.3 11.1 %copy-start.9 = (bf16[16,2,16,128]{3,2,1,0:T(8,128)(2,1)S(1)}, bf16[16,2,16,128]{3,2,1,0:T(8,128)(2,1)}, u32[]{:S(2)}) copy-start(bf16[16,2,16,128]{3,2,1,0:T(8,128)(2,1)} %copy-done.8) | copy-start | bytes 393220
  133.1 5.2 %copy-start = (bf16[8,16,2,16,128]{4,3,2,1,0:T(8,128)(2,1)S(1)}, bf16[8,16,2,16,128]{4,3,2,1,0:T(8,128)(2,1)}, u32[]{:S(2)}) copy-start(bf16[8,16,2,16,128]{4,3,2,1,0:T(8,128)(2,1)} %get-tuple-element.50) | copy-start | bytes 3145732
  138.3 6.9 %collective-permute-start.16 = (bf16[16,2,2,16,512]{4,3,2,1,0:T(8,128)(2,1)S(1)}, bf16[16,2,2,16,512]{4,3,2,1,0:T(8,128)(2,1)S(1)}, u32[]{:S(2)}, u32[]{:S(2)}) collective-permute-start(bf16[16,2,2,16,512]{4,3,2,1,0:T(8,128)(2,1)S(1)} %bitcast_dynamic-update-slice_fusion.16), channel_id=1, source_target_pairs={{0,1},{1,0},{2,3},{3,2},{4,5},{5,4},{6,7},{7,6},{8,9},{9,8},{10,11... | collective-permute-start | bytes 3145736 | tf_op jit(solution)/shard_map/ppermute | solution.py:192
  139.3 7.9 %collective-permute-start.17 = (bf16[16,2,16,128]{3,2,1,0:T(8,128)(2,1)S(1)}, bf16[16,2,16,128]{3,2,1,0:T(8,128)(2,1)S(1)}, u32[]{:S(2)}, u32[]{:S(2)}) collective-permute-start(bf16[16,2,16,128]{3,2,1,0:T(8,128)(2,1)S(1)} %get-tuple-element.93), channel_id=1, source_target_pairs={{0,2},{2,0},{4,6},{6,4},{8,10},{10,8},{12,14},{14,12},{1,3},{3,1},... | collective-permute-start | bytes 393224 | tf_op jit(solution)/shard_map/ppermute | solution.py:171
  140.6 10.5 %collective-permute-start.18 = (bf16[16,2,16,128]{3,2,1,0:T(8,128)(2,1)S(1)}, bf16[16,2,16,128]{3,2,1,0:T(8,128)(2,1)S(1)}, u32[]{:S(2)}, u32[]{:S(2)}) collective-permute-start(bf16[16,2,16,128]{3,2,1,0:T(8,128)(2,1)S(1)} %get-tuple-element.92), channel_id=1, source_target_pairs={{0,4},{2,6},{4,8},{6,10},{8,12},{10,14},{12,0},{14,2},{1,5},{3,7},... | collective-permute-start | bytes 393224 | tf_op jit(solution)/shard_map/ppermute | solution.py:171
  142.6 23.3 %collective-permute-start.19 = (bf16[16,2,16,128]{3,2,1,0:T(8,128)(2,1)}, bf16[16,2,16,128]{3,2,1,0:T(8,128)(2,1)}, u32[]{:S(2)}, u32[]{:S(2)}) collective-permute-start(bf16[16,2,16,128]{3,2,1,0:T(8,128)(2,1)} %get-tuple-element.91), channel_id=1, source_target_pairs={{0,6},{2,4},{4,10},{6,8},{8,14},{10,12},{12,2},{14,0},{1,7},{3,5},... | collective-permute-start | bytes 393224 | tf_op jit(solution)/shard_map/ppermute | solution.py:171
  143.4 22.5 %collective-permute-start.20 = (bf16[16,2,16,128]{3,2,1,0:T(8,128)(2,1)}, bf16[16,2,16,128]{3,2,1,0:T(8,128)(2,1)}, u32[]{:S(2)}, u32[]{:S(2)}) collective-permute-start(bf16[16,2,16,128]{3,2,1,0:T(8,128)(2,1)} %get-tuple-element.90), channel_id=1, source_target_pairs={{0,8},{2,10},{4,12},{6,14},{8,0},{10,2},{12,4},{14,6},{1,9},{3,11}... | collective-permute-start | bytes 393224 | tf_op jit(solution)/shard_map/ppermute | solution.py:171
  145.2 20.8 %collective-permute-start.21 = (bf16[16,2,16,128]{3,2,1,0:T(8,128)(2,1)}, bf16[16,2,16,128]{3,2,1,0:T(8,128)(2,1)}, u32[]{:S(2)}, u32[]{:S(2)}) collective-permute-start(bf16[16,2,16,128]{3,2,1,0:T(8,128)(2,1)} %get-tuple-element.89), channel_id=1, source_target_pairs={{0,10},{2,8},{4,14},{6,12},{8,2},{10,0},{12,6},{14,4},{1,11},{3,9}... | collective-permute-start | bytes 393224 | tf_op jit(solution)/shard_map/ppermute | solution.py:171
  147.2 4.8 %copy-start.2 = (bf16[16,2,16,128]{3,2,1,0:T(8,128)(2,1)}, bf16[16,2,16,128]{3,2,1,0:T(8,128)(2,1)S(1)}, u32[]{:S(2)}) copy-start(bf16[16,2,16,128]{3,2,1,0:T(8,128)(2,1)S(1)} %collective-permute-done.17) | copy-start | bytes 393220
  147.2 18.8 %collective-permute-start.22 = (bf16[16,2,16,128]{3,2,1,0:T(8,128)(2,1)S(1)}, bf16[16,2,16,128]{3,2,1,0:T(8,128)(2,1)}, u32[]{:S(2)}, u32[]{:S(2)}) collective-permute-start(bf16[16,2,16,128]{3,2,1,0:T(8,128)(2,1)S(1)} %get-tuple-element.88), channel_id=1, source_target_pairs={{0,12},{2,14},{4,0},{6,2},{8,4},{10,6},{12,8},{14,10},{1,13},{3,15... | collective-permute-start | bytes 393224 | tf_op jit(solution)/shard_map/ppermute | solution.py:171
  151.1 0.9 copy-start.4
  151.1 14.9 %collective-permute-start.23 = (bf16[16,2,16,128]{3,2,1,0:T(8,128)(2,1)S(1)}, bf16[16,2,16,128]{3,2,1,0:T(8,128)(2,1)}, u32[]{:S(2)}, u32[]{:S(2)}) collective-permute-start(bf16[16,2,16,128]{3,2,1,0:T(8,128)(2,1)S(1)} %get-tuple-element.87), channel_id=1, source_target_pairs={{0,14},{2,12},{4,2},{6,0},{8,6},{10,4},{12,10},{14,8},{1,15},{3,13... | collective-permute-start | bytes 393224 | tf_op jit(solution)/shard_map/ppermute | solution.py:171
  156.1 10.1 %copy-start.3 = (bf16[16,2,16,128]{3,2,1,0:T(8,128)(2,1)S(1)}, bf16[16,2,16,128]{3,2,1,0:T(8,128)(2,1)}, u32[]{:S(2)}) copy-start(bf16[16,2,16,128]{3,2,1,0:T(8,128)(2,1)} %copy-done.2) | copy-start | bytes 393220
  156.1 10.1 %copy-start.5 = (bf16[16,2,16,128]{3,2,1,0:T(8,128)(2,1)S(1)}, bf16[16,2,16,128]{3,2,1,0:T(8,128)(2,1)}, u32[]{:S(2)}) copy-start(bf16[16,2,16,128]{3,2,1,0:T(8,128)(2,1)} %copy-done.4) | copy-start | bytes 393220
  171.0 6.2 %collective-permute-start.24 = (bf16[16,2,2,16,512]{4,3,2,1,0:T(8,128)(2,1)S(1)}, bf16[16,2,2,16,512]{4,3,2,1,0:T(8,128)(2,1)S(1)}, u32[]{:S(2)}, u32[]{:S(2)}) collective-permute-start(bf16[16,2,2,16,512]{4,3,2,1,0:T(8,128)(2,1)S(1)} %bitcast_dynamic-update-slice_fusion.8), channel_id=1, source_target_pairs={{0,1},{1,0},{2,3},{3,2},{4,5},{5,4},{6,7},{7,6},{8,9},{9,8},{10,11... | collective-permute-start | bytes 3145736 | tf_op jit(solution)/shard_map/ppermute | solution.py:192
  171.3 8.5 %collective-permute-start.25 = (bf16[16,2,16,128]{3,2,1,0:T(8,128)(2,1)S(1)}, bf16[16,2,16,128]{3,2,1,0:T(8,128)(2,1)S(1)}, u32[]{:S(2)}, u32[]{:S(2)}) collective-permute-start(bf16[16,2,16,128]{3,2,1,0:T(8,128)(2,1)S(1)} %get-tuple-element.83), channel_id=1, source_target_pairs={{0,2},{2,0},{4,6},{6,4},{8,10},{10,8},{12,14},{14,12},{1,3},{3,1},... | collective-permute-start | bytes 393224 | tf_op jit(solution)/shard_map/ppermute | solution.py:171
  172.5 11.1 %collective-permute-start.26 = (bf16[16,2,16,128]{3,2,1,0:T(8,128)(2,1)S(1)}, bf16[16,2,16,128]{3,2,1,0:T(8,128)(2,1)S(1)}, u32[]{:S(2)}, u32[]{:S(2)}) collective-permute-start(bf16[16,2,16,128]{3,2,1,0:T(8,128)(2,1)S(1)} %get-tuple-element.82), channel_id=1, source_target_pairs={{0,4},{2,6},{4,8},{6,10},{8,12},{10,14},{12,0},{14,2},{1,5},{3,7},... | collective-permute-start | bytes 393224 | tf_op jit(solution)/shard_map/ppermute | solution.py:171
  175.2 22.6 %collective-permute-start.27 = (bf16[16,2,16,128]{3,2,1,0:T(8,128)(2,1)S(1)}, bf16[16,2,16,128]{3,2,1,0:T(8,128)(2,1)S(1)}, u32[]{:S(2)}, u32[]{:S(2)}) collective-permute-start(bf16[16,2,16,128]{3,2,1,0:T(8,128)(2,1)S(1)} %get-tuple-element.81), channel_id=1, source_target_pairs={{0,6},{2,4},{4,10},{6,8},{8,14},{10,12},{12,2},{14,0},{1,7},{3,5},... | collective-permute-start | bytes 393224 | tf_op jit(solution)/shard_map/ppermute | solution.py:171
  175.3 22.5 %collective-permute-start.28 = (bf16[16,2,16,128]{3,2,1,0:T(8,128)(2,1)S(1)}, bf16[16,2,16,128]{3,2,1,0:T(8,128)(2,1)S(1)}, u32[]{:S(2)}, u32[]{:S(2)}) collective-permute-start(bf16[16,2,16,128]{3,2,1,0:T(8,128)(2,1)S(1)} %get-tuple-element.80), channel_id=1, source_target_pairs={{0,8},{2,10},{4,12},{6,14},{8,0},{10,2},{12,4},{14,6},{1,9},{3,11}... | collective-permute-start | bytes 393224 | tf_op jit(solution)/shard_map/ppermute | solution.py:171
  177.2 20.6 %collective-permute-start.29 = (bf16[16,2,16,128]{3,2,1,0:T(8,128)(2,1)S(1)}, bf16[16,2,16,128]{3,2,1,0:T(8,128)(2,1)S(1)}, u32[]{:S(2)}, u32[]{:S(2)}) collective-permute-start(bf16[16,2,16,128]{3,2,1,0:T(8,128)(2,1)S(1)} %get-tuple-element.79), channel_id=1, source_target_pairs={{0,10},{2,8},{4,14},{6,12},{8,2},{10,0},{12,6},{14,4},{1,11},{3,9}... | collective-permute-start | bytes 393224 | tf_op jit(solution)/shard_map/ppermute | solution.py:171
  179.7 18.1 %collective-permute-start.30 = (bf16[16,2,16,128]{3,2,1,0:T(8,128)(2,1)S(1)}, bf16[16,2,16,128]{3,2,1,0:T(8,128)(2,1)}, u32[]{:S(2)}, u32[]{:S(2)}) collective-permute-start(bf16[16,2,16,128]{3,2,1,0:T(8,128)(2,1)S(1)} %get-tuple-element.78), channel_id=1, source_target_pairs={{0,12},{2,14},{4,0},{6,2},{8,4},{10,6},{12,8},{14,10},{1,13},{3,15... | collective-permute-start | bytes 393224 | tf_op jit(solution)/shard_map/ppermute | solution.py:171
  183.6 14.2 %collective-permute-start.31 = (bf16[16,2,16,128]{3,2,1,0:T(8,128)(2,1)S(1)}, bf16[16,2,16,128]{3,2,1,0:T(8,128)(2,1)}, u32[]{:S(2)}, u32[]{:S(2)}) collective-permute-start(bf16[16,2,16,128]{3,2,1,0:T(8,128)(2,1)S(1)} %get-tuple-element.77), channel_id=1, source_target_pairs={{0,14},{2,12},{4,2},{6,0},{8,6},{10,4},{12,10},{14,8},{1,15},{3,13... | collective-permute-start | bytes 393224 | tf_op jit(solution)/shard_map/ppermute | solution.py:171
  200.1 2.7 %collective-permute-start.32 = (bf16[16,2,2,16,512]{4,3,2,1,0:T(8,128)(2,1)S(1)}, bf16[16,2,2,16,512]{4,3,2,1,0:T(8,128)(2,1)S(1)}, u32[]{:S(2)}, u32[]{:S(2)}) collective-permute-start(bf16[16,2,2,16,512]{4,3,2,1,0:T(8,128)(2,1)S(1)} %bitcast_dynamic-update-slice_fusion), channel_id=1, source_target_pairs={{0,1},{1,0},{2,3},{3,2},{4,5},{5,4},{6,7},{7,6},{8,9},{9,8},{10,11... | collective-permute-start | bytes 3145736 | tf_op jit(solution)/shard_map/ppermute | solution.py:192

commit v10 on v9

--- a/solution.py
+++ b/solution.py
@@ -67,8 +67,16 @@
 def polyphase_filter(filter_taps, own, history, frame_len):
     inputs_here = own.shape[0]
     spectra_here = own.shape[1] // frame_len
+    rows = 32 if inputs_here % 32 == 0 else inputs_here
     return pl.pallas_call(
         filter_kernel,
+        grid=(inputs_here // rows,),
+        in_specs=[
+            pl.BlockSpec((TAPS, frame_len), lambda r: (0, 0)),
+            pl.BlockSpec((rows, spectra_here * frame_len), lambda r: (r, 0)),
+            pl.BlockSpec((rows, spectra_here * frame_len), lambda r: (r, 0)),
+        ],
+        out_specs=pl.BlockSpec((spectra_here, rows, frame_len), lambda r: (0, r, 0)),
         out_shape=jax.ShapeDtypeStruct((spectra_here, inputs_here, frame_len), jnp.bfloat16),
         cost_estimate=pl.CostEstimate(
             flops=2 * TAPS * own.size, bytes_accessed=3 * own.size * 2, transcendentals=0

time: 219 us -> 216 us (0.986)
  Pallas kernels: 55.5 us -> 52.4 us
    pallas_call x1, Pallas kernels: 16.2 us -> 13.1 us  [polyphase_filter(): pl.pallas_call(filter_kernel, grid=(inputs_here // rows,), in_specs=[pl.B...]
where the time goes in v10:
time: 216 us; the launch traced here: 214 us
  starting transfers between devices  85.9 us (40%)
  Pallas kernels  52.4 us (24%)
  local copies, waits for them, and re-layouts  40.6 us (19%)
  other arithmetic  14.9 us (7%)
  waiting for transfers between devices  12.3 us (6%)
  matrix products  6.95 us (3%)
    ppermute x28, starting transfers between devices, send_chunk(): block = lax.ppermute(block, ('inp', 'tm'), route)  81.3 us
    pallas_call x4, Pallas kernels, correlate(): pl.pallas_call(functools.partial(correlate_kernel, 1.0 / (depth // 2)), g...  39.3 us
    pallas_call x1, Pallas kernels, polyphase_filter(): pl.pallas_call(filter_kernel, grid=(inputs_here // rows,), in_specs=[pl.B...  13.1 us
    dynamic_update_slice x32, local copies, waits for them, and re-layouts, assemble_chunk(): lax.dynamic_update_slice(half, block[:, :, None], (0, 0, tm_step, 0, sour...  13 us
    ppermute x28, waiting for transfers between devices, send_chunk(): block = lax.ppermute(block, ('inp', 'tm'), route)  9.6 us
    transpose x4, local copies, waits for them, and re-layouts, finish_chunk(): lhs = lhs.transpose(0, 1, 3, 2).reshape(own_channels, 2 * rows_here, depth)  9.58 us
    another operation x1, other arithmetic  8.49 us
    dot_general x1, matrix products, per_device(): lax.dot_general(dft_table_t(frame_len), filtered.reshape(spectra_here * i...  6.95 us
  transfers between devices with their start and end apart: 33, of which 4 were waited for; matrix products, arithmetic and copies ran while one was open for 16% of the time, Pallas kernels for 14%

profile of v10, /device:TPU:0, one launch (start us, length us, event | category | flops | bytes accessed | tf_op | source)
XLA Modules:
  0.0 214.4 jit_solution(16557164518615723921)
XLA Ops:
  0.0 4.3 %collective-permute-start = (bf16[128,16384]{1,0:T(8,128)(2,1)}, bf16[128,16384]{1,0:T(8,128)(2,1)}, u32[]{:S(2)}, u32[]{:S(2)}) collective-permute-start(bf16[128,16384]{1,0:T(8,128)(2,1)} %own_ref.1), channel_id=1, source_target_pairs={{0,1},{1,2},{2,3},{4,5},{5,6},{6,7},{8,9},{9,10},{10,11},{12,13},{... | collective-permute-start | bytes 12582920 | tf_op jit(solution)/shard_map/ppermute | solution.py:17
  4.3 8.5 %negate_convert_fusion = (bf16[512,1,1024]{2,0,1:T(8,128)(2,1)S(1)}, bf16[512,1,1024]{2,0,1:T(8,128)(2,1)S(1)}) fusion(), kind=kLoop, calls=%fused_computation.24 | loop fusion | flops 8912896 | bytes 2097152 | tf_op jit(solution)/shard_map/convert.1
  13.0 2.2 %copy.51 = bf16[512,2,1024]{2,1,0:T(2,128)(2,1)S(1)} copy(bf16[512,2,1024]{2,0,1:T(8,128)(2,1)S(1)} %pad_maximum_fusion.4) | data formatting | bytes 4194304 | tf_op jit(solution)/shard_map/stack | solution.py:35
  15.2 2.3 %convert_element_type.36 = bf16[1024,1024]{1,0:T(8,128)(2,1)} reshape(bf16[512,2,1024]{2,1,0:T(2,128)(2,1)S(1)} %copy.51) | data formatting | bytes 4194304 | tf_op jit(solution)/shard_map/convert_element_type | solution.py:36
  17.4 1.1 fusion.14
  19.2 1.1 fusion.11.taps_ref
  20.3 13.1 %shard_map.17 = bf16[16,128,1024]{2,1,0:T(8,128)(2,1)} custom-call(f32[16,1024]{1,0:T(8,128)} %fusion.11.taps_ref, bf16[128,16384]{1,0:T(8,128)(2,1)} %own_ref.1, bf16[128,16384]{1,0:T(8,128)(2,1)} %collective-permute-done.history_ref), custom_call_target="tpu_custom_call" | custom-call | flops 67108864 | bytes 12582912 | tf_op jit(solution)/shard_map/pallas_call | solution.py:71
  33.5 7.0 %convert_bitcast_fusion = bf16[128,8,16,128]{3,1,2,0:T(8,128)(2,1)S(1)} fusion(bf16[1024,1024]{1,0:T(8,128)(2,1)S(1)} %copy-done.1, bf16[2048,1024]{1,0:T(8,128)(2,1)} %bitcast.185), kind=kOutput, calls=%fused_computation | convolution fusion | flops 4297064448 | bytes 10485760 | tf_op jit(solution)/shard_map/dot_general | solution.py:93
  40.4 1.4 copy.66
  41.8 2.2 %fusion.15 = (bf16[8,16,2,16,128]{4,3,2,1,0:T(8,128)(2,1)S(1)}, bf16[8,16,2,16,128]{4,3,2,1,0:T(8,128)(2,1)}, bf16[8,16,2,16,128]{4,3,2,1,0:T(8,128)(2,1)}, bf16[8,16,2,16,128]{4,3,2,1,0:T(8,128)(2,1)S(1)}) fusion(bf16[8,64,2,16,128]{4,3,2,1,0:T(8,128)(2,1)S(1)} %bitcast.167), kind=kLoop, calls=%fused_computation.111 | loop fusion | bytes 8388608 | tf_op jit(solution)/shard_map/slice | solution.py:111
  44.1 0.9 dynamic-slice_bitcast_fusion.24
  45.0 32.6 %collective-permute-start.1 = (bf16[16,2,16,128]{3,2,1,0:T(8,128)(2,1)}, bf16[16,2,16,128]{3,2,1,0:T(8,128)(2,1)}, u32[]{:S(2)}, u32[]{:S(2)}) collective-permute-start(bf16[16,2,16,128]{3,2,1,0:T(8,128)(2,1)} %get-tuple-element.113), channel_id=1, source_target_pairs={{0,2},{2,0},{4,6},{6,4},{8,10},{10,8},{12,14},{14,12},{1,3},{3,1},... | collective-permute-start | bytes 393224 | tf_op jit(solution)/shard_map/ppermute | solution.py:179
  77.6 1.6 collective-permute-start.2
  79.1 1.0 collective-permute-start.3
  80.2 1.6 collective-permute-start.4
  81.7 2.8 %collective-permute-start.5 = (bf16[16,2,16,128]{3,2,1,0:T(8,128)(2,1)S(1)}, bf16[16,2,16,128]{3,2,1,0:T(8,128)(2,1)S(1)}, u32[]{:S(2)}, u32[]{:S(2)}) collective-permute-start(bf16[16,2,16,128]{3,2,1,0:T(8,128)(2,1)S(1)} %get-tuple-element.109), channel_id=1, source_target_pairs={{0,10},{2,8},{4,14},{6,12},{8,2},{10,0},{12,6},{14,4},{1,11},{3,9}... | collective-permute-start | bytes 393224 | tf_op jit(solution)/shard_map/ppermute | solution.py:179
  84.7 2.3 %collective-permute-start.6 = (bf16[16,2,16,128]{3,2,1,0:T(8,128)(2,1)S(1)}, bf16[16,2,16,128]{3,2,1,0:T(8,128)(2,1)S(1)}, u32[]{:S(2)}, u32[]{:S(2)}) collective-permute-start(bf16[16,2,16,128]{3,2,1,0:T(8,128)(2,1)S(1)} %get-tuple-element.108), channel_id=1, source_target_pairs={{0,12},{2,14},{4,0},{6,2},{8,4},{10,6},{12,8},{14,10},{1,13},{3,15... | collective-permute-start | bytes 393224 | tf_op jit(solution)/shard_map/ppermute | solution.py:179
  87.0 0.9 bitcast_dynamic-update-slice_fusion.30
  88.8 6.3 %collective-permute-done.4 = bf16[16,2,16,128]{3,2,1,0:T(8,128)(2,1)S(1)} collective-permute-done((bf16[16,2,16,128]{3,2,1,0:T(8,128)(2,1)}, bf16[16,2,16,128]{3,2,1,0:T(8,128)(2,1)S(1)}, u32[]{:S(2)}, u32[]{:S(2)}) %collective-permute-start.4) | collective-permute-done | bytes 131104 | tf_op jit(solution)/shard_map/ppermute | solution.py:179
  95.1 2.9 %collective-permute-done.5 = bf16[16,2,16,128]{3,2,1,0:T(8,128)(2,1)S(1)} collective-permute-done((bf16[16,2,16,128]{3,2,1,0:T(8,128)(2,1)S(1)}, bf16[16,2,16,128]{3,2,1,0:T(8,128)(2,1)S(1)}, u32[]{:S(2)}, u32[]{:S(2)}) %collective-permute-start.5) | collective-permute-done | bytes 131104 | tf_op jit(solution)/shard_map/ppermute | solution.py:179
  98.6 2.1 %dynamic-slice_bitcast_fusion.16 = (bf16[16,2,16,128]{3,2,1,0:T(8,128)(2,1)S(1)}, bf16[16,2,16,128]{3,2,1,0:T(8,128)(2,1)}, bf16[16,2,16,128]{3,2,1,0:T(8,128)(2...) fusion(bf16[8,16,2,16,128]{4,3,2,1,0:T(8,128)(2,1)} %get-tuple-, ...), kind=kLoop, calls=%fused_computation.89 | loop fusion | bytes 2097184 | tf_op jit(solution)/shard_map/jit(dynamic_index_in_dim)/squeeze | solution.py:173
  100.8 5.6 %collective-permute-start.10 = (bf16[16,2,16,128]{3,2,1,0:T(8,128)(2,1)S(1)}, bf16[16,2,16,128]{3,2,1,0:T(8,128)(2,1)S(1)}, u32[]{:S(2)}, u32[]{:S(2)}) collective-permute-start(bf16[16,2,16,128]{3,2,1,0:T(8,128)(2,1)S(1)} %get-tuple-element.102), channel_id=1, source_target_pairs={{0,4},{2,6},{4,8},{6,10},{8,12},{10,14},{12,0},{14,2},{1,5},{3,7},... | collective-permute-start | bytes 393224 | tf_op jit(solution)/shard_map/ppermute | solution.py:179
  107.1 1.8 collective-permute-start.12
  108.9 1.3 collective-permute-start.13
  110.2 3.8 %collective-permute-start.14 = (bf16[16,2,16,128]{3,2,1,0:T(8,128)(2,1)}, bf16[16,2,16,128]{3,2,1,0:T(8,128)(2,1)}, u32[]{:S(2)}, u32[]{:S(2)}) collective-permute-start(bf16[16,2,16,128]{3,2,1,0:T(8,128)(2,1)} %get-tuple-element.98), channel_id=1, source_target_pairs={{0,12},{2,14},{4,0},{6,2},{8,4},{10,6},{12,8},{14,10},{1,13},{3,15... | collective-permute-start | bytes 393224 | tf_op jit(solution)/shard_map/ppermute | solution.py:179
  114.0 1.5 pad_maximum_fusion
  115.9 1.0 collective-permute-start.15
  117.8 2.4 %copy.53 = bf16[16,2,256,128]{3,2,1,0:T(8,128)(2,1)} copy(bf16[16,2,256,128]{2,3,0,1:T(8,128)(2,1)S(1)} %maximum_bitcast_fusion) | data formatting | bytes 4194304 | tf_op jit(solution)/shard_map/transpose | solution.py:211
  120.2 9.8 %shard_map.18.rest_0_ = f32[64,2,256,512]{3,2,1,0:T(8,128)} custom-call(bf16[16,512,128]{2,1,0:T(8,128)(2,1)} %bitcast.184, bf16[16,128,512]{2,1,0:T(8,128)(2,1)} %bitcast.183), custom_call_target="tpu_custom_call" | custom-call | flops 1073741824 | bytes 20971520 | tf_op jit(solution)/shard_map/pallas_call | solution.py:154
  130.2 1.0 bitcast_dynamic-update-slice_fusion.22
  131.4 0.9 bitcast_dynamic-update-slice_fusion.19
  132.3 0.9 bitcast_dynamic-update-slice_fusion.18
  133.3 0.9 bitcast_dynamic-update-slice_fusion.17
  134.2 0.9 bitcast_dynamic-update-slice_fusion.16
  135.3 0.9 dynamic-slice_bitcast_fusion.8
  136.2 1.3 collective-permute-start.17
  137.5 2.0 collective-permute-start.18
  139.5 0.8 collective-permute-start.19
  140.3 1.7 collective-permute-start.20
  142.1 1.3 collective-permute-start.21
  144.1 3.9 %collective-permute-start.22 = (bf16[16,2,16,128]{3,2,1,0:T(8,128)(2,1)S(1)}, bf16[16,2,16,128]{3,2,1,0:T(8,128)(2,1)}, u32[]{:S(2)}, u32[]{:S(2)}) collective-permute-start(bf16[16,2,16,128]{3,2,1,0:T(8,128)(2,1)S(1)} %get-tuple-element.88), channel_id=1, source_target_pairs={{0,12},{2,14},{4,0},{6,2},{8,4},{10,6},{12,8},{14,10},{1,13},{3,15... | collective-permute-start | bytes 393224 | tf_op jit(solution)/shard_map/ppermute | solution.py:179
  148.0 0.9 collective-permute-start.23
  149.1 1.6 copy.57
  150.6 2.4 %copy.56 = bf16[16,2,256,128]{3,2,1,0:T(8,128)(2,1)} copy(bf16[16,2,256,128]{2,3,0,1:T(8,128)(2,1)S(1)} %maximum_bitcast_fusion.1) | data formatting | bytes 4194304 | tf_op jit(solution)/shard_map/transpose | solution.py:211
  153.0 9.8 %shard_map.19.rest_0_ = f32[64,2,256,512]{3,2,1,0:T(8,128)} custom-call(bf16[16,512,128]{2,1,0:T(8,128)(2,1)} %bitcast.180, bf16[16,128,512]{2,1,0:T(8,128)(2,1)} %bitcast.178, f32[64,2,256,512]{3,2,1,0:T(8,128)} %shard_map.18.rest_0_), custom_call_target="tpu_custom_call", output_to_operand_aliasing={{}: (2, {})} | custom-call | flops 1073741824 | bytes 20971520 | tf_op jit(solution)/shard_map/pallas_call | solution.py:154
  163.2 0.9 bitcast_dynamic-update-slice_fusion.12
  164.1 0.9 bitcast_dynamic-update-slice_fusion.11
  165.1 0.9 bitcast_dynamic-update-slice_fusion.10
  166.0 0.9 bitcast_dynamic-update-slice_fusion.9
  167.0 0.9 bitcast_dynamic-update-slice_fusion.8
  168.1 1.2 collective-permute-start.25
  169.3 2.7 %collective-permute-start.26 = (bf16[16,2,16,128]{3,2,1,0:T(8,128)(2,1)S(1)}, bf16[16,2,16,128]{3,2,1,0:T(8,128)(2,1)S(1)}, u32[]{:S(2)}, u32[]{:S(2)}) collective-permute-start(bf16[16,2,16,128]{3,2,1,0:T(8,128)(2,1)S(1)} %get-tuple-element.82), channel_id=1, source_target_pairs={{0,4},{2,6},{4,8},{6,10},{8,12},{10,14},{12,0},{14,2},{1,5},{3,7},... | collective-permute-start | bytes 393224 | tf_op jit(solution)/shard_map/ppermute | solution.py:179
  172.2 1.8 collective-permute-start.28
  174.1 1.8 collective-permute-start.29
  176.6 3.9 %collective-permute-start.30 = (bf16[16,2,16,128]{3,2,1,0:T(8,128)(2,1)S(1)}, bf16[16,2,16,128]{3,2,1,0:T(8,128)(2,1)}, u32[]{:S(2)}, u32[]{:S(2)}) collective-permute-start(bf16[16,2,16,128]{3,2,1,0:T(8,128)(2,1)S(1)} %get-tuple-element.78), channel_id=1, source_target_pairs={{0,12},{2,14},{4,0},{6,2},{8,4},{10,6},{12,8},{14,10},{1,13},{3,15... | collective-permute-start | bytes 393224 | tf_op jit(solution)/shard_map/ppermute | solution.py:179
  180.9 1.6 copy.61
  182.5 2.4 %copy.60 = bf16[16,2,256,128]{3,2,1,0:T(8,128)(2,1)} copy(bf16[16,2,256,128]{2,3,0,1:T(8,128)(2,1)S(1)} %maximum_bitcast_fusion.2) | data formatting | bytes 4194304 | tf_op jit(solution)/shard_map/transpose | solution.py:211
  184.9 9.8 %shard_map.20.rest_0_ = f32[64,2,256,512]{3,2,1,0:T(8,128)} custom-call(bf16[16,512,128]{2,1,0:T(8,128)(2,1)} %bitcast.181, bf16[16,128,512]{2,1,0:T(8,128)(2,1)} %bitcast.179, f32[64,2,256,512]{3,2,1,0:T(8,128)} %shard_map.19.rest_0_), custom_call_target="tpu_custom_call", output_to_operand_aliasing={{}: (2, {})} | custom-call | flops 1073741824 | bytes 20971520 | tf_op jit(solution)/shard_map/pallas_call | solution.py:154
  195.1 0.9 bitcast_dynamic-update-slice_fusion.1
  196.1 0.9 bitcast_dynamic-update-slice_fusion
  197.1 2.6 %collective-permute-done.32 = bf16[16,2,2,16,512]{4,3,2,1,0:T(8,128)(2,1)S(1)} collective-permute-done((bf16[16,2,2,16,512]{4,3,2,1,0:T(8,128)(2,1)S(1)}, bf16[16,2,2,16,512]{4,3,2,1,0:T(8,128)(2,1)S(1)}, u32[]{:S(2)}, u32[]{:S(2)}) %collective-permute-start.32) | collective-permute-done | bytes 1048608 | tf_op jit(solution)/shard_map/ppermute | solution.py:200
  200.2 1.6 copy.65
  202.2 2.4 %copy.64 = bf16[16,2,256,128]{3,2,1,0:T(8,128)(2,1)} copy(bf16[16,2,256,128]{2,3,0,1:T(8,128)(2,1)S(1)} %maximum_bitcast_fusion.3) | data formatting | bytes 4194304 | tf_op jit(solution)/shard_map/transpose | solution.py:211
  204.6 9.8 %shard_map.21 = f32[64,2,256,512]{3,2,1,0:T(8,128)} custom-call(bf16[16,512,128]{2,1,0:T(8,128)(2,1)} %bitcast.182, bf16[16,128,512]{2,1,0:T(8,128)(2,1)} %bitcast.177, f32[64,2,256,512]{3,2,1,0:T(8,128)} %shard_map.20.rest_0_), custom_call_target="tpu_custom_call", output_to_operand_aliasing={{}: (2, {})} | custom-call | flops 1073741824 | bytes 20971520 | tf_op jit(solution)/shard_map/pallas_call | solution.py:154
  (109 shorter events, 8.0 us)
Async XLA Ops:
  0.0 20.3 %collective-permute-start = (bf16[128,16384]{1,0:T(8,128)(2,1)}, bf16[128,16384]{1,0:T(8,128)(2,1)}, u32[]{:S(2)}, u32[]{:S(2)}) collective-permute-start(bf16[128,16384]{1,0:T(8,128)(2,1)} %own_ref.1), channel_id=1, source_target_pairs={{0,1},{1,2},{2,3},{4,5},{5,6},{6,7},{8,9},{9,10},{10,11},{12,13},{... | collective-permute-start | bytes 12582920 | tf_op jit(solution)/shard_map/ppermute | solution.py:17
  20.3 13.1 %copy-start.1 = (bf16[1024,1024]{1,0:T(8,128)(2,1)S(1)}, bf16[1024,1024]{1,0:T(8,128)(2,1)}, u32[]{:S(2)}) copy-start(bf16[1024,1024]{1,0:T(8,128)(2,1)} %convert_element_type.36) | copy-start | bytes 6291460
  45.0 39.7 %collective-permute-start.1 = (bf16[16,2,16,128]{3,2,1,0:T(8,128)(2,1)}, bf16[16,2,16,128]{3,2,1,0:T(8,128)(2,1)}, u32[]{:S(2)}, u32[]{:S(2)}) collective-permute-start(bf16[16,2,16,128]{3,2,1,0:T(8,128)(2,1)} %get-tuple-element.113), channel_id=1, source_target_pairs={{0,2},{2,0},{4,6},{6,4},{8,10},{10,8},{12,14},{14,12},{1,3},{3,1},... | collective-permute-start | bytes 393224 | tf_op jit(solution)/shard_map/ppermute | solution.py:179
  77.6 10.4 %collective-permute-start.2 = (bf16[16,2,16,128]{3,2,1,0:T(8,128)(2,1)}, bf16[16,2,16,128]{3,2,1,0:T(8,128)(2,1)S(1)}, u32[]{:S(2)}, u32[]{:S(2)}) collective-permute-start(bf16[16,2,16,128]{3,2,1,0:T(8,128)(2,1)} %get-tuple-element.112), channel_id=1, source_target_pairs={{0,4},{2,6},{4,8},{6,10},{8,12},{10,14},{12,0},{14,2},{1,5},{3,7},... | collective-permute-start | bytes 393224 | tf_op jit(solution)/shard_map/ppermute | solution.py:179
  79.1 9.6 %collective-permute-start.3 = (bf16[16,2,16,128]{3,2,1,0:T(8,128)(2,1)}, bf16[16,2,16,128]{3,2,1,0:T(8,128)(2,1)S(1)}, u32[]{:S(2)}, u32[]{:S(2)}) collective-permute-start(bf16[16,2,16,128]{3,2,1,0:T(8,128)(2,1)} %get-tuple-element.111), channel_id=1, source_target_pairs={{0,6},{2,4},{4,10},{6,8},{8,14},{10,12},{12,2},{14,0},{1,7},{3,5},... | collective-permute-start | bytes 393224 | tf_op jit(solution)/shard_map/ppermute | solution.py:179
  80.2 15.0 %collective-permute-start.4 = (bf16[16,2,16,128]{3,2,1,0:T(8,128)(2,1)}, bf16[16,2,16,128]{3,2,1,0:T(8,128)(2,1)S(1)}, u32[]{:S(2)}, u32[]{:S(2)}) collective-permute-start(bf16[16,2,16,128]{3,2,1,0:T(8,128)(2,1)} %get-tuple-element.110), channel_id=1, source_target_pairs={{0,8},{2,10},{4,12},{6,14},{8,0},{10,2},{12,4},{14,6},{1,9},{3,11}... | collective-permute-start | bytes 393224 | tf_op jit(solution)/shard_map/ppermute | solution.py:179
  81.7 16.3 %collective-permute-start.5 = (bf16[16,2,16,128]{3,2,1,0:T(8,128)(2,1)S(1)}, bf16[16,2,16,128]{3,2,1,0:T(8,128)(2,1)S(1)}, u32[]{:S(2)}, u32[]{:S(2)}) collective-permute-start(bf16[16,2,16,128]{3,2,1,0:T(8,128)(2,1)S(1)} %get-tuple-element.109), channel_id=1, source_target_pairs={{0,10},{2,8},{4,14},{6,12},{8,2},{10,0},{12,6},{14,4},{1,11},{3,9}... | collective-permute-start | bytes 393224 | tf_op jit(solution)/shard_map/ppermute | solution.py:179
  84.7 13.3 %collective-permute-start.6 = (bf16[16,2,16,128]{3,2,1,0:T(8,128)(2,1)S(1)}, bf16[16,2,16,128]{3,2,1,0:T(8,128)(2,1)S(1)}, u32[]{:S(2)}, u32[]{:S(2)}) collective-permute-start(bf16[16,2,16,128]{3,2,1,0:T(8,128)(2,1)S(1)} %get-tuple-element.108), channel_id=1, source_target_pairs={{0,12},{2,14},{4,0},{6,2},{8,4},{10,6},{12,8},{14,10},{1,13},{3,15... | collective-permute-start | bytes 393224 | tf_op jit(solution)/shard_map/ppermute | solution.py:179
  88.0 10.5 %collective-permute-start.7 = (bf16[16,2,16,128]{3,2,1,0:T(8,128)(2,1)S(1)}, bf16[16,2,16,128]{3,2,1,0:T(8,128)(2,1)S(1)}, u32[]{:S(2)}, u32[]{:S(2)}) collective-permute-start(bf16[16,2,16,128]{3,2,1,0:T(8,128)(2,1)S(1)} %get-tuple-element.107), channel_id=1, source_target_pairs={{0,14},{2,12},{4,2},{6,0},{8,6},{10,4},{12,10},{14,8},{1,15},{3,13... | collective-permute-start | bytes 393224 | tf_op jit(solution)/shard_map/ppermute | solution.py:179
  98.5 11.7 %collective-permute-start.8 = (bf16[16,2,2,16,512]{4,3,2,1,0:T(8,128)(2,1)S(1)}, bf16[16,2,2,16,512]{4,3,2,1,0:T(8,128)(2,1)S(1)}, u32[]{:S(2)}, u32[]{:S(2)}) collective-permute-start(bf16[16,2,2,16,512]{4,3,2,1,0:T(8,128)(2,1)S(1)} %bitcast_dynamic-update-slice_fusion.24), channel_id=1, source_target_pairs={{0,1},{1,0},{2,3},{3,2},{4,5},{5,4},{6,7},{7,6},{8,9},{9,8},{10,11... | collective-permute-start | bytes 3145736 | tf_op jit(solution)/shard_map/ppermute | solution.py:200
  100.8 15.1 %collective-permute-start.10 = (bf16[16,2,16,128]{3,2,1,0:T(8,128)(2,1)S(1)}, bf16[16,2,16,128]{3,2,1,0:T(8,128)(2,1)S(1)}, u32[]{:S(2)}, u32[]{:S(2)}) collective-permute-start(bf16[16,2,16,128]{3,2,1,0:T(8,128)(2,1)S(1)} %get-tuple-element.102), channel_id=1, source_target_pairs={{0,4},{2,6},{4,8},{6,10},{8,12},{10,14},{12,0},{14,2},{1,5},{3,7},... | collective-permute-start | bytes 393224 | tf_op jit(solution)/shard_map/ppermute | solution.py:179
  106.4 10.5 %collective-permute-start.11 = (bf16[16,2,16,128]{3,2,1,0:T(8,128)(2,1)S(1)}, bf16[16,2,16,128]{3,2,1,0:T(8,128)(2,1)S(1)}, u32[]{:S(2)}, u32[]{:S(2)}) collective-permute-start(bf16[16,2,16,128]{3,2,1,0:T(8,128)(2,1)S(1)} %get-tuple-element.101), channel_id=1, source_target_pairs={{0,6},{2,4},{4,10},{6,8},{8,14},{10,12},{12,2},{14,0},{1,7},{3,5},... | collective-permute-start | bytes 393224 | tf_op jit(solution)/shard_map/ppermute | solution.py:179
  107.1 22.9 %collective-permute-start.12 = (bf16[16,2,16,128]{3,2,1,0:T(8,128)(2,1)}, bf16[16,2,16,128]{3,2,1,0:T(8,128)(2,1)}, u32[]{:S(2)}, u32[]{:S(2)}) collective-permute-start(bf16[16,2,16,128]{3,2,1,0:T(8,128)(2,1)} %get-tuple-element.100), channel_id=1, source_target_pairs={{0,8},{2,10},{4,12},{6,14},{8,0},{10,2},{12,4},{14,6},{1,9},{3,11}... | collective-permute-start | bytes 393224 | tf_op jit(solution)/shard_map/ppermute | solution.py:179
  108.9 21.2 %collective-permute-start.13 = (bf16[16,2,16,128]{3,2,1,0:T(8,128)(2,1)}, bf16[16,2,16,128]{3,2,1,0:T(8,128)(2,1)}, u32[]{:S(2)}, u32[]{:S(2)}) collective-permute-start(bf16[16,2,16,128]{3,2,1,0:T(8,128)(2,1)} %get-tuple-element.99), channel_id=1, source_target_pairs={{0,10},{2,8},{4,14},{6,12},{8,2},{10,0},{12,6},{14,4},{1,11},{3,9}... | collective-permute-start | bytes 393224 | tf_op jit(solution)/shard_map/ppermute | solution.py:179
  110.2 19.8 %collective-permute-start.14 = (bf16[16,2,16,128]{3,2,1,0:T(8,128)(2,1)}, bf16[16,2,16,128]{3,2,1,0:T(8,128)(2,1)}, u32[]{:S(2)}, u32[]{:S(2)}) collective-permute-start(bf16[16,2,16,128]{3,2,1,0:T(8,128)(2,1)} %get-tuple-element.98), channel_id=1, source_target_pairs={{0,12},{2,14},{4,0},{6,2},{8,4},{10,6},{12,8},{14,10},{1,13},{3,15... | collective-permute-start | bytes 393224 | tf_op jit(solution)/shard_map/ppermute | solution.py:179
  115.9 1.7 copy-start.6
  115.9 14.2 %collective-permute-start.15 = (bf16[16,2,16,128]{3,2,1,0:T(8,128)(2,1)S(1)}, bf16[16,2,16,128]{3,2,1,0:T(8,128)(2,1)}, u32[]{:S(2)}, u32[]{:S(2)}) collective-permute-start(bf16[16,2,16,128]{3,2,1,0:T(8,128)(2,1)S(1)} %get-tuple-element.97), channel_id=1, source_target_pairs={{0,14},{2,12},{4,2},{6,0},{8,6},{10,4},{12,10},{14,8},{1,15},{3,13... | collective-permute-start | bytes 393224 | tf_op jit(solution)/shard_map/ppermute | solution.py:179
  116.9 0.7 copy-start.8
  116.9 13.2 %collective-permute-start.9 = (bf16[16,2,16,128]{3,2,1,0:T(8,128)(2,1)S(1)}, bf16[16,2,16,128]{3,2,1,0:T(8,128)(2,1)}, u32[]{:S(2)}, u32[]{:S(2)}) collective-permute-start(bf16[16,2,16,128]{3,2,1,0:T(8,128)(2,1)S(1)} %get-tuple-element.103), channel_id=1, source_target_pairs={{0,2},{2,0},{4,6},{6,4},{8,10},{10,8},{12,14},{14,12},{1,3},{3,1},... | collective-permute-start | bytes 393224 | tf_op jit(solution)/shard_map/ppermute | solution.py:179
  120.2 11.1 %copy-start.7 = (bf16[16,2,16,128]{3,2,1,0:T(8,128)(2,1)S(1)}, bf16[16,2,16,128]{3,2,1,0:T(8,128)(2,1)}, u32[]{:S(2)}) copy-start(bf16[16,2,16,128]{3,2,1,0:T(8,128)(2,1)} %copy-done.6) | copy-start | bytes 393220
  120.2 11.2 %copy-start.9 = (bf16[16,2,16,128]{3,2,1,0:T(8,128)(2,1)S(1)}, bf16[16,2,16,128]{3,2,1,0:T(8,128)(2,1)}, u32[]{:S(2)}) copy-start(bf16[16,2,16,128]{3,2,1,0:T(8,128)(2,1)} %copy-done.8) | copy-start | bytes 393220
  130.0 5.2 %copy-start = (bf16[8,16,2,16,128]{4,3,2,1,0:T(8,128)(2,1)S(1)}, bf16[8,16,2,16,128]{4,3,2,1,0:T(8,128)(2,1)}, u32[]{:S(2)}) copy-start(bf16[8,16,2,16,128]{4,3,2,1,0:T(8,128)(2,1)} %get-tuple-element.50) | copy-start | bytes 3145732
  135.2 6.9 %collective-permute-start.16 = (bf16[16,2,2,16,512]{4,3,2,1,0:T(8,128)(2,1)S(1)}, bf16[16,2,2,16,512]{4,3,2,1,0:T(8,128)(2,1)S(1)}, u32[]{:S(2)}, u32[]{:S(2)}) collective-permute-start(bf16[16,2,2,16,512]{4,3,2,1,0:T(8,128)(2,1)S(1)} %bitcast_dynamic-update-slice_fusion.16), channel_id=1, source_target_pairs={{0,1},{1,0},{2,3},{3,2},{4,5},{5,4},{6,7},{7,6},{8,9},{9,8},{10,11... | collective-permute-start | bytes 3145736 | tf_op jit(solution)/shard_map/ppermute | solution.py:200
  136.2 7.9 %collective-permute-start.17 = (bf16[16,2,16,128]{3,2,1,0:T(8,128)(2,1)S(1)}, bf16[16,2,16,128]{3,2,1,0:T(8,128)(2,1)S(1)}, u32[]{:S(2)}, u32[]{:S(2)}) collective-permute-start(bf16[16,2,16,128]{3,2,1,0:T(8,128)(2,1)S(1)} %get-tuple-element.93), channel_id=1, source_target_pairs={{0,2},{2,0},{4,6},{6,4},{8,10},{10,8},{12,14},{14,12},{1,3},{3,1},... | collective-permute-start | bytes 393224 | tf_op jit(solution)/shard_map/ppermute | solution.py:179
  137.5 10.5 %collective-permute-start.18 = (bf16[16,2,16,128]{3,2,1,0:T(8,128)(2,1)S(1)}, bf16[16,2,16,128]{3,2,1,0:T(8,128)(2,1)S(1)}, u32[]{:S(2)}, u32[]{:S(2)}) collective-permute-start(bf16[16,2,16,128]{3,2,1,0:T(8,128)(2,1)S(1)} %get-tuple-element.92), channel_id=1, source_target_pairs={{0,4},{2,6},{4,8},{6,10},{8,12},{10,14},{12,0},{14,2},{1,5},{3,7},... | collective-permute-start | bytes 393224 | tf_op jit(solution)/shard_map/ppermute | solution.py:179
  139.5 23.3 %collective-permute-start.19 = (bf16[16,2,16,128]{3,2,1,0:T(8,128)(2,1)}, bf16[16,2,16,128]{3,2,1,0:T(8,128)(2,1)}, u32[]{:S(2)}, u32[]{:S(2)}) collective-permute-start(bf16[16,2,16,128]{3,2,1,0:T(8,128)(2,1)} %get-tuple-element.91), channel_id=1, source_target_pairs={{0,6},{2,4},{4,10},{6,8},{8,14},{10,12},{12,2},{14,0},{1,7},{3,5},... | collective-permute-start | bytes 393224 | tf_op jit(solution)/shard_map/ppermute | solution.py:179
  140.3 22.5 %collective-permute-start.20 = (bf16[16,2,16,128]{3,2,1,0:T(8,128)(2,1)}, bf16[16,2,16,128]{3,2,1,0:T(8,128)(2,1)}, u32[]{:S(2)}, u32[]{:S(2)}) collective-permute-start(bf16[16,2,16,128]{3,2,1,0:T(8,128)(2,1)} %get-tuple-element.90), channel_id=1, source_target_pairs={{0,8},{2,10},{4,12},{6,14},{8,0},{10,2},{12,4},{14,6},{1,9},{3,11}... | collective-permute-start | bytes 393224 | tf_op jit(solution)/shard_map/ppermute | solution.py:179
  142.1 20.8 %collective-permute-start.21 = (bf16[16,2,16,128]{3,2,1,0:T(8,128)(2,1)}, bf16[16,2,16,128]{3,2,1,0:T(8,128)(2,1)}, u32[]{:S(2)}, u32[]{:S(2)}) collective-permute-start(bf16[16,2,16,128]{3,2,1,0:T(8,128)(2,1)} %get-tuple-element.89), channel_id=1, source_target_pairs={{0,10},{2,8},{4,14},{6,12},{8,2},{10,0},{12,6},{14,4},{1,11},{3,9}... | collective-permute-start | bytes 393224 | tf_op jit(solution)/shard_map/ppermute | solution.py:179
  144.1 4.8 %copy-start.2 = (bf16[16,2,16,128]{3,2,1,0:T(8,128)(2,1)}, bf16[16,2,16,128]{3,2,1,0:T(8,128)(2,1)S(1)}, u32[]{:S(2)}) copy-start(bf16[16,2,16,128]{3,2,1,0:T(8,128)(2,1)S(1)} %collective-permute-done.17) | copy-start | bytes 393220
  144.1 18.8 %collective-permute-start.22 = (bf16[16,2,16,128]{3,2,1,0:T(8,128)(2,1)S(1)}, bf16[16,2,16,128]{3,2,1,0:T(8,128)(2,1)}, u32[]{:S(2)}, u32[]{:S(2)}) collective-permute-start(bf16[16,2,16,128]{3,2,1,0:T(8,128)(2,1)S(1)} %get-tuple-element.88), channel_id=1, source_target_pairs={{0,12},{2,14},{4,0},{6,2},{8,4},{10,6},{12,8},{14,10},{1,13},{3,15... | collective-permute-start | bytes 393224 | tf_op jit(solution)/shard_map/ppermute | solution.py:179
  148.0 0.9 copy-start.4
  148.0 14.9 %collective-permute-start.23 = (bf16[16,2,16,128]{3,2,1,0:T(8,128)(2,1)S(1)}, bf16[16,2,16,128]{3,2,1,0:T(8,128)(2,1)}, u32[]{:S(2)}, u32[]{:S(2)}) collective-permute-start(bf16[16,2,16,128]{3,2,1,0:T(8,128)(2,1)S(1)} %get-tuple-element.87), channel_id=1, source_target_pairs={{0,14},{2,12},{4,2},{6,0},{8,6},{10,4},{12,10},{14,8},{1,15},{3,13... | collective-permute-start | bytes 393224 | tf_op jit(solution)/shard_map/ppermute | solution.py:179
  153.0 10.1 %copy-start.3 = (bf16[16,2,16,128]{3,2,1,0:T(8,128)(2,1)S(1)}, bf16[16,2,16,128]{3,2,1,0:T(8,128)(2,1)}, u32[]{:S(2)}) copy-start(bf16[16,2,16,128]{3,2,1,0:T(8,128)(2,1)} %copy-done.2) | copy-start | bytes 393220
  153.0 10.1 %copy-start.5 = (bf16[16,2,16,128]{3,2,1,0:T(8,128)(2,1)S(1)}, bf16[16,2,16,128]{3,2,1,0:T(8,128)(2,1)}, u32[]{:S(2)}) copy-start(bf16[16,2,16,128]{3,2,1,0:T(8,128)(2,1)} %copy-done.4) | copy-start | bytes 393220
  167.9 6.2 %collective-permute-start.24 = (bf16[16,2,2,16,512]{4,3,2,1,0:T(8,128)(2,1)S(1)}, bf16[16,2,2,16,512]{4,3,2,1,0:T(8,128)(2,1)S(1)}, u32[]{:S(2)}, u32[]{:S(2)}) collective-permute-start(bf16[16,2,2,16,512]{4,3,2,1,0:T(8,128)(2,1)S(1)} %bitcast_dynamic-update-slice_fusion.8), channel_id=1, source_target_pairs={{0,1},{1,0},{2,3},{3,2},{4,5},{5,4},{6,7},{7,6},{8,9},{9,8},{10,11... | collective-permute-start | bytes 3145736 | tf_op jit(solution)/shard_map/ppermute | solution.py:200
  168.1 8.5 %collective-permute-start.25 = (bf16[16,2,16,128]{3,2,1,0:T(8,128)(2,1)S(1)}, bf16[16,2,16,128]{3,2,1,0:T(8,128)(2,1)S(1)}, u32[]{:S(2)}, u32[]{:S(2)}) collective-permute-start(bf16[16,2,16,128]{3,2,1,0:T(8,128)(2,1)S(1)} %get-tuple-element.83), channel_id=1, source_target_pairs={{0,2},{2,0},{4,6},{6,4},{8,10},{10,8},{12,14},{14,12},{1,3},{3,1},... | collective-permute-start | bytes 393224 | tf_op jit(solution)/shard_map/ppermute | solution.py:179
  169.3 11.2 %collective-permute-start.26 = (bf16[16,2,16,128]{3,2,1,0:T(8,128)(2,1)S(1)}, bf16[16,2,16,128]{3,2,1,0:T(8,128)(2,1)S(1)}, u32[]{:S(2)}, u32[]{:S(2)}) collective-permute-start(bf16[16,2,16,128]{3,2,1,0:T(8,128)(2,1)S(1)} %get-tuple-element.82), channel_id=1, source_target_pairs={{0,4},{2,6},{4,8},{6,10},{8,12},{10,14},{12,0},{14,2},{1,5},{3,7},... | collective-permute-start | bytes 393224 | tf_op jit(solution)/shard_map/ppermute | solution.py:179
  172.0 22.6 %collective-permute-start.27 = (bf16[16,2,16,128]{3,2,1,0:T(8,128)(2,1)S(1)}, bf16[16,2,16,128]{3,2,1,0:T(8,128)(2,1)S(1)}, u32[]{:S(2)}, u32[]{:S(2)}) collective-permute-start(bf16[16,2,16,128]{3,2,1,0:T(8,128)(2,1)S(1)} %get-tuple-element.81), channel_id=1, source_target_pairs={{0,6},{2,4},{4,10},{6,8},{8,14},{10,12},{12,2},{14,0},{1,7},{3,5},... | collective-permute-start | bytes 393224 | tf_op jit(solution)/shard_map/ppermute | solution.py:179
  172.2 22.5 %collective-permute-start.28 = (bf16[16,2,16,128]{3,2,1,0:T(8,128)(2,1)S(1)}, bf16[16,2,16,128]{3,2,1,0:T(8,128)(2,1)S(1)}, u32[]{:S(2)}, u32[]{:S(2)}) collective-permute-start(bf16[16,2,16,128]{3,2,1,0:T(8,128)(2,1)S(1)} %get-tuple-element.80), channel_id=1, source_target_pairs={{0,8},{2,10},{4,12},{6,14},{8,0},{10,2},{12,4},{14,6},{1,9},{3,11}... | collective-permute-start | bytes 393224 | tf_op jit(solution)/shard_map/ppermute | solution.py:179
  174.1 20.6 %collective-permute-start.29 = (bf16[16,2,16,128]{3,2,1,0:T(8,128)(2,1)S(1)}, bf16[16,2,16,128]{3,2,1,0:T(8,128)(2,1)S(1)}, u32[]{:S(2)}, u32[]{:S(2)}) collective-permute-start(bf16[16,2,16,128]{3,2,1,0:T(8,128)(2,1)S(1)} %get-tuple-element.79), channel_id=1, source_target_pairs={{0,10},{2,8},{4,14},{6,12},{8,2},{10,0},{12,6},{14,4},{1,11},{3,9}... | collective-permute-start | bytes 393224 | tf_op jit(solution)/shard_map/ppermute | solution.py:179
  176.6 18.1 %collective-permute-start.30 = (bf16[16,2,16,128]{3,2,1,0:T(8,128)(2,1)S(1)}, bf16[16,2,16,128]{3,2,1,0:T(8,128)(2,1)}, u32[]{:S(2)}, u32[]{:S(2)}) collective-permute-start(bf16[16,2,16,128]{3,2,1,0:T(8,128)(2,1)S(1)} %get-tuple-element.78), channel_id=1, source_target_pairs={{0,12},{2,14},{4,0},{6,2},{8,4},{10,6},{12,8},{14,10},{1,13},{3,15... | collective-permute-start | bytes 393224 | tf_op jit(solution)/shard_map/ppermute | solution.py:179
  180.5 14.2 %collective-permute-start.31 = (bf16[16,2,16,128]{3,2,1,0:T(8,128)(2,1)S(1)}, bf16[16,2,16,128]{3,2,1,0:T(8,128)(2,1)}, u32[]{:S(2)}, u32[]{:S(2)}) collective-permute-start(bf16[16,2,16,128]{3,2,1,0:T(8,128)(2,1)S(1)} %get-tuple-element.77), channel_id=1, source_target_pairs={{0,14},{2,12},{4,2},{6,0},{8,6},{10,4},{12,10},{14,8},{1,15},{3,13... | collective-permute-start | bytes 393224 | tf_op jit(solution)/shard_map/ppermute | solution.py:179
  197.0 2.7 %collective-permute-start.32 = (bf16[16,2,2,16,512]{4,3,2,1,0:T(8,128)(2,1)S(1)}, bf16[16,2,2,16,512]{4,3,2,1,0:T(8,128)(2,1)S(1)}, u32[]{:S(2)}, u32[]{:S(2)}) collective-permute-start(bf16[16,2,2,16,512]{4,3,2,1,0:T(8,128)(2,1)S(1)} %bitcast_dynamic-update-slice_fusion), channel_id=1, source_target_pairs={{0,1},{1,0},{2,3},{3,2},{4,5},{5,4},{6,7},{7,6},{8,9},{9,8},{10,11... | collective-permute-start | bytes 3145736 | tf_op jit(solution)/shard_map/ppermute | solution.py:200

commit v11 on v9

--- a/solution.py
+++ b/solution.py
@@ -36,7 +36,8 @@
     return table.reshape(frame_len, frame_len).astype(jnp.bfloat16)
 
 
-def filter_kernel(taps_ref, own_ref, history_ref, out_ref):
+def filter_kernel(taps_ref, own_ref, history_ref, *rest):
+    out_ref = rest[-1]
     spectra_here, inputs_here, frame_len = out_ref.shape
     tile_rows, tile_cols = 16, 128
     col_tiles = frame_len // tile_cols
@@ -64,24 +65,50 @@
     lax.fori_loop(0, (inputs_here // tile_rows) * col_tiles, body, 0)
 
 
-def polyphase_filter(filter_taps, own, history, frame_len):
+def polyphase_filter(filter_taps, own, history, frame_len, prev, part, inputs_total):
     inputs_here = own.shape[0]
     spectra_here = own.shape[1] // frame_len
+    rows = 32 if inputs_here % 32 == 0 else inputs_here
+    offset = part * (inputs_here // rows)
+    in_specs = [
+        pl.BlockSpec((TAPS, frame_len), lambda r: (0, 0)),
+        pl.BlockSpec((rows, spectra_here * frame_len), lambda r: (r, 0)),
+        pl.BlockSpec((rows, spectra_here * frame_len), lambda r: (r, 0)),
+    ]
+    args = [filter_taps, own, history]
+    aliases = {}
+    if prev is not None:
+        in_specs.append(pl.BlockSpec(memory_space=pl.ANY))
+        args.append(prev)
+        aliases = {3: 0}
     return pl.pallas_call(
         filter_kernel,
-        out_shape=jax.ShapeDtypeStruct((spectra_here, inputs_here, frame_len), jnp.bfloat16),
+        grid=(inputs_here // rows,),
+        in_specs=in_specs,
+        out_specs=pl.BlockSpec((spectra_here, rows, frame_len), lambda r: (0, r + offset, 0)),
+        out_shape=jax.ShapeDtypeStruct((spectra_here, inputs_total, frame_len), jnp.bfloat16),
+        input_output_aliases=aliases,
         cost_estimate=pl.CostEstimate(
             flops=2 * TAPS * own.size, bytes_accessed=3 * own.size * 2, transcendentals=0
         ),
-    )(filter_taps, own, history)
+    )(*args)
 
 
 def per_device(voltages):
     inputs_here = voltages.shape[0]
     frame_len = 2 * CH
     spectra_here = voltages.shape[1] // frame_len
-    history = shifted(voltages, ("tm", "pol"), 1)
-    filtered = polyphase_filter(prototype(TAPS, frame_len), voltages, history, frame_len)
+    filter_taps = prototype(TAPS, frame_len)
+    halves = 2 if inputs_here % 64 == 0 else 1
+    half_rows = inputs_here // halves
+    filtered = None
+    history = None
+    for half in range(halves):
+        rows = voltages[half * half_rows : (half + 1) * half_rows]
+        if half:
+            history, rows = lax.optimization_barrier((history, rows))
+        history = shifted(rows, ("tm", "pol"), 1)
+        filtered = polyphase_filter(filter_taps, rows, history, frame_len, filtered, half, inputs_here)
     spectra = lax.dot_general(
         dft_table_t(frame_len),
         filtered.reshape(spectra_here * inputs_here, frame_len),

time: 219 us -> 223 us (1.018)
  starting transfers between devices: 86 us -> 78.5 us
  local copies, waits for them, and re-layouts: 40.6 us -> 48 us
  waiting for transfers between devices: 12.3 us -> 17 us
    ppermute x28, starting transfers between devices: 81.4 us -> 50.7 us  [send_chunk(): block = lax.ppermute(block, ('inp', 'tm'), route)]
    ppermute x1 -> x2, starting transfers between devices: 4.31 us -> 27.5 us  [shifted(): return lax.ppermute(block, axis, route)]
    slice x0 -> x1, local copies, waits for them, and re-layouts: none -> 3.94 us  [per_device(): rows = voltages[half * half_rows:(half + 1) * half_rows]]
    ppermute x1 -> x2, waiting for transfers between devices: 0.01 us -> 3.64 us  [shifted(): return lax.ppermute(block, axis, route)]
    unnamed x21 -> x25, local copies, waits for them, and re-layouts: 1.45 us -> 5 us
    pallas_call x1 -> x2, Pallas kernels: 16.2 us -> 15.6 us  [polyphase_filter(): pl.pallas_call(filter_kernel, grid=(inputs_here // rows,), in_specs=in_sp...]
  transfers between devices with their start and end apart: 33 -> 34, of which waited for: 4 -> 6; matrix products, arithmetic and copies ran while one was open for 16% -> 15% of each run, Pallas kernels for 14% -> 17%
where the time goes in v11:
time: 223 us; the launch traced here: 222 us
  starting transfers between devices  78.5 us (35%)
  Pallas kernels  54.9 us (25%)
  local copies, waits for them, and re-layouts  48 us (22%)
  waiting for transfers between devices  17 us (8%)
  other arithmetic  14.9 us (7%)
  matrix products  6.95 us (3%)
    ppermute x28, starting transfers between devices, send_chunk(): block = lax.ppermute(block, ('inp', 'tm'), route)  50.7 us
    pallas_call x4, Pallas kernels, correlate(): pl.pallas_call(functools.partial(correlate_kernel, 1.0 / (depth // 2)), g...  39.3 us
    ppermute x2, starting transfers between devices, shifted(): return lax.ppermute(block, axis, route)  27.5 us
    pallas_call x2, Pallas kernels, polyphase_filter(): pl.pallas_call(filter_kernel, grid=(inputs_here // rows,), in_specs=in_sp...  15.6 us
    dynamic_update_slice x32, local copies, waits for them, and re-layouts, assemble_chunk(): lax.dynamic_update_slice(half, block[:, :, None], (0, 0, tm_step, 0, sour...  12.9 us
    ppermute x28, waiting for transfers between devices, send_chunk(): block = lax.ppermute(block, ('inp', 'tm'), route)  10.7 us
    transpose x4, local copies, waits for them, and re-layouts, finish_chunk(): lhs = lhs.transpose(0, 1, 3, 2).reshape(own_channels, 2 * rows_here, depth)  9.51 us
    another operation x1, other arithmetic  8.5 us
  transfers between devices with their start and end apart: 34, of which 6 were waited for; matrix products, arithmetic and copies ran while one was open for 15% of the time, Pallas kernels for 17%

profile of v11, /device:TPU:0, one launch (start us, length us, event | category | flops | bytes accessed | tf_op | source)
XLA Modules:
  0.0 221.6 jit_solution(17991540886131021291)
XLA Ops:
  0.0 3.9 %fusion.16 = (bf16[64,16384]{1,0:T(8,128)(2,1)}, bf16[64,16384]{1,0:T(8,128)(2,1)S(1)}) fusion(bf16[128,16384]{1,0:T(8,128)(2,1)} %param.1), kind=kLoop, calls=%fused_computation.112 | loop fusion | bytes 8388608 | tf_op jit(solution)/shard_map/slice | solution.py:107
  3.9 1.4 copy-done
  5.3 2.5 %collective-permute-start = (bf16[64,16384]{1,0:T(8,128)(2,1)S(1)}, bf16[64,16384]{1,0:T(8,128)(2,1)S(1)}, u32[]{:S(2)}, u32[]{:S(2)}) collective-permute-start(bf16[64,16384]{1,0:T(8,128)(2,1)S(1)} %get-tuple-element.78.own_ref), channel_id=1, source_target_pairs={{0,1},{1,2},{2,3},{4,5},{5,6},{6,7},{8,9},{9,10},{10,11},{12,13},{... | collective-permute-start | bytes 6291464 | tf_op jit(solution)/shard_map/ppermute | solution.py:17
  7.8 3.6 %collective-permute-done.history_ref = bf16[64,16384]{1,0:T(8,128)(2,1)S(1)} collective-permute-done((bf16[64,16384]{1,0:T(8,128)(2,1)S(1)}, bf16[64,16384]{1,0:T(8,128)(2,1)S(1)}, u32[]{:S(2)}, u32[]{:S(2)}) %collective-permute-start) | collective-permute-done | bytes 2097184 | tf_op jit(solution)/shard_map/ppermute | solution.py:17
  11.4 1.3 copy-done.3
  12.8 25.0 %collective-permute-start.1 = (bf16[64,16384]{1,0:T(8,128)(2,1)}, bf16[64,16384]{1,0:T(8,128)(2,1)}, u32[]{:S(2)}, u32[]{:S(2)}) collective-permute-start(bf16[64,16384]{1,0:T(8,128)(2,1)} %get-tuple-element.39.own_ref), channel_id=1, source_target_pairs={{0,1},{1,2},{2,3},{4,5},{5,6},{6,7},{8,9},{9,10},{10,11},{12,13},{... | collective-permute-start | bytes 6291464 | tf_op jit(solution)/shard_map/ppermute | solution.py:17
  37.8 1.1 fusion.14
  39.6 8.5 %negate_convert_fusion = (bf16[512,1,1024]{2,0,1:T(8,128)(2,1)S(1)}, bf16[512,1,1024]{2,0,1:T(8,128)(2,1)S(1)}) fusion(), kind=kLoop, calls=%fused_computation.24 | loop fusion | flops 8912896 | bytes 2097152 | tf_op jit(solution)/shard_map/convert.1
  48.3 2.2 copy.52
  50.4 2.2 %convert_element_type.36 = bf16[1024,1024]{1,0:T(8,128)(2,1)} reshape(bf16[512,2,1024]{2,1,0:T(2,128)(2,1)S(1)} %copy.52) | data formatting | bytes 4194304 | tf_op jit(solution)/shard_map/convert_element_type | solution.py:36
  52.7 1.1 fusion.11.taps_ref
  53.8 7.7 %shard_map.17.rest_0_ = bf16[16,128,1024]{2,1,0:T(8,128)(2,1)} custom-call(f32[16,1024]{1,0:T(8,128)} %fusion.11.taps_ref, bf16[64,16384]{1,0:T(8,128)(2,1)} %copy-done, bf16[64,16384]{1,0:T(8,128)(2,1)} %copy-done.3), custom_call_target="tpu_custom_call" | custom-call | flops 33554432 | bytes 6291456 | tf_op jit(solution)/shard_map/pallas_call | solution.py:84
  61.5 7.9 %shard_map.18 = bf16[16,128,1024]{2,1,0:T(8,128)(2,1)} custom-call(f32[16,1024]{1,0:T(8,128)} %fusion.11.taps_ref, bf16[64,16384]{1,0:T(8,128)(2,1)} %get-tuple-element.39.own_ref, bf16[64,16384]{1,0:T(8,128)(2,1)} %collective-permute-done.1.history_ref, bf16[16,128,1024]{2,1,0:T(8,128)(2,1)} %shard_map.17.rest_0_), custom_call_target="tpu_custom_call", output_to_operand_aliasing={{}: (3, {})} | custom-call | flops 33554432 | bytes 6291456 | tf_op jit(solution)/shard_map/pallas_call | solution.py:84
  69.4 7.0 %convert_bitcast_fusion = bf16[128,8,16,128]{3,1,2,0:T(8,128)(2,1)S(1)} fusion(bf16[1024,1024]{1,0:T(8,128)(2,1)S(1)} %copy-done.2, bf16[2048,1024]{1,0:T(8,128)(2,1)} %bitcast.167), kind=kOutput, calls=%fused_computation | convolution fusion | flops 4297064448 | bytes 10485760 | tf_op jit(solution)/shard_map/dot_general | solution.py:112
  76.4 1.4 copy.67
  77.8 2.2 %fusion.15 = (bf16[8,16,2,16,128]{4,3,2,1,0:T(8,128)(2,1)S(1)}, bf16[8,16,2,16,128]{4,3,2,1,0:T(8,128)(2,1)}, bf16[8,16,2,16,128]{4,3,2,1,0:T(8,128)(2,1)}, bf16[8,16,2,16,128]{4,3,2,1,0:T(8,128)(2,1)S(1)}) fusion(bf16[8,64,2,16,128]{4,3,2,1,0:T(8,128)(2,1)S(1)} %bitcast.168), kind=kLoop, calls=%fused_computation.111 | loop fusion | bytes 8388608 | tf_op jit(solution)/shard_map/slice | solution.py:130
  80.9 2.9 %collective-permute-start.2 = (bf16[16,2,16,128]{3,2,1,0:T(8,128)(2,1)}, bf16[16,2,16,128]{3,2,1,0:T(8,128)(2,1)}, u32[]{:S(2)}, u32[]{:S(2)}) collective-permute-start(bf16[16,2,16,128]{3,2,1,0:T(8,128)(2,1)} %get-tuple-element.117), channel_id=1, source_target_pairs={{0,2},{2,0},{4,6},{6,4},{8,10},{10,8},{12,14},{14,12},{1,3},{3,1},... | collective-permute-start | bytes 393224 | tf_op jit(solution)/shard_map/ppermute | solution.py:198
  83.8 1.6 collective-permute-start.3
  85.4 1.0 collective-permute-start.4
  86.4 1.6 collective-permute-start.5
  88.0 2.8 %collective-permute-start.6 = (bf16[16,2,16,128]{3,2,1,0:T(8,128)(2,1)S(1)}, bf16[16,2,16,128]{3,2,1,0:T(8,128)(2,1)S(1)}, u32[]{:S(2)}, u32[]{:S(2)}) collective-permute-start(bf16[16,2,16,128]{3,2,1,0:T(8,128)(2,1)S(1)} %get-tuple-element.113), channel_id=1, source_target_pairs={{0,10},{2,8},{4,14},{6,12},{8,2},{10,0},{12,6},{14,4},{1,11},{3,9}... | collective-permute-start | bytes 393224 | tf_op jit(solution)/shard_map/ppermute | solution.py:198
  91.0 2.3 %collective-permute-start.7 = (bf16[16,2,16,128]{3,2,1,0:T(8,128)(2,1)S(1)}, bf16[16,2,16,128]{3,2,1,0:T(8,128)(2,1)S(1)}, u32[]{:S(2)}, u32[]{:S(2)}) collective-permute-start(bf16[16,2,16,128]{3,2,1,0:T(8,128)(2,1)S(1)} %get-tuple-element.112), channel_id=1, source_target_pairs={{0,12},{2,14},{4,0},{6,2},{8,4},{10,6},{12,8},{14,10},{1,13},{3,15... | collective-permute-start | bytes 393224 | tf_op jit(solution)/shard_map/ppermute | solution.py:198
  94.8 7.2 %collective-permute-done.5 = bf16[16,2,16,128]{3,2,1,0:T(8,128)(2,1)S(1)} collective-permute-done((bf16[16,2,16,128]{3,2,1,0:T(8,128)(2,1)}, bf16[16,2,16,128]{3,2,1,0:T(8,128)(2,1)S(1)}, u32[]{:S(2)}, u32[]{:S(2)}) %collective-permute-start.5) | collective-permute-done | bytes 131104 | tf_op jit(solution)/shard_map/ppermute | solution.py:198
  102.1 2.9 %collective-permute-done.6 = bf16[16,2,16,128]{3,2,1,0:T(8,128)(2,1)S(1)} collective-permute-done((bf16[16,2,16,128]{3,2,1,0:T(8,128)(2,1)S(1)}, bf16[16,2,16,128]{3,2,1,0:T(8,128)(2,1)S(1)}, u32[]{:S(2)}, u32[]{:S(2)}) %collective-permute-start.6) | collective-permute-done | bytes 131104 | tf_op jit(solution)/shard_map/ppermute | solution.py:198
  105.6 2.2 dynamic-slice_bitcast_fusion.16
  107.7 0.9 collective-permute-start.10
  108.7 6.0 %collective-permute-start.11 = (bf16[16,2,16,128]{3,2,1,0:T(8,128)(2,1)S(1)}, bf16[16,2,16,128]{3,2,1,0:T(8,128)(2,1)S(1)}, u32[]{:S(2)}, u32[]{:S(2)}) collective-permute-start(bf16[16,2,16,128]{3,2,1,0:T(8,128)(2,1)S(1)} %get-tuple-element.106), channel_id=1, source_target_pairs={{0,4},{2,6},{4,8},{6,10},{8,12},{10,14},{12,0},{14,2},{1,5},{3,7},... | collective-permute-start | bytes 393224 | tf_op jit(solution)/shard_map/ppermute | solution.py:198
  114.8 1.7 collective-permute-start.13
  116.5 2.0 collective-permute-start.14
  118.5 1.5 pad_maximum_fusion
  120.3 3.9 %collective-permute-start.15 = (bf16[16,2,16,128]{3,2,1,0:T(8,128)(2,1)S(1)}, bf16[16,2,16,128]{3,2,1,0:T(8,128)(2,1)}, u32[]{:S(2)}, u32[]{:S(2)}) collective-permute-start(bf16[16,2,16,128]{3,2,1,0:T(8,128)(2,1)S(1)} %get-tuple-element.102), channel_id=1, source_target_pairs={{0,12},{2,14},{4,0},{6,2},{8,4},{10,6},{12,8},{14,10},{1,13},{3,15... | collective-permute-start | bytes 393224 | tf_op jit(solution)/shard_map/ppermute | solution.py:198
  125.0 2.4 %copy.54 = bf16[16,2,256,128]{3,2,1,0:T(8,128)(2,1)} copy(bf16[16,2,256,128]{2,3,0,1:T(8,128)(2,1)S(1)} %maximum_bitcast_fusion) | data formatting | bytes 4194304 | tf_op jit(solution)/shard_map/transpose | solution.py:230
  127.5 9.8 %shard_map.19.rest_0_ = f32[64,2,256,512]{3,2,1,0:T(8,128)} custom-call(bf16[16,512,128]{2,1,0:T(8,128)(2,1)} %bitcast.185, bf16[16,128,512]{2,1,0:T(8,128)(2,1)} %bitcast.184), custom_call_target="tpu_custom_call" | custom-call | flops 1073741824 | bytes 20971520 | tf_op jit(solution)/shard_map/pallas_call | solution.py:173
  137.6 0.9 bitcast_dynamic-update-slice_fusion.20
  138.6 0.9 bitcast_dynamic-update-slice_fusion.19
  139.5 0.9 bitcast_dynamic-update-slice_fusion.18
  140.5 0.9 bitcast_dynamic-update-slice_fusion.17
  141.4 0.9 bitcast_dynamic-update-slice_fusion.16
  144.3 3.3 %collective-permute-start.19 = (bf16[16,2,16,128]{3,2,1,0:T(8,128)(2,1)S(1)}, bf16[16,2,16,128]{3,2,1,0:T(8,128)(2,1)S(1)}, u32[]{:S(2)}, u32[]{:S(2)}) collective-permute-start(bf16[16,2,16,128]{3,2,1,0:T(8,128)(2,1)S(1)} %get-tuple-element.96), channel_id=1, source_target_pairs={{0,4},{2,6},{4,8},{6,10},{8,12},{10,14},{12,0},{14,2},{1,5},{3,7},... | collective-permute-start | bytes 393224 | tf_op jit(solution)/shard_map/ppermute | solution.py:198
  147.6 1.6 collective-permute-start.21
  149.2 2.2 collective-permute-start.22
  152.1 3.9 %collective-permute-start.23 = (bf16[16,2,16,128]{3,2,1,0:T(8,128)(2,1)S(1)}, bf16[16,2,16,128]{3,2,1,0:T(8,128)(2,1)}, u32[]{:S(2)}, u32[]{:S(2)}) collective-permute-start(bf16[16,2,16,128]{3,2,1,0:T(8,128)(2,1)S(1)} %get-tuple-element.92), channel_id=1, source_target_pairs={{0,12},{2,14},{4,0},{6,2},{8,4},{10,6},{12,8},{14,10},{1,13},{3,15... | collective-permute-start | bytes 393224 | tf_op jit(solution)/shard_map/ppermute | solution.py:198
  156.8 1.6 copy.58
  158.4 2.4 %copy.57 = bf16[16,2,256,128]{3,2,1,0:T(8,128)(2,1)} copy(bf16[16,2,256,128]{2,3,0,1:T(8,128)(2,1)S(1)} %maximum_bitcast_fusion.1) | data formatting | bytes 4194304 | tf_op jit(solution)/shard_map/transpose | solution.py:230
  160.8 9.8 %shard_map.20.rest_0_ = f32[64,2,256,512]{3,2,1,0:T(8,128)} custom-call(bf16[16,512,128]{2,1,0:T(8,128)(2,1)} %bitcast.181, bf16[16,128,512]{2,1,0:T(8,128)(2,1)} %bitcast.179, f32[64,2,256,512]{3,2,1,0:T(8,128)} %shard_map.19.rest_0_), custom_call_target="tpu_custom_call", output_to_operand_aliasing={{}: (2, {})} | custom-call | flops 1073741824 | bytes 20971520 | tf_op jit(solution)/shard_map/pallas_call | solution.py:173
  171.0 0.9 bitcast_dynamic-update-slice_fusion.12
  171.9 0.9 bitcast_dynamic-update-slice_fusion.11
  172.8 0.9 bitcast_dynamic-update-slice_fusion.10
  173.8 0.9 bitcast_dynamic-update-slice_fusion.9
  174.7 0.9 bitcast_dynamic-update-slice_fusion.8
  175.9 1.0 collective-permute-start.26
  176.9 2.2 collective-permute-start.27
  179.4 2.5 %collective-permute-start.29 = (bf16[16,2,16,128]{3,2,1,0:T(8,128)(2,1)S(1)}, bf16[16,2,16,128]{3,2,1,0:T(8,128)(2,1)S(1)}, u32[]{:S(2)}, u32[]{:S(2)}) collective-permute-start(bf16[16,2,16,128]{3,2,1,0:T(8,128)(2,1)S(1)} %get-tuple-element.84), channel_id=1, source_target_pairs={{0,8},{2,10},{4,12},{6,14},{8,0},{10,2},{12,4},{14,6},{1,9},{3,11}... | collective-permute-start | bytes 393224 | tf_op jit(solution)/shard_map/ppermute | solution.py:198
  181.8 1.1 collective-permute-start.30
  183.7 3.9 %collective-permute-start.31 = (bf16[16,2,16,128]{3,2,1,0:T(8,128)(2,1)S(1)}, bf16[16,2,16,128]{3,2,1,0:T(8,128)(2,1)}, u32[]{:S(2)}, u32[]{:S(2)}) collective-permute-start(bf16[16,2,16,128]{3,2,1,0:T(8,128)(2,1)S(1)} %get-tuple-element.82), channel_id=1, source_target_pairs={{0,12},{2,14},{4,0},{6,2},{8,4},{10,6},{12,8},{14,10},{1,13},{3,15... | collective-permute-start | bytes 393224 | tf_op jit(solution)/shard_map/ppermute | solution.py:198
  188.1 1.6 copy.62
  189.7 2.4 %copy.61 = bf16[16,2,256,128]{3,2,1,0:T(8,128)(2,1)} copy(bf16[16,2,256,128]{2,3,0,1:T(8,128)(2,1)S(1)} %maximum_bitcast_fusion.2) | data formatting | bytes 4194304 | tf_op jit(solution)/shard_map/transpose | solution.py:230
  192.1 9.8 %shard_map.21.rest_0_ = f32[64,2,256,512]{3,2,1,0:T(8,128)} custom-call(bf16[16,512,128]{2,1,0:T(8,128)(2,1)} %bitcast.182, bf16[16,128,512]{2,1,0:T(8,128)(2,1)} %bitcast.180, f32[64,2,256,512]{3,2,1,0:T(8,128)} %shard_map.20.rest_0_), custom_call_target="tpu_custom_call", output_to_operand_aliasing={{}: (2, {})} | custom-call | flops 1073741824 | bytes 20971520 | tf_op jit(solution)/shard_map/pallas_call | solution.py:173
  202.3 0.9 bitcast_dynamic-update-slice_fusion.1
  203.2 0.9 bitcast_dynamic-update-slice_fusion
  204.3 2.6 %collective-permute-done.33 = bf16[16,2,2,16,512]{4,3,2,1,0:T(8,128)(2,1)S(1)} collective-permute-done((bf16[16,2,2,16,512]{4,3,2,1,0:T(8,128)(2,1)S(1)}, bf16[16,2,2,16,512]{4,3,2,1,0:T(8,128)(2,1)S(1)}, u32[]{:S(2)}, u32[]{:S(2)}) %collective-permute-start.33) | collective-permute-done | bytes 1048608 | tf_op jit(solution)/shard_map/ppermute | solution.py:219
  207.4 1.6 copy.66
  209.4 2.4 %copy.65 = bf16[16,2,256,128]{3,2,1,0:T(8,128)(2,1)} copy(bf16[16,2,256,128]{2,3,0,1:T(8,128)(2,1)S(1)} %maximum_bitcast_fusion.3) | data formatting | bytes 4194304 | tf_op jit(solution)/shard_map/transpose | solution.py:230
  211.8 9.8 %shard_map.22 = f32[64,2,256,512]{3,2,1,0:T(8,128)} custom-call(bf16[16,512,128]{2,1,0:T(8,128)(2,1)} %bitcast.183, bf16[16,128,512]{2,1,0:T(8,128)(2,1)} %bitcast.178, f32[64,2,256,512]{3,2,1,0:T(8,128)} %shard_map.21.rest_0_), custom_call_target="tpu_custom_call", output_to_operand_aliasing={{}: (2, {})} | custom-call | flops 1073741824 | bytes 20971520 | tf_op jit(solution)/shard_map/pallas_call | solution.py:173
  (117 shorter events, 11.7 us)
Async XLA Ops:
  3.9 1.4 copy-start
  5.3 6.1 %collective-permute-start = (bf16[64,16384]{1,0:T(8,128)(2,1)S(1)}, bf16[64,16384]{1,0:T(8,128)(2,1)S(1)}, u32[]{:S(2)}, u32[]{:S(2)}) collective-permute-start(bf16[64,16384]{1,0:T(8,128)(2,1)S(1)} %get-tuple-element.78.own_ref), channel_id=1, source_target_pairs={{0,1},{1,2},{2,3},{4,5},{5,6},{6,7},{8,9},{9,10},{10,11},{12,13},{... | collective-permute-start | bytes 6291464 | tf_op jit(solution)/shard_map/ppermute | solution.py:17
  11.4 1.3 copy-start.3
  12.8 48.7 %collective-permute-start.1 = (bf16[64,16384]{1,0:T(8,128)(2,1)}, bf16[64,16384]{1,0:T(8,128)(2,1)}, u32[]{:S(2)}, u32[]{:S(2)}) collective-permute-start(bf16[64,16384]{1,0:T(8,128)(2,1)} %get-tuple-element.39.own_ref), channel_id=1, source_target_pairs={{0,1},{1,2},{2,3},{4,5},{5,6},{6,7},{8,9},{9,10},{10,11},{12,13},{... | collective-permute-start | bytes 6291464 | tf_op jit(solution)/shard_map/ppermute | solution.py:17
  61.5 7.9 %copy-start.2 = (bf16[1024,1024]{1,0:T(8,128)(2,1)S(1)}, bf16[1024,1024]{1,0:T(8,128)(2,1)}, u32[]{:S(2)}) copy-start(bf16[1024,1024]{1,0:T(8,128)(2,1)} %convert_element_type.36) | copy-start | bytes 6291460
  80.9 10.1 %collective-permute-start.2 = (bf16[16,2,16,128]{3,2,1,0:T(8,128)(2,1)}, bf16[16,2,16,128]{3,2,1,0:T(8,128)(2,1)}, u32[]{:S(2)}, u32[]{:S(2)}) collective-permute-start(bf16[16,2,16,128]{3,2,1,0:T(8,128)(2,1)} %get-tuple-element.117), channel_id=1, source_target_pairs={{0,2},{2,0},{4,6},{6,4},{8,10},{10,8},{12,14},{14,12},{1,3},{3,1},... | collective-permute-start | bytes 393224 | tf_op jit(solution)/shard_map/ppermute | solution.py:198
  83.8 10.4 %collective-permute-start.3 = (bf16[16,2,16,128]{3,2,1,0:T(8,128)(2,1)}, bf16[16,2,16,128]{3,2,1,0:T(8,128)(2,1)S(1)}, u32[]{:S(2)}, u32[]{:S(2)}) collective-permute-start(bf16[16,2,16,128]{3,2,1,0:T(8,128)(2,1)} %get-tuple-element.116), channel_id=1, source_target_pairs={{0,4},{2,6},{4,8},{6,10},{8,12},{10,14},{12,0},{14,2},{1,5},{3,7},... | collective-permute-start | bytes 393224 | tf_op jit(solution)/shard_map/ppermute | solution.py:198
  85.4 9.4 %collective-permute-start.4 = (bf16[16,2,16,128]{3,2,1,0:T(8,128)(2,1)}, bf16[16,2,16,128]{3,2,1,0:T(8,128)(2,1)S(1)}, u32[]{:S(2)}, u32[]{:S(2)}) collective-permute-start(bf16[16,2,16,128]{3,2,1,0:T(8,128)(2,1)} %get-tuple-element.115), channel_id=1, source_target_pairs={{0,6},{2,4},{4,10},{6,8},{8,14},{10,12},{12,2},{14,0},{1,7},{3,5},... | collective-permute-start | bytes 393224 | tf_op jit(solution)/shard_map/ppermute | solution.py:198
  86.4 15.6 %collective-permute-start.5 = (bf16[16,2,16,128]{3,2,1,0:T(8,128)(2,1)}, bf16[16,2,16,128]{3,2,1,0:T(8,128)(2,1)S(1)}, u32[]{:S(2)}, u32[]{:S(2)}) collective-permute-start(bf16[16,2,16,128]{3,2,1,0:T(8,128)(2,1)} %get-tuple-element.114), channel_id=1, source_target_pairs={{0,8},{2,10},{4,12},{6,14},{8,0},{10,2},{12,4},{14,6},{1,9},{3,11}... | collective-permute-start | bytes 393224 | tf_op jit(solution)/shard_map/ppermute | solution.py:198
  88.0 17.0 %collective-permute-start.6 = (bf16[16,2,16,128]{3,2,1,0:T(8,128)(2,1)S(1)}, bf16[16,2,16,128]{3,2,1,0:T(8,128)(2,1)S(1)}, u32[]{:S(2)}, u32[]{:S(2)}) collective-permute-start(bf16[16,2,16,128]{3,2,1,0:T(8,128)(2,1)S(1)} %get-tuple-element.113), channel_id=1, source_target_pairs={{0,10},{2,8},{4,14},{6,12},{8,2},{10,0},{12,6},{14,4},{1,11},{3,9}... | collective-permute-start | bytes 393224 | tf_op jit(solution)/shard_map/ppermute | solution.py:198
  91.0 14.0 %collective-permute-start.7 = (bf16[16,2,16,128]{3,2,1,0:T(8,128)(2,1)S(1)}, bf16[16,2,16,128]{3,2,1,0:T(8,128)(2,1)S(1)}, u32[]{:S(2)}, u32[]{:S(2)}) collective-permute-start(bf16[16,2,16,128]{3,2,1,0:T(8,128)(2,1)S(1)} %get-tuple-element.112), channel_id=1, source_target_pairs={{0,12},{2,14},{4,0},{6,2},{8,4},{10,6},{12,8},{14,10},{1,13},{3,15... | collective-permute-start | bytes 393224 | tf_op jit(solution)/shard_map/ppermute | solution.py:198
  94.2 11.2 %collective-permute-start.8 = (bf16[16,2,16,128]{3,2,1,0:T(8,128)(2,1)S(1)}, bf16[16,2,16,128]{3,2,1,0:T(8,128)(2,1)S(1)}, u32[]{:S(2)}, u32[]{:S(2)}) collective-permute-start(bf16[16,2,16,128]{3,2,1,0:T(8,128)(2,1)S(1)} %get-tuple-element.111), channel_id=1, source_target_pairs={{0,14},{2,12},{4,2},{6,0},{8,6},{10,4},{12,10},{14,8},{1,15},{3,13... | collective-permute-start | bytes 393224 | tf_op jit(solution)/shard_map/ppermute | solution.py:198
  105.5 11.0 %collective-permute-start.9 = (bf16[16,2,2,16,512]{4,3,2,1,0:T(8,128)(2,1)S(1)}, bf16[16,2,2,16,512]{4,3,2,1,0:T(8,128)(2,1)S(1)}, u32[]{:S(2)}, u32[]{:S(2)}) collective-permute-start(bf16[16,2,2,16,512]{4,3,2,1,0:T(8,128)(2,1)S(1)} %bitcast_dynamic-update-slice_fusion.24), channel_id=1, source_target_pairs={{0,1},{1,0},{2,3},{3,2},{4,5},{5,4},{6,7},{7,6},{8,9},{9,8},{10,11... | collective-permute-start | bytes 3145736 | tf_op jit(solution)/shard_map/ppermute | solution.py:219
  107.7 12.6 %collective-permute-start.10 = (bf16[16,2,16,128]{3,2,1,0:T(8,128)(2,1)S(1)}, bf16[16,2,16,128]{3,2,1,0:T(8,128)(2,1)S(1)}, u32[]{:S(2)}, u32[]{:S(2)}) collective-permute-start(bf16[16,2,16,128]{3,2,1,0:T(8,128)(2,1)S(1)} %get-tuple-element.107), channel_id=1, source_target_pairs={{0,2},{2,0},{4,6},{6,4},{8,10},{10,8},{12,14},{14,12},{1,3},{3,1},... | collective-permute-start | bytes 393224 | tf_op jit(solution)/shard_map/ppermute | solution.py:198
  108.7 15.5 %collective-permute-start.11 = (bf16[16,2,16,128]{3,2,1,0:T(8,128)(2,1)S(1)}, bf16[16,2,16,128]{3,2,1,0:T(8,128)(2,1)S(1)}, u32[]{:S(2)}, u32[]{:S(2)}) collective-permute-start(bf16[16,2,16,128]{3,2,1,0:T(8,128)(2,1)S(1)} %get-tuple-element.106), channel_id=1, source_target_pairs={{0,4},{2,6},{4,8},{6,10},{8,12},{10,14},{12,0},{14,2},{1,5},{3,7},... | collective-permute-start | bytes 393224 | tf_op jit(solution)/shard_map/ppermute | solution.py:198
  114.6 22.7 %collective-permute-start.12 = (bf16[16,2,16,128]{3,2,1,0:T(8,128)(2,1)}, bf16[16,2,16,128]{3,2,1,0:T(8,128)(2,1)}, u32[]{:S(2)}, u32[]{:S(2)}) collective-permute-start(bf16[16,2,16,128]{3,2,1,0:T(8,128)(2,1)} %get-tuple-element.105), channel_id=1, source_target_pairs={{0,6},{2,4},{4,10},{6,8},{8,14},{10,12},{12,2},{14,0},{1,7},{3,5},... | collective-permute-start | bytes 393224 | tf_op jit(solution)/shard_map/ppermute | solution.py:198
  114.8 22.5 %collective-permute-start.13 = (bf16[16,2,16,128]{3,2,1,0:T(8,128)(2,1)}, bf16[16,2,16,128]{3,2,1,0:T(8,128)(2,1)}, u32[]{:S(2)}, u32[]{:S(2)}) collective-permute-start(bf16[16,2,16,128]{3,2,1,0:T(8,128)(2,1)} %get-tuple-element.104), channel_id=1, source_target_pairs={{0,8},{2,10},{4,12},{6,14},{8,0},{10,2},{12,4},{14,6},{1,9},{3,11}... | collective-permute-start | bytes 393224 | tf_op jit(solution)/shard_map/ppermute | solution.py:198
  116.5 20.8 %collective-permute-start.14 = (bf16[16,2,16,128]{3,2,1,0:T(8,128)(2,1)}, bf16[16,2,16,128]{3,2,1,0:T(8,128)(2,1)}, u32[]{:S(2)}, u32[]{:S(2)}) collective-permute-start(bf16[16,2,16,128]{3,2,1,0:T(8,128)(2,1)} %get-tuple-element.103), channel_id=1, source_target_pairs={{0,10},{2,8},{4,14},{6,12},{8,2},{10,0},{12,6},{14,4},{1,11},{3,9}... | collective-permute-start | bytes 393224 | tf_op jit(solution)/shard_map/ppermute | solution.py:198
  120.3 4.1 %copy-start.8 = (bf16[16,2,16,128]{3,2,1,0:T(8,128)(2,1)}, bf16[16,2,16,128]{3,2,1,0:T(8,128)(2,1)S(1)}, u32[]{:S(2)}) copy-start(bf16[16,2,16,128]{3,2,1,0:T(8,128)(2,1)S(1)} %collective-permute-done.10) | copy-start | bytes 393220
  120.3 17.0 %collective-permute-start.15 = (bf16[16,2,16,128]{3,2,1,0:T(8,128)(2,1)S(1)}, bf16[16,2,16,128]{3,2,1,0:T(8,128)(2,1)}, u32[]{:S(2)}, u32[]{:S(2)}) collective-permute-start(bf16[16,2,16,128]{3,2,1,0:T(8,128)(2,1)S(1)} %get-tuple-element.102), channel_id=1, source_target_pairs={{0,12},{2,14},{4,0},{6,2},{8,4},{10,6},{12,8},{14,10},{1,13},{3,15... | collective-permute-start | bytes 393224 | tf_op jit(solution)/shard_map/ppermute | solution.py:198
  124.2 0.7 copy-start.10
  124.2 13.1 %collective-permute-start.16 = (bf16[16,2,16,128]{3,2,1,0:T(8,128)(2,1)S(1)}, bf16[16,2,16,128]{3,2,1,0:T(8,128)(2,1)}, u32[]{:S(2)}, u32[]{:S(2)}) collective-permute-start(bf16[16,2,16,128]{3,2,1,0:T(8,128)(2,1)S(1)} %get-tuple-element.101), channel_id=1, source_target_pairs={{0,14},{2,12},{4,2},{6,0},{8,6},{10,4},{12,10},{14,8},{1,15},{3,13... | collective-permute-start | bytes 393224 | tf_op jit(solution)/shard_map/ppermute | solution.py:198
  127.4 10.1 %copy-start.9 = (bf16[16,2,16,128]{3,2,1,0:T(8,128)(2,1)S(1)}, bf16[16,2,16,128]{3,2,1,0:T(8,128)(2,1)}, u32[]{:S(2)}) copy-start(bf16[16,2,16,128]{3,2,1,0:T(8,128)(2,1)} %copy-done.8) | copy-start | bytes 393220
  127.5 10.1 %copy-start.11 = (bf16[16,2,16,128]{3,2,1,0:T(8,128)(2,1)S(1)}, bf16[16,2,16,128]{3,2,1,0:T(8,128)(2,1)}, u32[]{:S(2)}) copy-start(bf16[16,2,16,128]{3,2,1,0:T(8,128)(2,1)} %copy-done.10) | copy-start | bytes 393220
  137.3 5.1 %copy-start.1 = (bf16[8,16,2,16,128]{4,3,2,1,0:T(8,128)(2,1)S(1)}, bf16[8,16,2,16,128]{4,3,2,1,0:T(8,128)(2,1)}, u32[]{:S(2)}) copy-start(bf16[8,16,2,16,128]{4,3,2,1,0:T(8,128)(2,1)} %get-tuple-element.52) | copy-start | bytes 3145732
  142.4 6.9 %collective-permute-start.17 = (bf16[16,2,2,16,512]{4,3,2,1,0:T(8,128)(2,1)S(1)}, bf16[16,2,2,16,512]{4,3,2,1,0:T(8,128)(2,1)S(1)}, u32[]{:S(2)}, u32[]{:S(2)}) collective-permute-start(bf16[16,2,2,16,512]{4,3,2,1,0:T(8,128)(2,1)S(1)} %bitcast_dynamic-update-slice_fusion.16), channel_id=1, source_target_pairs={{0,1},{1,0},{2,3},{3,2},{4,5},{5,4},{6,7},{7,6},{8,9},{9,8},{10,11... | collective-permute-start | bytes 3145736 | tf_op jit(solution)/shard_map/ppermute | solution.py:219
  143.4 8.7 %collective-permute-start.18 = (bf16[16,2,16,128]{3,2,1,0:T(8,128)(2,1)S(1)}, bf16[16,2,16,128]{3,2,1,0:T(8,128)(2,1)S(1)}, u32[]{:S(2)}, u32[]{:S(2)}) collective-permute-start(bf16[16,2,16,128]{3,2,1,0:T(8,128)(2,1)S(1)} %get-tuple-element.97), channel_id=1, source_target_pairs={{0,2},{2,0},{4,6},{6,4},{8,10},{10,8},{12,14},{14,12},{1,3},{3,1},... | collective-permute-start | bytes 393224 | tf_op jit(solution)/shard_map/ppermute | solution.py:198
  144.3 11.7 %collective-permute-start.19 = (bf16[16,2,16,128]{3,2,1,0:T(8,128)(2,1)S(1)}, bf16[16,2,16,128]{3,2,1,0:T(8,128)(2,1)S(1)}, u32[]{:S(2)}, u32[]{:S(2)}) collective-permute-start(bf16[16,2,16,128]{3,2,1,0:T(8,128)(2,1)S(1)} %get-tuple-element.96), channel_id=1, source_target_pairs={{0,4},{2,6},{4,8},{6,10},{8,12},{10,14},{12,0},{14,2},{1,5},{3,7},... | collective-permute-start | bytes 393224 | tf_op jit(solution)/shard_map/ppermute | solution.py:198
  147.5 23.1 %collective-permute-start.20 = (bf16[16,2,16,128]{3,2,1,0:T(8,128)(2,1)}, bf16[16,2,16,128]{3,2,1,0:T(8,128)(2,1)}, u32[]{:S(2)}, u32[]{:S(2)}) collective-permute-start(bf16[16,2,16,128]{3,2,1,0:T(8,128)(2,1)} %get-tuple-element.95), channel_id=1, source_target_pairs={{0,6},{2,4},{4,10},{6,8},{8,14},{10,12},{12,2},{14,0},{1,7},{3,5},... | collective-permute-start | bytes 393224 | tf_op jit(solution)/shard_map/ppermute | solution.py:198
  147.6 23.0 %collective-permute-start.21 = (bf16[16,2,16,128]{3,2,1,0:T(8,128)(2,1)}, bf16[16,2,16,128]{3,2,1,0:T(8,128)(2,1)}, u32[]{:S(2)}, u32[]{:S(2)}) collective-permute-start(bf16[16,2,16,128]{3,2,1,0:T(8,128)(2,1)} %get-tuple-element.94), channel_id=1, source_target_pairs={{0,8},{2,10},{4,12},{6,14},{8,0},{10,2},{12,4},{14,6},{1,9},{3,11}... | collective-permute-start | bytes 393224 | tf_op jit(solution)/shard_map/ppermute | solution.py:198
  149.2 21.4 %collective-permute-start.22 = (bf16[16,2,16,128]{3,2,1,0:T(8,128)(2,1)}, bf16[16,2,16,128]{3,2,1,0:T(8,128)(2,1)}, u32[]{:S(2)}, u32[]{:S(2)}) collective-permute-start(bf16[16,2,16,128]{3,2,1,0:T(8,128)(2,1)} %get-tuple-element.93), channel_id=1, source_target_pairs={{0,10},{2,8},{4,14},{6,12},{8,2},{10,0},{12,6},{14,4},{1,11},{3,9}... | collective-permute-start | bytes 393224 | tf_op jit(solution)/shard_map/ppermute | solution.py:198
  152.1 4.1 %copy-start.4 = (bf16[16,2,16,128]{3,2,1,0:T(8,128)(2,1)}, bf16[16,2,16,128]{3,2,1,0:T(8,128)(2,1)S(1)}, u32[]{:S(2)}) copy-start(bf16[16,2,16,128]{3,2,1,0:T(8,128)(2,1)S(1)} %collective-permute-done.18) | copy-start | bytes 393220
  152.1 18.5 %collective-permute-start.23 = (bf16[16,2,16,128]{3,2,1,0:T(8,128)(2,1)S(1)}, bf16[16,2,16,128]{3,2,1,0:T(8,128)(2,1)}, u32[]{:S(2)}, u32[]{:S(2)}) collective-permute-start(bf16[16,2,16,128]{3,2,1,0:T(8,128)(2,1)S(1)} %get-tuple-element.92), channel_id=1, source_target_pairs={{0,12},{2,14},{4,0},{6,2},{8,4},{10,6},{12,8},{14,10},{1,13},{3,15... | collective-permute-start | bytes 393224 | tf_op jit(solution)/shard_map/ppermute | solution.py:198
  156.0 0.6 copy-start.6
  156.0 14.7 %collective-permute-start.24 = (bf16[16,2,16,128]{3,2,1,0:T(8,128)(2,1)S(1)}, bf16[16,2,16,128]{3,2,1,0:T(8,128)(2,1)}, u32[]{:S(2)}, u32[]{:S(2)}) collective-permute-start(bf16[16,2,16,128]{3,2,1,0:T(8,128)(2,1)S(1)} %get-tuple-element.91), channel_id=1, source_target_pairs={{0,14},{2,12},{4,2},{6,0},{8,6},{10,4},{12,10},{14,8},{1,15},{3,13... | collective-permute-start | bytes 393224 | tf_op jit(solution)/shard_map/ppermute | solution.py:198
  160.8 10.1 %copy-start.5 = (bf16[16,2,16,128]{3,2,1,0:T(8,128)(2,1)S(1)}, bf16[16,2,16,128]{3,2,1,0:T(8,128)(2,1)}, u32[]{:S(2)}) copy-start(bf16[16,2,16,128]{3,2,1,0:T(8,128)(2,1)} %copy-done.4) | copy-start | bytes 393220
  160.8 10.1 %copy-start.7 = (bf16[16,2,16,128]{3,2,1,0:T(8,128)(2,1)S(1)}, bf16[16,2,16,128]{3,2,1,0:T(8,128)(2,1)}, u32[]{:S(2)}) copy-start(bf16[16,2,16,128]{3,2,1,0:T(8,128)(2,1)} %copy-done.6) | copy-start | bytes 393220
  175.7 6.2 %collective-permute-start.25 = (bf16[16,2,2,16,512]{4,3,2,1,0:T(8,128)(2,1)S(1)}, bf16[16,2,2,16,512]{4,3,2,1,0:T(8,128)(2,1)S(1)}, u32[]{:S(2)}, u32[]{:S(2)}) collective-permute-start(bf16[16,2,2,16,512]{4,3,2,1,0:T(8,128)(2,1)S(1)} %bitcast_dynamic-update-slice_fusion.8), channel_id=1, source_target_pairs={{0,1},{1,0},{2,3},{3,2},{4,5},{5,4},{6,7},{7,6},{8,9},{9,8},{10,11... | collective-permute-start | bytes 3145736 | tf_op jit(solution)/shard_map/ppermute | solution.py:219
  175.9 7.7 %collective-permute-start.26 = (bf16[16,2,16,128]{3,2,1,0:T(8,128)(2,1)S(1)}, bf16[16,2,16,128]{3,2,1,0:T(8,128)(2,1)S(1)}, u32[]{:S(2)}, u32[]{:S(2)}) collective-permute-start(bf16[16,2,16,128]{3,2,1,0:T(8,128)(2,1)S(1)} %get-tuple-element.87), channel_id=1, source_target_pairs={{0,2},{2,0},{4,6},{6,4},{8,10},{10,8},{12,14},{14,12},{1,3},{3,1},... | collective-permute-start | bytes 393224 | tf_op jit(solution)/shard_map/ppermute | solution.py:198
  176.9 10.7 %collective-permute-start.27 = (bf16[16,2,16,128]{3,2,1,0:T(8,128)(2,1)S(1)}, bf16[16,2,16,128]{3,2,1,0:T(8,128)(2,1)S(1)}, u32[]{:S(2)}, u32[]{:S(2)}) collective-permute-start(bf16[16,2,16,128]{3,2,1,0:T(8,128)(2,1)S(1)} %get-tuple-element.86), channel_id=1, source_target_pairs={{0,4},{2,6},{4,8},{6,10},{8,12},{10,14},{12,0},{14,2},{1,5},{3,7},... | collective-permute-start | bytes 393224 | tf_op jit(solution)/shard_map/ppermute | solution.py:198
  179.1 22.8 %collective-permute-start.28 = (bf16[16,2,16,128]{3,2,1,0:T(8,128)(2,1)S(1)}, bf16[16,2,16,128]{3,2,1,0:T(8,128)(2,1)S(1)}, u32[]{:S(2)}, u32[]{:S(2)}) collective-permute-start(bf16[16,2,16,128]{3,2,1,0:T(8,128)(2,1)S(1)} %get-tuple-element.85), channel_id=1, source_target_pairs={{0,6},{2,4},{4,10},{6,8},{8,14},{10,12},{12,2},{14,0},{1,7},{3,5},... | collective-permute-start | bytes 393224 | tf_op jit(solution)/shard_map/ppermute | solution.py:198
  179.4 22.5 %collective-permute-start.29 = (bf16[16,2,16,128]{3,2,1,0:T(8,128)(2,1)S(1)}, bf16[16,2,16,128]{3,2,1,0:T(8,128)(2,1)S(1)}, u32[]{:S(2)}, u32[]{:S(2)}) collective-permute-start(bf16[16,2,16,128]{3,2,1,0:T(8,128)(2,1)S(1)} %get-tuple-element.84), channel_id=1, source_target_pairs={{0,8},{2,10},{4,12},{6,14},{8,0},{10,2},{12,4},{14,6},{1,9},{3,11}... | collective-permute-start | bytes 393224 | tf_op jit(solution)/shard_map/ppermute | solution.py:198
  181.8 20.0 %collective-permute-start.30 = (bf16[16,2,16,128]{3,2,1,0:T(8,128)(2,1)S(1)}, bf16[16,2,16,128]{3,2,1,0:T(8,128)(2,1)S(1)}, u32[]{:S(2)}, u32[]{:S(2)}) collective-permute-start(bf16[16,2,16,128]{3,2,1,0:T(8,128)(2,1)S(1)} %get-tuple-element.83), channel_id=1, source_target_pairs={{0,10},{2,8},{4,14},{6,12},{8,2},{10,0},{12,6},{14,4},{1,11},{3,9}... | collective-permute-start | bytes 393224 | tf_op jit(solution)/shard_map/ppermute | solution.py:198
  183.7 18.2 %collective-permute-start.31 = (bf16[16,2,16,128]{3,2,1,0:T(8,128)(2,1)S(1)}, bf16[16,2,16,128]{3,2,1,0:T(8,128)(2,1)}, u32[]{:S(2)}, u32[]{:S(2)}) collective-permute-start(bf16[16,2,16,128]{3,2,1,0:T(8,128)(2,1)S(1)} %get-tuple-element.82), channel_id=1, source_target_pairs={{0,12},{2,14},{4,0},{6,2},{8,4},{10,6},{12,8},{14,10},{1,13},{3,15... | collective-permute-start | bytes 393224 | tf_op jit(solution)/shard_map/ppermute | solution.py:198
  187.5 14.3 %collective-permute-start.32 = (bf16[16,2,16,128]{3,2,1,0:T(8,128)(2,1)S(1)}, bf16[16,2,16,128]{3,2,1,0:T(8,128)(2,1)}, u32[]{:S(2)}, u32[]{:S(2)}) collective-permute-start(bf16[16,2,16,128]{3,2,1,0:T(8,128)(2,1)S(1)} %get-tuple-element.81), channel_id=1, source_target_pairs={{0,14},{2,12},{4,2},{6,0},{8,6},{10,4},{12,10},{14,8},{1,15},{3,13... | collective-permute-start | bytes 393224 | tf_op jit(solution)/shard_map/ppermute | solution.py:198
  204.2 2.7 %collective-permute-start.33 = (bf16[16,2,2,16,512]{4,3,2,1,0:T(8,128)(2,1)S(1)}, bf16[16,2,2,16,512]{4,3,2,1,0:T(8,128)(2,1)S(1)}, u32[]{:S(2)}, u32[]{:S(2)}) collective-permute-start(bf16[16,2,2,16,512]{4,3,2,1,0:T(8,128)(2,1)S(1)} %bitcast_dynamic-update-slice_fusion), channel_id=1, source_target_pairs={{0,1},{1,0},{2,3},{3,2},{4,5},{5,4},{6,7},{7,6},{8,9},{9,8},{10,11... | collective-permute-start | bytes 3145736 | tf_op jit(solution)/shard_map/ppermute | solution.py:219

commit v12 on v10

--- a/solution.py
+++ b/solution.py
@@ -106,7 +106,7 @@
     inp_at = lax.axis_index("inp")
     tm_at = lax.axis_index("tm")
     cols = inp_size * inputs_here
-    chunks = 4 if own_channels % 8 == 0 else 1
+    chunks = 8 if own_channels % 16 == 0 else 1
     per_chunk = own_channels // chunks
     parts = [blocks[:, chunk * per_chunk : (chunk + 1) * per_chunk] for chunk in range(chunks)]
     out = None

time: 216 us -> 249 us (1.15)
  starting transfers between devices: 85.9 us -> 126 us
  local copies, waits for them, and re-layouts: 40.6 us -> 31 us
  Pallas kernels: 52.4 us -> 60.1 us
  waiting for transfers between devices: 12.3 us -> 6.85 us
    ppermute x28 -> x56, starting transfers between devices: 81.3 us -> 121 us  [send_chunk(): block = lax.ppermute(block, ('inp', 'tm'), route)]
    dynamic_update_slice x32 -> x64, local copies, waits for them, and re-layouts: 13 us -> 4.04 us  [assemble_chunk(): lax.dynamic_update_slice(half, block[:, :, None], (0, 0, tm_step, 0, sour...]
    pallas_call x4 -> x8, Pallas kernels: 39.3 us -> 47 us  [correlate(): pl.pallas_call(functools.partial(correlate_kernel, 1.0 / (depth // 2)), g...]
    ppermute x28 -> x56, waiting for transfers between devices: 9.6 us -> 4.93 us  [send_chunk(): block = lax.ppermute(block, ('inp', 'tm'), route)]
    squeeze x4 -> x8, local copies, waits for them, and re-layouts: 4.11 us -> 0.4 us  [send_chunk(): block = lax.dynamic_index_in_dim(blocks, target, 0, keepdims=False)]
    another operation x3 -> x7, local copies, waits for them, and re-layouts: 4.67 us -> 7.48 us  [finish_chunk(): both = jnp.stack([half, partner], axis=1)]
    transpose x4 -> x8, local copies, waits for them, and re-layouts: 9.58 us -> 10.5 us  [finish_chunk(): lhs = lhs.transpose(0, 1, 3, 2).reshape(own_channels, 2 * rows_here, depth)]
  transfers between devices with their start and end apart: 33 -> 65, of which waited for: 4 -> 4; matrix products, arithmetic and copies ran while one was open for 16% -> 14% of each run, Pallas kernels for 14% -> 17%
where the time goes in v12:
time: 249 us; the launch traced here: 248 us
  starting transfers between devices  126 us (51%)
  Pallas kernels  60.1 us (24%)
  local copies, waits for them, and re-layouts  31 us (12%)
  other arithmetic  14.5 us (6%)
  matrix products  6.95 us (3%)
  waiting for transfers between devices  6.85 us (3%)
    ppermute x56, starting transfers between devices, send_chunk(): block = lax.ppermute(block, ('inp', 'tm'), route)  121 us
    pallas_call x8, Pallas kernels, correlate(): pl.pallas_call(functools.partial(correlate_kernel, 1.0 / (depth // 2)), g...  47 us
    pallas_call x1, Pallas kernels, polyphase_filter(): pl.pallas_call(filter_kernel, grid=(inputs_here // rows,), in_specs=[pl.B...  13.1 us
    transpose x8, local copies, waits for them, and re-layouts, finish_chunk(): lhs = lhs.transpose(0, 1, 3, 2).reshape(own_channels, 2 * rows_here, depth)  10.5 us
    another operation x1, other arithmetic  8.49 us
    another operation x7, local copies, waits for them, and re-layouts, finish_chunk(): both = jnp.stack([half, partner], axis=1)  7.48 us
    dot_general x1, matrix products, per_device(): lax.dot_general(dft_table_t(frame_len), filtered.reshape(spectra_here * i...  6.95 us
  transfers between devices with their start and end apart: 65, of which 4 were waited for; matrix products, arithmetic and copies ran while one was open for 14% of the time, Pallas kernels for 17%

profile of v12, /device:TPU:0, one launch (start us, length us, event | category | flops | bytes accessed | tf_op | source)
XLA Modules:
  0.0 247.5 jit_solution(17523151986780046802)
XLA Ops:
  0.0 4.4 %collective-permute-start = (bf16[128,16384]{1,0:T(8,128)(2,1)}, bf16[128,16384]{1,0:T(8,128)(2,1)}, u32[]{:S(2)}, u32[]{:S(2)}) collective-permute-start(bf16[128,16384]{1,0:T(8,128)(2,1)} %own_ref.1), channel_id=1, source_target_pairs={{0,1},{1,2},{2,3},{4,5},{5,6},{6,7},{8,9},{9,10},{10,11},{12,13},{... | collective-permute-start | bytes 12582920 | tf_op jit(solution)/shard_map/ppermute | solution.py:17
  4.4 8.5 %negate_convert_fusion = (bf16[512,1,1024]{2,0,1:T(8,128)(2,1)S(1)}, bf16[512,1,1024]{2,0,1:T(8,128)(2,1)S(1)}) fusion(), kind=kLoop, calls=%fused_computation.8 | loop fusion | flops 8912896 | bytes 2097152 | tf_op jit(solution)/shard_map/convert.1
  13.1 2.2 copy.107
  15.3 2.2 convert_element_type.36
  19.3 1.1 fusion.15.taps_ref
  20.4 13.1 %shard_map.17 = bf16[16,128,1024]{2,1,0:T(8,128)(2,1)} custom-call(f32[16,1024]{1,0:T(8,128)} %fusion.15.taps_ref, bf16[128,16384]{1,0:T(8,128)(2,1)} %own_ref.1, bf16[128,16384]{1,0:T(8,128)(2,1)} %collective-permute-done.history_ref), custom_call_target="tpu_custom_call" | custom-call | flops 67108864 | bytes 12582912 | tf_op jit(solution)/shard_map/pallas_call | solution.py:71
  33.6 7.0 %convert_bitcast_fusion = bf16[128,8,16,128]{3,1,2,0:T(8,128)(2,1)S(1)} fusion(bf16[1024,1024]{1,0:T(8,128)(2,1)S(1)} %copy-done.3, bf16[2048,1024]{1,0:T(8,128)(2,1)} %bitcast.361), kind=kOutput, calls=%fused_computation | convolution fusion | flops 4297064448 | bytes 10485760 | tf_op jit(solution)/shard_map/dot_general | solution.py:93
  40.5 1.4 copy.138
  41.9 1.8 fusion.19
  43.8 32.6 %collective-permute-start.1 = (bf16[8,2,16,128]{3,2,1,0:T(8,128)(2,1)S(1)}, bf16[8,2,16,128]{3,2,1,0:T(8,128)(2,1)S(1)}, u32[]{:S(2)}, u32[]{:S(2)}) collective-permute-start(bf16[8,2,16,128]{3,2,1,0:T(8,128)(2,1)S(1)} %get-tuple-element.245), channel_id=1, source_target_pairs={{0,2},{2,0},{4,6},{6,4},{8,10},{10,8},{12,14},{14,12},{1,3},{3,1},... | collective-permute-start | bytes 196616 | tf_op jit(solution)/shard_map/ppermute | solution.py:179
  76.4 1.6 collective-permute-start.2
  78.0 1.1 collective-permute-start.3
  79.0 1.5 collective-permute-start.4
  80.5 2.8 %collective-permute-start.5 = (bf16[8,2,16,128]{3,2,1,0:T(8,128)(2,1)S(1)}, bf16[8,2,16,128]{3,2,1,0:T(8,128)(2,1)S(1)}, u32[]{:S(2)}, u32[]{:S(2)}) collective-permute-start(bf16[8,2,16,128]{3,2,1,0:T(8,128)(2,1)S(1)} %get-tuple-element.241), channel_id=1, source_target_pairs={{0,10},{2,8},{4,14},{6,12},{8,2},{10,0},{12,6},{14,4},{1,11},{3,9}... | collective-permute-start | bytes 196616 | tf_op jit(solution)/shard_map/ppermute | solution.py:179
  83.5 2.3 collective-permute-start.6
  86.7 3.1 %collective-permute-done.5 = bf16[8,2,16,128]{3,2,1,0:T(8,128)(2,1)S(1)} collective-permute-done((bf16[8,2,16,128]{3,2,1,0:T(8,128)(2,1)S(1)}, bf16[8,2,16,128]{3,2,1,0:T(8,128)(2,1)S(1)}, u32[]{:S(2)}, u32[]{:S(2)}) %collective-permute-start.5) | collective-permute-done | bytes 65568 | tf_op jit(solution)/shard_map/ppermute | solution.py:179
  89.9 1.2 collective-permute-done.7
  92.0 1.2 collective-permute-start.11
  93.2 2.3 collective-permute-start.12
  96.5 3.1 %collective-permute-start.14 = (bf16[8,2,16,128]{3,2,1,0:T(8,128)(2,1)S(1)}, bf16[8,2,16,128]{3,2,1,0:T(8,128)(2,1)}, u32[]{:S(2)}, u32[]{:S(2)}) collective-permute-start(bf16[8,2,16,128]{3,2,1,0:T(8,128)(2,1)S(1)} %get-tuple-element.230), channel_id=1, source_target_pairs={{0,12},{2,14},{4,0},{6,2},{8,4},{10,6},{12,8},{14,10},{1,13},{3,15... | collective-permute-start | bytes 196616 | tf_op jit(solution)/shard_map/ppermute | solution.py:179
  100.9 1.4 collective-permute-start.15
  102.2 1.6 collective-permute-start.9
  104.0 1.3 copy.109
  105.3 5.9 %shard_map.18.rest_0_ = f32[64,2,256,512]{3,2,1,0:T(8,128)} custom-call(bf16[8,512,128]{2,1,0:T(8,128)(2,1)} %bitcast.360, bf16[8,128,512]{2,1,0:T(8,128)(2,1)} %bitcast.345), custom_call_target="tpu_custom_call" | custom-call | flops 536870912 | bytes 10485760 | tf_op jit(solution)/shard_map/pallas_call | solution.py:154
  114.9 1.8 collective-permute-start.18
  116.7 3.4 %collective-permute-start.20 = (bf16[8,2,16,128]{3,2,1,0:T(8,128)(2,1)S(1)}, bf16[8,2,16,128]{3,2,1,0:T(8,128)(2,1)S(1)}, u32[]{:S(2)}, u32[]{:S(2)}) collective-permute-start(bf16[8,2,16,128]{3,2,1,0:T(8,128)(2,1)S(1)} %get-tuple-element.222), channel_id=1, source_target_pairs={{0,8},{2,10},{4,12},{6,14},{8,0},{10,2},{12,4},{14,6},{1,9},{3,11}... | collective-permute-start | bytes 196616 | tf_op jit(solution)/shard_map/ppermute | solution.py:179
  120.9 3.9 %collective-permute-start.22 = (bf16[8,2,16,128]{3,2,1,0:T(8,128)(2,1)S(1)}, bf16[8,2,16,128]{3,2,1,0:T(8,128)(2,1)S(1)}, u32[]{:S(2)}, u32[]{:S(2)}) collective-permute-start(bf16[8,2,16,128]{3,2,1,0:T(8,128)(2,1)S(1)} %get-tuple-element.220), channel_id=1, source_target_pairs={{0,12},{2,14},{4,0},{6,2},{8,4},{10,6},{12,8},{14,10},{1,13},{3,15... | collective-permute-start | bytes 196616 | tf_op jit(solution)/shard_map/ppermute | solution.py:179
  125.9 1.1 copy.113
  127.0 1.3 copy.112
  128.3 5.8 %shard_map.19.rest_0_ = f32[64,2,256,512]{3,2,1,0:T(8,128)} custom-call(bf16[8,512,128]{2,1,0:T(8,128)(2,1)} %bitcast.353, bf16[8,128,512]{2,1,0:T(8,128)(2,1)} %bitcast.347, f32[64,2,256,512]{3,2,1,0:T(8,128)} %shard_map.18.rest_0_), custom_call_target="tpu_custom_call", output_to_operand_aliasing={{}: (2, {})} | custom-call | flops 536870912 | bytes 10485760 | tf_op jit(solution)/shard_map/pallas_call | solution.py:154
  135.3 1.8 collective-permute-start.26
  137.2 3.4 %collective-permute-start.28 = (bf16[8,2,16,128]{3,2,1,0:T(8,128)(2,1)S(1)}, bf16[8,2,16,128]{3,2,1,0:T(8,128)(2,1)S(1)}, u32[]{:S(2)}, u32[]{:S(2)}) collective-permute-start(bf16[8,2,16,128]{3,2,1,0:T(8,128)(2,1)S(1)} %get-tuple-element.212), channel_id=1, source_target_pairs={{0,8},{2,10},{4,12},{6,14},{8,0},{10,2},{12,4},{14,6},{1,9},{3,11}... | collective-permute-start | bytes 196616 | tf_op jit(solution)/shard_map/ppermute | solution.py:179
  141.3 3.9 %collective-permute-start.30 = (bf16[8,2,16,128]{3,2,1,0:T(8,128)(2,1)S(1)}, bf16[8,2,16,128]{3,2,1,0:T(8,128)(2,1)S(1)}, u32[]{:S(2)}, u32[]{:S(2)}) collective-permute-start(bf16[8,2,16,128]{3,2,1,0:T(8,128)(2,1)S(1)} %get-tuple-element.210), channel_id=1, source_target_pairs={{0,12},{2,14},{4,0},{6,2},{8,4},{10,6},{12,8},{14,10},{1,13},{3,15... | collective-permute-start | bytes 196616 | tf_op jit(solution)/shard_map/ppermute | solution.py:179
  146.3 1.1 copy.117
  147.4 1.3 copy.116
  148.7 5.8 %shard_map.20.rest_0_ = f32[64,2,256,512]{3,2,1,0:T(8,128)} custom-call(bf16[8,512,128]{2,1,0:T(8,128)(2,1)} %bitcast.354, bf16[8,128,512]{2,1,0:T(8,128)(2,1)} %bitcast.348, f32[64,2,256,512]{3,2,1,0:T(8,128)} %shard_map.19.rest_0_), custom_call_target="tpu_custom_call", output_to_operand_aliasing={{}: (2, {})} | custom-call | flops 536870912 | bytes 10485760 | tf_op jit(solution)/shard_map/pallas_call | solution.py:154
  155.7 1.8 collective-permute-start.34
  157.6 3.4 %collective-permute-start.36 = (bf16[8,2,16,128]{3,2,1,0:T(8,128)(2,1)S(1)}, bf16[8,2,16,128]{3,2,1,0:T(8,128)(2,1)S(1)}, u32[]{:S(2)}, u32[]{:S(2)}) collective-permute-start(bf16[8,2,16,128]{3,2,1,0:T(8,128)(2,1)S(1)} %get-tuple-element.202), channel_id=1, source_target_pairs={{0,8},{2,10},{4,12},{6,14},{8,0},{10,2},{12,4},{14,6},{1,9},{3,11}... | collective-permute-start | bytes 196616 | tf_op jit(solution)/shard_map/ppermute | solution.py:179
  161.8 3.9 %collective-permute-start.38 = (bf16[8,2,16,128]{3,2,1,0:T(8,128)(2,1)S(1)}, bf16[8,2,16,128]{3,2,1,0:T(8,128)(2,1)S(1)}, u32[]{:S(2)}, u32[]{:S(2)}) collective-permute-start(bf16[8,2,16,128]{3,2,1,0:T(8,128)(2,1)S(1)} %get-tuple-element.200), channel_id=1, source_target_pairs={{0,12},{2,14},{4,0},{6,2},{8,4},{10,6},{12,8},{14,10},{1,13},{3,15... | collective-permute-start | bytes 196616 | tf_op jit(solution)/shard_map/ppermute | solution.py:179
  166.8 1.1 copy.121
  167.9 1.3 copy.120
  169.2 5.9 %shard_map.21.rest_0_ = f32[64,2,256,512]{3,2,1,0:T(8,128)} custom-call(bf16[8,512,128]{2,1,0:T(8,128)(2,1)} %bitcast.355, bf16[8,128,512]{2,1,0:T(8,128)(2,1)} %bitcast.349, f32[64,2,256,512]{3,2,1,0:T(8,128)} %shard_map.20.rest_0_), custom_call_target="tpu_custom_call", output_to_operand_aliasing={{}: (2, {})} | custom-call | flops 536870912 | bytes 10485760 | tf_op jit(solution)/shard_map/pallas_call | solution.py:154
  176.2 1.8 collective-permute-start.42
  178.1 3.4 %collective-permute-start.44 = (bf16[8,2,16,128]{3,2,1,0:T(8,128)(2,1)S(1)}, bf16[8,2,16,128]{3,2,1,0:T(8,128)(2,1)S(1)}, u32[]{:S(2)}, u32[]{:S(2)}) collective-permute-start(bf16[8,2,16,128]{3,2,1,0:T(8,128)(2,1)S(1)} %get-tuple-element.192), channel_id=1, source_target_pairs={{0,8},{2,10},{4,12},{6,14},{8,0},{10,2},{12,4},{14,6},{1,9},{3,11}... | collective-permute-start | bytes 196616 | tf_op jit(solution)/shard_map/ppermute | solution.py:179
  182.3 3.9 %collective-permute-start.46 = (bf16[8,2,16,128]{3,2,1,0:T(8,128)(2,1)S(1)}, bf16[8,2,16,128]{3,2,1,0:T(8,128)(2,1)S(1)}, u32[]{:S(2)}, u32[]{:S(2)}) collective-permute-start(bf16[8,2,16,128]{3,2,1,0:T(8,128)(2,1)S(1)} %get-tuple-element.190), channel_id=1, source_target_pairs={{0,12},{2,14},{4,0},{6,2},{8,4},{10,6},{12,8},{14,10},{1,13},{3,15... | collective-permute-start | bytes 196616 | tf_op jit(solution)/shard_map/ppermute | solution.py:179
  187.3 1.1 copy.125
  188.4 1.3 copy.124
  189.7 5.9 %shard_map.22.rest_0_ = f32[64,2,256,512]{3,2,1,0:T(8,128)} custom-call(bf16[8,512,128]{2,1,0:T(8,128)(2,1)} %bitcast.356, bf16[8,128,512]{2,1,0:T(8,128)(2,1)} %bitcast.350, f32[64,2,256,512]{3,2,1,0:T(8,128)} %shard_map.21.rest_0_), custom_call_target="tpu_custom_call", output_to_operand_aliasing={{}: (2, {})} | custom-call | flops 536870912 | bytes 10485760 | tf_op jit(solution)/shard_map/pallas_call | solution.py:154
  196.7 1.8 collective-permute-start.50
  198.6 3.4 %collective-permute-start.52 = (bf16[8,2,16,128]{3,2,1,0:T(8,128)(2,1)S(1)}, bf16[8,2,16,128]{3,2,1,0:T(8,128)(2,1)S(1)}, u32[]{:S(2)}, u32[]{:S(2)}) collective-permute-start(bf16[8,2,16,128]{3,2,1,0:T(8,128)(2,1)S(1)} %get-tuple-element.182), channel_id=1, source_target_pairs={{0,8},{2,10},{4,12},{6,14},{8,0},{10,2},{12,4},{14,6},{1,9},{3,11}... | collective-permute-start | bytes 196616 | tf_op jit(solution)/shard_map/ppermute | solution.py:179
  202.8 3.9 %collective-permute-start.54 = (bf16[8,2,16,128]{3,2,1,0:T(8,128)(2,1)S(1)}, bf16[8,2,16,128]{3,2,1,0:T(8,128)(2,1)S(1)}, u32[]{:S(2)}, u32[]{:S(2)}) collective-permute-start(bf16[8,2,16,128]{3,2,1,0:T(8,128)(2,1)S(1)} %get-tuple-element.180), channel_id=1, source_target_pairs={{0,12},{2,14},{4,0},{6,2},{8,4},{10,6},{12,8},{14,10},{1,13},{3,15... | collective-permute-start | bytes 196616 | tf_op jit(solution)/shard_map/ppermute | solution.py:179
  207.8 1.1 copy.129
  208.9 1.3 copy.128
  210.2 5.9 %shard_map.23.rest_0_ = f32[64,2,256,512]{3,2,1,0:T(8,128)} custom-call(bf16[8,512,128]{2,1,0:T(8,128)(2,1)} %bitcast.357, bf16[8,128,512]{2,1,0:T(8,128)(2,1)} %bitcast.351, f32[64,2,256,512]{3,2,1,0:T(8,128)} %shard_map.22.rest_0_), custom_call_target="tpu_custom_call", output_to_operand_aliasing={{}: (2, {})} | custom-call | flops 536870912 | bytes 10485760 | tf_op jit(solution)/shard_map/pallas_call | solution.py:154
  217.3 1.8 collective-permute-start.58
  219.1 3.4 %collective-permute-start.60 = (bf16[8,2,16,128]{3,2,1,0:T(8,128)(2,1)S(1)}, bf16[8,2,16,128]{3,2,1,0:T(8,128)(2,1)S(1)}, u32[]{:S(2)}, u32[]{:S(2)}) collective-permute-start(bf16[8,2,16,128]{3,2,1,0:T(8,128)(2,1)S(1)} %get-tuple-element.172), channel_id=1, source_target_pairs={{0,8},{2,10},{4,12},{6,14},{8,0},{10,2},{12,4},{14,6},{1,9},{3,11}... | collective-permute-start | bytes 196616 | tf_op jit(solution)/shard_map/ppermute | solution.py:179
  223.3 3.9 %collective-permute-start.62 = (bf16[8,2,16,128]{3,2,1,0:T(8,128)(2,1)S(1)}, bf16[8,2,16,128]{3,2,1,0:T(8,128)(2,1)S(1)}, u32[]{:S(2)}, u32[]{:S(2)}) collective-permute-start(bf16[8,2,16,128]{3,2,1,0:T(8,128)(2,1)S(1)} %get-tuple-element.170), channel_id=1, source_target_pairs={{0,12},{2,14},{4,0},{6,2},{8,4},{10,6},{12,8},{14,10},{1,13},{3,15... | collective-permute-start | bytes 196616 | tf_op jit(solution)/shard_map/ppermute | solution.py:179
  228.3 1.1 copy.133
  229.4 1.3 copy.132
  230.7 5.8 %shard_map.24.rest_0_ = f32[64,2,256,512]{3,2,1,0:T(8,128)} custom-call(bf16[8,512,128]{2,1,0:T(8,128)(2,1)} %bitcast.358, bf16[8,128,512]{2,1,0:T(8,128)(2,1)} %bitcast.352, f32[64,2,256,512]{3,2,1,0:T(8,128)} %shard_map.23.rest_0_), custom_call_target="tpu_custom_call", output_to_operand_aliasing={{}: (2, {})} | custom-call | flops 536870912 | bytes 10485760 | tf_op jit(solution)/shard_map/pallas_call | solution.py:154
  237.0 1.9 collective-permute-done.64
  239.1 1.1 copy.137
  240.4 1.3 copy.136
  241.7 5.8 %shard_map.25 = f32[64,2,256,512]{3,2,1,0:T(8,128)} custom-call(bf16[8,512,128]{2,1,0:T(8,128)(2,1)} %bitcast.359, bf16[8,128,512]{2,1,0:T(8,128)(2,1)} %bitcast.346, f32[64,2,256,512]{3,2,1,0:T(8,128)} %shard_map.24.rest_0_), custom_call_target="tpu_custom_call", output_to_operand_aliasing={{}: (2, {})} | custom-call | flops 536870912 | bytes 10485760 | tf_op jit(solution)/shard_map/pallas_call | solution.py:154
  (249 shorter events, 26.8 us)
Async XLA Ops:
  0.0 20.4 %collective-permute-start = (bf16[128,16384]{1,0:T(8,128)(2,1)}, bf16[128,16384]{1,0:T(8,128)(2,1)}, u32[]{:S(2)}, u32[]{:S(2)}) collective-permute-start(bf16[128,16384]{1,0:T(8,128)(2,1)} %own_ref.1), channel_id=1, source_target_pairs={{0,1},{1,2},{2,3},{4,5},{5,6},{6,7},{8,9},{9,10},{10,11},{12,13},{... | collective-permute-start | bytes 12582920 | tf_op jit(solution)/shard_map/ppermute | solution.py:17
  43.8 39.6 %collective-permute-start.1 = (bf16[8,2,16,128]{3,2,1,0:T(8,128)(2,1)S(1)}, bf16[8,2,16,128]{3,2,1,0:T(8,128)(2,1)S(1)}, u32[]{:S(2)}, u32[]{:S(2)}) collective-permute-start(bf16[8,2,16,128]{3,2,1,0:T(8,128)(2,1)S(1)} %get-tuple-element.245), channel_id=1, source_target_pairs={{0,2},{2,0},{4,6},{6,4},{8,10},{10,8},{12,14},{14,12},{1,3},{3,1},... | collective-permute-start | bytes 196616 | tf_op jit(solution)/shard_map/ppermute | solution.py:179
  76.4 9.4 %collective-permute-start.2 = (bf16[8,2,16,128]{3,2,1,0:T(8,128)(2,1)S(1)}, bf16[8,2,16,128]{3,2,1,0:T(8,128)(2,1)S(1)}, u32[]{:S(2)}, u32[]{:S(2)}) collective-permute-start(bf16[8,2,16,128]{3,2,1,0:T(8,128)(2,1)S(1)} %get-tuple-element.244), channel_id=1, source_target_pairs={{0,4},{2,6},{4,8},{6,10},{8,12},{10,14},{12,0},{14,2},{1,5},{3,7},... | collective-permute-start | bytes 196616 | tf_op jit(solution)/shard_map/ppermute | solution.py:179
  78.0 8.1 %collective-permute-start.3 = (bf16[8,2,16,128]{3,2,1,0:T(8,128)(2,1)S(1)}, bf16[8,2,16,128]{3,2,1,0:T(8,128)(2,1)S(1)}, u32[]{:S(2)}, u32[]{:S(2)}) collective-permute-start(bf16[8,2,16,128]{3,2,1,0:T(8,128)(2,1)S(1)} %get-tuple-element.243), channel_id=1, source_target_pairs={{0,6},{2,4},{4,10},{6,8},{8,14},{10,12},{12,2},{14,0},{1,7},{3,5},... | collective-permute-start | bytes 196616 | tf_op jit(solution)/shard_map/ppermute | solution.py:179
  79.0 7.6 %collective-permute-start.4 = (bf16[8,2,16,128]{3,2,1,0:T(8,128)(2,1)S(1)}, bf16[8,2,16,128]{3,2,1,0:T(8,128)(2,1)S(1)}, u32[]{:S(2)}, u32[]{:S(2)}) collective-permute-start(bf16[8,2,16,128]{3,2,1,0:T(8,128)(2,1)S(1)} %get-tuple-element.242), channel_id=1, source_target_pairs={{0,8},{2,10},{4,12},{6,14},{8,0},{10,2},{12,4},{14,6},{1,9},{3,11}... | collective-permute-start | bytes 196616 | tf_op jit(solution)/shard_map/ppermute | solution.py:179
  80.5 9.2 %collective-permute-start.5 = (bf16[8,2,16,128]{3,2,1,0:T(8,128)(2,1)S(1)}, bf16[8,2,16,128]{3,2,1,0:T(8,128)(2,1)S(1)}, u32[]{:S(2)}, u32[]{:S(2)}) collective-permute-start(bf16[8,2,16,128]{3,2,1,0:T(8,128)(2,1)S(1)} %get-tuple-element.241), channel_id=1, source_target_pairs={{0,10},{2,8},{4,14},{6,12},{8,2},{10,0},{12,6},{14,4},{1,11},{3,9}... | collective-permute-start | bytes 196616 | tf_op jit(solution)/shard_map/ppermute | solution.py:179
  83.5 6.4 %collective-permute-start.6 = (bf16[8,2,16,128]{3,2,1,0:T(8,128)(2,1)S(1)}, bf16[8,2,16,128]{3,2,1,0:T(8,128)(2,1)S(1)}, u32[]{:S(2)}, u32[]{:S(2)}) collective-permute-start(bf16[8,2,16,128]{3,2,1,0:T(8,128)(2,1)S(1)} %get-tuple-element.240), channel_id=1, source_target_pairs={{0,12},{2,14},{4,0},{6,2},{8,4},{10,6},{12,8},{14,10},{1,13},{3,15... | collective-permute-start | bytes 196616 | tf_op jit(solution)/shard_map/ppermute | solution.py:179
  85.8 5.2 %collective-permute-start.7 = (bf16[8,2,16,128]{3,2,1,0:T(8,128)(2,1)S(1)}, bf16[8,2,16,128]{3,2,1,0:T(8,128)(2,1)S(1)}, u32[]{:S(2)}, u32[]{:S(2)}) collective-permute-start(bf16[8,2,16,128]{3,2,1,0:T(8,128)(2,1)S(1)} %get-tuple-element.239), channel_id=1, source_target_pairs={{0,14},{2,12},{4,2},{6,0},{8,6},{10,4},{12,10},{14,8},{1,15},{3,13... | collective-permute-start | bytes 196616 | tf_op jit(solution)/shard_map/ppermute | solution.py:179
  91.0 5.5 %collective-permute-start.8 = (bf16[8,2,2,16,512]{4,3,2,1,0:T(8,128)(2,1)S(1)}, bf16[8,2,2,16,512]{4,3,2,1,0:T(8,128)(2,1)S(1)}, u32[]{:S(2)}, u32[]{:S(2)}) collective-permute-start(bf16[8,2,2,16,512]{4,3,2,1,0:T(8,128)(2,1)S(1)} %bitcast_dynamic-update-slice_fusion.56), channel_id=1, source_target_pairs={{0,1},{1,0},{2,3},{3,2},{4,5},{5,4},{6,7},{7,6},{8,9},{9,8},{10,11... | collective-permute-start | bytes 1572872 | tf_op jit(solution)/shard_map/ppermute | solution.py:200
  91.2 9.7 %collective-permute-start.10 = (bf16[8,2,16,128]{3,2,1,0:T(8,128)(2,1)S(1)}, bf16[8,2,16,128]{3,2,1,0:T(8,128)(2,1)S(1)}, u32[]{:S(2)}, u32[]{:S(2)}) collective-permute-start(bf16[8,2,16,128]{3,2,1,0:T(8,128)(2,1)S(1)} %get-tuple-element.234), channel_id=1, source_target_pairs={{0,4},{2,6},{4,8},{6,10},{8,12},{10,14},{12,0},{14,2},{1,5},{3,7},... | collective-permute-start | bytes 196616 | tf_op jit(solution)/shard_map/ppermute | solution.py:179
  92.0 10.2 %collective-permute-start.11 = (bf16[8,2,16,128]{3,2,1,0:T(8,128)(2,1)S(1)}, bf16[8,2,16,128]{3,2,1,0:T(8,128)(2,1)S(1)}, u32[]{:S(2)}, u32[]{:S(2)}) collective-permute-start(bf16[8,2,16,128]{3,2,1,0:T(8,128)(2,1)S(1)} %get-tuple-element.233), channel_id=1, source_target_pairs={{0,6},{2,4},{4,10},{6,8},{8,14},{10,12},{12,2},{14,0},{1,7},{3,5},... | collective-permute-start | bytes 196616 | tf_op jit(solution)/shard_map/ppermute | solution.py:179
  93.2 18.0 %collective-permute-start.12 = (bf16[8,2,16,128]{3,2,1,0:T(8,128)(2,1)S(1)}, bf16[8,2,16,128]{3,2,1,0:T(8,128)(2,1)}, u32[]{:S(2)}, u32[]{:S(2)}) collective-permute-start(bf16[8,2,16,128]{3,2,1,0:T(8,128)(2,1)S(1)} %get-tuple-element.232), channel_id=1, source_target_pairs={{0,8},{2,10},{4,12},{6,14},{8,0},{10,2},{12,4},{14,6},{1,9},{3,11}... | collective-permute-start | bytes 196616 | tf_op jit(solution)/shard_map/ppermute | solution.py:179
  95.5 15.7 %collective-permute-start.13 = (bf16[8,2,16,128]{3,2,1,0:T(8,128)(2,1)S(1)}, bf16[8,2,16,128]{3,2,1,0:T(8,128)(2,1)}, u32[]{:S(2)}, u32[]{:S(2)}) collective-permute-start(bf16[8,2,16,128]{3,2,1,0:T(8,128)(2,1)S(1)} %get-tuple-element.231), channel_id=1, source_target_pairs={{0,10},{2,8},{4,14},{6,12},{8,2},{10,0},{12,6},{14,4},{1,11},{3,9}... | collective-permute-start | bytes 196616 | tf_op jit(solution)/shard_map/ppermute | solution.py:179
  96.5 14.7 %collective-permute-start.14 = (bf16[8,2,16,128]{3,2,1,0:T(8,128)(2,1)S(1)}, bf16[8,2,16,128]{3,2,1,0:T(8,128)(2,1)}, u32[]{:S(2)}, u32[]{:S(2)}) collective-permute-start(bf16[8,2,16,128]{3,2,1,0:T(8,128)(2,1)S(1)} %get-tuple-element.230), channel_id=1, source_target_pairs={{0,12},{2,14},{4,0},{6,2},{8,4},{10,6},{12,8},{14,10},{1,13},{3,15... | collective-permute-start | bytes 196616 | tf_op jit(solution)/shard_map/ppermute | solution.py:179
  100.9 10.3 %collective-permute-start.15 = (bf16[8,2,16,128]{3,2,1,0:T(8,128)(2,1)S(1)}, bf16[8,2,16,128]{3,2,1,0:T(8,128)(2,1)S(1)}, u32[]{:S(2)}, u32[]{:S(2)}) collective-permute-start(bf16[8,2,16,128]{3,2,1,0:T(8,128)(2,1)S(1)} %get-tuple-element.229), channel_id=1, source_target_pairs={{0,14},{2,12},{4,2},{6,0},{8,6},{10,4},{12,10},{14,8},{1,15},{3,13... | collective-permute-start | bytes 196616 | tf_op jit(solution)/shard_map/ppermute | solution.py:179
  102.2 9.0 %collective-permute-start.9 = (bf16[8,2,16,128]{3,2,1,0:T(8,128)(2,1)S(1)}, bf16[8,2,16,128]{3,2,1,0:T(8,128)(2,1)S(1)}, u32[]{:S(2)}, u32[]{:S(2)}) collective-permute-start(bf16[8,2,16,128]{3,2,1,0:T(8,128)(2,1)S(1)} %get-tuple-element.235), channel_id=1, source_target_pairs={{0,2},{2,0},{4,6},{6,4},{8,10},{10,8},{12,14},{14,12},{1,3},{3,1},... | collective-permute-start | bytes 196616 | tf_op jit(solution)/shard_map/ppermute | solution.py:179
  114.0 6.1 %collective-permute-start.16 = (bf16[8,2,2,16,512]{4,3,2,1,0:T(8,128)(2,1)S(1)}, bf16[8,2,2,16,512]{4,3,2,1,0:T(8,128)(2,1)S(1)}, u32[]{:S(2)}, u32[]{:S(2)}) collective-permute-start(bf16[8,2,2,16,512]{4,3,2,1,0:T(8,128)(2,1)S(1)} %bitcast_dynamic-update-slice_fusion.48), channel_id=1, source_target_pairs={{0,1},{1,0},{2,3},{3,2},{4,5},{5,4},{6,7},{7,6},{8,9},{9,8},{10,11... | collective-permute-start | bytes 1572872 | tf_op jit(solution)/shard_map/ppermute | solution.py:200
  114.2 6.7 %collective-permute-start.17 = (bf16[8,2,16,128]{3,2,1,0:T(8,128)(2,1)S(1)}, bf16[8,2,16,128]{3,2,1,0:T(8,128)(2,1)S(1)}, u32[]{:S(2)}, u32[]{:S(2)}) collective-permute-start(bf16[8,2,16,128]{3,2,1,0:T(8,128)(2,1)S(1)} %get-tuple-element.225), channel_id=1, source_target_pairs={{0,2},{2,0},{4,6},{6,4},{8,10},{10,8},{12,14},{14,12},{1,3},{3,1},... | collective-permute-start | bytes 196616 | tf_op jit(solution)/shard_map/ppermute | solution.py:179
  114.9 9.9 %collective-permute-start.18 = (bf16[8,2,16,128]{3,2,1,0:T(8,128)(2,1)S(1)}, bf16[8,2,16,128]{3,2,1,0:T(8,128)(2,1)S(1)}, u32[]{:S(2)}, u32[]{:S(2)}) collective-permute-start(bf16[8,2,16,128]{3,2,1,0:T(8,128)(2,1)S(1)} %get-tuple-element.224), channel_id=1, source_target_pairs={{0,4},{2,6},{4,8},{6,10},{8,12},{10,14},{12,0},{14,2},{1,5},{3,7},... | collective-permute-start | bytes 196616 | tf_op jit(solution)/shard_map/ppermute | solution.py:179
  116.7 17.5 %collective-permute-start.19 = (bf16[8,2,16,128]{3,2,1,0:T(8,128)(2,1)S(1)}, bf16[8,2,16,128]{3,2,1,0:T(8,128)(2,1)S(1)}, u32[]{:S(2)}, u32[]{:S(2)}) collective-permute-start(bf16[8,2,16,128]{3,2,1,0:T(8,128)(2,1)S(1)} %get-tuple-element.223), channel_id=1, source_target_pairs={{0,6},{2,4},{4,10},{6,8},{8,14},{10,12},{12,2},{14,0},{1,7},{3,5},... | collective-permute-start | bytes 196616 | tf_op jit(solution)/shard_map/ppermute | solution.py:179
  116.7 17.4 %collective-permute-start.20 = (bf16[8,2,16,128]{3,2,1,0:T(8,128)(2,1)S(1)}, bf16[8,2,16,128]{3,2,1,0:T(8,128)(2,1)S(1)}, u32[]{:S(2)}, u32[]{:S(2)}) collective-permute-start(bf16[8,2,16,128]{3,2,1,0:T(8,128)(2,1)S(1)} %get-tuple-element.222), channel_id=1, source_target_pairs={{0,8},{2,10},{4,12},{6,14},{8,0},{10,2},{12,4},{14,6},{1,9},{3,11}... | collective-permute-start | bytes 196616 | tf_op jit(solution)/shard_map/ppermute | solution.py:179
  120.1 14.0 %collective-permute-start.21 = (bf16[8,2,16,128]{3,2,1,0:T(8,128)(2,1)S(1)}, bf16[8,2,16,128]{3,2,1,0:T(8,128)(2,1)S(1)}, u32[]{:S(2)}, u32[]{:S(2)}) collective-permute-start(bf16[8,2,16,128]{3,2,1,0:T(8,128)(2,1)S(1)} %get-tuple-element.221), channel_id=1, source_target_pairs={{0,10},{2,8},{4,14},{6,12},{8,2},{10,0},{12,6},{14,4},{1,11},{3,9}... | collective-permute-start | bytes 196616 | tf_op jit(solution)/shard_map/ppermute | solution.py:179
  120.9 13.3 %collective-permute-start.22 = (bf16[8,2,16,128]{3,2,1,0:T(8,128)(2,1)S(1)}, bf16[8,2,16,128]{3,2,1,0:T(8,128)(2,1)S(1)}, u32[]{:S(2)}, u32[]{:S(2)}) collective-permute-start(bf16[8,2,16,128]{3,2,1,0:T(8,128)(2,1)S(1)} %get-tuple-element.220), channel_id=1, source_target_pairs={{0,12},{2,14},{4,0},{6,2},{8,4},{10,6},{12,8},{14,10},{1,13},{3,15... | collective-permute-start | bytes 196616 | tf_op jit(solution)/shard_map/ppermute | solution.py:179
  124.8 9.4 %collective-permute-start.23 = (bf16[8,2,16,128]{3,2,1,0:T(8,128)(2,1)S(1)}, bf16[8,2,16,128]{3,2,1,0:T(8,128)(2,1)S(1)}, u32[]{:S(2)}, u32[]{:S(2)}) collective-permute-start(bf16[8,2,16,128]{3,2,1,0:T(8,128)(2,1)S(1)} %get-tuple-element.219), channel_id=1, source_target_pairs={{0,14},{2,12},{4,2},{6,0},{8,6},{10,4},{12,10},{14,8},{1,15},{3,13... | collective-permute-start | bytes 196616 | tf_op jit(solution)/shard_map/ppermute | solution.py:179
  134.5 6.1 %collective-permute-start.24 = (bf16[8,2,2,16,512]{4,3,2,1,0:T(8,128)(2,1)S(1)}, bf16[8,2,2,16,512]{4,3,2,1,0:T(8,128)(2,1)S(1)}, u32[]{:S(2)}, u32[]{:S(2)}) collective-permute-start(bf16[8,2,2,16,512]{4,3,2,1,0:T(8,128)(2,1)S(1)} %bitcast_dynamic-update-slice_fusion.40), channel_id=1, source_target_pairs={{0,1},{1,0},{2,3},{3,2},{4,5},{5,4},{6,7},{7,6},{8,9},{9,8},{10,11... | collective-permute-start | bytes 1572872 | tf_op jit(solution)/shard_map/ppermute | solution.py:200
  134.6 6.7 %collective-permute-start.25 = (bf16[8,2,16,128]{3,2,1,0:T(8,128)(2,1)S(1)}, bf16[8,2,16,128]{3,2,1,0:T(8,128)(2,1)S(1)}, u32[]{:S(2)}, u32[]{:S(2)}) collective-permute-start(bf16[8,2,16,128]{3,2,1,0:T(8,128)(2,1)S(1)} %get-tuple-element.215), channel_id=1, source_target_pairs={{0,2},{2,0},{4,6},{6,4},{8,10},{10,8},{12,14},{14,12},{1,3},{3,1},... | collective-permute-start | bytes 196616 | tf_op jit(solution)/shard_map/ppermute | solution.py:179
  135.3 9.9 %collective-permute-start.26 = (bf16[8,2,16,128]{3,2,1,0:T(8,128)(2,1)S(1)}, bf16[8,2,16,128]{3,2,1,0:T(8,128)(2,1)S(1)}, u32[]{:S(2)}, u32[]{:S(2)}) collective-permute-start(bf16[8,2,16,128]{3,2,1,0:T(8,128)(2,1)S(1)} %get-tuple-element.214), channel_id=1, source_target_pairs={{0,4},{2,6},{4,8},{6,10},{8,12},{10,14},{12,0},{14,2},{1,5},{3,7},... | collective-permute-start | bytes 196616 | tf_op jit(solution)/shard_map/ppermute | solution.py:179
  137.1 17.5 %collective-permute-start.27 = (bf16[8,2,16,128]{3,2,1,0:T(8,128)(2,1)S(1)}, bf16[8,2,16,128]{3,2,1,0:T(8,128)(2,1)S(1)}, u32[]{:S(2)}, u32[]{:S(2)}) collective-permute-start(bf16[8,2,16,128]{3,2,1,0:T(8,128)(2,1)S(1)} %get-tuple-element.213), channel_id=1, source_target_pairs={{0,6},{2,4},{4,10},{6,8},{8,14},{10,12},{12,2},{14,0},{1,7},{3,5},... | collective-permute-start | bytes 196616 | tf_op jit(solution)/shard_map/ppermute | solution.py:179
  137.2 17.4 %collective-permute-start.28 = (bf16[8,2,16,128]{3,2,1,0:T(8,128)(2,1)S(1)}, bf16[8,2,16,128]{3,2,1,0:T(8,128)(2,1)S(1)}, u32[]{:S(2)}, u32[]{:S(2)}) collective-permute-start(bf16[8,2,16,128]{3,2,1,0:T(8,128)(2,1)S(1)} %get-tuple-element.212), channel_id=1, source_target_pairs={{0,8},{2,10},{4,12},{6,14},{8,0},{10,2},{12,4},{14,6},{1,9},{3,11}... | collective-permute-start | bytes 196616 | tf_op jit(solution)/shard_map/ppermute | solution.py:179
  140.5 14.0 %collective-permute-start.29 = (bf16[8,2,16,128]{3,2,1,0:T(8,128)(2,1)S(1)}, bf16[8,2,16,128]{3,2,1,0:T(8,128)(2,1)S(1)}, u32[]{:S(2)}, u32[]{:S(2)}) collective-permute-start(bf16[8,2,16,128]{3,2,1,0:T(8,128)(2,1)S(1)} %get-tuple-element.211), channel_id=1, source_target_pairs={{0,10},{2,8},{4,14},{6,12},{8,2},{10,0},{12,6},{14,4},{1,11},{3,9}... | collective-permute-start | bytes 196616 | tf_op jit(solution)/shard_map/ppermute | solution.py:179
  141.3 13.3 %collective-permute-start.30 = (bf16[8,2,16,128]{3,2,1,0:T(8,128)(2,1)S(1)}, bf16[8,2,16,128]{3,2,1,0:T(8,128)(2,1)S(1)}, u32[]{:S(2)}, u32[]{:S(2)}) collective-permute-start(bf16[8,2,16,128]{3,2,1,0:T(8,128)(2,1)S(1)} %get-tuple-element.210), channel_id=1, source_target_pairs={{0,12},{2,14},{4,0},{6,2},{8,4},{10,6},{12,8},{14,10},{1,13},{3,15... | collective-permute-start | bytes 196616 | tf_op jit(solution)/shard_map/ppermute | solution.py:179
  145.2 9.4 %collective-permute-start.31 = (bf16[8,2,16,128]{3,2,1,0:T(8,128)(2,1)S(1)}, bf16[8,2,16,128]{3,2,1,0:T(8,128)(2,1)S(1)}, u32[]{:S(2)}, u32[]{:S(2)}) collective-permute-start(bf16[8,2,16,128]{3,2,1,0:T(8,128)(2,1)S(1)} %get-tuple-element.209), channel_id=1, source_target_pairs={{0,14},{2,12},{4,2},{6,0},{8,6},{10,4},{12,10},{14,8},{1,15},{3,13... | collective-permute-start | bytes 196616 | tf_op jit(solution)/shard_map/ppermute | solution.py:179
  154.9 6.1 %collective-permute-start.32 = (bf16[8,2,2,16,512]{4,3,2,1,0:T(8,128)(2,1)S(1)}, bf16[8,2,2,16,512]{4,3,2,1,0:T(8,128)(2,1)S(1)}, u32[]{:S(2)}, u32[]{:S(2)}) collective-permute-start(bf16[8,2,2,16,512]{4,3,2,1,0:T(8,128)(2,1)S(1)} %bitcast_dynamic-update-slice_fusion.32), channel_id=1, source_target_pairs={{0,1},{1,0},{2,3},{3,2},{4,5},{5,4},{6,7},{7,6},{8,9},{9,8},{10,11... | collective-permute-start | bytes 1572872 | tf_op jit(solution)/shard_map/ppermute | solution.py:200
  155.1 6.7 %collective-permute-start.33 = (bf16[8,2,16,128]{3,2,1,0:T(8,128)(2,1)S(1)}, bf16[8,2,16,128]{3,2,1,0:T(8,128)(2,1)S(1)}, u32[]{:S(2)}, u32[]{:S(2)}) collective-permute-start(bf16[8,2,16,128]{3,2,1,0:T(8,128)(2,1)S(1)} %get-tuple-element.205), channel_id=1, source_target_pairs={{0,2},{2,0},{4,6},{6,4},{8,10},{10,8},{12,14},{14,12},{1,3},{3,1},... | collective-permute-start | bytes 196616 | tf_op jit(solution)/shard_map/ppermute | solution.py:179
  155.7 9.9 %collective-permute-start.34 = (bf16[8,2,16,128]{3,2,1,0:T(8,128)(2,1)S(1)}, bf16[8,2,16,128]{3,2,1,0:T(8,128)(2,1)S(1)}, u32[]{:S(2)}, u32[]{:S(2)}) collective-permute-start(bf16[8,2,16,128]{3,2,1,0:T(8,128)(2,1)S(1)} %get-tuple-element.204), channel_id=1, source_target_pairs={{0,4},{2,6},{4,8},{6,10},{8,12},{10,14},{12,0},{14,2},{1,5},{3,7},... | collective-permute-start | bytes 196616 | tf_op jit(solution)/shard_map/ppermute | solution.py:179
  157.6 17.5 %collective-permute-start.35 = (bf16[8,2,16,128]{3,2,1,0:T(8,128)(2,1)S(1)}, bf16[8,2,16,128]{3,2,1,0:T(8,128)(2,1)S(1)}, u32[]{:S(2)}, u32[]{:S(2)}) collective-permute-start(bf16[8,2,16,128]{3,2,1,0:T(8,128)(2,1)S(1)} %get-tuple-element.203), channel_id=1, source_target_pairs={{0,6},{2,4},{4,10},{6,8},{8,14},{10,12},{12,2},{14,0},{1,7},{3,5},... | collective-permute-start | bytes 196616 | tf_op jit(solution)/shard_map/ppermute | solution.py:179
  157.6 17.5 %collective-permute-start.36 = (bf16[8,2,16,128]{3,2,1,0:T(8,128)(2,1)S(1)}, bf16[8,2,16,128]{3,2,1,0:T(8,128)(2,1)S(1)}, u32[]{:S(2)}, u32[]{:S(2)}) collective-permute-start(bf16[8,2,16,128]{3,2,1,0:T(8,128)(2,1)S(1)} %get-tuple-element.202), channel_id=1, source_target_pairs={{0,8},{2,10},{4,12},{6,14},{8,0},{10,2},{12,4},{14,6},{1,9},{3,11}... | collective-permute-start | bytes 196616 | tf_op jit(solution)/shard_map/ppermute | solution.py:179
  161.0 14.1 %collective-permute-start.37 = (bf16[8,2,16,128]{3,2,1,0:T(8,128)(2,1)S(1)}, bf16[8,2,16,128]{3,2,1,0:T(8,128)(2,1)S(1)}, u32[]{:S(2)}, u32[]{:S(2)}) collective-permute-start(bf16[8,2,16,128]{3,2,1,0:T(8,128)(2,1)S(1)} %get-tuple-element.201), channel_id=1, source_target_pairs={{0,10},{2,8},{4,14},{6,12},{8,2},{10,0},{12,6},{14,4},{1,11},{3,9}... | collective-permute-start | bytes 196616 | tf_op jit(solution)/shard_map/ppermute | solution.py:179
  161.8 13.3 %collective-permute-start.38 = (bf16[8,2,16,128]{3,2,1,0:T(8,128)(2,1)S(1)}, bf16[8,2,16,128]{3,2,1,0:T(8,128)(2,1)S(1)}, u32[]{:S(2)}, u32[]{:S(2)}) collective-permute-start(bf16[8,2,16,128]{3,2,1,0:T(8,128)(2,1)S(1)} %get-tuple-element.200), channel_id=1, source_target_pairs={{0,12},{2,14},{4,0},{6,2},{8,4},{10,6},{12,8},{14,10},{1,13},{3,15... | collective-permute-start | bytes 196616 | tf_op jit(solution)/shard_map/ppermute | solution.py:179
  165.6 9.5 %collective-permute-start.39 = (bf16[8,2,16,128]{3,2,1,0:T(8,128)(2,1)S(1)}, bf16[8,2,16,128]{3,2,1,0:T(8,128)(2,1)S(1)}, u32[]{:S(2)}, u32[]{:S(2)}) collective-permute-start(bf16[8,2,16,128]{3,2,1,0:T(8,128)(2,1)S(1)} %get-tuple-element.199), channel_id=1, source_target_pairs={{0,14},{2,12},{4,2},{6,0},{8,6},{10,4},{12,10},{14,8},{1,15},{3,13... | collective-permute-start | bytes 196616 | tf_op jit(solution)/shard_map/ppermute | solution.py:179
  175.4 6.1 %collective-permute-start.40 = (bf16[8,2,2,16,512]{4,3,2,1,0:T(8,128)(2,1)S(1)}, bf16[8,2,2,16,512]{4,3,2,1,0:T(8,128)(2,1)S(1)}, u32[]{:S(2)}, u32[]{:S(2)}) collective-permute-start(bf16[8,2,2,16,512]{4,3,2,1,0:T(8,128)(2,1)S(1)} %bitcast_dynamic-update-slice_fusion.24), channel_id=1, source_target_pairs={{0,1},{1,0},{2,3},{3,2},{4,5},{5,4},{6,7},{7,6},{8,9},{9,8},{10,11... | collective-permute-start | bytes 1572872 | tf_op jit(solution)/shard_map/ppermute | solution.py:200
  175.6 6.7 %collective-permute-start.41 = (bf16[8,2,16,128]{3,2,1,0:T(8,128)(2,1)S(1)}, bf16[8,2,16,128]{3,2,1,0:T(8,128)(2,1)S(1)}, u32[]{:S(2)}, u32[]{:S(2)}) collective-permute-start(bf16[8,2,16,128]{3,2,1,0:T(8,128)(2,1)S(1)} %get-tuple-element.195), channel_id=1, source_target_pairs={{0,2},{2,0},{4,6},{6,4},{8,10},{10,8},{12,14},{14,12},{1,3},{3,1},... | collective-permute-start | bytes 196616 | tf_op jit(solution)/shard_map/ppermute | solution.py:179
  176.2 9.9 %collective-permute-start.42 = (bf16[8,2,16,128]{3,2,1,0:T(8,128)(2,1)S(1)}, bf16[8,2,16,128]{3,2,1,0:T(8,128)(2,1)S(1)}, u32[]{:S(2)}, u32[]{:S(2)}) collective-permute-start(bf16[8,2,16,128]{3,2,1,0:T(8,128)(2,1)S(1)} %get-tuple-element.194), channel_id=1, source_target_pairs={{0,4},{2,6},{4,8},{6,10},{8,12},{10,14},{12,0},{14,2},{1,5},{3,7},... | collective-permute-start | bytes 196616 | tf_op jit(solution)/shard_map/ppermute | solution.py:179
  178.1 17.5 %collective-permute-start.43 = (bf16[8,2,16,128]{3,2,1,0:T(8,128)(2,1)S(1)}, bf16[8,2,16,128]{3,2,1,0:T(8,128)(2,1)S(1)}, u32[]{:S(2)}, u32[]{:S(2)}) collective-permute-start(bf16[8,2,16,128]{3,2,1,0:T(8,128)(2,1)S(1)} %get-tuple-element.193), channel_id=1, source_target_pairs={{0,6},{2,4},{4,10},{6,8},{8,14},{10,12},{12,2},{14,0},{1,7},{3,5},... | collective-permute-start | bytes 196616 | tf_op jit(solution)/shard_map/ppermute | solution.py:179
  178.1 17.5 %collective-permute-start.44 = (bf16[8,2,16,128]{3,2,1,0:T(8,128)(2,1)S(1)}, bf16[8,2,16,128]{3,2,1,0:T(8,128)(2,1)S(1)}, u32[]{:S(2)}, u32[]{:S(2)}) collective-permute-start(bf16[8,2,16,128]{3,2,1,0:T(8,128)(2,1)S(1)} %get-tuple-element.192), channel_id=1, source_target_pairs={{0,8},{2,10},{4,12},{6,14},{8,0},{10,2},{12,4},{14,6},{1,9},{3,11}... | collective-permute-start | bytes 196616 | tf_op jit(solution)/shard_map/ppermute | solution.py:179
  181.5 14.1 %collective-permute-start.45 = (bf16[8,2,16,128]{3,2,1,0:T(8,128)(2,1)S(1)}, bf16[8,2,16,128]{3,2,1,0:T(8,128)(2,1)S(1)}, u32[]{:S(2)}, u32[]{:S(2)}) collective-permute-start(bf16[8,2,16,128]{3,2,1,0:T(8,128)(2,1)S(1)} %get-tuple-element.191), channel_id=1, source_target_pairs={{0,10},{2,8},{4,14},{6,12},{8,2},{10,0},{12,6},{14,4},{1,11},{3,9}... | collective-permute-start | bytes 196616 | tf_op jit(solution)/shard_map/ppermute | solution.py:179
  182.3 13.3 %collective-permute-start.46 = (bf16[8,2,16,128]{3,2,1,0:T(8,128)(2,1)S(1)}, bf16[8,2,16,128]{3,2,1,0:T(8,128)(2,1)S(1)}, u32[]{:S(2)}, u32[]{:S(2)}) collective-permute-start(bf16[8,2,16,128]{3,2,1,0:T(8,128)(2,1)S(1)} %get-tuple-element.190), channel_id=1, source_target_pairs={{0,12},{2,14},{4,0},{6,2},{8,4},{10,6},{12,8},{14,10},{1,13},{3,15... | collective-permute-start | bytes 196616 | tf_op jit(solution)/shard_map/ppermute | solution.py:179
  186.1 9.5 %collective-permute-start.47 = (bf16[8,2,16,128]{3,2,1,0:T(8,128)(2,1)S(1)}, bf16[8,2,16,128]{3,2,1,0:T(8,128)(2,1)S(1)}, u32[]{:S(2)}, u32[]{:S(2)}) collective-permute-start(bf16[8,2,16,128]{3,2,1,0:T(8,128)(2,1)S(1)} %get-tuple-element.189), channel_id=1, source_target_pairs={{0,14},{2,12},{4,2},{6,0},{8,6},{10,4},{12,10},{14,8},{1,15},{3,13... | collective-permute-start | bytes 196616 | tf_op jit(solution)/shard_map/ppermute | solution.py:179
  195.9 6.1 %collective-permute-start.48 = (bf16[8,2,2,16,512]{4,3,2,1,0:T(8,128)(2,1)S(1)}, bf16[8,2,2,16,512]{4,3,2,1,0:T(8,128)(2,1)S(1)}, u32[]{:S(2)}, u32[]{:S(2)}) collective-permute-start(bf16[8,2,2,16,512]{4,3,2,1,0:T(8,128)(2,1)S(1)} %bitcast_dynamic-update-slice_fusion.16), channel_id=1, source_target_pairs={{0,1},{1,0},{2,3},{3,2},{4,5},{5,4},{6,7},{7,6},{8,9},{9,8},{10,11... | collective-permute-start | bytes 1572872 | tf_op jit(solution)/shard_map/ppermute | solution.py:200
  196.1 6.7 %collective-permute-start.49 = (bf16[8,2,16,128]{3,2,1,0:T(8,128)(2,1)S(1)}, bf16[8,2,16,128]{3,2,1,0:T(8,128)(2,1)S(1)}, u32[]{:S(2)}, u32[]{:S(2)}) collective-permute-start(bf16[8,2,16,128]{3,2,1,0:T(8,128)(2,1)S(1)} %get-tuple-element.185), channel_id=1, source_target_pairs={{0,2},{2,0},{4,6},{6,4},{8,10},{10,8},{12,14},{14,12},{1,3},{3,1},... | collective-permute-start | bytes 196616 | tf_op jit(solution)/shard_map/ppermute | solution.py:179
  196.7 9.9 %collective-permute-start.50 = (bf16[8,2,16,128]{3,2,1,0:T(8,128)(2,1)S(1)}, bf16[8,2,16,128]{3,2,1,0:T(8,128)(2,1)S(1)}, u32[]{:S(2)}, u32[]{:S(2)}) collective-permute-start(bf16[8,2,16,128]{3,2,1,0:T(8,128)(2,1)S(1)} %get-tuple-element.184), channel_id=1, source_target_pairs={{0,4},{2,6},{4,8},{6,10},{8,12},{10,14},{12,0},{14,2},{1,5},{3,7},... | collective-permute-start | bytes 196616 | tf_op jit(solution)/shard_map/ppermute | solution.py:179
  198.6 17.5 %collective-permute-start.51 = (bf16[8,2,16,128]{3,2,1,0:T(8,128)(2,1)S(1)}, bf16[8,2,16,128]{3,2,1,0:T(8,128)(2,1)S(1)}, u32[]{:S(2)}, u32[]{:S(2)}) collective-permute-start(bf16[8,2,16,128]{3,2,1,0:T(8,128)(2,1)S(1)} %get-tuple-element.183), channel_id=1, source_target_pairs={{0,6},{2,4},{4,10},{6,8},{8,14},{10,12},{12,2},{14,0},{1,7},{3,5},... | collective-permute-start | bytes 196616 | tf_op jit(solution)/shard_map/ppermute | solution.py:179
  198.6 17.5 %collective-permute-start.52 = (bf16[8,2,16,128]{3,2,1,0:T(8,128)(2,1)S(1)}, bf16[8,2,16,128]{3,2,1,0:T(8,128)(2,1)S(1)}, u32[]{:S(2)}, u32[]{:S(2)}) collective-permute-start(bf16[8,2,16,128]{3,2,1,0:T(8,128)(2,1)S(1)} %get-tuple-element.182), channel_id=1, source_target_pairs={{0,8},{2,10},{4,12},{6,14},{8,0},{10,2},{12,4},{14,6},{1,9},{3,11}... | collective-permute-start | bytes 196616 | tf_op jit(solution)/shard_map/ppermute | solution.py:179
  202.0 14.1 %collective-permute-start.53 = (bf16[8,2,16,128]{3,2,1,0:T(8,128)(2,1)S(1)}, bf16[8,2,16,128]{3,2,1,0:T(8,128)(2,1)S(1)}, u32[]{:S(2)}, u32[]{:S(2)}) collective-permute-start(bf16[8,2,16,128]{3,2,1,0:T(8,128)(2,1)S(1)} %get-tuple-element.181), channel_id=1, source_target_pairs={{0,10},{2,8},{4,14},{6,12},{8,2},{10,0},{12,6},{14,4},{1,11},{3,9}... | collective-permute-start | bytes 196616 | tf_op jit(solution)/shard_map/ppermute | solution.py:179
  202.8 13.3 %collective-permute-start.54 = (bf16[8,2,16,128]{3,2,1,0:T(8,128)(2,1)S(1)}, bf16[8,2,16,128]{3,2,1,0:T(8,128)(2,1)S(1)}, u32[]{:S(2)}, u32[]{:S(2)}) collective-permute-start(bf16[8,2,16,128]{3,2,1,0:T(8,128)(2,1)S(1)} %get-tuple-element.180), channel_id=1, source_target_pairs={{0,12},{2,14},{4,0},{6,2},{8,4},{10,6},{12,8},{14,10},{1,13},{3,15... | collective-permute-start | bytes 196616 | tf_op jit(solution)/shard_map/ppermute | solution.py:179
  206.6 9.5 %collective-permute-start.55 = (bf16[8,2,16,128]{3,2,1,0:T(8,128)(2,1)S(1)}, bf16[8,2,16,128]{3,2,1,0:T(8,128)(2,1)S(1)}, u32[]{:S(2)}, u32[]{:S(2)}) collective-permute-start(bf16[8,2,16,128]{3,2,1,0:T(8,128)(2,1)S(1)} %get-tuple-element.179), channel_id=1, source_target_pairs={{0,14},{2,12},{4,2},{6,0},{8,6},{10,4},{12,10},{14,8},{1,15},{3,13... | collective-permute-start | bytes 196616 | tf_op jit(solution)/shard_map/ppermute | solution.py:179
  216.4 6.1 %collective-permute-start.56 = (bf16[8,2,2,16,512]{4,3,2,1,0:T(8,128)(2,1)S(1)}, bf16[8,2,2,16,512]{4,3,2,1,0:T(8,128)(2,1)S(1)}, u32[]{:S(2)}, u32[]{:S(2)}) collective-permute-start(bf16[8,2,2,16,512]{4,3,2,1,0:T(8,128)(2,1)S(1)} %bitcast_dynamic-update-slice_fusion.8), channel_id=1, source_target_pairs={{0,1},{1,0},{2,3},{3,2},{4,5},{5,4},{6,7},{7,6},{8,9},{9,8},{10,11... | collective-permute-start | bytes 1572872 | tf_op jit(solution)/shard_map/ppermute | solution.py:200
  216.6 6.7 %collective-permute-start.57 = (bf16[8,2,16,128]{3,2,1,0:T(8,128)(2,1)S(1)}, bf16[8,2,16,128]{3,2,1,0:T(8,128)(2,1)S(1)}, u32[]{:S(2)}, u32[]{:S(2)}) collective-permute-start(bf16[8,2,16,128]{3,2,1,0:T(8,128)(2,1)S(1)} %get-tuple-element.175), channel_id=1, source_target_pairs={{0,2},{2,0},{4,6},{6,4},{8,10},{10,8},{12,14},{14,12},{1,3},{3,1},... | collective-permute-start | bytes 196616 | tf_op jit(solution)/shard_map/ppermute | solution.py:179
  217.3 9.9 %collective-permute-start.58 = (bf16[8,2,16,128]{3,2,1,0:T(8,128)(2,1)S(1)}, bf16[8,2,16,128]{3,2,1,0:T(8,128)(2,1)S(1)}, u32[]{:S(2)}, u32[]{:S(2)}) collective-permute-start(bf16[8,2,16,128]{3,2,1,0:T(8,128)(2,1)S(1)} %get-tuple-element.174), channel_id=1, source_target_pairs={{0,4},{2,6},{4,8},{6,10},{8,12},{10,14},{12,0},{14,2},{1,5},{3,7},... | collective-permute-start | bytes 196616 | tf_op jit(solution)/shard_map/ppermute | solution.py:179
  219.1 17.5 %collective-permute-start.59 = (bf16[8,2,16,128]{3,2,1,0:T(8,128)(2,1)S(1)}, bf16[8,2,16,128]{3,2,1,0:T(8,128)(2,1)S(1)}, u32[]{:S(2)}, u32[]{:S(2)}) collective-permute-start(bf16[8,2,16,128]{3,2,1,0:T(8,128)(2,1)S(1)} %get-tuple-element.173), channel_id=1, source_target_pairs={{0,6},{2,4},{4,10},{6,8},{8,14},{10,12},{12,2},{14,0},{1,7},{3,5},... | collective-permute-start | bytes 196616 | tf_op jit(solution)/shard_map/ppermute | solution.py:179
  219.1 17.4 %collective-permute-start.60 = (bf16[8,2,16,128]{3,2,1,0:T(8,128)(2,1)S(1)}, bf16[8,2,16,128]{3,2,1,0:T(8,128)(2,1)S(1)}, u32[]{:S(2)}, u32[]{:S(2)}) collective-permute-start(bf16[8,2,16,128]{3,2,1,0:T(8,128)(2,1)S(1)} %get-tuple-element.172), channel_id=1, source_target_pairs={{0,8},{2,10},{4,12},{6,14},{8,0},{10,2},{12,4},{14,6},{1,9},{3,11}... | collective-permute-start | bytes 196616 | tf_op jit(solution)/shard_map/ppermute | solution.py:179
  222.5 14.0 %collective-permute-start.61 = (bf16[8,2,16,128]{3,2,1,0:T(8,128)(2,1)S(1)}, bf16[8,2,16,128]{3,2,1,0:T(8,128)(2,1)S(1)}, u32[]{:S(2)}, u32[]{:S(2)}) collective-permute-start(bf16[8,2,16,128]{3,2,1,0:T(8,128)(2,1)S(1)} %get-tuple-element.171), channel_id=1, source_target_pairs={{0,10},{2,8},{4,14},{6,12},{8,2},{10,0},{12,6},{14,4},{1,11},{3,9}... | collective-permute-start | bytes 196616 | tf_op jit(solution)/shard_map/ppermute | solution.py:179
  223.3 13.3 %collective-permute-start.62 = (bf16[8,2,16,128]{3,2,1,0:T(8,128)(2,1)S(1)}, bf16[8,2,16,128]{3,2,1,0:T(8,128)(2,1)S(1)}, u32[]{:S(2)}, u32[]{:S(2)}) collective-permute-start(bf16[8,2,16,128]{3,2,1,0:T(8,128)(2,1)S(1)} %get-tuple-element.170), channel_id=1, source_target_pairs={{0,12},{2,14},{4,0},{6,2},{8,4},{10,6},{12,8},{14,10},{1,13},{3,15... | collective-permute-start | bytes 196616 | tf_op jit(solution)/shard_map/ppermute | solution.py:179
  227.2 9.4 %collective-permute-start.63 = (bf16[8,2,16,128]{3,2,1,0:T(8,128)(2,1)S(1)}, bf16[8,2,16,128]{3,2,1,0:T(8,128)(2,1)S(1)}, u32[]{:S(2)}, u32[]{:S(2)}) collective-permute-start(bf16[8,2,16,128]{3,2,1,0:T(8,128)(2,1)S(1)} %get-tuple-element.169), channel_id=1, source_target_pairs={{0,14},{2,12},{4,2},{6,0},{8,6},{10,4},{12,10},{14,8},{1,15},{3,13... | collective-permute-start | bytes 196616 | tf_op jit(solution)/shard_map/ppermute | solution.py:179
  (9 other events, 50.9 us)

commit v13 on v10

--- a/solution.py
+++ b/solution.py
@@ -137,7 +137,7 @@
     count, two_rows, depth = lhs.shape
     cols = rhs.shape[2]
     rows = two_rows // 2
-    step = 2 if count % 2 == 0 else 1
+    step = 4 if count % 4 == 0 else (2 if count % 2 == 0 else 1)
     offset = first_channel // step
     in_specs = [
         pl.BlockSpec((step, two_rows, depth), lambda c: (c, 0, 0)),

time: 216 us -> 214 us (level)
  Pallas kernels: 52.4 us -> 47.4 us
  starting transfers between devices: 85.9 us -> 88.1 us
    pallas_call x4, Pallas kernels: 39.3 us -> 34.3 us  [correlate(): pl.pallas_call(functools.partial(correlate_kernel, 1.0 / (depth // 2)), g...]
    ppermute x28, starting transfers between devices: 81.3 us -> 83.5 us  [send_chunk(): block = lax.ppermute(block, ('inp', 'tm'), route)]
  transfers between devices with their start and end apart: 33 -> 33, of which waited for: 4 -> 4; matrix products, arithmetic and copies ran while one was open for 16% -> 16% of each run, Pallas kernels for 14% -> 12%
where the time goes in v13:
time: 214 us; the launch traced here: 212 us
  starting transfers between devices  88.1 us (41%)
  Pallas kernels  47.4 us (22%)
  local copies, waits for them, and re-layouts  40.6 us (19%)
  other arithmetic  14.9 us (7%)
  waiting for transfers between devices  12.3 us (6%)
  matrix products  6.95 us (3%)
    ppermute x28, starting transfers between devices, send_chunk(): block = lax.ppermute(block, ('inp', 'tm'), route)  83.5 us
    pallas_call x4, Pallas kernels, correlate(): pl.pallas_call(functools.partial(correlate_kernel, 1.0 / (depth // 2)), g...  34.3 us
    pallas_call x1, Pallas kernels, polyphase_filter(): pl.pallas_call(filter_kernel, grid=(inputs_here // rows,), in_specs=[pl.B...  13.1 us
    dynamic_update_slice x32, local copies, waits for them, and re-layouts, assemble_chunk(): lax.dynamic_update_slice(half, block[:, :, None], (0, 0, tm_step, 0, sour...  13 us
    ppermute x28, waiting for transfers between devices, send_chunk(): block = lax.ppermute(block, ('inp', 'tm'), route)  9.6 us
    transpose x4, local copies, waits for them, and re-layouts, finish_chunk(): lhs = lhs.transpose(0, 1, 3, 2).reshape(own_channels, 2 * rows_here, depth)  9.58 us
    another operation x1, other arithmetic  8.49 us
    dot_general x1, matrix products, per_device(): lax.dot_general(dft_table_t(frame_len), filtered.reshape(spectra_here * i...  6.95 us
  transfers between devices with their start and end apart: 33, of which 4 were waited for; matrix products, arithmetic and copies ran while one was open for 16% of the time, Pallas kernels for 12%

profile of v13, /device:TPU:0, one launch (start us, length us, event | category | flops | bytes accessed | tf_op | source)
XLA Modules:
  0.0 211.6 jit_solution(9925694160594882296)
XLA Ops:
  0.0 4.3 %collective-permute-start = (bf16[128,16384]{1,0:T(8,128)(2,1)}, bf16[128,16384]{1,0:T(8,128)(2,1)}, u32[]{:S(2)}, u32[]{:S(2)}) collective-permute-start(bf16[128,16384]{1,0:T(8,128)(2,1)} %own_ref.1), channel_id=1, source_target_pairs={{0,1},{1,2},{2,3},{4,5},{5,6},{6,7},{8,9},{9,10},{10,11},{12,13},{... | collective-permute-start | bytes 12582920 | tf_op jit(solution)/shard_map/ppermute | solution.py:17
  4.3 8.5 %negate_convert_fusion = (bf16[512,1,1024]{2,0,1:T(8,128)(2,1)S(1)}, bf16[512,1,1024]{2,0,1:T(8,128)(2,1)S(1)}) fusion(), kind=kLoop, calls=%fused_computation.24 | loop fusion | flops 8912896 | bytes 2097152 | tf_op jit(solution)/shard_map/convert.1
  13.0 2.2 %copy.51 = bf16[512,2,1024]{2,1,0:T(2,128)(2,1)S(1)} copy(bf16[512,2,1024]{2,0,1:T(8,128)(2,1)S(1)} %pad_maximum_fusion.4) | data formatting | bytes 4194304 | tf_op jit(solution)/shard_map/stack | solution.py:35
  15.2 2.3 %convert_element_type.36 = bf16[1024,1024]{1,0:T(8,128)(2,1)} reshape(bf16[512,2,1024]{2,1,0:T(2,128)(2,1)S(1)} %copy.51) | data formatting | bytes 4194304 | tf_op jit(solution)/shard_map/convert_element_type | solution.py:36
  17.4 1.1 fusion.14
  19.2 1.1 fusion.11.taps_ref
  20.3 13.1 %shard_map.17 = bf16[16,128,1024]{2,1,0:T(8,128)(2,1)} custom-call(f32[16,1024]{1,0:T(8,128)} %fusion.11.taps_ref, bf16[128,16384]{1,0:T(8,128)(2,1)} %own_ref.1, bf16[128,16384]{1,0:T(8,128)(2,1)} %collective-permute-done.history_ref), custom_call_target="tpu_custom_call" | custom-call | flops 67108864 | bytes 12582912 | tf_op jit(solution)/shard_map/pallas_call | solution.py:71
  33.5 7.0 %convert_bitcast_fusion = bf16[128,8,16,128]{3,1,2,0:T(8,128)(2,1)S(1)} fusion(bf16[1024,1024]{1,0:T(8,128)(2,1)S(1)} %copy-done.1, bf16[2048,1024]{1,0:T(8,128)(2,1)} %bitcast.185), kind=kOutput, calls=%fused_computation | convolution fusion | flops 4297064448 | bytes 10485760 | tf_op jit(solution)/shard_map/dot_general | solution.py:93
  40.4 1.4 copy.66
  41.8 2.2 %fusion.15 = (bf16[8,16,2,16,128]{4,3,2,1,0:T(8,128)(2,1)S(1)}, bf16[8,16,2,16,128]{4,3,2,1,0:T(8,128)(2,1)}, bf16[8,16,2,16,128]{4,3,2,1,0:T(8,128)(2,1)}, bf16[8,16,2,16,128]{4,3,2,1,0:T(8,128)(2,1)S(1)}) fusion(bf16[8,64,2,16,128]{4,3,2,1,0:T(8,128)(2,1)S(1)} %bitcast.167), kind=kLoop, calls=%fused_computation.111 | loop fusion | bytes 8388608 | tf_op jit(solution)/shard_map/slice | solution.py:111
  44.1 0.9 dynamic-slice_bitcast_fusion.24
  45.0 32.6 %collective-permute-start.1 = (bf16[16,2,16,128]{3,2,1,0:T(8,128)(2,1)}, bf16[16,2,16,128]{3,2,1,0:T(8,128)(2,1)}, u32[]{:S(2)}, u32[]{:S(2)}) collective-permute-start(bf16[16,2,16,128]{3,2,1,0:T(8,128)(2,1)} %get-tuple-element.113), channel_id=1, source_target_pairs={{0,2},{2,0},{4,6},{6,4},{8,10},{10,8},{12,14},{14,12},{1,3},{3,1},... | collective-permute-start | bytes 393224 | tf_op jit(solution)/shard_map/ppermute | solution.py:179
  77.6 1.6 collective-permute-start.2
  79.1 1.0 collective-permute-start.3
  80.2 1.6 collective-permute-start.4
  81.7 2.8 %collective-permute-start.5 = (bf16[16,2,16,128]{3,2,1,0:T(8,128)(2,1)S(1)}, bf16[16,2,16,128]{3,2,1,0:T(8,128)(2,1)S(1)}, u32[]{:S(2)}, u32[]{:S(2)}) collective-permute-start(bf16[16,2,16,128]{3,2,1,0:T(8,128)(2,1)S(1)} %get-tuple-element.109), channel_id=1, source_target_pairs={{0,10},{2,8},{4,14},{6,12},{8,2},{10,0},{12,6},{14,4},{1,11},{3,9}... | collective-permute-start | bytes 393224 | tf_op jit(solution)/shard_map/ppermute | solution.py:179
  84.7 2.3 %collective-permute-start.6 = (bf16[16,2,16,128]{3,2,1,0:T(8,128)(2,1)S(1)}, bf16[16,2,16,128]{3,2,1,0:T(8,128)(2,1)S(1)}, u32[]{:S(2)}, u32[]{:S(2)}) collective-permute-start(bf16[16,2,16,128]{3,2,1,0:T(8,128)(2,1)S(1)} %get-tuple-element.108), channel_id=1, source_target_pairs={{0,12},{2,14},{4,0},{6,2},{8,4},{10,6},{12,8},{14,10},{1,13},{3,15... | collective-permute-start | bytes 393224 | tf_op jit(solution)/shard_map/ppermute | solution.py:179
  87.0 0.9 bitcast_dynamic-update-slice_fusion.30
  88.8 6.3 %collective-permute-done.4 = bf16[16,2,16,128]{3,2,1,0:T(8,128)(2,1)S(1)} collective-permute-done((bf16[16,2,16,128]{3,2,1,0:T(8,128)(2,1)}, bf16[16,2,16,128]{3,2,1,0:T(8,128)(2,1)S(1)}, u32[]{:S(2)}, u32[]{:S(2)}) %collective-permute-start.4) | collective-permute-done | bytes 131104 | tf_op jit(solution)/shard_map/ppermute | solution.py:179
  95.1 2.9 %collective-permute-done.5 = bf16[16,2,16,128]{3,2,1,0:T(8,128)(2,1)S(1)} collective-permute-done((bf16[16,2,16,128]{3,2,1,0:T(8,128)(2,1)S(1)}, bf16[16,2,16,128]{3,2,1,0:T(8,128)(2,1)S(1)}, u32[]{:S(2)}, u32[]{:S(2)}) %collective-permute-start.5) | collective-permute-done | bytes 131104 | tf_op jit(solution)/shard_map/ppermute | solution.py:179
  98.6 2.1 %dynamic-slice_bitcast_fusion.16 = (bf16[16,2,16,128]{3,2,1,0:T(8,128)(2,1)S(1)}, bf16[16,2,16,128]{3,2,1,0:T(8,128)(2,1)}, bf16[16,2,16,128]{3,2,1,0:T(8,128)(2...) fusion(bf16[8,16,2,16,128]{4,3,2,1,0:T(8,128)(2,1)} %get-tuple-, ...), kind=kLoop, calls=%fused_computation.89 | loop fusion | bytes 2097184 | tf_op jit(solution)/shard_map/jit(dynamic_index_in_dim)/squeeze | solution.py:173
  100.8 5.6 %collective-permute-start.10 = (bf16[16,2,16,128]{3,2,1,0:T(8,128)(2,1)S(1)}, bf16[16,2,16,128]{3,2,1,0:T(8,128)(2,1)S(1)}, u32[]{:S(2)}, u32[]{:S(2)}) collective-permute-start(bf16[16,2,16,128]{3,2,1,0:T(8,128)(2,1)S(1)} %get-tuple-element.102), channel_id=1, source_target_pairs={{0,4},{2,6},{4,8},{6,10},{8,12},{10,14},{12,0},{14,2},{1,5},{3,7},... | collective-permute-start | bytes 393224 | tf_op jit(solution)/shard_map/ppermute | solution.py:179
  107.1 1.8 collective-permute-start.12
  108.9 1.3 collective-permute-start.13
  110.2 3.8 %collective-permute-start.14 = (bf16[16,2,16,128]{3,2,1,0:T(8,128)(2,1)}, bf16[16,2,16,128]{3,2,1,0:T(8,128)(2,1)}, u32[]{:S(2)}, u32[]{:S(2)}) collective-permute-start(bf16[16,2,16,128]{3,2,1,0:T(8,128)(2,1)} %get-tuple-element.98), channel_id=1, source_target_pairs={{0,12},{2,14},{4,0},{6,2},{8,4},{10,6},{12,8},{14,10},{1,13},{3,15... | collective-permute-start | bytes 393224 | tf_op jit(solution)/shard_map/ppermute | solution.py:179
  114.0 1.5 pad_maximum_fusion
  115.9 1.0 collective-permute-start.15
  117.8 2.4 %copy.53 = bf16[16,2,256,128]{3,2,1,0:T(8,128)(2,1)} copy(bf16[16,2,256,128]{2,3,0,1:T(8,128)(2,1)S(1)} %maximum_bitcast_fusion) | data formatting | bytes 4194304 | tf_op jit(solution)/shard_map/transpose | solution.py:211
  120.2 8.6 %shard_map.18.rest_0_ = f32[64,2,256,512]{3,2,1,0:T(8,128)} custom-call(bf16[16,512,128]{2,1,0:T(8,128)(2,1)} %bitcast.184, bf16[16,128,512]{2,1,0:T(8,128)(2,1)} %bitcast.183), custom_call_target="tpu_custom_call" | custom-call | flops 1073741824 | bytes 20971520 | tf_op jit(solution)/shard_map/pallas_call | solution.py:154
  129.0 1.0 bitcast_dynamic-update-slice_fusion.22
  130.1 0.9 bitcast_dynamic-update-slice_fusion.19
  131.1 0.9 bitcast_dynamic-update-slice_fusion.18
  132.0 0.9 bitcast_dynamic-update-slice_fusion.17
  133.0 0.9 bitcast_dynamic-update-slice_fusion.16
  134.0 0.9 dynamic-slice_bitcast_fusion.8
  134.9 1.3 collective-permute-start.17
  136.2 3.2 %collective-permute-start.18 = (bf16[16,2,16,128]{3,2,1,0:T(8,128)(2,1)S(1)}, bf16[16,2,16,128]{3,2,1,0:T(8,128)(2,1)S(1)}, u32[]{:S(2)}, u32[]{:S(2)}) collective-permute-start(bf16[16,2,16,128]{3,2,1,0:T(8,128)(2,1)S(1)} %get-tuple-element.92), channel_id=1, source_target_pairs={{0,4},{2,6},{4,8},{6,10},{8,12},{10,14},{12,0},{14,2},{1,5},{3,7},... | collective-permute-start | bytes 393224 | tf_op jit(solution)/shard_map/ppermute | solution.py:179
  139.5 0.8 collective-permute-start.19
  140.3 1.1 collective-permute-start.20
  141.5 1.9 collective-permute-start.21
  144.1 3.9 %collective-permute-start.22 = (bf16[16,2,16,128]{3,2,1,0:T(8,128)(2,1)S(1)}, bf16[16,2,16,128]{3,2,1,0:T(8,128)(2,1)}, u32[]{:S(2)}, u32[]{:S(2)}) collective-permute-start(bf16[16,2,16,128]{3,2,1,0:T(8,128)(2,1)S(1)} %get-tuple-element.88), channel_id=1, source_target_pairs={{0,12},{2,14},{4,0},{6,2},{8,4},{10,6},{12,8},{14,10},{1,13},{3,15... | collective-permute-start | bytes 393224 | tf_op jit(solution)/shard_map/ppermute | solution.py:179
  147.9 0.9 collective-permute-start.23
  149.1 1.6 copy.57
  150.6 2.4 %copy.56 = bf16[16,2,256,128]{3,2,1,0:T(8,128)(2,1)} copy(bf16[16,2,256,128]{2,3,0,1:T(8,128)(2,1)S(1)} %maximum_bitcast_fusion.1) | data formatting | bytes 4194304 | tf_op jit(solution)/shard_map/transpose | solution.py:211
  153.0 8.6 %shard_map.19.rest_0_ = f32[64,2,256,512]{3,2,1,0:T(8,128)} custom-call(bf16[16,512,128]{2,1,0:T(8,128)(2,1)} %bitcast.180, bf16[16,128,512]{2,1,0:T(8,128)(2,1)} %bitcast.178, f32[64,2,256,512]{3,2,1,0:T(8,128)} %shard_map.18.rest_0_), custom_call_target="tpu_custom_call", output_to_operand_aliasing={{}: (2, {})} | custom-call | flops 1073741824 | bytes 20971520 | tf_op jit(solution)/shard_map/pallas_call | solution.py:154
  161.9 0.9 bitcast_dynamic-update-slice_fusion.12
  162.9 0.9 bitcast_dynamic-update-slice_fusion.11
  163.8 0.9 bitcast_dynamic-update-slice_fusion.10
  164.8 0.9 bitcast_dynamic-update-slice_fusion.9
  165.7 0.9 bitcast_dynamic-update-slice_fusion.8
  166.9 1.2 collective-permute-start.25
  168.1 3.1 %collective-permute-start.26 = (bf16[16,2,16,128]{3,2,1,0:T(8,128)(2,1)S(1)}, bf16[16,2,16,128]{3,2,1,0:T(8,128)(2,1)S(1)}, u32[]{:S(2)}, u32[]{:S(2)}) collective-permute-start(bf16[16,2,16,128]{3,2,1,0:T(8,128)(2,1)S(1)} %get-tuple-element.82), channel_id=1, source_target_pairs={{0,4},{2,6},{4,8},{6,10},{8,12},{10,14},{12,0},{14,2},{1,5},{3,7},... | collective-permute-start | bytes 393224 | tf_op jit(solution)/shard_map/ppermute | solution.py:179
  171.9 1.8 collective-permute-start.28
  173.7 1.3 collective-permute-start.29
  175.7 3.9 %collective-permute-start.30 = (bf16[16,2,16,128]{3,2,1,0:T(8,128)(2,1)S(1)}, bf16[16,2,16,128]{3,2,1,0:T(8,128)(2,1)}, u32[]{:S(2)}, u32[]{:S(2)}) collective-permute-start(bf16[16,2,16,128]{3,2,1,0:T(8,128)(2,1)S(1)} %get-tuple-element.78), channel_id=1, source_target_pairs={{0,12},{2,14},{4,0},{6,2},{8,4},{10,6},{12,8},{14,10},{1,13},{3,15... | collective-permute-start | bytes 393224 | tf_op jit(solution)/shard_map/ppermute | solution.py:179
  180.6 1.6 copy.61
  182.2 2.4 %copy.60 = bf16[16,2,256,128]{3,2,1,0:T(8,128)(2,1)} copy(bf16[16,2,256,128]{2,3,0,1:T(8,128)(2,1)S(1)} %maximum_bitcast_fusion.2) | data formatting | bytes 4194304 | tf_op jit(solution)/shard_map/transpose | solution.py:211
  184.6 8.5 %shard_map.20.rest_0_ = f32[64,2,256,512]{3,2,1,0:T(8,128)} custom-call(bf16[16,512,128]{2,1,0:T(8,128)(2,1)} %bitcast.181, bf16[16,128,512]{2,1,0:T(8,128)(2,1)} %bitcast.179, f32[64,2,256,512]{3,2,1,0:T(8,128)} %shard_map.19.rest_0_), custom_call_target="tpu_custom_call", output_to_operand_aliasing={{}: (2, {})} | custom-call | flops 1073741824 | bytes 20971520 | tf_op jit(solution)/shard_map/pallas_call | solution.py:154
  193.5 0.9 bitcast_dynamic-update-slice_fusion.1
  194.5 0.9 bitcast_dynamic-update-slice_fusion
  195.5 2.6 %collective-permute-done.32 = bf16[16,2,2,16,512]{4,3,2,1,0:T(8,128)(2,1)S(1)} collective-permute-done((bf16[16,2,2,16,512]{4,3,2,1,0:T(8,128)(2,1)S(1)}, bf16[16,2,2,16,512]{4,3,2,1,0:T(8,128)(2,1)S(1)}, u32[]{:S(2)}, u32[]{:S(2)}) %collective-permute-start.32) | collective-permute-done | bytes 1048608 | tf_op jit(solution)/shard_map/ppermute | solution.py:200
  198.7 1.6 copy.65
  200.6 2.4 %copy.64 = bf16[16,2,256,128]{3,2,1,0:T(8,128)(2,1)} copy(bf16[16,2,256,128]{2,3,0,1:T(8,128)(2,1)S(1)} %maximum_bitcast_fusion.3) | data formatting | bytes 4194304 | tf_op jit(solution)/shard_map/transpose | solution.py:211
  203.1 8.6 %shard_map.21 = f32[64,2,256,512]{3,2,1,0:T(8,128)} custom-call(bf16[16,512,128]{2,1,0:T(8,128)(2,1)} %bitcast.182, bf16[16,128,512]{2,1,0:T(8,128)(2,1)} %bitcast.177, f32[64,2,256,512]{3,2,1,0:T(8,128)} %shard_map.20.rest_0_), custom_call_target="tpu_custom_call", output_to_operand_aliasing={{}: (2, {})} | custom-call | flops 1073741824 | bytes 20971520 | tf_op jit(solution)/shard_map/pallas_call | solution.py:154
  (109 shorter events, 9.1 us)
Async XLA Ops:
  0.0 20.3 %collective-permute-start = (bf16[128,16384]{1,0:T(8,128)(2,1)}, bf16[128,16384]{1,0:T(8,128)(2,1)}, u32[]{:S(2)}, u32[]{:S(2)}) collective-permute-start(bf16[128,16384]{1,0:T(8,128)(2,1)} %own_ref.1), channel_id=1, source_target_pairs={{0,1},{1,2},{2,3},{4,5},{5,6},{6,7},{8,9},{9,10},{10,11},{12,13},{... | collective-permute-start | bytes 12582920 | tf_op jit(solution)/shard_map/ppermute | solution.py:17
  20.3 13.1 %copy-start.1 = (bf16[1024,1024]{1,0:T(8,128)(2,1)S(1)}, bf16[1024,1024]{1,0:T(8,128)(2,1)}, u32[]{:S(2)}) copy-start(bf16[1024,1024]{1,0:T(8,128)(2,1)} %convert_element_type.36) | copy-start | bytes 6291460
  45.0 39.7 %collective-permute-start.1 = (bf16[16,2,16,128]{3,2,1,0:T(8,128)(2,1)}, bf16[16,2,16,128]{3,2,1,0:T(8,128)(2,1)}, u32[]{:S(2)}, u32[]{:S(2)}) collective-permute-start(bf16[16,2,16,128]{3,2,1,0:T(8,128)(2,1)} %get-tuple-element.113), channel_id=1, source_target_pairs={{0,2},{2,0},{4,6},{6,4},{8,10},{10,8},{12,14},{14,12},{1,3},{3,1},... | collective-permute-start | bytes 393224 | tf_op jit(solution)/shard_map/ppermute | solution.py:179
  77.6 10.4 %collective-permute-start.2 = (bf16[16,2,16,128]{3,2,1,0:T(8,128)(2,1)}, bf16[16,2,16,128]{3,2,1,0:T(8,128)(2,1)S(1)}, u32[]{:S(2)}, u32[]{:S(2)}) collective-permute-start(bf16[16,2,16,128]{3,2,1,0:T(8,128)(2,1)} %get-tuple-element.112), channel_id=1, source_target_pairs={{0,4},{2,6},{4,8},{6,10},{8,12},{10,14},{12,0},{14,2},{1,5},{3,7},... | collective-permute-start | bytes 393224 | tf_op jit(solution)/shard_map/ppermute | solution.py:179
  79.1 9.6 %collective-permute-start.3 = (bf16[16,2,16,128]{3,2,1,0:T(8,128)(2,1)}, bf16[16,2,16,128]{3,2,1,0:T(8,128)(2,1)S(1)}, u32[]{:S(2)}, u32[]{:S(2)}) collective-permute-start(bf16[16,2,16,128]{3,2,1,0:T(8,128)(2,1)} %get-tuple-element.111), channel_id=1, source_target_pairs={{0,6},{2,4},{4,10},{6,8},{8,14},{10,12},{12,2},{14,0},{1,7},{3,5},... | collective-permute-start | bytes 393224 | tf_op jit(solution)/shard_map/ppermute | solution.py:179
  80.2 15.0 %collective-permute-start.4 = (bf16[16,2,16,128]{3,2,1,0:T(8,128)(2,1)}, bf16[16,2,16,128]{3,2,1,0:T(8,128)(2,1)S(1)}, u32[]{:S(2)}, u32[]{:S(2)}) collective-permute-start(bf16[16,2,16,128]{3,2,1,0:T(8,128)(2,1)} %get-tuple-element.110), channel_id=1, source_target_pairs={{0,8},{2,10},{4,12},{6,14},{8,0},{10,2},{12,4},{14,6},{1,9},{3,11}... | collective-permute-start | bytes 393224 | tf_op jit(solution)/shard_map/ppermute | solution.py:179
  81.7 16.3 %collective-permute-start.5 = (bf16[16,2,16,128]{3,2,1,0:T(8,128)(2,1)S(1)}, bf16[16,2,16,128]{3,2,1,0:T(8,128)(2,1)S(1)}, u32[]{:S(2)}, u32[]{:S(2)}) collective-permute-start(bf16[16,2,16,128]{3,2,1,0:T(8,128)(2,1)S(1)} %get-tuple-element.109), channel_id=1, source_target_pairs={{0,10},{2,8},{4,14},{6,12},{8,2},{10,0},{12,6},{14,4},{1,11},{3,9}... | collective-permute-start | bytes 393224 | tf_op jit(solution)/shard_map/ppermute | solution.py:179
  84.7 13.3 %collective-permute-start.6 = (bf16[16,2,16,128]{3,2,1,0:T(8,128)(2,1)S(1)}, bf16[16,2,16,128]{3,2,1,0:T(8,128)(2,1)S(1)}, u32[]{:S(2)}, u32[]{:S(2)}) collective-permute-start(bf16[16,2,16,128]{3,2,1,0:T(8,128)(2,1)S(1)} %get-tuple-element.108), channel_id=1, source_target_pairs={{0,12},{2,14},{4,0},{6,2},{8,4},{10,6},{12,8},{14,10},{1,13},{3,15... | collective-permute-start | bytes 393224 | tf_op jit(solution)/shard_map/ppermute | solution.py:179
  88.0 10.5 %collective-permute-start.7 = (bf16[16,2,16,128]{3,2,1,0:T(8,128)(2,1)S(1)}, bf16[16,2,16,128]{3,2,1,0:T(8,128)(2,1)S(1)}, u32[]{:S(2)}, u32[]{:S(2)}) collective-permute-start(bf16[16,2,16,128]{3,2,1,0:T(8,128)(2,1)S(1)} %get-tuple-element.107), channel_id=1, source_target_pairs={{0,14},{2,12},{4,2},{6,0},{8,6},{10,4},{12,10},{14,8},{1,15},{3,13... | collective-permute-start | bytes 393224 | tf_op jit(solution)/shard_map/ppermute | solution.py:179
  98.5 11.7 %collective-permute-start.8 = (bf16[16,2,2,16,512]{4,3,2,1,0:T(8,128)(2,1)S(1)}, bf16[16,2,2,16,512]{4,3,2,1,0:T(8,128)(2,1)S(1)}, u32[]{:S(2)}, u32[]{:S(2)}) collective-permute-start(bf16[16,2,2,16,512]{4,3,2,1,0:T(8,128)(2,1)S(1)} %bitcast_dynamic-update-slice_fusion.24), channel_id=1, source_target_pairs={{0,1},{1,0},{2,3},{3,2},{4,5},{5,4},{6,7},{7,6},{8,9},{9,8},{10,11... | collective-permute-start | bytes 3145736 | tf_op jit(solution)/shard_map/ppermute | solution.py:200
  100.8 15.1 %collective-permute-start.10 = (bf16[16,2,16,128]{3,2,1,0:T(8,128)(2,1)S(1)}, bf16[16,2,16,128]{3,2,1,0:T(8,128)(2,1)S(1)}, u32[]{:S(2)}, u32[]{:S(2)}) collective-permute-start(bf16[16,2,16,128]{3,2,1,0:T(8,128)(2,1)S(1)} %get-tuple-element.102), channel_id=1, source_target_pairs={{0,4},{2,6},{4,8},{6,10},{8,12},{10,14},{12,0},{14,2},{1,5},{3,7},... | collective-permute-start | bytes 393224 | tf_op jit(solution)/shard_map/ppermute | solution.py:179
  106.4 10.5 %collective-permute-start.11 = (bf16[16,2,16,128]{3,2,1,0:T(8,128)(2,1)S(1)}, bf16[16,2,16,128]{3,2,1,0:T(8,128)(2,1)S(1)}, u32[]{:S(2)}, u32[]{:S(2)}) collective-permute-start(bf16[16,2,16,128]{3,2,1,0:T(8,128)(2,1)S(1)} %get-tuple-element.101), channel_id=1, source_target_pairs={{0,6},{2,4},{4,10},{6,8},{8,14},{10,12},{12,2},{14,0},{1,7},{3,5},... | collective-permute-start | bytes 393224 | tf_op jit(solution)/shard_map/ppermute | solution.py:179
  107.1 21.7 %collective-permute-start.12 = (bf16[16,2,16,128]{3,2,1,0:T(8,128)(2,1)}, bf16[16,2,16,128]{3,2,1,0:T(8,128)(2,1)}, u32[]{:S(2)}, u32[]{:S(2)}) collective-permute-start(bf16[16,2,16,128]{3,2,1,0:T(8,128)(2,1)} %get-tuple-element.100), channel_id=1, source_target_pairs={{0,8},{2,10},{4,12},{6,14},{8,0},{10,2},{12,4},{14,6},{1,9},{3,11}... | collective-permute-start | bytes 393224 | tf_op jit(solution)/shard_map/ppermute | solution.py:179
  108.9 19.9 %collective-permute-start.13 = (bf16[16,2,16,128]{3,2,1,0:T(8,128)(2,1)}, bf16[16,2,16,128]{3,2,1,0:T(8,128)(2,1)}, u32[]{:S(2)}, u32[]{:S(2)}) collective-permute-start(bf16[16,2,16,128]{3,2,1,0:T(8,128)(2,1)} %get-tuple-element.99), channel_id=1, source_target_pairs={{0,10},{2,8},{4,14},{6,12},{8,2},{10,0},{12,6},{14,4},{1,11},{3,9}... | collective-permute-start | bytes 393224 | tf_op jit(solution)/shard_map/ppermute | solution.py:179
  110.2 18.6 %collective-permute-start.14 = (bf16[16,2,16,128]{3,2,1,0:T(8,128)(2,1)}, bf16[16,2,16,128]{3,2,1,0:T(8,128)(2,1)}, u32[]{:S(2)}, u32[]{:S(2)}) collective-permute-start(bf16[16,2,16,128]{3,2,1,0:T(8,128)(2,1)} %get-tuple-element.98), channel_id=1, source_target_pairs={{0,12},{2,14},{4,0},{6,2},{8,4},{10,6},{12,8},{14,10},{1,13},{3,15... | collective-permute-start | bytes 393224 | tf_op jit(solution)/shard_map/ppermute | solution.py:179
  115.9 1.7 copy-start.6
  115.9 12.9 %collective-permute-start.15 = (bf16[16,2,16,128]{3,2,1,0:T(8,128)(2,1)S(1)}, bf16[16,2,16,128]{3,2,1,0:T(8,128)(2,1)}, u32[]{:S(2)}, u32[]{:S(2)}) collective-permute-start(bf16[16,2,16,128]{3,2,1,0:T(8,128)(2,1)S(1)} %get-tuple-element.97), channel_id=1, source_target_pairs={{0,14},{2,12},{4,2},{6,0},{8,6},{10,4},{12,10},{14,8},{1,15},{3,13... | collective-permute-start | bytes 393224 | tf_op jit(solution)/shard_map/ppermute | solution.py:179
  116.9 0.7 copy-start.8
  116.9 11.9 %collective-permute-start.9 = (bf16[16,2,16,128]{3,2,1,0:T(8,128)(2,1)S(1)}, bf16[16,2,16,128]{3,2,1,0:T(8,128)(2,1)}, u32[]{:S(2)}, u32[]{:S(2)}) collective-permute-start(bf16[16,2,16,128]{3,2,1,0:T(8,128)(2,1)S(1)} %get-tuple-element.103), channel_id=1, source_target_pairs={{0,2},{2,0},{4,6},{6,4},{8,10},{10,8},{12,14},{14,12},{1,3},{3,1},... | collective-permute-start | bytes 393224 | tf_op jit(solution)/shard_map/ppermute | solution.py:179
  120.2 9.8 %copy-start.7 = (bf16[16,2,16,128]{3,2,1,0:T(8,128)(2,1)S(1)}, bf16[16,2,16,128]{3,2,1,0:T(8,128)(2,1)}, u32[]{:S(2)}) copy-start(bf16[16,2,16,128]{3,2,1,0:T(8,128)(2,1)} %copy-done.6) | copy-start | bytes 393220
  120.2 9.9 %copy-start.9 = (bf16[16,2,16,128]{3,2,1,0:T(8,128)(2,1)S(1)}, bf16[16,2,16,128]{3,2,1,0:T(8,128)(2,1)}, u32[]{:S(2)}) copy-start(bf16[16,2,16,128]{3,2,1,0:T(8,128)(2,1)} %copy-done.8) | copy-start | bytes 393220
  128.8 5.2 %copy-start = (bf16[8,16,2,16,128]{4,3,2,1,0:T(8,128)(2,1)S(1)}, bf16[8,16,2,16,128]{4,3,2,1,0:T(8,128)(2,1)}, u32[]{:S(2)}) copy-start(bf16[8,16,2,16,128]{4,3,2,1,0:T(8,128)(2,1)} %get-tuple-element.50) | copy-start | bytes 3145732
  133.9 7.5 %collective-permute-start.16 = (bf16[16,2,2,16,512]{4,3,2,1,0:T(8,128)(2,1)S(1)}, bf16[16,2,2,16,512]{4,3,2,1,0:T(8,128)(2,1)S(1)}, u32[]{:S(2)}, u32[]{:S(2)}) collective-permute-start(bf16[16,2,2,16,512]{4,3,2,1,0:T(8,128)(2,1)S(1)} %bitcast_dynamic-update-slice_fusion.16), channel_id=1, source_target_pairs={{0,1},{1,0},{2,3},{3,2},{4,5},{5,4},{6,7},{7,6},{8,9},{9,8},{10,11... | collective-permute-start | bytes 3145736 | tf_op jit(solution)/shard_map/ppermute | solution.py:200
  134.9 9.1 %collective-permute-start.17 = (bf16[16,2,16,128]{3,2,1,0:T(8,128)(2,1)S(1)}, bf16[16,2,16,128]{3,2,1,0:T(8,128)(2,1)S(1)}, u32[]{:S(2)}, u32[]{:S(2)}) collective-permute-start(bf16[16,2,16,128]{3,2,1,0:T(8,128)(2,1)S(1)} %get-tuple-element.93), channel_id=1, source_target_pairs={{0,2},{2,0},{4,6},{6,4},{8,10},{10,8},{12,14},{14,12},{1,3},{3,1},... | collective-permute-start | bytes 393224 | tf_op jit(solution)/shard_map/ppermute | solution.py:179
  136.2 11.7 %collective-permute-start.18 = (bf16[16,2,16,128]{3,2,1,0:T(8,128)(2,1)S(1)}, bf16[16,2,16,128]{3,2,1,0:T(8,128)(2,1)S(1)}, u32[]{:S(2)}, u32[]{:S(2)}) collective-permute-start(bf16[16,2,16,128]{3,2,1,0:T(8,128)(2,1)S(1)} %get-tuple-element.92), channel_id=1, source_target_pairs={{0,4},{2,6},{4,8},{6,10},{8,12},{10,14},{12,0},{14,2},{1,5},{3,7},... | collective-permute-start | bytes 393224 | tf_op jit(solution)/shard_map/ppermute | solution.py:179
  139.5 22.1 %collective-permute-start.19 = (bf16[16,2,16,128]{3,2,1,0:T(8,128)(2,1)}, bf16[16,2,16,128]{3,2,1,0:T(8,128)(2,1)}, u32[]{:S(2)}, u32[]{:S(2)}) collective-permute-start(bf16[16,2,16,128]{3,2,1,0:T(8,128)(2,1)} %get-tuple-element.91), channel_id=1, source_target_pairs={{0,6},{2,4},{4,10},{6,8},{8,14},{10,12},{12,2},{14,0},{1,7},{3,5},... | collective-permute-start | bytes 393224 | tf_op jit(solution)/shard_map/ppermute | solution.py:179
  140.3 21.3 %collective-permute-start.20 = (bf16[16,2,16,128]{3,2,1,0:T(8,128)(2,1)}, bf16[16,2,16,128]{3,2,1,0:T(8,128)(2,1)}, u32[]{:S(2)}, u32[]{:S(2)}) collective-permute-start(bf16[16,2,16,128]{3,2,1,0:T(8,128)(2,1)} %get-tuple-element.90), channel_id=1, source_target_pairs={{0,8},{2,10},{4,12},{6,14},{8,0},{10,2},{12,4},{14,6},{1,9},{3,11}... | collective-permute-start | bytes 393224 | tf_op jit(solution)/shard_map/ppermute | solution.py:179
  141.5 20.2 %collective-permute-start.21 = (bf16[16,2,16,128]{3,2,1,0:T(8,128)(2,1)}, bf16[16,2,16,128]{3,2,1,0:T(8,128)(2,1)}, u32[]{:S(2)}, u32[]{:S(2)}) collective-permute-start(bf16[16,2,16,128]{3,2,1,0:T(8,128)(2,1)} %get-tuple-element.89), channel_id=1, source_target_pairs={{0,10},{2,8},{4,14},{6,12},{8,2},{10,0},{12,6},{14,4},{1,11},{3,9}... | collective-permute-start | bytes 393224 | tf_op jit(solution)/shard_map/ppermute | solution.py:179
  144.1 4.8 %copy-start.2 = (bf16[16,2,16,128]{3,2,1,0:T(8,128)(2,1)}, bf16[16,2,16,128]{3,2,1,0:T(8,128)(2,1)S(1)}, u32[]{:S(2)}) copy-start(bf16[16,2,16,128]{3,2,1,0:T(8,128)(2,1)S(1)} %collective-permute-done.17) | copy-start | bytes 393220
  144.1 17.6 %collective-permute-start.22 = (bf16[16,2,16,128]{3,2,1,0:T(8,128)(2,1)S(1)}, bf16[16,2,16,128]{3,2,1,0:T(8,128)(2,1)}, u32[]{:S(2)}, u32[]{:S(2)}) collective-permute-start(bf16[16,2,16,128]{3,2,1,0:T(8,128)(2,1)S(1)} %get-tuple-element.88), channel_id=1, source_target_pairs={{0,12},{2,14},{4,0},{6,2},{8,4},{10,6},{12,8},{14,10},{1,13},{3,15... | collective-permute-start | bytes 393224 | tf_op jit(solution)/shard_map/ppermute | solution.py:179
  147.9 0.9 copy-start.4
  147.9 13.7 %collective-permute-start.23 = (bf16[16,2,16,128]{3,2,1,0:T(8,128)(2,1)S(1)}, bf16[16,2,16,128]{3,2,1,0:T(8,128)(2,1)}, u32[]{:S(2)}, u32[]{:S(2)}) collective-permute-start(bf16[16,2,16,128]{3,2,1,0:T(8,128)(2,1)S(1)} %get-tuple-element.87), channel_id=1, source_target_pairs={{0,14},{2,12},{4,2},{6,0},{8,6},{10,4},{12,10},{14,8},{1,15},{3,13... | collective-permute-start | bytes 393224 | tf_op jit(solution)/shard_map/ppermute | solution.py:179
  153.0 8.8 %copy-start.3 = (bf16[16,2,16,128]{3,2,1,0:T(8,128)(2,1)S(1)}, bf16[16,2,16,128]{3,2,1,0:T(8,128)(2,1)}, u32[]{:S(2)}) copy-start(bf16[16,2,16,128]{3,2,1,0:T(8,128)(2,1)} %copy-done.2) | copy-start | bytes 393220
  153.0 8.9 %copy-start.5 = (bf16[16,2,16,128]{3,2,1,0:T(8,128)(2,1)S(1)}, bf16[16,2,16,128]{3,2,1,0:T(8,128)(2,1)}, u32[]{:S(2)}) copy-start(bf16[16,2,16,128]{3,2,1,0:T(8,128)(2,1)} %copy-done.4) | copy-start | bytes 393220
  166.7 7.0 %collective-permute-start.24 = (bf16[16,2,2,16,512]{4,3,2,1,0:T(8,128)(2,1)S(1)}, bf16[16,2,2,16,512]{4,3,2,1,0:T(8,128)(2,1)S(1)}, u32[]{:S(2)}, u32[]{:S(2)}) collective-permute-start(bf16[16,2,2,16,512]{4,3,2,1,0:T(8,128)(2,1)S(1)} %bitcast_dynamic-update-slice_fusion.8), channel_id=1, source_target_pairs={{0,1},{1,0},{2,3},{3,2},{4,5},{5,4},{6,7},{7,6},{8,9},{9,8},{10,11... | collective-permute-start | bytes 3145736 | tf_op jit(solution)/shard_map/ppermute | solution.py:200
  166.9 8.8 %collective-permute-start.25 = (bf16[16,2,16,128]{3,2,1,0:T(8,128)(2,1)S(1)}, bf16[16,2,16,128]{3,2,1,0:T(8,128)(2,1)S(1)}, u32[]{:S(2)}, u32[]{:S(2)}) collective-permute-start(bf16[16,2,16,128]{3,2,1,0:T(8,128)(2,1)S(1)} %get-tuple-element.83), channel_id=1, source_target_pairs={{0,2},{2,0},{4,6},{6,4},{8,10},{10,8},{12,14},{14,12},{1,3},{3,1},... | collective-permute-start | bytes 393224 | tf_op jit(solution)/shard_map/ppermute | solution.py:179
  168.1 11.5 %collective-permute-start.26 = (bf16[16,2,16,128]{3,2,1,0:T(8,128)(2,1)S(1)}, bf16[16,2,16,128]{3,2,1,0:T(8,128)(2,1)S(1)}, u32[]{:S(2)}, u32[]{:S(2)}) collective-permute-start(bf16[16,2,16,128]{3,2,1,0:T(8,128)(2,1)S(1)} %get-tuple-element.82), channel_id=1, source_target_pairs={{0,4},{2,6},{4,8},{6,10},{8,12},{10,14},{12,0},{14,2},{1,5},{3,7},... | collective-permute-start | bytes 393224 | tf_op jit(solution)/shard_map/ppermute | solution.py:179
  171.2 21.9 %collective-permute-start.27 = (bf16[16,2,16,128]{3,2,1,0:T(8,128)(2,1)S(1)}, bf16[16,2,16,128]{3,2,1,0:T(8,128)(2,1)S(1)}, u32[]{:S(2)}, u32[]{:S(2)}) collective-permute-start(bf16[16,2,16,128]{3,2,1,0:T(8,128)(2,1)S(1)} %get-tuple-element.81), channel_id=1, source_target_pairs={{0,6},{2,4},{4,10},{6,8},{8,14},{10,12},{12,2},{14,0},{1,7},{3,5},... | collective-permute-start | bytes 393224 | tf_op jit(solution)/shard_map/ppermute | solution.py:179
  171.9 21.2 %collective-permute-start.28 = (bf16[16,2,16,128]{3,2,1,0:T(8,128)(2,1)S(1)}, bf16[16,2,16,128]{3,2,1,0:T(8,128)(2,1)S(1)}, u32[]{:S(2)}, u32[]{:S(2)}) collective-permute-start(bf16[16,2,16,128]{3,2,1,0:T(8,128)(2,1)S(1)} %get-tuple-element.80), channel_id=1, source_target_pairs={{0,8},{2,10},{4,12},{6,14},{8,0},{10,2},{12,4},{14,6},{1,9},{3,11}... | collective-permute-start | bytes 393224 | tf_op jit(solution)/shard_map/ppermute | solution.py:179
  173.7 19.5 %collective-permute-start.29 = (bf16[16,2,16,128]{3,2,1,0:T(8,128)(2,1)S(1)}, bf16[16,2,16,128]{3,2,1,0:T(8,128)(2,1)S(1)}, u32[]{:S(2)}, u32[]{:S(2)}) collective-permute-start(bf16[16,2,16,128]{3,2,1,0:T(8,128)(2,1)S(1)} %get-tuple-element.79), channel_id=1, source_target_pairs={{0,10},{2,8},{4,14},{6,12},{8,2},{10,0},{12,6},{14,4},{1,11},{3,9}... | collective-permute-start | bytes 393224 | tf_op jit(solution)/shard_map/ppermute | solution.py:179
  175.7 17.4 %collective-permute-start.30 = (bf16[16,2,16,128]{3,2,1,0:T(8,128)(2,1)S(1)}, bf16[16,2,16,128]{3,2,1,0:T(8,128)(2,1)}, u32[]{:S(2)}, u32[]{:S(2)}) collective-permute-start(bf16[16,2,16,128]{3,2,1,0:T(8,128)(2,1)S(1)} %get-tuple-element.78), channel_id=1, source_target_pairs={{0,12},{2,14},{4,0},{6,2},{8,4},{10,6},{12,8},{14,10},{1,13},{3,15... | collective-permute-start | bytes 393224 | tf_op jit(solution)/shard_map/ppermute | solution.py:179
  179.6 13.5 %collective-permute-start.31 = (bf16[16,2,16,128]{3,2,1,0:T(8,128)(2,1)S(1)}, bf16[16,2,16,128]{3,2,1,0:T(8,128)(2,1)}, u32[]{:S(2)}, u32[]{:S(2)}) collective-permute-start(bf16[16,2,16,128]{3,2,1,0:T(8,128)(2,1)S(1)} %get-tuple-element.77), channel_id=1, source_target_pairs={{0,14},{2,12},{4,2},{6,0},{8,6},{10,4},{12,10},{14,8},{1,15},{3,13... | collective-permute-start | bytes 393224 | tf_op jit(solution)/shard_map/ppermute | solution.py:179
  195.4 2.7 %collective-permute-start.32 = (bf16[16,2,2,16,512]{4,3,2,1,0:T(8,128)(2,1)S(1)}, bf16[16,2,2,16,512]{4,3,2,1,0:T(8,128)(2,1)S(1)}, u32[]{:S(2)}, u32[]{:S(2)}) collective-permute-start(bf16[16,2,2,16,512]{4,3,2,1,0:T(8,128)(2,1)S(1)} %bitcast_dynamic-update-slice_fusion), channel_id=1, source_target_pairs={{0,1},{1,0},{2,3},{3,2},{4,5},{5,4},{6,7},{7,6},{8,9},{9,8},{10,11... | collective-permute-start | bytes 3145736 | tf_op jit(solution)/shard_map/ppermute | solution.py:200

commit v14 on v13

--- a/solution.py
+++ b/solution.py
@@ -128,19 +128,21 @@
     out_ref = rest[-1]
     rows = out_ref.shape[2]
     for k in range(lhs_ref.shape[0]):
-        acc = jnp.dot(lhs_ref[k], rhs_ref[k], preferred_element_type=jnp.float32) * scale
+        acc = lax.dot_general(
+            lhs_ref[k], rhs_ref[k], (((0,), (0,)), ((), ())), preferred_element_type=jnp.float32
+        ) * scale
         out_ref[k, 0] = acc[:rows]
         out_ref[k, 1] = acc[rows:]
 
 
 def correlate(lhs, rhs, prev, first_channel, own_channels):
-    count, two_rows, depth = lhs.shape
+    count, depth, two_rows = lhs.shape
     cols = rhs.shape[2]
     rows = two_rows // 2
     step = 4 if count % 4 == 0 else (2 if count % 2 == 0 else 1)
     offset = first_channel // step
     in_specs = [
-        pl.BlockSpec((step, two_rows, depth), lambda c: (c, 0, 0)),
+        pl.BlockSpec((step, depth, two_rows), lambda c: (c, 0, 0)),
         pl.BlockSpec((step, depth, cols), lambda c: (c, 0, 0)),
     ]
     args = [lhs, rhs]
@@ -207,8 +209,7 @@
     row_start = lax.axis_index("pol") * rows_here
     own_rows = lax.dynamic_slice_in_dim(both, row_start, rows_here, 5)
     swapped = jnp.stack([own_rows[:, :, 1], -own_rows[:, :, 0]], axis=2)
-    lhs = jnp.stack([own_rows, swapped], axis=1).reshape(own_channels, 2, depth, rows_here)
-    lhs = lhs.transpose(0, 1, 3, 2).reshape(own_channels, 2 * rows_here, depth)
+    lhs = jnp.concatenate([own_rows, swapped], axis=5).reshape(own_channels, depth, 2 * rows_here)
     return lhs, left_all
 
 

time: 214 us -> 203 us (0.949)
  local copies, waits for them, and re-layouts: 40.6 us -> 25.9 us
    transpose x4 -> x0, local copies, waits for them, and re-layouts: 9.58 us -> none  [finish_chunk(): lhs = lhs.transpose(0, 1, 3, 2).reshape(own_channels, 2 * rows_here, depth)]
    dynamic_update_slice x32, local copies, waits for them, and re-layouts: 13 us -> 4.8 us  [assemble_chunk(): lax.dynamic_update_slice(half, block[:, :, None], (0, 0, tm_step, 0, sour...]
    concatenate x0 -> x3, local copies, waits for them, and re-layouts: none -> 4.57 us  [finish_chunk(): jnp.concatenate([own_rows, swapped], axis=5)]
    concatenate x0 -> x4, other arithmetic: none -> 2.41 us  [finish_chunk(): jnp.concatenate([own_rows, swapped], axis=5)]
    another operation x5 -> x1, other arithmetic: 8.89 us -> 8.49 us
  transfers between devices with their start and end apart: 33 -> 33, of which waited for: 4 -> 5; matrix products, arithmetic and copies ran while one was open for 16% -> 15% of each run, Pallas kernels for 12% -> 13%
where the time goes in v14:
time: 203 us; the launch traced here: 200 us
  starting transfers between devices  89.8 us (44%)
  Pallas kernels  47.7 us (23%)
  local copies, waits for them, and re-layouts  25.9 us (13%)
  other arithmetic  16.1 us (8%)
  waiting for transfers between devices  12.4 us (6%)
  matrix products  6.95 us (3%)
    ppermute x28, starting transfers between devices, send_chunk(): block = lax.ppermute(block, ('inp', 'tm'), route)  85.2 us
    pallas_call x4, Pallas kernels, correlate(): pl.pallas_call(functools.partial(correlate_kernel, 1.0 / (depth // 2)), g...  34.5 us
    pallas_call x1, Pallas kernels, polyphase_filter(): pl.pallas_call(filter_kernel, grid=(inputs_here // rows,), in_specs=[pl.B...  13.1 us
    ppermute x28, waiting for transfers between devices, send_chunk(): block = lax.ppermute(block, ('inp', 'tm'), route)  9.74 us
    another operation x1, other arithmetic  8.49 us
    dot_general x1, matrix products, per_device(): lax.dot_general(dft_table_t(frame_len), filtered.reshape(spectra_here * i...  6.95 us
    dynamic_update_slice x32, local copies, waits for them, and re-layouts, assemble_chunk(): lax.dynamic_update_slice(half, block[:, :, None], (0, 0, tm_step, 0, sour...  4.8 us
    concatenate x3, local copies, waits for them, and re-layouts, finish_chunk(): jnp.concatenate([own_rows, swapped], axis=5)  4.57 us
  transfers between devices with their start and end apart: 33, of which 5 were waited for; matrix products, arithmetic and copies ran while one was open for 15% of the time, Pallas kernels for 13%

profile of v14, /device:TPU:0, one launch (start us, length us, event | category | flops | bytes accessed | tf_op | source)
XLA Modules:
  0.0 200.1 jit_solution(11911862692154971145)
XLA Ops:
  0.0 4.3 %collective-permute-start = (bf16[128,16384]{1,0:T(8,128)(2,1)}, bf16[128,16384]{1,0:T(8,128)(2,1)}, u32[]{:S(2)}, u32[]{:S(2)}) collective-permute-start(bf16[128,16384]{1,0:T(8,128)(2,1)} %own_ref.1), channel_id=1, source_target_pairs={{0,1},{1,2},{2,3},{4,5},{5,6},{6,7},{8,9},{9,10},{10,11},{12,13},{... | collective-permute-start | bytes 12582920 | tf_op jit(solution)/shard_map/ppermute | solution.py:17
  4.3 8.5 %negate_convert_fusion = (bf16[512,1,1024]{2,0,1:T(8,128)(2,1)S(1)}, bf16[512,1,1024]{2,0,1:T(8,128)(2,1)S(1)}) fusion(), kind=kLoop, calls=%fused_computation.24 | loop fusion | flops 8912896 | bytes 2097152 | tf_op jit(solution)/shard_map/convert.1
  12.8 0.2 pad_maximum_fusion.4
  13.0 2.2 %copy.19 = bf16[512,2,1024]{2,1,0:T(2,128)(2,1)S(1)} copy(bf16[512,2,1024]{2,0,1:T(8,128)(2,1)S(1)} %pad_maximum_fusion.4) | data formatting | bytes 4194304 | tf_op jit(solution)/shard_map/stack | solution.py:35
  15.2 2.3 %convert_element_type.36 = bf16[1024,1024]{1,0:T(8,128)(2,1)} reshape(bf16[512,2,1024]{2,1,0:T(2,128)(2,1)S(1)} %copy.19) | data formatting | bytes 4194304 | tf_op jit(solution)/shard_map/convert_element_type | solution.py:36
  17.4 1.1 fusion.14
  19.2 1.1 fusion.11.taps_ref
  20.3 13.1 %shard_map.17 = bf16[16,128,1024]{2,1,0:T(8,128)(2,1)} custom-call(f32[16,1024]{1,0:T(8,128)} %fusion.11.taps_ref, bf16[128,16384]{1,0:T(8,128)(2,1)} %own_ref.1, bf16[128,16384]{1,0:T(8,128)(2,1)} %collective-permute-done.history_ref), custom_call_target="tpu_custom_call" | custom-call | flops 67108864 | bytes 12582912 | tf_op jit(solution)/shard_map/pallas_call | solution.py:71
  33.5 7.0 %convert_bitcast_fusion = bf16[128,8,16,128]{3,1,2,0:T(8,128)(2,1)S(1)} fusion(bf16[1024,1024]{1,0:T(8,128)(2,1)S(1)} %copy-done.1, bf16[2048,1024]{1,0:T(8,128)(2,1)} %bitcast.168), kind=kOutput, calls=%fused_computation | convolution fusion | flops 4297064448 | bytes 10485760 | tf_op jit(solution)/shard_map/dot_general | solution.py:93
  40.4 1.4 copy.27
  41.8 2.2 %fusion.15 = (bf16[8,16,2,16,128]{4,3,2,1,0:T(8,128)(2,1)S(1)}, bf16[8,16,2,16,128]{4,3,2,1,0:T(8,128)(2,1)}, bf16[8,16,2,16,128]{4,3,2,1,0:T(8,128)(2,1)}, bf16[8,16,2,16,128]{4,3,2,1,0:T(8,128)(2,1)S(1)}) fusion(bf16[8,64,2,16,128]{4,3,2,1,0:T(8,128)(2,1)S(1)} %bitcast.151), kind=kLoop, calls=%fused_computation.107 | loop fusion | bytes 8388608 | tf_op jit(solution)/shard_map/slice | solution.py:111
  44.1 0.9 dynamic-slice_bitcast_fusion.24
  45.0 32.6 %collective-permute-start.1 = (bf16[16,2,16,128]{3,2,1,0:T(8,128)(2,1)}, bf16[16,2,16,128]{3,2,1,0:T(8,128)(2,1)}, u32[]{:S(2)}, u32[]{:S(2)}) collective-permute-start(bf16[16,2,16,128]{3,2,1,0:T(8,128)(2,1)} %get-tuple-element.113), channel_id=1, source_target_pairs={{0,2},{2,0},{4,6},{6,4},{8,10},{10,8},{12,14},{14,12},{1,3},{3,1},... | collective-permute-start | bytes 393224 | tf_op jit(solution)/shard_map/ppermute | solution.py:181
  77.6 1.6 collective-permute-start.2
  79.1 1.0 collective-permute-start.3
  80.2 1.6 collective-permute-start.4
  81.7 2.8 %collective-permute-start.5 = (bf16[16,2,16,128]{3,2,1,0:T(8,128)(2,1)S(1)}, bf16[16,2,16,128]{3,2,1,0:T(8,128)(2,1)S(1)}, u32[]{:S(2)}, u32[]{:S(2)}) collective-permute-start(bf16[16,2,16,128]{3,2,1,0:T(8,128)(2,1)S(1)} %get-tuple-element.109), channel_id=1, source_target_pairs={{0,10},{2,8},{4,14},{6,12},{8,2},{10,0},{12,6},{14,4},{1,11},{3,9}... | collective-permute-start | bytes 393224 | tf_op jit(solution)/shard_map/ppermute | solution.py:181
  84.7 2.3 %collective-permute-start.6 = (bf16[16,2,16,128]{3,2,1,0:T(8,128)(2,1)S(1)}, bf16[16,2,16,128]{3,2,1,0:T(8,128)(2,1)S(1)}, u32[]{:S(2)}, u32[]{:S(2)}) collective-permute-start(bf16[16,2,16,128]{3,2,1,0:T(8,128)(2,1)S(1)} %get-tuple-element.108), channel_id=1, source_target_pairs={{0,12},{2,14},{4,0},{6,2},{8,4},{10,6},{12,8},{14,10},{1,13},{3,15... | collective-permute-start | bytes 393224 | tf_op jit(solution)/shard_map/ppermute | solution.py:181
  87.0 0.9 bitcast_dynamic-update-slice_fusion.30
  88.0 0.8 collective-permute-start.7
  88.8 6.3 %collective-permute-done.4 = bf16[16,2,16,128]{3,2,1,0:T(8,128)(2,1)S(1)} collective-permute-done((bf16[16,2,16,128]{3,2,1,0:T(8,128)(2,1)}, bf16[16,2,16,128]{3,2,1,0:T(8,128)(2,1)S(1)}, u32[]{:S(2)}, u32[]{:S(2)}) %collective-permute-start.4) | collective-permute-done | bytes 131104 | tf_op jit(solution)/shard_map/ppermute | solution.py:181
  95.2 2.9 %collective-permute-done.5 = bf16[16,2,16,128]{3,2,1,0:T(8,128)(2,1)S(1)} collective-permute-done((bf16[16,2,16,128]{3,2,1,0:T(8,128)(2,1)S(1)}, bf16[16,2,16,128]{3,2,1,0:T(8,128)(2,1)S(1)}, u32[]{:S(2)}, u32[]{:S(2)}) %collective-permute-start.5) | collective-permute-done | bytes 131104 | tf_op jit(solution)/shard_map/ppermute | solution.py:181
  98.1 0.4 collective-permute-done.7
  98.6 2.1 %dynamic-slice_bitcast_fusion.16 = (bf16[16,2,16,128]{3,2,1,0:T(8,128)(2,1)S(1)}, bf16[16,2,16,128]{3,2,1,0:T(8,128)(2,1)}, bf16[16,2,16,128]{3,2,1,0:T(8,128)(2...) fusion(bf16[8,16,2,16,128]{4,3,2,1,0:T(8,128)(2,1)} %get-tuple-, ...), kind=kLoop, calls=%fused_computation.85 | loop fusion | bytes 2097184 | tf_op jit(solution)/shard_map/jit(dynamic_index_in_dim)/squeeze | solution.py:175
  100.8 5.6 %collective-permute-start.10 = (bf16[16,2,16,128]{3,2,1,0:T(8,128)(2,1)S(1)}, bf16[16,2,16,128]{3,2,1,0:T(8,128)(2,1)S(1)}, u32[]{:S(2)}, u32[]{:S(2)}) collective-permute-start(bf16[16,2,16,128]{3,2,1,0:T(8,128)(2,1)S(1)} %get-tuple-element.102), channel_id=1, source_target_pairs={{0,4},{2,6},{4,8},{6,10},{8,12},{10,14},{12,0},{14,2},{1,5},{3,7},... | collective-permute-start | bytes 393224 | tf_op jit(solution)/shard_map/ppermute | solution.py:181
  106.4 0.7 collective-permute-start.11
  107.1 1.8 collective-permute-start.12
  108.9 1.3 collective-permute-start.13
  110.2 3.8 %collective-permute-start.14 = (bf16[16,2,16,128]{3,2,1,0:T(8,128)(2,1)}, bf16[16,2,16,128]{3,2,1,0:T(8,128)(2,1)}, u32[]{:S(2)}, u32[]{:S(2)}) collective-permute-start(bf16[16,2,16,128]{3,2,1,0:T(8,128)(2,1)} %get-tuple-element.98), channel_id=1, source_target_pairs={{0,12},{2,14},{4,0},{6,2},{8,4},{10,6},{12,8},{14,10},{1,13},{3,15... | collective-permute-start | bytes 393224 | tf_op jit(solution)/shard_map/ppermute | solution.py:181
  114.5 1.0 collective-permute-start.15
  115.6 1.2 collective-permute-start.9
  116.8 0.3 maximum_maximum_fusion
  117.1 1.5 copy.21
  118.6 1.5 copy.20
  120.1 8.7 %shard_map.18.rest_0_ = f32[64,2,256,512]{3,2,1,0:T(8,128)} custom-call(bf16[16,128,512]{2,1,0:T(8,128)(2,1)} %bitcast.167, bf16[16,128,512]{2,1,0:T(8,128)(2,1)} %bitcast.166), custom_call_target="tpu_custom_call" | custom-call | flops 1073741824 | bytes 20971520 | tf_op jit(solution)/shard_map/pallas_call | solution.py:156
  129.1 0.9 bitcast_dynamic-update-slice_fusion.19
  130.1 0.9 bitcast_dynamic-update-slice_fusion.18
  131.0 0.9 bitcast_dynamic-update-slice_fusion.17
  132.3 0.9 collective-permute-start.17
  133.2 3.7 %collective-permute-start.18 = (bf16[16,2,16,128]{3,2,1,0:T(8,128)(2,1)S(1)}, bf16[16,2,16,128]{3,2,1,0:T(8,128)(2,1)S(1)}, u32[]{:S(2)}, u32[]{:S(2)}) collective-permute-start(bf16[16,2,16,128]{3,2,1,0:T(8,128)(2,1)S(1)} %get-tuple-element.92), channel_id=1, source_target_pairs={{0,4},{2,6},{4,8},{6,10},{8,12},{10,14},{12,0},{14,2},{1,5},{3,7},... | collective-permute-start | bytes 393224 | tf_op jit(solution)/shard_map/ppermute | solution.py:181
  136.9 0.8 collective-permute-start.19
  137.7 1.3 collective-permute-start.20
  139.0 1.8 collective-permute-start.21
  141.2 3.9 %collective-permute-start.22 = (bf16[16,2,16,128]{3,2,1,0:T(8,128)(2,1)S(1)}, bf16[16,2,16,128]{3,2,1,0:T(8,128)(2,1)S(1)}, u32[]{:S(2)}, u32[]{:S(2)}) collective-permute-start(bf16[16,2,16,128]{3,2,1,0:T(8,128)(2,1)S(1)} %get-tuple-element.88), channel_id=1, source_target_pairs={{0,12},{2,14},{4,0},{6,2},{8,4},{10,6},{12,8},{14,10},{1,13},{3,15... | collective-permute-start | bytes 393224 | tf_op jit(solution)/shard_map/ppermute | solution.py:181
  145.0 0.9 collective-permute-start.23
  145.9 0.3 maximum_maximum_fusion.1
  146.2 1.5 copy.23
  147.7 1.5 copy.22
  149.2 8.6 %shard_map.19.rest_0_ = f32[64,2,256,512]{3,2,1,0:T(8,128)} custom-call(bf16[16,128,512]{2,1,0:T(8,128)(2,1)} %bitcast.164, bf16[16,128,512]{2,1,0:T(8,128)(2,1)} %bitcast.162, f32[64,2,256,512]{3,2,1,0:T(8,128)} %shard_map.18.rest_0_), custom_call_target="tpu_custom_call", output_to_operand_aliasing={{}: (2, {})} | custom-call | flops 1073741824 | bytes 20971520 | tf_op jit(solution)/shard_map/pallas_call | solution.py:156
  158.6 0.7 collective-permute-start.25
  159.3 4.7 %collective-permute-start.26 = (bf16[16,2,16,128]{3,2,1,0:T(8,128)(2,1)S(1)}, bf16[16,2,16,128]{3,2,1,0:T(8,128)(2,1)S(1)}, u32[]{:S(2)}, u32[]{:S(2)}) collective-permute-start(bf16[16,2,16,128]{3,2,1,0:T(8,128)(2,1)S(1)} %get-tuple-element.82), channel_id=1, source_target_pairs={{0,4},{2,6},{4,8},{6,10},{8,12},{10,14},{12,0},{14,2},{1,5},{3,7},... | collective-permute-start | bytes 393224 | tf_op jit(solution)/shard_map/ppermute | solution.py:181
  164.1 0.7 collective-permute-start.27
  164.8 1.6 collective-permute-start.28
  166.4 1.5 collective-permute-start.29
  168.3 3.9 %collective-permute-start.30 = (bf16[16,2,16,128]{3,2,1,0:T(8,128)(2,1)S(1)}, bf16[16,2,16,128]{3,2,1,0:T(8,128)(2,1)S(1)}, u32[]{:S(2)}, u32[]{:S(2)}) collective-permute-start(bf16[16,2,16,128]{3,2,1,0:T(8,128)(2,1)S(1)} %get-tuple-element.78), channel_id=1, source_target_pairs={{0,12},{2,14},{4,0},{6,2},{8,4},{10,6},{12,8},{14,10},{1,13},{3,15... | collective-permute-start | bytes 393224 | tf_op jit(solution)/shard_map/ppermute | solution.py:181
  172.2 0.8 collective-permute-start.31
  173.0 0.3 maximum_maximum_fusion.2
  173.3 1.5 copy.25
  174.8 1.5 copy.24
  176.3 8.6 %shard_map.20.rest_0_ = f32[64,2,256,512]{3,2,1,0:T(8,128)} custom-call(bf16[16,128,512]{2,1,0:T(8,128)(2,1)} %bitcast.165, bf16[16,128,512]{2,1,0:T(8,128)(2,1)} %bitcast.163, f32[64,2,256,512]{3,2,1,0:T(8,128)} %shard_map.19.rest_0_), custom_call_target="tpu_custom_call", output_to_operand_aliasing={{}: (2, {})} | custom-call | flops 1073741824 | bytes 20971520 | tf_op jit(solution)/shard_map/pallas_call | solution.py:156
  185.5 2.6 %collective-permute-done.32 = bf16[16,2,2,16,512]{4,3,2,1,0:T(8,128)(2,1)S(1)} collective-permute-done((bf16[16,2,2,16,512]{4,3,2,1,0:T(8,128)(2,1)S(1)}, bf16[16,2,2,16,512]{4,3,2,1,0:T(8,128)(2,1)S(1)}, u32[]{:S(2)}, u32[]{:S(2)}) %collective-permute-start.32) | collective-permute-done | bytes 1048608 | tf_op jit(solution)/shard_map/ppermute | solution.py:202
  188.2 1.5 pad_maximum_fusion.3
  189.9 1.6 maximum_maximum_fusion.3
  191.5 8.6 %shard_map.21 = f32[64,2,256,512]{3,2,1,0:T(8,128)} custom-call(bf16[16,128,512]{2,1,0:T(8,128)(2,1)} %bitcast.161, bf16[16,128,512]{2,1,0:T(8,128)(2,1)} %bitcast.160, f32[64,2,256,512]{3,2,1,0:T(8,128)} %shard_map.20.rest_0_), custom_call_target="tpu_custom_call", output_to_operand_aliasing={{}: (2, {})} | custom-call | flops 1073741824 | bytes 20971520 | tf_op jit(solution)/shard_map/pallas_call | solution.py:156
  (90 shorter events, 3.7 us)
Async XLA Ops:
  0.0 20.3 %collective-permute-start = (bf16[128,16384]{1,0:T(8,128)(2,1)}, bf16[128,16384]{1,0:T(8,128)(2,1)}, u32[]{:S(2)}, u32[]{:S(2)}) collective-permute-start(bf16[128,16384]{1,0:T(8,128)(2,1)} %own_ref.1), channel_id=1, source_target_pairs={{0,1},{1,2},{2,3},{4,5},{5,6},{6,7},{8,9},{9,10},{10,11},{12,13},{... | collective-permute-start | bytes 12582920 | tf_op jit(solution)/shard_map/ppermute | solution.py:17
  20.3 13.1 %copy-start.1 = (bf16[1024,1024]{1,0:T(8,128)(2,1)S(1)}, bf16[1024,1024]{1,0:T(8,128)(2,1)}, u32[]{:S(2)}) copy-start(bf16[1024,1024]{1,0:T(8,128)(2,1)} %convert_element_type.36) | copy-start | bytes 6291460
  45.0 39.7 %collective-permute-start.1 = (bf16[16,2,16,128]{3,2,1,0:T(8,128)(2,1)}, bf16[16,2,16,128]{3,2,1,0:T(8,128)(2,1)}, u32[]{:S(2)}, u32[]{:S(2)}) collective-permute-start(bf16[16,2,16,128]{3,2,1,0:T(8,128)(2,1)} %get-tuple-element.113), channel_id=1, source_target_pairs={{0,2},{2,0},{4,6},{6,4},{8,10},{10,8},{12,14},{14,12},{1,3},{3,1},... | collective-permute-start | bytes 393224 | tf_op jit(solution)/shard_map/ppermute | solution.py:181
  77.6 10.4 %collective-permute-start.2 = (bf16[16,2,16,128]{3,2,1,0:T(8,128)(2,1)}, bf16[16,2,16,128]{3,2,1,0:T(8,128)(2,1)S(1)}, u32[]{:S(2)}, u32[]{:S(2)}) collective-permute-start(bf16[16,2,16,128]{3,2,1,0:T(8,128)(2,1)} %get-tuple-element.112), channel_id=1, source_target_pairs={{0,4},{2,6},{4,8},{6,10},{8,12},{10,14},{12,0},{14,2},{1,5},{3,7},... | collective-permute-start | bytes 393224 | tf_op jit(solution)/shard_map/ppermute | solution.py:181
  79.1 9.6 %collective-permute-start.3 = (bf16[16,2,16,128]{3,2,1,0:T(8,128)(2,1)}, bf16[16,2,16,128]{3,2,1,0:T(8,128)(2,1)S(1)}, u32[]{:S(2)}, u32[]{:S(2)}) collective-permute-start(bf16[16,2,16,128]{3,2,1,0:T(8,128)(2,1)} %get-tuple-element.111), channel_id=1, source_target_pairs={{0,6},{2,4},{4,10},{6,8},{8,14},{10,12},{12,2},{14,0},{1,7},{3,5},... | collective-permute-start | bytes 393224 | tf_op jit(solution)/shard_map/ppermute | solution.py:181
  80.2 15.0 %collective-permute-start.4 = (bf16[16,2,16,128]{3,2,1,0:T(8,128)(2,1)}, bf16[16,2,16,128]{3,2,1,0:T(8,128)(2,1)S(1)}, u32[]{:S(2)}, u32[]{:S(2)}) collective-permute-start(bf16[16,2,16,128]{3,2,1,0:T(8,128)(2,1)} %get-tuple-element.110), channel_id=1, source_target_pairs={{0,8},{2,10},{4,12},{6,14},{8,0},{10,2},{12,4},{14,6},{1,9},{3,11}... | collective-permute-start | bytes 393224 | tf_op jit(solution)/shard_map/ppermute | solution.py:181
  81.7 16.3 %collective-permute-start.5 = (bf16[16,2,16,128]{3,2,1,0:T(8,128)(2,1)S(1)}, bf16[16,2,16,128]{3,2,1,0:T(8,128)(2,1)S(1)}, u32[]{:S(2)}, u32[]{:S(2)}) collective-permute-start(bf16[16,2,16,128]{3,2,1,0:T(8,128)(2,1)S(1)} %get-tuple-element.109), channel_id=1, source_target_pairs={{0,10},{2,8},{4,14},{6,12},{8,2},{10,0},{12,6},{14,4},{1,11},{3,9}... | collective-permute-start | bytes 393224 | tf_op jit(solution)/shard_map/ppermute | solution.py:181
  84.7 13.3 %collective-permute-start.6 = (bf16[16,2,16,128]{3,2,1,0:T(8,128)(2,1)S(1)}, bf16[16,2,16,128]{3,2,1,0:T(8,128)(2,1)S(1)}, u32[]{:S(2)}, u32[]{:S(2)}) collective-permute-start(bf16[16,2,16,128]{3,2,1,0:T(8,128)(2,1)S(1)} %get-tuple-element.108), channel_id=1, source_target_pairs={{0,12},{2,14},{4,0},{6,2},{8,4},{10,6},{12,8},{14,10},{1,13},{3,15... | collective-permute-start | bytes 393224 | tf_op jit(solution)/shard_map/ppermute | solution.py:181
  88.0 10.5 %collective-permute-start.7 = (bf16[16,2,16,128]{3,2,1,0:T(8,128)(2,1)S(1)}, bf16[16,2,16,128]{3,2,1,0:T(8,128)(2,1)S(1)}, u32[]{:S(2)}, u32[]{:S(2)}) collective-permute-start(bf16[16,2,16,128]{3,2,1,0:T(8,128)(2,1)S(1)} %get-tuple-element.107), channel_id=1, source_target_pairs={{0,14},{2,12},{4,2},{6,0},{8,6},{10,4},{12,10},{14,8},{1,15},{3,13... | collective-permute-start | bytes 393224 | tf_op jit(solution)/shard_map/ppermute | solution.py:181
  98.5 11.7 %collective-permute-start.8 = (bf16[16,2,2,16,512]{4,3,2,1,0:T(8,128)(2,1)S(1)}, bf16[16,2,2,16,512]{4,3,2,1,0:T(8,128)(2,1)S(1)}, u32[]{:S(2)}, u32[]{:S(2)}) collective-permute-start(bf16[16,2,2,16,512]{4,3,2,1,0:T(8,128)(2,1)S(1)} %bitcast_dynamic-update-slice_fusion.24), channel_id=1, source_target_pairs={{0,1},{1,0},{2,3},{3,2},{4,5},{5,4},{6,7},{7,6},{8,9},{9,8},{10,11... | collective-permute-start | bytes 3145736 | tf_op jit(solution)/shard_map/ppermute | solution.py:202
  100.8 13.7 %collective-permute-start.10 = (bf16[16,2,16,128]{3,2,1,0:T(8,128)(2,1)S(1)}, bf16[16,2,16,128]{3,2,1,0:T(8,128)(2,1)S(1)}, u32[]{:S(2)}, u32[]{:S(2)}) collective-permute-start(bf16[16,2,16,128]{3,2,1,0:T(8,128)(2,1)S(1)} %get-tuple-element.102), channel_id=1, source_target_pairs={{0,4},{2,6},{4,8},{6,10},{8,12},{10,14},{12,0},{14,2},{1,5},{3,7},... | collective-permute-start | bytes 393224 | tf_op jit(solution)/shard_map/ppermute | solution.py:181
  106.4 9.2 %collective-permute-start.11 = (bf16[16,2,16,128]{3,2,1,0:T(8,128)(2,1)S(1)}, bf16[16,2,16,128]{3,2,1,0:T(8,128)(2,1)S(1)}, u32[]{:S(2)}, u32[]{:S(2)}) collective-permute-start(bf16[16,2,16,128]{3,2,1,0:T(8,128)(2,1)S(1)} %get-tuple-element.101), channel_id=1, source_target_pairs={{0,6},{2,4},{4,10},{6,8},{8,14},{10,12},{12,2},{14,0},{1,7},{3,5},... | collective-permute-start | bytes 393224 | tf_op jit(solution)/shard_map/ppermute | solution.py:181
  107.1 21.6 %collective-permute-start.12 = (bf16[16,2,16,128]{3,2,1,0:T(8,128)(2,1)}, bf16[16,2,16,128]{3,2,1,0:T(8,128)(2,1)}, u32[]{:S(2)}, u32[]{:S(2)}) collective-permute-start(bf16[16,2,16,128]{3,2,1,0:T(8,128)(2,1)} %get-tuple-element.100), channel_id=1, source_target_pairs={{0,8},{2,10},{4,12},{6,14},{8,0},{10,2},{12,4},{14,6},{1,9},{3,11}... | collective-permute-start | bytes 393224 | tf_op jit(solution)/shard_map/ppermute | solution.py:181
  108.9 19.9 %collective-permute-start.13 = (bf16[16,2,16,128]{3,2,1,0:T(8,128)(2,1)}, bf16[16,2,16,128]{3,2,1,0:T(8,128)(2,1)}, u32[]{:S(2)}, u32[]{:S(2)}) collective-permute-start(bf16[16,2,16,128]{3,2,1,0:T(8,128)(2,1)} %get-tuple-element.99), channel_id=1, source_target_pairs={{0,10},{2,8},{4,14},{6,12},{8,2},{10,0},{12,6},{14,4},{1,11},{3,9}... | collective-permute-start | bytes 393224 | tf_op jit(solution)/shard_map/ppermute | solution.py:181
  110.2 18.5 %collective-permute-start.14 = (bf16[16,2,16,128]{3,2,1,0:T(8,128)(2,1)}, bf16[16,2,16,128]{3,2,1,0:T(8,128)(2,1)}, u32[]{:S(2)}, u32[]{:S(2)}) collective-permute-start(bf16[16,2,16,128]{3,2,1,0:T(8,128)(2,1)} %get-tuple-element.98), channel_id=1, source_target_pairs={{0,12},{2,14},{4,0},{6,2},{8,4},{10,6},{12,8},{14,10},{1,13},{3,15... | collective-permute-start | bytes 393224 | tf_op jit(solution)/shard_map/ppermute | solution.py:181
  114.5 2.3 %copy-start.2 = (bf16[16,2,16,128]{3,2,1,0:T(8,128)(2,1)}, bf16[16,2,16,128]{3,2,1,0:T(8,128)(2,1)S(1)}, u32[]{:S(2)}) copy-start(bf16[16,2,16,128]{3,2,1,0:T(8,128)(2,1)S(1)} %collective-permute-done.10) | copy-start | bytes 393220
  114.5 14.3 %collective-permute-start.15 = (bf16[16,2,16,128]{3,2,1,0:T(8,128)(2,1)S(1)}, bf16[16,2,16,128]{3,2,1,0:T(8,128)(2,1)S(1)}, u32[]{:S(2)}, u32[]{:S(2)}) collective-permute-start(bf16[16,2,16,128]{3,2,1,0:T(8,128)(2,1)S(1)} %get-tuple-element.97), channel_id=1, source_target_pairs={{0,14},{2,12},{4,2},{6,0},{8,6},{10,4},{12,10},{14,8},{1,15},{3,13... | collective-permute-start | bytes 393224 | tf_op jit(solution)/shard_map/ppermute | solution.py:181
  115.6 1.2 copy-start.4
  115.6 13.2 %collective-permute-start.9 = (bf16[16,2,16,128]{3,2,1,0:T(8,128)(2,1)S(1)}, bf16[16,2,16,128]{3,2,1,0:T(8,128)(2,1)S(1)}, u32[]{:S(2)}, u32[]{:S(2)}) collective-permute-start(bf16[16,2,16,128]{3,2,1,0:T(8,128)(2,1)S(1)} %get-tuple-element.103), channel_id=1, source_target_pairs={{0,2},{2,0},{4,6},{6,4},{8,10},{10,8},{12,14},{14,12},{1,3},{3,1},... | collective-permute-start | bytes 393224 | tf_op jit(solution)/shard_map/ppermute | solution.py:181
  120.1 8.9 %copy-start.3 = (bf16[16,2,16,128]{3,2,1,0:T(8,128)(2,1)S(1)}, bf16[16,2,16,128]{3,2,1,0:T(8,128)(2,1)}, u32[]{:S(2)}) copy-start(bf16[16,2,16,128]{3,2,1,0:T(8,128)(2,1)} %copy-done.2) | copy-start | bytes 393220
  120.1 9.0 %copy-start.5 = (bf16[16,2,16,128]{3,2,1,0:T(8,128)(2,1)S(1)}, bf16[16,2,16,128]{3,2,1,0:T(8,128)(2,1)}, u32[]{:S(2)}) copy-start(bf16[16,2,16,128]{3,2,1,0:T(8,128)(2,1)} %copy-done.4) | copy-start | bytes 393220
  128.8 3.3 %copy-start = (bf16[8,16,2,16,128]{4,3,2,1,0:T(8,128)(2,1)S(1)}, bf16[8,16,2,16,128]{4,3,2,1,0:T(8,128)(2,1)}, u32[]{:S(2)}) copy-start(bf16[8,16,2,16,128]{4,3,2,1,0:T(8,128)(2,1)} %get-tuple-element.50) | copy-start | bytes 3145732
  132.0 7.0 %collective-permute-start.16 = (bf16[16,2,2,16,512]{4,3,2,1,0:T(8,128)(2,1)S(1)}, bf16[16,2,2,16,512]{4,3,2,1,0:T(8,128)(2,1)S(1)}, u32[]{:S(2)}, u32[]{:S(2)}) collective-permute-start(bf16[16,2,2,16,512]{4,3,2,1,0:T(8,128)(2,1)S(1)} %bitcast_dynamic-update-slice_fusion.16), channel_id=1, source_target_pairs={{0,1},{1,0},{2,3},{3,2},{4,5},{5,4},{6,7},{7,6},{8,9},{9,8},{10,11... | collective-permute-start | bytes 3145736 | tf_op jit(solution)/shard_map/ppermute | solution.py:202
  132.3 8.9 %collective-permute-start.17 = (bf16[16,2,16,128]{3,2,1,0:T(8,128)(2,1)S(1)}, bf16[16,2,16,128]{3,2,1,0:T(8,128)(2,1)S(1)}, u32[]{:S(2)}, u32[]{:S(2)}) collective-permute-start(bf16[16,2,16,128]{3,2,1,0:T(8,128)(2,1)S(1)} %get-tuple-element.93), channel_id=1, source_target_pairs={{0,2},{2,0},{4,6},{6,4},{8,10},{10,8},{12,14},{14,12},{1,3},{3,1},... | collective-permute-start | bytes 393224 | tf_op jit(solution)/shard_map/ppermute | solution.py:181
  133.2 11.8 %collective-permute-start.18 = (bf16[16,2,16,128]{3,2,1,0:T(8,128)(2,1)S(1)}, bf16[16,2,16,128]{3,2,1,0:T(8,128)(2,1)S(1)}, u32[]{:S(2)}, u32[]{:S(2)}) collective-permute-start(bf16[16,2,16,128]{3,2,1,0:T(8,128)(2,1)S(1)} %get-tuple-element.92), channel_id=1, source_target_pairs={{0,4},{2,6},{4,8},{6,10},{8,12},{10,14},{12,0},{14,2},{1,5},{3,7},... | collective-permute-start | bytes 393224 | tf_op jit(solution)/shard_map/ppermute | solution.py:181
  136.9 20.9 %collective-permute-start.19 = (bf16[16,2,16,128]{3,2,1,0:T(8,128)(2,1)S(1)}, bf16[16,2,16,128]{3,2,1,0:T(8,128)(2,1)S(1)}, u32[]{:S(2)}, u32[]{:S(2)}) collective-permute-start(bf16[16,2,16,128]{3,2,1,0:T(8,128)(2,1)S(1)} %get-tuple-element.91), channel_id=1, source_target_pairs={{0,6},{2,4},{4,10},{6,8},{8,14},{10,12},{12,2},{14,0},{1,7},{3,5},... | collective-permute-start | bytes 393224 | tf_op jit(solution)/shard_map/ppermute | solution.py:181
  137.7 20.1 %collective-permute-start.20 = (bf16[16,2,16,128]{3,2,1,0:T(8,128)(2,1)S(1)}, bf16[16,2,16,128]{3,2,1,0:T(8,128)(2,1)S(1)}, u32[]{:S(2)}, u32[]{:S(2)}) collective-permute-start(bf16[16,2,16,128]{3,2,1,0:T(8,128)(2,1)S(1)} %get-tuple-element.90), channel_id=1, source_target_pairs={{0,8},{2,10},{4,12},{6,14},{8,0},{10,2},{12,4},{14,6},{1,9},{3,11}... | collective-permute-start | bytes 393224 | tf_op jit(solution)/shard_map/ppermute | solution.py:181
  139.0 18.9 %collective-permute-start.21 = (bf16[16,2,16,128]{3,2,1,0:T(8,128)(2,1)S(1)}, bf16[16,2,16,128]{3,2,1,0:T(8,128)(2,1)S(1)}, u32[]{:S(2)}, u32[]{:S(2)}) collective-permute-start(bf16[16,2,16,128]{3,2,1,0:T(8,128)(2,1)S(1)} %get-tuple-element.89), channel_id=1, source_target_pairs={{0,10},{2,8},{4,14},{6,12},{8,2},{10,0},{12,6},{14,4},{1,11},{3,9}... | collective-permute-start | bytes 393224 | tf_op jit(solution)/shard_map/ppermute | solution.py:181
  141.2 16.7 %collective-permute-start.22 = (bf16[16,2,16,128]{3,2,1,0:T(8,128)(2,1)S(1)}, bf16[16,2,16,128]{3,2,1,0:T(8,128)(2,1)S(1)}, u32[]{:S(2)}, u32[]{:S(2)}) collective-permute-start(bf16[16,2,16,128]{3,2,1,0:T(8,128)(2,1)S(1)} %get-tuple-element.88), channel_id=1, source_target_pairs={{0,12},{2,14},{4,0},{6,2},{8,4},{10,6},{12,8},{14,10},{1,13},{3,15... | collective-permute-start | bytes 393224 | tf_op jit(solution)/shard_map/ppermute | solution.py:181
  145.0 12.8 %collective-permute-start.23 = (bf16[16,2,16,128]{3,2,1,0:T(8,128)(2,1)S(1)}, bf16[16,2,16,128]{3,2,1,0:T(8,128)(2,1)S(1)}, u32[]{:S(2)}, u32[]{:S(2)}) collective-permute-start(bf16[16,2,16,128]{3,2,1,0:T(8,128)(2,1)S(1)} %get-tuple-element.87), channel_id=1, source_target_pairs={{0,14},{2,12},{4,2},{6,0},{8,6},{10,4},{12,10},{14,8},{1,15},{3,13... | collective-permute-start | bytes 393224 | tf_op jit(solution)/shard_map/ppermute | solution.py:181
  158.4 8.1 %collective-permute-start.24 = (bf16[16,2,2,16,512]{4,3,2,1,0:T(8,128)(2,1)S(1)}, bf16[16,2,2,16,512]{4,3,2,1,0:T(8,128)(2,1)S(1)}, u32[]{:S(2)}, u32[]{:S(2)}) collective-permute-start(bf16[16,2,2,16,512]{4,3,2,1,0:T(8,128)(2,1)S(1)} %bitcast_dynamic-update-slice_fusion.8), channel_id=1, source_target_pairs={{0,1},{1,0},{2,3},{3,2},{4,5},{5,4},{6,7},{7,6},{8,9},{9,8},{10,11... | collective-permute-start | bytes 3145736 | tf_op jit(solution)/shard_map/ppermute | solution.py:202
  158.6 9.7 %collective-permute-start.25 = (bf16[16,2,16,128]{3,2,1,0:T(8,128)(2,1)S(1)}, bf16[16,2,16,128]{3,2,1,0:T(8,128)(2,1)S(1)}, u32[]{:S(2)}, u32[]{:S(2)}) collective-permute-start(bf16[16,2,16,128]{3,2,1,0:T(8,128)(2,1)S(1)} %get-tuple-element.83), channel_id=1, source_target_pairs={{0,2},{2,0},{4,6},{6,4},{8,10},{10,8},{12,14},{14,12},{1,3},{3,1},... | collective-permute-start | bytes 393224 | tf_op jit(solution)/shard_map/ppermute | solution.py:181
  159.3 12.8 %collective-permute-start.26 = (bf16[16,2,16,128]{3,2,1,0:T(8,128)(2,1)S(1)}, bf16[16,2,16,128]{3,2,1,0:T(8,128)(2,1)S(1)}, u32[]{:S(2)}, u32[]{:S(2)}) collective-permute-start(bf16[16,2,16,128]{3,2,1,0:T(8,128)(2,1)S(1)} %get-tuple-element.82), channel_id=1, source_target_pairs={{0,4},{2,6},{4,8},{6,10},{8,12},{10,14},{12,0},{14,2},{1,5},{3,7},... | collective-permute-start | bytes 393224 | tf_op jit(solution)/shard_map/ppermute | solution.py:181
  164.1 20.9 %collective-permute-start.27 = (bf16[16,2,16,128]{3,2,1,0:T(8,128)(2,1)S(1)}, bf16[16,2,16,128]{3,2,1,0:T(8,128)(2,1)S(1)}, u32[]{:S(2)}, u32[]{:S(2)}) collective-permute-start(bf16[16,2,16,128]{3,2,1,0:T(8,128)(2,1)S(1)} %get-tuple-element.81), channel_id=1, source_target_pairs={{0,6},{2,4},{4,10},{6,8},{8,14},{10,12},{12,2},{14,0},{1,7},{3,5},... | collective-permute-start | bytes 393224 | tf_op jit(solution)/shard_map/ppermute | solution.py:181
  164.8 20.1 %collective-permute-start.28 = (bf16[16,2,16,128]{3,2,1,0:T(8,128)(2,1)S(1)}, bf16[16,2,16,128]{3,2,1,0:T(8,128)(2,1)S(1)}, u32[]{:S(2)}, u32[]{:S(2)}) collective-permute-start(bf16[16,2,16,128]{3,2,1,0:T(8,128)(2,1)S(1)} %get-tuple-element.80), channel_id=1, source_target_pairs={{0,8},{2,10},{4,12},{6,14},{8,0},{10,2},{12,4},{14,6},{1,9},{3,11}... | collective-permute-start | bytes 393224 | tf_op jit(solution)/shard_map/ppermute | solution.py:181
  166.4 18.5 %collective-permute-start.29 = (bf16[16,2,16,128]{3,2,1,0:T(8,128)(2,1)S(1)}, bf16[16,2,16,128]{3,2,1,0:T(8,128)(2,1)S(1)}, u32[]{:S(2)}, u32[]{:S(2)}) collective-permute-start(bf16[16,2,16,128]{3,2,1,0:T(8,128)(2,1)S(1)} %get-tuple-element.79), channel_id=1, source_target_pairs={{0,10},{2,8},{4,14},{6,12},{8,2},{10,0},{12,6},{14,4},{1,11},{3,9}... | collective-permute-start | bytes 393224 | tf_op jit(solution)/shard_map/ppermute | solution.py:181
  168.3 16.6 %collective-permute-start.30 = (bf16[16,2,16,128]{3,2,1,0:T(8,128)(2,1)S(1)}, bf16[16,2,16,128]{3,2,1,0:T(8,128)(2,1)S(1)}, u32[]{:S(2)}, u32[]{:S(2)}) collective-permute-start(bf16[16,2,16,128]{3,2,1,0:T(8,128)(2,1)S(1)} %get-tuple-element.78), channel_id=1, source_target_pairs={{0,12},{2,14},{4,0},{6,2},{8,4},{10,6},{12,8},{14,10},{1,13},{3,15... | collective-permute-start | bytes 393224 | tf_op jit(solution)/shard_map/ppermute | solution.py:181
  172.2 12.8 %collective-permute-start.31 = (bf16[16,2,16,128]{3,2,1,0:T(8,128)(2,1)S(1)}, bf16[16,2,16,128]{3,2,1,0:T(8,128)(2,1)S(1)}, u32[]{:S(2)}, u32[]{:S(2)}) collective-permute-start(bf16[16,2,16,128]{3,2,1,0:T(8,128)(2,1)S(1)} %get-tuple-element.77), channel_id=1, source_target_pairs={{0,14},{2,12},{4,2},{6,0},{8,6},{10,4},{12,10},{14,8},{1,15},{3,13... | collective-permute-start | bytes 393224 | tf_op jit(solution)/shard_map/ppermute | solution.py:181
  185.5 2.7 %collective-permute-start.32 = (bf16[16,2,2,16,512]{4,3,2,1,0:T(8,128)(2,1)S(1)}, bf16[16,2,2,16,512]{4,3,2,1,0:T(8,128)(2,1)S(1)}, u32[]{:S(2)}, u32[]{:S(2)}) collective-permute-start(bf16[16,2,2,16,512]{4,3,2,1,0:T(8,128)(2,1)S(1)} %bitcast_dynamic-update-slice_fusion), channel_id=1, source_target_pairs={{0,1},{1,0},{2,3},{3,2},{4,5},{5,4},{6,7},{7,6},{8,9},{9,8},{10,11... | collective-permute-start | bytes 3145736 | tf_op jit(solution)/shard_map/ppermute | solution.py:202

commit v15 on v14

--- a/solution.py
+++ b/solution.py
@@ -124,44 +124,46 @@
     return correlate(lhs, rhs, out, (chunks - 1) * per_chunk, own_channels)
 
 
-def correlate_kernel(scale, lhs_ref, rhs_ref, *rest):
+def correlate_kernel(scale, lhs_ref, lhs2_ref, rhs_ref, rhs2_ref, *rest):
     out_ref = rest[-1]
     rows = out_ref.shape[2]
     for k in range(lhs_ref.shape[0]):
         acc = lax.dot_general(
             lhs_ref[k], rhs_ref[k], (((0,), (0,)), ((), ())), preferred_element_type=jnp.float32
-        ) * scale
+        ) + lax.dot_general(
+            lhs2_ref[k], rhs2_ref[k], (((0,), (0,)), ((), ())), preferred_element_type=jnp.float32
+        )
+        acc = acc * scale
         out_ref[k, 0] = acc[:rows]
         out_ref[k, 1] = acc[rows:]
 
 
 def correlate(lhs, rhs, prev, first_channel, own_channels):
-    count, depth, two_rows = lhs.shape
-    cols = rhs.shape[2]
+    count, depth, two_rows = lhs[0].shape
+    cols = rhs[0].shape[2]
     rows = two_rows // 2
     step = 4 if count % 4 == 0 else (2 if count % 2 == 0 else 1)
     offset = first_channel // step
-    in_specs = [
-        pl.BlockSpec((step, depth, two_rows), lambda c: (c, 0, 0)),
-        pl.BlockSpec((step, depth, cols), lambda c: (c, 0, 0)),
-    ]
-    args = [lhs, rhs]
+    in_specs = [pl.BlockSpec((step, depth, two_rows), lambda c: (c, 0, 0))] * 2 + [
+        pl.BlockSpec((step, depth, cols), lambda c: (c, 0, 0))
+    ] * 2
+    args = [lhs[0], lhs[1], rhs[0], rhs[1]]
     aliases = {}
     if prev is not None:
         in_specs.append(pl.BlockSpec(memory_space=pl.ANY))
         args.append(prev)
-        aliases = {2: 0}
-    flops = 2 * count * two_rows * depth * cols
+        aliases = {4: 0}
+    flops = 4 * count * two_rows * depth * cols
     out_bytes = count * two_rows * cols * 4
     return pl.pallas_call(
-        functools.partial(correlate_kernel, 1.0 / (depth // 2)),
+        functools.partial(correlate_kernel, 1.0 / depth),
         grid=(count // step,),
         in_specs=in_specs,
         out_specs=pl.BlockSpec((step, 2, rows, cols), lambda c: (c + offset, 0, 0, 0)),
         out_shape=jax.ShapeDtypeStruct((own_channels, 2, rows, cols), jnp.float32),
         input_output_aliases=aliases,
         cost_estimate=pl.CostEstimate(
-            flops=flops, bytes_accessed=out_bytes + lhs.size * 2 + rhs.size * 2, transcendentals=0
+            flops=flops, bytes_accessed=out_bytes + 2 * (lhs[0].size + rhs[0].size) * 2, transcendentals=0
         ),
     )(*args)
 
@@ -198,19 +200,19 @@
 
 def finish_chunk(half, pol_size, cols):
     own_channels, _, tm_size, spectra_here, _ = half.shape
-    if pol_size == 2:
-        partner = lax.ppermute(half, "pol", [(0, 1), (1, 0)])
-        both = jnp.stack([half, partner], axis=1)
-    else:
-        both = lax.all_gather(half, "pol", axis=1, tiled=False)
-    depth = pol_size * 2 * tm_size * spectra_here
-    left_all = both.reshape(own_channels, depth, cols)
+    if pol_size != 2:
+        raise ValueError("pol size")
+    partner = lax.ppermute(half, "pol", [(0, 1), (1, 0)])
+    depth = 2 * tm_size * spectra_here
     rows_here = cols // pol_size
     row_start = lax.axis_index("pol") * rows_here
-    own_rows = lax.dynamic_slice_in_dim(both, row_start, rows_here, 5)
-    swapped = jnp.stack([own_rows[:, :, 1], -own_rows[:, :, 0]], axis=2)
-    lhs = jnp.concatenate([own_rows, swapped], axis=5).reshape(own_channels, depth, 2 * rows_here)
-    return lhs, left_all
+    lhs, rhs = [], []
+    for part in (half, partner):
+        own_rows = lax.dynamic_slice_in_dim(part, row_start, rows_here, 4)
+        swapped = jnp.stack([own_rows[:, 1], -own_rows[:, 0]], axis=1)
+        lhs.append(jnp.concatenate([own_rows, swapped], axis=4).reshape(own_channels, depth, 2 * rows_here))
+        rhs.append(part.reshape(own_channels, depth, cols))
+    return lhs, rhs
 
 
 def solution(mesh):

time: 203 us -> 201 us (level)
  local copies, waits for them, and re-layouts: 25.9 us -> 16.4 us
  other arithmetic: 16.1 us -> 20.6 us
  Pallas kernels: 47.7 us -> 52.1 us
    concatenate x4 -> x8, other arithmetic: 2.41 us -> 9.11 us  [finish_chunk(): jnp.concatenate([own_rows, swapped], axis=4)]
    concatenate x3 -> x0, local copies, waits for them, and re-layouts: 4.57 us -> none  [finish_chunk(): jnp.concatenate([own_rows, swapped], axis=5)]
    another operation x7 -> x4, local copies, waits for them, and re-layouts: 5.02 us -> 0.47 us  [the longest x3 4.55 us: finish_chunk(): both = jnp.stack([half, partner], axis=1)]
    pallas_call x4, Pallas kernels: 34.5 us -> 39 us  [correlate(): pl.pallas_call(functools.partial(correlate_kernel, 1.0 / depth), grid=(co...]
    another operation x9 -> x1, other arithmetic: 11 us -> 8.49 us
  transfers between devices with their start and end apart: 33 -> 33, of which waited for: 5 -> 4; matrix products, arithmetic and copies ran while one was open for 15% -> 14% of each run, Pallas kernels for 13% -> 15%
where the time goes in v15:
time: 201 us; the launch traced here: 198 us
  starting transfers between devices  89.7 us (45%)
  Pallas kernels  52.1 us (26%)
  other arithmetic  20.6 us (10%)
  local copies, waits for them, and re-layouts  16.4 us (8%)
  waiting for transfers between devices  10.9 us (5%)
  matrix products  6.95 us (3%)
    ppermute x28, starting transfers between devices, send_chunk(): block = lax.ppermute(block, ('inp', 'tm'), route)  85.1 us
    pallas_call x4, Pallas kernels, correlate(): pl.pallas_call(functools.partial(correlate_kernel, 1.0 / depth), grid=(co...  39 us
    pallas_call x1, Pallas kernels, polyphase_filter(): pl.pallas_call(filter_kernel, grid=(inputs_here // rows,), in_specs=[pl.B...  13.1 us
    ppermute x28, waiting for transfers between devices, send_chunk(): block = lax.ppermute(block, ('inp', 'tm'), route)  9.6 us
    concatenate x8, other arithmetic, finish_chunk(): jnp.concatenate([own_rows, swapped], axis=4)  9.11 us
    another operation x1, other arithmetic  8.49 us
    dot_general x1, matrix products, per_device(): lax.dot_general(dft_table_t(frame_len), filtered.reshape(spectra_here * i...  6.95 us
    ppermute x1, starting transfers between devices, shifted(): return lax.ppermute(block, axis, route)  4.34 us
  transfers between devices with their start and end apart: 33, of which 4 were waited for; matrix products, arithmetic and copies ran while one was open for 14% of the time, Pallas kernels for 15%

profile of v15, /device:TPU:0, one launch (start us, length us, event | category | flops | bytes accessed | tf_op | source)
XLA Modules:
  0.0 198.3 jit_solution(219167970803072107)
XLA Ops:
  0.0 4.3 %collective-permute-start = (bf16[128,16384]{1,0:T(8,128)(2,1)}, bf16[128,16384]{1,0:T(8,128)(2,1)}, u32[]{:S(2)}, u32[]{:S(2)}) collective-permute-start(bf16[128,16384]{1,0:T(8,128)(2,1)} %own_ref.1), channel_id=1, source_target_pairs={{0,1},{1,2},{2,3},{4,5},{5,6},{6,7},{8,9},{9,10},{10,11},{12,13},{... | collective-permute-start | bytes 12582920 | tf_op jit(solution)/shard_map/ppermute | solution.py:17
  4.3 8.5 %negate_convert_fusion = (bf16[512,1,1024]{2,0,1:T(8,128)(2,1)S(1)}, bf16[512,1,1024]{2,0,1:T(8,128)(2,1)S(1)}) fusion(), kind=kLoop, calls=%fused_computation.8 | loop fusion | flops 8912896 | bytes 2097152 | tf_op jit(solution)/shard_map/convert.1
  12.8 0.2 pad_maximum_fusion
  13.0 2.2 %copy.5 = bf16[512,2,1024]{2,1,0:T(2,128)(2,1)S(1)} copy(bf16[512,2,1024]{2,0,1:T(8,128)(2,1)S(1)} %pad_maximum_fusion) | data formatting | bytes 4194304 | tf_op jit(solution)/shard_map/stack | solution.py:35
  15.2 2.2 %convert_element_type.36 = bf16[1024,1024]{1,0:T(8,128)(2,1)} reshape(bf16[512,2,1024]{2,1,0:T(2,128)(2,1)S(1)} %copy.5) | data formatting | bytes 4194304 | tf_op jit(solution)/shard_map/convert_element_type | solution.py:36
  17.4 1.1 fusion.10
  19.2 1.1 fusion.7.taps_ref
  20.3 13.1 %shard_map.17 = bf16[16,128,1024]{2,1,0:T(8,128)(2,1)} custom-call(f32[16,1024]{1,0:T(8,128)} %fusion.7.taps_ref, bf16[128,16384]{1,0:T(8,128)(2,1)} %own_ref.1, bf16[128,16384]{1,0:T(8,128)(2,1)} %collective-permute-done.history_ref), custom_call_target="tpu_custom_call" | custom-call | flops 67108864 | bytes 12582912 | tf_op jit(solution)/shard_map/pallas_call | solution.py:71
  33.5 7.0 %convert_bitcast_fusion = bf16[128,8,16,128]{3,1,2,0:T(8,128)(2,1)S(1)} fusion(bf16[1024,1024]{1,0:T(8,128)(2,1)S(1)} %copy-done.9, bf16[2048,1024]{1,0:T(8,128)(2,1)} %bitcast.166), kind=kOutput, calls=%fused_computation | convolution fusion | flops 4297064448 | bytes 10485760 | tf_op jit(solution)/shard_map/dot_general | solution.py:93
  40.4 1.4 copy.6
  41.9 2.2 %fusion.11 = (bf16[8,16,2,16,128]{4,3,2,1,0:T(8,128)(2,1)S(1)}, bf16[8,16,2,16,128]{4,3,2,1,0:T(8,128)(2,1)}, bf16[8,16,2,16,128]{4,3,2,1,0:T(8,128)(2,1)}, bf16[8,16,2,16,128]{4,3,2,1,0:T(8,128)(2,1)S(1)}) fusion(bf16[8,64,2,16,128]{4,3,2,1,0:T(8,128)(2,1)S(1)} %bitcast.149), kind=kLoop, calls=%fused_computation.115 | loop fusion | bytes 8388608 | tf_op jit(solution)/shard_map/slice | solution.py:111
  44.1 0.9 dynamic-slice_bitcast_fusion.24
  45.0 32.6 %collective-permute-start.1 = (bf16[16,2,16,128]{3,2,1,0:T(8,128)(2,1)}, bf16[16,2,16,128]{3,2,1,0:T(8,128)(2,1)}, u32[]{:S(2)}, u32[]{:S(2)}) collective-permute-start(bf16[16,2,16,128]{3,2,1,0:T(8,128)(2,1)} %get-tuple-element.121), channel_id=1, source_target_pairs={{0,2},{2,0},{4,6},{6,4},{8,10},{10,8},{12,14},{14,12},{1,3},{3,1},... | collective-permute-start | bytes 393224 | tf_op jit(solution)/shard_map/ppermute | solution.py:183
  77.6 1.6 collective-permute-start.2
  79.1 1.0 collective-permute-start.3
  80.2 1.6 collective-permute-start.4
  81.7 2.8 %collective-permute-start.5 = (bf16[16,2,16,128]{3,2,1,0:T(8,128)(2,1)S(1)}, bf16[16,2,16,128]{3,2,1,0:T(8,128)(2,1)S(1)}, u32[]{:S(2)}, u32[]{:S(2)}) collective-permute-start(bf16[16,2,16,128]{3,2,1,0:T(8,128)(2,1)S(1)} %get-tuple-element.117), channel_id=1, source_target_pairs={{0,10},{2,8},{4,14},{6,12},{8,2},{10,0},{12,6},{14,4},{1,11},{3,9}... | collective-permute-start | bytes 393224 | tf_op jit(solution)/shard_map/ppermute | solution.py:183
  84.7 2.3 %collective-permute-start.6 = (bf16[16,2,16,128]{3,2,1,0:T(8,128)(2,1)S(1)}, bf16[16,2,16,128]{3,2,1,0:T(8,128)(2,1)S(1)}, u32[]{:S(2)}, u32[]{:S(2)}) collective-permute-start(bf16[16,2,16,128]{3,2,1,0:T(8,128)(2,1)S(1)} %get-tuple-element.116), channel_id=1, source_target_pairs={{0,12},{2,14},{4,0},{6,2},{8,4},{10,6},{12,8},{14,10},{1,13},{3,15... | collective-permute-start | bytes 393224 | tf_op jit(solution)/shard_map/ppermute | solution.py:183
  87.0 0.9 bitcast_dynamic-update-slice_fusion.30
  88.0 0.8 collective-permute-start.7
  88.8 6.3 %collective-permute-done.4 = bf16[16,2,16,128]{3,2,1,0:T(8,128)(2,1)S(1)} collective-permute-done((bf16[16,2,16,128]{3,2,1,0:T(8,128)(2,1)}, bf16[16,2,16,128]{3,2,1,0:T(8,128)(2,1)S(1)}, u32[]{:S(2)}, u32[]{:S(2)}) %collective-permute-start.4) | collective-permute-done | bytes 131104 | tf_op jit(solution)/shard_map/ppermute | solution.py:183
  95.1 2.9 %collective-permute-done.5 = bf16[16,2,16,128]{3,2,1,0:T(8,128)(2,1)S(1)} collective-permute-done((bf16[16,2,16,128]{3,2,1,0:T(8,128)(2,1)S(1)}, bf16[16,2,16,128]{3,2,1,0:T(8,128)(2,1)S(1)}, u32[]{:S(2)}, u32[]{:S(2)}) %collective-permute-start.5) | collective-permute-done | bytes 131104 | tf_op jit(solution)/shard_map/ppermute | solution.py:183
  98.1 0.4 collective-permute-done.7
  98.6 2.4 %dynamic-slice_bitcast_fusion.16 = (bf16[16,2,16,128]{3,2,1,0:T(8,128)(2,1)S(1)}, bf16[16,2,16,128]{3,2,1,0:T(8,128)(2,1)}, bf16[16,2,16,128]{3,2,1,0:T(8,128)(2...) fusion(bf16[8,16,2,16,128]{4,3,2,1,0:T(8,128)(2,1)} %get-tuple-, ...), kind=kLoop, calls=%fused_computation.77 | loop fusion | bytes 2097184 | tf_op jit(solution)/shard_map/jit(dynamic_index_in_dim)/squeeze | solution.py:177
  101.0 5.6 %collective-permute-start.10 = (bf16[16,2,16,128]{3,2,1,0:T(8,128)(2,1)S(1)}, bf16[16,2,16,128]{3,2,1,0:T(8,128)(2,1)S(1)}, u32[]{:S(2)}, u32[]{:S(2)}) collective-permute-start(bf16[16,2,16,128]{3,2,1,0:T(8,128)(2,1)S(1)} %get-tuple-element.108), channel_id=1, source_target_pairs={{0,4},{2,6},{4,8},{6,10},{8,12},{10,14},{12,0},{14,2},{1,5},{3,7},... | collective-permute-start | bytes 393224 | tf_op jit(solution)/shard_map/ppermute | solution.py:183
  106.7 0.7 collective-permute-start.11
  107.4 1.8 collective-permute-start.12
  109.2 1.3 collective-permute-start.13
  110.6 1.1 maximum_maximum_fusion
  111.8 3.8 %collective-permute-start.14 = (bf16[16,2,16,128]{3,2,1,0:T(8,128)(2,1)}, bf16[16,2,16,128]{3,2,1,0:T(8,128)(2,1)S(1)}, u32[]{:S(2)}, u32[]{:S(2)}) collective-permute-start(bf16[16,2,16,128]{3,2,1,0:T(8,128)(2,1)} %get-tuple-element.104), channel_id=1, source_target_pairs={{0,12},{2,14},{4,0},{6,2},{8,4},{10,6},{12,8},{14,10},{1,13},{3,15... | collective-permute-start | bytes 393224 | tf_op jit(solution)/shard_map/ppermute | solution.py:183
  115.7 1.0 collective-permute-start.15
  116.7 0.7 collective-permute-start.9
  117.4 1.1 maximum_maximum_fusion.1
  118.6 9.8 %shard_map.18.rest_0_ = f32[64,2,256,512]{3,2,1,0:T(8,128)} custom-call(bf16[16,64,512]{2,1,0:T(8,128)(2,1)} %bitcast.159, bf16[16,64,512]{2,1,0:T(8,128)(2,1)} %bitcast.165, bf16[16,64,512]{2,1,0:T(8,128)(2,1)} %bitcast.151, bf16[16,64,512]{2,1,0:T(8,128)(2,1)} %bitcast.154), custom_call_target="tpu_custom_call" | custom-call | flops 1073741824 | bytes 20971520 | tf_op jit(solution)/shard_map/pallas_call | solution.py:158
  128.5 0.1 broadcast.108.clone.1
  128.8 0.9 bitcast_dynamic-update-slice_fusion.19
  129.7 0.9 bitcast_dynamic-update-slice_fusion.18
  130.9 0.2 dynamic-slice_bitcast_fusion.8
  131.0 1.4 collective-permute-start.17
  132.4 3.6 %collective-permute-start.18 = (bf16[16,2,16,128]{3,2,1,0:T(8,128)(2,1)S(1)}, bf16[16,2,16,128]{3,2,1,0:T(8,128)(2,1)S(1)}, u32[]{:S(2)}, u32[]{:S(2)}) collective-permute-start(bf16[16,2,16,128]{3,2,1,0:T(8,128)(2,1)S(1)} %get-tuple-element.96), channel_id=1, source_target_pairs={{0,4},{2,6},{4,8},{6,10},{8,12},{10,14},{12,0},{14,2},{1,5},{3,7},... | collective-permute-start | bytes 393224 | tf_op jit(solution)/shard_map/ppermute | solution.py:183
  136.0 0.8 collective-permute-start.19
  136.8 1.2 collective-permute-start.20
  138.2 1.2 maximum_maximum_fusion.2
  139.4 1.8 collective-permute-start.21
  141.3 3.9 %collective-permute-start.22 = (bf16[16,2,16,128]{3,2,1,0:T(8,128)(2,1)S(1)}, bf16[16,2,16,128]{3,2,1,0:T(8,128)(2,1)S(1)}, u32[]{:S(2)}, u32[]{:S(2)}) collective-permute-start(bf16[16,2,16,128]{3,2,1,0:T(8,128)(2,1)S(1)} %get-tuple-element.92), channel_id=1, source_target_pairs={{0,12},{2,14},{4,0},{6,2},{8,4},{10,6},{12,8},{14,10},{1,13},{3,15... | collective-permute-start | bytes 393224 | tf_op jit(solution)/shard_map/ppermute | solution.py:183
  145.2 0.9 collective-permute-start.23
  146.1 1.1 maximum_maximum_fusion.3
  147.2 9.7 %shard_map.19.rest_0_ = f32[64,2,256,512]{3,2,1,0:T(8,128)} custom-call(bf16[16,64,512]{2,1,0:T(8,128)(2,1)} %bitcast.157, bf16[16,64,512]{2,1,0:T(8,128)(2,1)} %bitcast.162, bf16[16,64,512]{2,1,0:T(8,128)(2,1)} %bitcast.152, bf16[16,64,512]{2,1,0:T(8,128)(2,1)} %bitcast.156, f32[64,2,256,512]{3,2,1,0:T(8,128)} %shard_map.18.rest_0_), custom_call_target="tpu_custom_call", output_to_operand_aliasing={{}: (4, {})} | custom-call | flops 1073741824 | bytes 20971520 | tf_op jit(solution)/shard_map/pallas_call | solution.py:158
  157.0 0.1 broadcast.108.clone
  157.6 0.1 dynamic-slice_bitcast_fusion
  157.7 0.7 collective-permute-start.25
  158.4 4.7 %collective-permute-start.26 = (bf16[16,2,16,128]{3,2,1,0:T(8,128)(2,1)S(1)}, bf16[16,2,16,128]{3,2,1,0:T(8,128)(2,1)S(1)}, u32[]{:S(2)}, u32[]{:S(2)}) collective-permute-start(bf16[16,2,16,128]{3,2,1,0:T(8,128)(2,1)S(1)} %get-tuple-element.84), channel_id=1, source_target_pairs={{0,4},{2,6},{4,8},{6,10},{8,12},{10,14},{12,0},{14,2},{1,5},{3,7},... | collective-permute-start | bytes 393224 | tf_op jit(solution)/shard_map/ppermute | solution.py:183
  163.1 0.7 collective-permute-start.27
  163.9 1.7 collective-permute-start.28
  165.7 1.2 maximum_maximum_fusion.4
  166.9 1.4 collective-permute-start.29
  168.5 3.9 %collective-permute-start.30 = (bf16[16,2,16,128]{3,2,1,0:T(8,128)(2,1)S(1)}, bf16[16,2,16,128]{3,2,1,0:T(8,128)(2,1)S(1)}, u32[]{:S(2)}, u32[]{:S(2)}) collective-permute-start(bf16[16,2,16,128]{3,2,1,0:T(8,128)(2,1)S(1)} %get-tuple-element.80), channel_id=1, source_target_pairs={{0,12},{2,14},{4,0},{6,2},{8,4},{10,6},{12,8},{14,10},{1,13},{3,15... | collective-permute-start | bytes 393224 | tf_op jit(solution)/shard_map/ppermute | solution.py:183
  172.3 0.8 collective-permute-start.31
  173.1 1.1 maximum_maximum_fusion.5
  174.3 9.7 %shard_map.20.rest_0_ = f32[64,2,256,512]{3,2,1,0:T(8,128)} custom-call(bf16[16,64,512]{2,1,0:T(8,128)(2,1)} %bitcast.158, bf16[16,64,512]{2,1,0:T(8,128)(2,1)} %bitcast.163, bf16[16,64,512]{2,1,0:T(8,128)(2,1)} %bitcast.153, bf16[16,64,512]{2,1,0:T(8,128)(2,1)} %bitcast.155, f32[64,2,256,512]{3,2,1,0:T(8,128)} %shard_map.19.rest_0_), custom_call_target="tpu_custom_call", output_to_operand_aliasing={{}: (4, {})} | custom-call | flops 1073741824 | bytes 20971520 | tf_op jit(solution)/shard_map/pallas_call | solution.py:158
  184.8 1.2 maximum_maximum_fusion.6
  185.9 1.3 collective-permute-done.32
  187.4 1.2 maximum_maximum_fusion.7
  188.6 9.7 %shard_map.21 = f32[64,2,256,512]{3,2,1,0:T(8,128)} custom-call(bf16[16,64,512]{2,1,0:T(8,128)(2,1)} %bitcast.161, bf16[16,64,512]{2,1,0:T(8,128)(2,1)} %bitcast.164, bf16[16,64,512]{2,1,0:T(8,128)(2,1)} %bitcast.150, bf16[16,64,512]{2,1,0:T(8,128)(2,1)} %bitcast.160, f32[64,2,256,512]{3,2,1,0:T(8,128)} %shard_map.20.rest_0_), custom_call_target="tpu_custom_call", output_to_operand_aliasing={{}: (4, {})} | custom-call | flops 1073741824 | bytes 20971520 | tf_op jit(solution)/shard_map/pallas_call | solution.py:158
  (108 shorter events, 2.8 us)
Async XLA Ops:
  0.0 20.3 %collective-permute-start = (bf16[128,16384]{1,0:T(8,128)(2,1)}, bf16[128,16384]{1,0:T(8,128)(2,1)}, u32[]{:S(2)}, u32[]{:S(2)}) collective-permute-start(bf16[128,16384]{1,0:T(8,128)(2,1)} %own_ref.1), channel_id=1, source_target_pairs={{0,1},{1,2},{2,3},{4,5},{5,6},{6,7},{8,9},{9,10},{10,11},{12,13},{... | collective-permute-start | bytes 12582920 | tf_op jit(solution)/shard_map/ppermute | solution.py:17
  20.3 13.1 %copy-start.9 = (bf16[1024,1024]{1,0:T(8,128)(2,1)S(1)}, bf16[1024,1024]{1,0:T(8,128)(2,1)}, u32[]{:S(2)}) copy-start(bf16[1024,1024]{1,0:T(8,128)(2,1)} %convert_element_type.36) | copy-start | bytes 6291460
  45.0 39.7 %collective-permute-start.1 = (bf16[16,2,16,128]{3,2,1,0:T(8,128)(2,1)}, bf16[16,2,16,128]{3,2,1,0:T(8,128)(2,1)}, u32[]{:S(2)}, u32[]{:S(2)}) collective-permute-start(bf16[16,2,16,128]{3,2,1,0:T(8,128)(2,1)} %get-tuple-element.121), channel_id=1, source_target_pairs={{0,2},{2,0},{4,6},{6,4},{8,10},{10,8},{12,14},{14,12},{1,3},{3,1},... | collective-permute-start | bytes 393224 | tf_op jit(solution)/shard_map/ppermute | solution.py:183
  77.6 10.4 %collective-permute-start.2 = (bf16[16,2,16,128]{3,2,1,0:T(8,128)(2,1)}, bf16[16,2,16,128]{3,2,1,0:T(8,128)(2,1)S(1)}, u32[]{:S(2)}, u32[]{:S(2)}) collective-permute-start(bf16[16,2,16,128]{3,2,1,0:T(8,128)(2,1)} %get-tuple-element.120), channel_id=1, source_target_pairs={{0,4},{2,6},{4,8},{6,10},{8,12},{10,14},{12,0},{14,2},{1,5},{3,7},... | collective-permute-start | bytes 393224 | tf_op jit(solution)/shard_map/ppermute | solution.py:183
  79.1 9.6 %collective-permute-start.3 = (bf16[16,2,16,128]{3,2,1,0:T(8,128)(2,1)}, bf16[16,2,16,128]{3,2,1,0:T(8,128)(2,1)S(1)}, u32[]{:S(2)}, u32[]{:S(2)}) collective-permute-start(bf16[16,2,16,128]{3,2,1,0:T(8,128)(2,1)} %get-tuple-element.119), channel_id=1, source_target_pairs={{0,6},{2,4},{4,10},{6,8},{8,14},{10,12},{12,2},{14,0},{1,7},{3,5},... | collective-permute-start | bytes 393224 | tf_op jit(solution)/shard_map/ppermute | solution.py:183
  80.2 15.0 %collective-permute-start.4 = (bf16[16,2,16,128]{3,2,1,0:T(8,128)(2,1)}, bf16[16,2,16,128]{3,2,1,0:T(8,128)(2,1)S(1)}, u32[]{:S(2)}, u32[]{:S(2)}) collective-permute-start(bf16[16,2,16,128]{3,2,1,0:T(8,128)(2,1)} %get-tuple-element.118), channel_id=1, source_target_pairs={{0,8},{2,10},{4,12},{6,14},{8,0},{10,2},{12,4},{14,6},{1,9},{3,11}... | collective-permute-start | bytes 393224 | tf_op jit(solution)/shard_map/ppermute | solution.py:183
  81.7 16.3 %collective-permute-start.5 = (bf16[16,2,16,128]{3,2,1,0:T(8,128)(2,1)S(1)}, bf16[16,2,16,128]{3,2,1,0:T(8,128)(2,1)S(1)}, u32[]{:S(2)}, u32[]{:S(2)}) collective-permute-start(bf16[16,2,16,128]{3,2,1,0:T(8,128)(2,1)S(1)} %get-tuple-element.117), channel_id=1, source_target_pairs={{0,10},{2,8},{4,14},{6,12},{8,2},{10,0},{12,6},{14,4},{1,11},{3,9}... | collective-permute-start | bytes 393224 | tf_op jit(solution)/shard_map/ppermute | solution.py:183
  84.7 13.3 %collective-permute-start.6 = (bf16[16,2,16,128]{3,2,1,0:T(8,128)(2,1)S(1)}, bf16[16,2,16,128]{3,2,1,0:T(8,128)(2,1)S(1)}, u32[]{:S(2)}, u32[]{:S(2)}) collective-permute-start(bf16[16,2,16,128]{3,2,1,0:T(8,128)(2,1)S(1)} %get-tuple-element.116), channel_id=1, source_target_pairs={{0,12},{2,14},{4,0},{6,2},{8,4},{10,6},{12,8},{14,10},{1,13},{3,15... | collective-permute-start | bytes 393224 | tf_op jit(solution)/shard_map/ppermute | solution.py:183
  88.0 10.5 %collective-permute-start.7 = (bf16[16,2,16,128]{3,2,1,0:T(8,128)(2,1)S(1)}, bf16[16,2,16,128]{3,2,1,0:T(8,128)(2,1)S(1)}, u32[]{:S(2)}, u32[]{:S(2)}) collective-permute-start(bf16[16,2,16,128]{3,2,1,0:T(8,128)(2,1)S(1)} %get-tuple-element.115), channel_id=1, source_target_pairs={{0,14},{2,12},{4,2},{6,0},{8,6},{10,4},{12,10},{14,8},{1,15},{3,13... | collective-permute-start | bytes 393224 | tf_op jit(solution)/shard_map/ppermute | solution.py:183
  98.5 12.1 %copy-start.1 = (bf16[16,2,2,16,512]{4,3,2,1,0:T(8,128)(2,1)}, bf16[16,2,2,16,512]{4,3,2,1,0:T(8,128)(2,1)S(1)}, u32[]{:S(2)}) copy-start(bf16[16,2,2,16,512]{4,3,2,1,0:T(8,128)(2,1)S(1)} %bitcast_dynamic-update-slice_fusion.24) | copy-start | bytes 3145732
  98.5 13.2 %collective-permute-start.8 = (bf16[16,2,2,16,512]{4,3,2,1,0:T(8,128)(2,1)S(1)}, bf16[16,2,2,16,512]{4,3,2,1,0:T(8,128)(2,1)S(1)}, u32[]{:S(2)}, u32[]{:S(2)}) collective-permute-start(bf16[16,2,2,16,512]{4,3,2,1,0:T(8,128)(2,1)S(1)} %bitcast_dynamic-update-slice_fusion.24), channel_id=1, source_target_pairs={{0,1},{1,0},{2,3},{3,2},{4,5},{5,4},{6,7},{7,6},{8,9},{9,8},{10,11... | collective-permute-start | bytes 3145736 | tf_op jit(solution)/shard_map/ppermute | solution.py:205
  101.0 14.7 %collective-permute-start.10 = (bf16[16,2,16,128]{3,2,1,0:T(8,128)(2,1)S(1)}, bf16[16,2,16,128]{3,2,1,0:T(8,128)(2,1)S(1)}, u32[]{:S(2)}, u32[]{:S(2)}) collective-permute-start(bf16[16,2,16,128]{3,2,1,0:T(8,128)(2,1)S(1)} %get-tuple-element.108), channel_id=1, source_target_pairs={{0,4},{2,6},{4,8},{6,10},{8,12},{10,14},{12,0},{14,2},{1,5},{3,7},... | collective-permute-start | bytes 393224 | tf_op jit(solution)/shard_map/ppermute | solution.py:183
  106.7 10.1 %collective-permute-start.11 = (bf16[16,2,16,128]{3,2,1,0:T(8,128)(2,1)S(1)}, bf16[16,2,16,128]{3,2,1,0:T(8,128)(2,1)S(1)}, u32[]{:S(2)}, u32[]{:S(2)}) collective-permute-start(bf16[16,2,16,128]{3,2,1,0:T(8,128)(2,1)S(1)} %get-tuple-element.107), channel_id=1, source_target_pairs={{0,6},{2,4},{4,10},{6,8},{8,14},{10,12},{12,2},{14,0},{1,7},{3,5},... | collective-permute-start | bytes 393224 | tf_op jit(solution)/shard_map/ppermute | solution.py:183
  107.4 21.0 %collective-permute-start.12 = (bf16[16,2,16,128]{3,2,1,0:T(8,128)(2,1)}, bf16[16,2,16,128]{3,2,1,0:T(8,128)(2,1)}, u32[]{:S(2)}, u32[]{:S(2)}) collective-permute-start(bf16[16,2,16,128]{3,2,1,0:T(8,128)(2,1)} %get-tuple-element.106), channel_id=1, source_target_pairs={{0,8},{2,10},{4,12},{6,14},{8,0},{10,2},{12,4},{14,6},{1,9},{3,11}... | collective-permute-start | bytes 393224 | tf_op jit(solution)/shard_map/ppermute | solution.py:183
  109.2 19.3 %collective-permute-start.13 = (bf16[16,2,16,128]{3,2,1,0:T(8,128)(2,1)}, bf16[16,2,16,128]{3,2,1,0:T(8,128)(2,1)}, u32[]{:S(2)}, u32[]{:S(2)}) collective-permute-start(bf16[16,2,16,128]{3,2,1,0:T(8,128)(2,1)} %get-tuple-element.105), channel_id=1, source_target_pairs={{0,10},{2,8},{4,14},{6,12},{8,2},{10,0},{12,6},{14,4},{1,11},{3,9}... | collective-permute-start | bytes 393224 | tf_op jit(solution)/shard_map/ppermute | solution.py:183
  111.7 6.8 %copy-start.4 = (bf16[16,2,2,16,512]{4,3,2,1,0:T(8,128)(2,1)}, bf16[16,2,2,16,512]{4,3,2,1,0:T(8,128)(2,1)S(1)}, u32[]{:S(2)}) copy-start(bf16[16,2,2,16,512]{4,3,2,1,0:T(8,128)(2,1)S(1)} %collective-permute-done.8) | copy-start | bytes 3145732
  111.8 16.7 %collective-permute-start.14 = (bf16[16,2,16,128]{3,2,1,0:T(8,128)(2,1)}, bf16[16,2,16,128]{3,2,1,0:T(8,128)(2,1)S(1)}, u32[]{:S(2)}, u32[]{:S(2)}) collective-permute-start(bf16[16,2,16,128]{3,2,1,0:T(8,128)(2,1)} %get-tuple-element.104), channel_id=1, source_target_pairs={{0,12},{2,14},{4,0},{6,2},{8,4},{10,6},{12,8},{14,10},{1,13},{3,15... | collective-permute-start | bytes 393224 | tf_op jit(solution)/shard_map/ppermute | solution.py:183
  115.7 2.9 %copy-start.10 = (bf16[16,2,16,128]{3,2,1,0:T(8,128)(2,1)}, bf16[16,2,16,128]{3,2,1,0:T(8,128)(2,1)S(1)}, u32[]{:S(2)}) copy-start(bf16[16,2,16,128]{3,2,1,0:T(8,128)(2,1)S(1)} %collective-permute-done.10) | copy-start | bytes 393220
  115.7 12.7 %collective-permute-start.15 = (bf16[16,2,16,128]{3,2,1,0:T(8,128)(2,1)S(1)}, bf16[16,2,16,128]{3,2,1,0:T(8,128)(2,1)S(1)}, u32[]{:S(2)}, u32[]{:S(2)}) collective-permute-start(bf16[16,2,16,128]{3,2,1,0:T(8,128)(2,1)S(1)} %get-tuple-element.103), channel_id=1, source_target_pairs={{0,14},{2,12},{4,2},{6,0},{8,6},{10,4},{12,10},{14,8},{1,15},{3,13... | collective-permute-start | bytes 393224 | tf_op jit(solution)/shard_map/ppermute | solution.py:183
  116.7 1.9 copy-start.12
  116.7 11.7 %collective-permute-start.9 = (bf16[16,2,16,128]{3,2,1,0:T(8,128)(2,1)S(1)}, bf16[16,2,16,128]{3,2,1,0:T(8,128)(2,1)S(1)}, u32[]{:S(2)}, u32[]{:S(2)}) collective-permute-start(bf16[16,2,16,128]{3,2,1,0:T(8,128)(2,1)S(1)} %get-tuple-element.109), channel_id=1, source_target_pairs={{0,2},{2,0},{4,6},{6,4},{8,10},{10,8},{12,14},{14,12},{1,3},{3,1},... | collective-permute-start | bytes 393224 | tf_op jit(solution)/shard_map/ppermute | solution.py:183
  118.6 10.1 %copy-start.11 = (bf16[16,2,16,128]{3,2,1,0:T(8,128)(2,1)S(1)}, bf16[16,2,16,128]{3,2,1,0:T(8,128)(2,1)}, u32[]{:S(2)}) copy-start(bf16[16,2,16,128]{3,2,1,0:T(8,128)(2,1)} %copy-done.10) | copy-start | bytes 393220
  118.6 10.2 %copy-start.13 = (bf16[16,2,16,128]{3,2,1,0:T(8,128)(2,1)S(1)}, bf16[16,2,16,128]{3,2,1,0:T(8,128)(2,1)}, u32[]{:S(2)}) copy-start(bf16[16,2,16,128]{3,2,1,0:T(8,128)(2,1)} %copy-done.12) | copy-start | bytes 393220
  128.4 2.5 %copy-start.8 = (bf16[8,16,2,16,128]{4,3,2,1,0:T(8,128)(2,1)S(1)}, bf16[8,16,2,16,128]{4,3,2,1,0:T(8,128)(2,1)}, u32[]{:S(2)}) copy-start(bf16[8,16,2,16,128]{4,3,2,1,0:T(8,128)(2,1)} %get-tuple-element.50) | copy-start | bytes 3145732
  130.8 7.4 %copy-start.2 = (bf16[16,2,2,16,512]{4,3,2,1,0:T(8,128)(2,1)}, bf16[16,2,2,16,512]{4,3,2,1,0:T(8,128)(2,1)S(1)}, u32[]{:S(2)}) copy-start(bf16[16,2,2,16,512]{4,3,2,1,0:T(8,128)(2,1)S(1)} %bitcast_dynamic-update-slice_fusion.16) | copy-start | bytes 3145732
  130.8 8.6 %collective-permute-start.16 = (bf16[16,2,2,16,512]{4,3,2,1,0:T(8,128)(2,1)S(1)}, bf16[16,2,2,16,512]{4,3,2,1,0:T(8,128)(2,1)S(1)}, u32[]{:S(2)}, u32[]{:S(2)}) collective-permute-start(bf16[16,2,2,16,512]{4,3,2,1,0:T(8,128)(2,1)S(1)} %bitcast_dynamic-update-slice_fusion.16), channel_id=1, source_target_pairs={{0,1},{1,0},{2,3},{3,2},{4,5},{5,4},{6,7},{7,6},{8,9},{9,8},{10,11... | collective-permute-start | bytes 3145736 | tf_op jit(solution)/shard_map/ppermute | solution.py:205
  131.0 10.3 %collective-permute-start.17 = (bf16[16,2,16,128]{3,2,1,0:T(8,128)(2,1)S(1)}, bf16[16,2,16,128]{3,2,1,0:T(8,128)(2,1)S(1)}, u32[]{:S(2)}, u32[]{:S(2)}) collective-permute-start(bf16[16,2,16,128]{3,2,1,0:T(8,128)(2,1)S(1)} %get-tuple-element.97), channel_id=1, source_target_pairs={{0,2},{2,0},{4,6},{6,4},{8,10},{10,8},{12,14},{14,12},{1,3},{3,1},... | collective-permute-start | bytes 393224 | tf_op jit(solution)/shard_map/ppermute | solution.py:183
  132.4 12.8 %collective-permute-start.18 = (bf16[16,2,16,128]{3,2,1,0:T(8,128)(2,1)S(1)}, bf16[16,2,16,128]{3,2,1,0:T(8,128)(2,1)S(1)}, u32[]{:S(2)}, u32[]{:S(2)}) collective-permute-start(bf16[16,2,16,128]{3,2,1,0:T(8,128)(2,1)S(1)} %get-tuple-element.96), channel_id=1, source_target_pairs={{0,4},{2,6},{4,8},{6,10},{8,12},{10,14},{12,0},{14,2},{1,5},{3,7},... | collective-permute-start | bytes 393224 | tf_op jit(solution)/shard_map/ppermute | solution.py:183
  136.0 20.9 %collective-permute-start.19 = (bf16[16,2,16,128]{3,2,1,0:T(8,128)(2,1)S(1)}, bf16[16,2,16,128]{3,2,1,0:T(8,128)(2,1)S(1)}, u32[]{:S(2)}, u32[]{:S(2)}) collective-permute-start(bf16[16,2,16,128]{3,2,1,0:T(8,128)(2,1)S(1)} %get-tuple-element.95), channel_id=1, source_target_pairs={{0,6},{2,4},{4,10},{6,8},{8,14},{10,12},{12,2},{14,0},{1,7},{3,5},... | collective-permute-start | bytes 393224 | tf_op jit(solution)/shard_map/ppermute | solution.py:183
  136.8 20.1 %collective-permute-start.20 = (bf16[16,2,16,128]{3,2,1,0:T(8,128)(2,1)S(1)}, bf16[16,2,16,128]{3,2,1,0:T(8,128)(2,1)S(1)}, u32[]{:S(2)}, u32[]{:S(2)}) collective-permute-start(bf16[16,2,16,128]{3,2,1,0:T(8,128)(2,1)S(1)} %get-tuple-element.94), channel_id=1, source_target_pairs={{0,8},{2,10},{4,12},{6,14},{8,0},{10,2},{12,4},{14,6},{1,9},{3,11}... | collective-permute-start | bytes 393224 | tf_op jit(solution)/shard_map/ppermute | solution.py:183
  139.4 7.8 %copy-start.6 = (bf16[16,2,2,16,512]{4,3,2,1,0:T(8,128)(2,1)}, bf16[16,2,2,16,512]{4,3,2,1,0:T(8,128)(2,1)S(1)}, u32[]{:S(2)}) copy-start(bf16[16,2,2,16,512]{4,3,2,1,0:T(8,128)(2,1)S(1)} %collective-permute-done.16) | copy-start | bytes 3145732
  139.4 17.6 %collective-permute-start.21 = (bf16[16,2,16,128]{3,2,1,0:T(8,128)(2,1)S(1)}, bf16[16,2,16,128]{3,2,1,0:T(8,128)(2,1)S(1)}, u32[]{:S(2)}, u32[]{:S(2)}) collective-permute-start(bf16[16,2,16,128]{3,2,1,0:T(8,128)(2,1)S(1)} %get-tuple-element.93), channel_id=1, source_target_pairs={{0,10},{2,8},{4,14},{6,12},{8,2},{10,0},{12,6},{14,4},{1,11},{3,9}... | collective-permute-start | bytes 393224 | tf_op jit(solution)/shard_map/ppermute | solution.py:183
  141.3 15.6 %collective-permute-start.22 = (bf16[16,2,16,128]{3,2,1,0:T(8,128)(2,1)S(1)}, bf16[16,2,16,128]{3,2,1,0:T(8,128)(2,1)S(1)}, u32[]{:S(2)}, u32[]{:S(2)}) collective-permute-start(bf16[16,2,16,128]{3,2,1,0:T(8,128)(2,1)S(1)} %get-tuple-element.92), channel_id=1, source_target_pairs={{0,12},{2,14},{4,0},{6,2},{8,4},{10,6},{12,8},{14,10},{1,13},{3,15... | collective-permute-start | bytes 393224 | tf_op jit(solution)/shard_map/ppermute | solution.py:183
  145.2 11.8 %collective-permute-start.23 = (bf16[16,2,16,128]{3,2,1,0:T(8,128)(2,1)S(1)}, bf16[16,2,16,128]{3,2,1,0:T(8,128)(2,1)S(1)}, u32[]{:S(2)}, u32[]{:S(2)}) collective-permute-start(bf16[16,2,16,128]{3,2,1,0:T(8,128)(2,1)S(1)} %get-tuple-element.91), channel_id=1, source_target_pairs={{0,14},{2,12},{4,2},{6,0},{8,6},{10,4},{12,10},{14,8},{1,15},{3,13... | collective-permute-start | bytes 393224 | tf_op jit(solution)/shard_map/ppermute | solution.py:183
  157.5 8.2 %copy-start.3 = (bf16[16,2,2,16,512]{4,3,2,1,0:T(8,128)(2,1)}, bf16[16,2,2,16,512]{4,3,2,1,0:T(8,128)(2,1)S(1)}, u32[]{:S(2)}) copy-start(bf16[16,2,2,16,512]{4,3,2,1,0:T(8,128)(2,1)S(1)} %bitcast_dynamic-update-slice_fusion.8) | copy-start | bytes 3145732
  157.5 9.4 %collective-permute-start.24 = (bf16[16,2,2,16,512]{4,3,2,1,0:T(8,128)(2,1)S(1)}, bf16[16,2,2,16,512]{4,3,2,1,0:T(8,128)(2,1)S(1)}, u32[]{:S(2)}, u32[]{:S(2)}) collective-permute-start(bf16[16,2,2,16,512]{4,3,2,1,0:T(8,128)(2,1)S(1)} %bitcast_dynamic-update-slice_fusion.8), channel_id=1, source_target_pairs={{0,1},{1,0},{2,3},{3,2},{4,5},{5,4},{6,7},{7,6},{8,9},{9,8},{10,11... | collective-permute-start | bytes 3145736 | tf_op jit(solution)/shard_map/ppermute | solution.py:205
  157.7 10.7 %collective-permute-start.25 = (bf16[16,2,16,128]{3,2,1,0:T(8,128)(2,1)S(1)}, bf16[16,2,16,128]{3,2,1,0:T(8,128)(2,1)S(1)}, u32[]{:S(2)}, u32[]{:S(2)}) collective-permute-start(bf16[16,2,16,128]{3,2,1,0:T(8,128)(2,1)S(1)} %get-tuple-element.85), channel_id=1, source_target_pairs={{0,2},{2,0},{4,6},{6,4},{8,10},{10,8},{12,14},{14,12},{1,3},{3,1},... | collective-permute-start | bytes 393224 | tf_op jit(solution)/shard_map/ppermute | solution.py:183
  158.4 13.9 %collective-permute-start.26 = (bf16[16,2,16,128]{3,2,1,0:T(8,128)(2,1)S(1)}, bf16[16,2,16,128]{3,2,1,0:T(8,128)(2,1)S(1)}, u32[]{:S(2)}, u32[]{:S(2)}) collective-permute-start(bf16[16,2,16,128]{3,2,1,0:T(8,128)(2,1)S(1)} %get-tuple-element.84), channel_id=1, source_target_pairs={{0,4},{2,6},{4,8},{6,10},{8,12},{10,14},{12,0},{14,2},{1,5},{3,7},... | collective-permute-start | bytes 393224 | tf_op jit(solution)/shard_map/ppermute | solution.py:183
  163.1 20.8 %collective-permute-start.27 = (bf16[16,2,16,128]{3,2,1,0:T(8,128)(2,1)S(1)}, bf16[16,2,16,128]{3,2,1,0:T(8,128)(2,1)S(1)}, u32[]{:S(2)}, u32[]{:S(2)}) collective-permute-start(bf16[16,2,16,128]{3,2,1,0:T(8,128)(2,1)S(1)} %get-tuple-element.83), channel_id=1, source_target_pairs={{0,6},{2,4},{4,10},{6,8},{8,14},{10,12},{12,2},{14,0},{1,7},{3,5},... | collective-permute-start | bytes 393224 | tf_op jit(solution)/shard_map/ppermute | solution.py:183
  163.9 20.1 %collective-permute-start.28 = (bf16[16,2,16,128]{3,2,1,0:T(8,128)(2,1)S(1)}, bf16[16,2,16,128]{3,2,1,0:T(8,128)(2,1)S(1)}, u32[]{:S(2)}, u32[]{:S(2)}) collective-permute-start(bf16[16,2,16,128]{3,2,1,0:T(8,128)(2,1)S(1)} %get-tuple-element.82), channel_id=1, source_target_pairs={{0,8},{2,10},{4,12},{6,14},{8,0},{10,2},{12,4},{14,6},{1,9},{3,11}... | collective-permute-start | bytes 393224 | tf_op jit(solution)/shard_map/ppermute | solution.py:183
  166.9 7.4 %copy-start.5 = (bf16[16,2,2,16,512]{4,3,2,1,0:T(8,128)(2,1)}, bf16[16,2,2,16,512]{4,3,2,1,0:T(8,128)(2,1)S(1)}, u32[]{:S(2)}) copy-start(bf16[16,2,2,16,512]{4,3,2,1,0:T(8,128)(2,1)S(1)} %collective-permute-done.24) | copy-start | bytes 3145732
  166.9 17.1 %collective-permute-start.29 = (bf16[16,2,16,128]{3,2,1,0:T(8,128)(2,1)S(1)}, bf16[16,2,16,128]{3,2,1,0:T(8,128)(2,1)S(1)}, u32[]{:S(2)}, u32[]{:S(2)}) collective-permute-start(bf16[16,2,16,128]{3,2,1,0:T(8,128)(2,1)S(1)} %get-tuple-element.81), channel_id=1, source_target_pairs={{0,10},{2,8},{4,14},{6,12},{8,2},{10,0},{12,6},{14,4},{1,11},{3,9}... | collective-permute-start | bytes 393224 | tf_op jit(solution)/shard_map/ppermute | solution.py:183
  168.5 15.5 %collective-permute-start.30 = (bf16[16,2,16,128]{3,2,1,0:T(8,128)(2,1)S(1)}, bf16[16,2,16,128]{3,2,1,0:T(8,128)(2,1)S(1)}, u32[]{:S(2)}, u32[]{:S(2)}) collective-permute-start(bf16[16,2,16,128]{3,2,1,0:T(8,128)(2,1)S(1)} %get-tuple-element.80), channel_id=1, source_target_pairs={{0,12},{2,14},{4,0},{6,2},{8,4},{10,6},{12,8},{14,10},{1,13},{3,15... | collective-permute-start | bytes 393224 | tf_op jit(solution)/shard_map/ppermute | solution.py:183
  172.3 11.7 %collective-permute-start.31 = (bf16[16,2,16,128]{3,2,1,0:T(8,128)(2,1)S(1)}, bf16[16,2,16,128]{3,2,1,0:T(8,128)(2,1)S(1)}, u32[]{:S(2)}, u32[]{:S(2)}) collective-permute-start(bf16[16,2,16,128]{3,2,1,0:T(8,128)(2,1)S(1)} %get-tuple-element.79), channel_id=1, source_target_pairs={{0,14},{2,12},{4,2},{6,0},{8,6},{10,4},{12,10},{14,8},{1,15},{3,13... | collective-permute-start | bytes 393224 | tf_op jit(solution)/shard_map/ppermute | solution.py:183
  184.5 1.4 copy-start
  184.5 2.7 %collective-permute-start.32 = (bf16[16,2,2,16,512]{4,3,2,1,0:T(8,128)(2,1)S(1)}, bf16[16,2,2,16,512]{4,3,2,1,0:T(8,128)(2,1)S(1)}, u32[]{:S(2)}, u32[]{:S(2)}) collective-permute-start(bf16[16,2,2,16,512]{4,3,2,1,0:T(8,128)(2,1)S(1)} %bitcast_dynamic-update-slice_fusion), channel_id=1, source_target_pairs={{0,1},{1,0},{2,3},{3,2},{4,5},{5,4},{6,7},{7,6},{8,9},{9,8},{10,11... | collective-permute-start | bytes 3145736 | tf_op jit(solution)/shard_map/ppermute | solution.py:205
  187.3 1.3 copy-start.7

commit v16 on v15

--- a/solution.py
+++ b/solution.py
@@ -142,7 +142,7 @@
     count, depth, two_rows = lhs[0].shape
     cols = rhs[0].shape[2]
     rows = two_rows // 2
-    step = 4 if count % 4 == 0 else (2 if count % 2 == 0 else 1)
+    step = 8 if count % 8 == 0 else (4 if count % 4 == 0 else (2 if count % 2 == 0 else 1))
     offset = first_channel // step
     in_specs = [pl.BlockSpec((step, depth, two_rows), lambda c: (c, 0, 0))] * 2 + [
         pl.BlockSpec((step, depth, cols), lambda c: (c, 0, 0))

time: 201 us -> 201 us (level)
  no operation moved by 1% of the time
where the time goes in v16:
time: 201 us; the launch traced here: 199 us
  starting transfers between devices  89 us (44%)
  Pallas kernels  53.5 us (27%)
  other arithmetic  20.6 us (10%)
  local copies, waits for them, and re-layouts  16.4 us (8%)
  waiting for transfers between devices  10.9 us (5%)
  matrix products  6.95 us (3%)
    ppermute x28, starting transfers between devices, send_chunk(): block = lax.ppermute(block, ('inp', 'tm'), route)  84.4 us
    pallas_call x4, Pallas kernels, correlate(): pl.pallas_call(functools.partial(correlate_kernel, 1.0 / depth), grid=(co...  40.4 us
    pallas_call x1, Pallas kernels, polyphase_filter(): pl.pallas_call(filter_kernel, grid=(inputs_here // rows,), in_specs=[pl.B...  13.1 us
    ppermute x28, waiting for transfers between devices, send_chunk(): block = lax.ppermute(block, ('inp', 'tm'), route)  9.6 us
    concatenate x8, other arithmetic, finish_chunk(): jnp.concatenate([own_rows, swapped], axis=4)  9.11 us
    another operation x1, other arithmetic  8.49 us
    dot_general x1, matrix products, per_device(): lax.dot_general(dft_table_t(frame_len), filtered.reshape(spectra_here * i...  6.95 us
    ppermute x1, starting transfers between devices, shifted(): return lax.ppermute(block, axis, route)  4.34 us
  transfers between devices with their start and end apart: 33, of which 4 were waited for; matrix products, arithmetic and copies ran while one was open for 14% of the time, Pallas kernels for 15%

profile of v16, /device:TPU:0, one launch (start us, length us, event | category | flops | bytes accessed | tf_op | source)
XLA Modules:
  0.0 199.0 jit_solution(10994274797917963895)
XLA Ops:
  0.0 4.3 %collective-permute-start = (bf16[128,16384]{1,0:T(8,128)(2,1)}, bf16[128,16384]{1,0:T(8,128)(2,1)}, u32[]{:S(2)}, u32[]{:S(2)}) collective-permute-start(bf16[128,16384]{1,0:T(8,128)(2,1)} %own_ref.1), channel_id=1, source_target_pairs={{0,1},{1,2},{2,3},{4,5},{5,6},{6,7},{8,9},{9,10},{10,11},{12,13},{... | collective-permute-start | bytes 12582920 | tf_op jit(solution)/shard_map/ppermute | solution.py:17
  4.3 8.5 %negate_convert_fusion = (bf16[512,1,1024]{2,0,1:T(8,128)(2,1)S(1)}, bf16[512,1,1024]{2,0,1:T(8,128)(2,1)S(1)}) fusion(), kind=kLoop, calls=%fused_computation.8 | loop fusion | flops 8912896 | bytes 2097152 | tf_op jit(solution)/shard_map/convert.1
  12.8 0.2 pad_maximum_fusion
  13.0 2.2 %copy.5 = bf16[512,2,1024]{2,1,0:T(2,128)(2,1)S(1)} copy(bf16[512,2,1024]{2,0,1:T(8,128)(2,1)S(1)} %pad_maximum_fusion) | data formatting | bytes 4194304 | tf_op jit(solution)/shard_map/stack | solution.py:35
  15.2 2.2 %convert_element_type.36 = bf16[1024,1024]{1,0:T(8,128)(2,1)} reshape(bf16[512,2,1024]{2,1,0:T(2,128)(2,1)S(1)} %copy.5) | data formatting | bytes 4194304 | tf_op jit(solution)/shard_map/convert_element_type | solution.py:36
  17.4 1.1 fusion.10
  19.2 1.1 fusion.7.taps_ref
  20.3 13.1 %shard_map.17 = bf16[16,128,1024]{2,1,0:T(8,128)(2,1)} custom-call(f32[16,1024]{1,0:T(8,128)} %fusion.7.taps_ref, bf16[128,16384]{1,0:T(8,128)(2,1)} %own_ref.1, bf16[128,16384]{1,0:T(8,128)(2,1)} %collective-permute-done.history_ref), custom_call_target="tpu_custom_call" | custom-call | flops 67108864 | bytes 12582912 | tf_op jit(solution)/shard_map/pallas_call | solution.py:71
  33.5 7.0 %convert_bitcast_fusion = bf16[128,8,16,128]{3,1,2,0:T(8,128)(2,1)S(1)} fusion(bf16[1024,1024]{1,0:T(8,128)(2,1)S(1)} %copy-done.9, bf16[2048,1024]{1,0:T(8,128)(2,1)} %bitcast.166), kind=kOutput, calls=%fused_computation | convolution fusion | flops 4297064448 | bytes 10485760 | tf_op jit(solution)/shard_map/dot_general | solution.py:93
  40.4 1.4 copy.6
  41.9 2.2 %fusion.11 = (bf16[8,16,2,16,128]{4,3,2,1,0:T(8,128)(2,1)S(1)}, bf16[8,16,2,16,128]{4,3,2,1,0:T(8,128)(2,1)}, bf16[8,16,2,16,128]{4,3,2,1,0:T(8,128)(2,1)}, bf16[8,16,2,16,128]{4,3,2,1,0:T(8,128)(2,1)S(1)}) fusion(bf16[8,64,2,16,128]{4,3,2,1,0:T(8,128)(2,1)S(1)} %bitcast.149), kind=kLoop, calls=%fused_computation.115 | loop fusion | bytes 8388608 | tf_op jit(solution)/shard_map/slice | solution.py:111
  44.1 0.9 dynamic-slice_bitcast_fusion.24
  45.0 32.6 %collective-permute-start.1 = (bf16[16,2,16,128]{3,2,1,0:T(8,128)(2,1)}, bf16[16,2,16,128]{3,2,1,0:T(8,128)(2,1)}, u32[]{:S(2)}, u32[]{:S(2)}) collective-permute-start(bf16[16,2,16,128]{3,2,1,0:T(8,128)(2,1)} %get-tuple-element.121), channel_id=1, source_target_pairs={{0,2},{2,0},{4,6},{6,4},{8,10},{10,8},{12,14},{14,12},{1,3},{3,1},... | collective-permute-start | bytes 393224 | tf_op jit(solution)/shard_map/ppermute | solution.py:183
  77.6 1.6 collective-permute-start.2
  79.1 1.0 collective-permute-start.3
  80.2 1.6 collective-permute-start.4
  81.7 2.8 %collective-permute-start.5 = (bf16[16,2,16,128]{3,2,1,0:T(8,128)(2,1)S(1)}, bf16[16,2,16,128]{3,2,1,0:T(8,128)(2,1)S(1)}, u32[]{:S(2)}, u32[]{:S(2)}) collective-permute-start(bf16[16,2,16,128]{3,2,1,0:T(8,128)(2,1)S(1)} %get-tuple-element.117), channel_id=1, source_target_pairs={{0,10},{2,8},{4,14},{6,12},{8,2},{10,0},{12,6},{14,4},{1,11},{3,9}... | collective-permute-start | bytes 393224 | tf_op jit(solution)/shard_map/ppermute | solution.py:183
  84.7 2.3 %collective-permute-start.6 = (bf16[16,2,16,128]{3,2,1,0:T(8,128)(2,1)S(1)}, bf16[16,2,16,128]{3,2,1,0:T(8,128)(2,1)S(1)}, u32[]{:S(2)}, u32[]{:S(2)}) collective-permute-start(bf16[16,2,16,128]{3,2,1,0:T(8,128)(2,1)S(1)} %get-tuple-element.116), channel_id=1, source_target_pairs={{0,12},{2,14},{4,0},{6,2},{8,4},{10,6},{12,8},{14,10},{1,13},{3,15... | collective-permute-start | bytes 393224 | tf_op jit(solution)/shard_map/ppermute | solution.py:183
  87.0 0.9 bitcast_dynamic-update-slice_fusion.30
  88.0 0.8 collective-permute-start.7
  88.8 6.3 %collective-permute-done.4 = bf16[16,2,16,128]{3,2,1,0:T(8,128)(2,1)S(1)} collective-permute-done((bf16[16,2,16,128]{3,2,1,0:T(8,128)(2,1)}, bf16[16,2,16,128]{3,2,1,0:T(8,128)(2,1)S(1)}, u32[]{:S(2)}, u32[]{:S(2)}) %collective-permute-start.4) | collective-permute-done | bytes 131104 | tf_op jit(solution)/shard_map/ppermute | solution.py:183
  95.1 2.9 %collective-permute-done.5 = bf16[16,2,16,128]{3,2,1,0:T(8,128)(2,1)S(1)} collective-permute-done((bf16[16,2,16,128]{3,2,1,0:T(8,128)(2,1)S(1)}, bf16[16,2,16,128]{3,2,1,0:T(8,128)(2,1)S(1)}, u32[]{:S(2)}, u32[]{:S(2)}) %collective-permute-start.5) | collective-permute-done | bytes 131104 | tf_op jit(solution)/shard_map/ppermute | solution.py:183
  98.1 0.4 collective-permute-done.7
  98.6 2.4 %dynamic-slice_bitcast_fusion.16 = (bf16[16,2,16,128]{3,2,1,0:T(8,128)(2,1)S(1)}, bf16[16,2,16,128]{3,2,1,0:T(8,128)(2,1)}, bf16[16,2,16,128]{3,2,1,0:T(8,128)(2...) fusion(bf16[8,16,2,16,128]{4,3,2,1,0:T(8,128)(2,1)} %get-tuple-, ...), kind=kLoop, calls=%fused_computation.77 | loop fusion | bytes 2097184 | tf_op jit(solution)/shard_map/jit(dynamic_index_in_dim)/squeeze | solution.py:177
  101.0 5.6 %collective-permute-start.10 = (bf16[16,2,16,128]{3,2,1,0:T(8,128)(2,1)S(1)}, bf16[16,2,16,128]{3,2,1,0:T(8,128)(2,1)S(1)}, u32[]{:S(2)}, u32[]{:S(2)}) collective-permute-start(bf16[16,2,16,128]{3,2,1,0:T(8,128)(2,1)S(1)} %get-tuple-element.108), channel_id=1, source_target_pairs={{0,4},{2,6},{4,8},{6,10},{8,12},{10,14},{12,0},{14,2},{1,5},{3,7},... | collective-permute-start | bytes 393224 | tf_op jit(solution)/shard_map/ppermute | solution.py:183
  106.7 0.7 collective-permute-start.11
  107.4 1.8 collective-permute-start.12
  109.2 1.3 collective-permute-start.13
  110.6 1.1 maximum_maximum_fusion
  111.8 3.8 %collective-permute-start.14 = (bf16[16,2,16,128]{3,2,1,0:T(8,128)(2,1)}, bf16[16,2,16,128]{3,2,1,0:T(8,128)(2,1)S(1)}, u32[]{:S(2)}, u32[]{:S(2)}) collective-permute-start(bf16[16,2,16,128]{3,2,1,0:T(8,128)(2,1)} %get-tuple-element.104), channel_id=1, source_target_pairs={{0,12},{2,14},{4,0},{6,2},{8,4},{10,6},{12,8},{14,10},{1,13},{3,15... | collective-permute-start | bytes 393224 | tf_op jit(solution)/shard_map/ppermute | solution.py:183
  115.7 1.0 collective-permute-start.15
  116.7 0.7 collective-permute-start.9
  117.4 1.1 maximum_maximum_fusion.1
  118.6 10.2 %shard_map.18.rest_0_ = f32[64,2,256,512]{3,2,1,0:T(8,128)} custom-call(bf16[16,64,512]{2,1,0:T(8,128)(2,1)} %bitcast.159, bf16[16,64,512]{2,1,0:T(8,128)(2,1)} %bitcast.165, bf16[16,64,512]{2,1,0:T(8,128)(2,1)} %bitcast.151, bf16[16,64,512]{2,1,0:T(8,128)(2,1)} %bitcast.154), custom_call_target="tpu_custom_call" | custom-call | flops 1073741824 | bytes 20971520 | tf_op jit(solution)/shard_map/pallas_call | solution.py:158
  128.8 0.1 broadcast.108.clone.1
  129.1 0.9 bitcast_dynamic-update-slice_fusion.19
  130.1 0.9 bitcast_dynamic-update-slice_fusion.18
  131.2 0.2 dynamic-slice_bitcast_fusion.8
  131.4 1.4 collective-permute-start.17
  132.7 3.3 %collective-permute-start.18 = (bf16[16,2,16,128]{3,2,1,0:T(8,128)(2,1)S(1)}, bf16[16,2,16,128]{3,2,1,0:T(8,128)(2,1)S(1)}, u32[]{:S(2)}, u32[]{:S(2)}) collective-permute-start(bf16[16,2,16,128]{3,2,1,0:T(8,128)(2,1)S(1)} %get-tuple-element.96), channel_id=1, source_target_pairs={{0,4},{2,6},{4,8},{6,10},{8,12},{10,14},{12,0},{14,2},{1,5},{3,7},... | collective-permute-start | bytes 393224 | tf_op jit(solution)/shard_map/ppermute | solution.py:183
  136.0 0.8 collective-permute-start.19
  136.8 1.2 collective-permute-start.20
  138.2 1.2 maximum_maximum_fusion.2
  139.4 1.8 collective-permute-start.21
  141.3 3.9 %collective-permute-start.22 = (bf16[16,2,16,128]{3,2,1,0:T(8,128)(2,1)S(1)}, bf16[16,2,16,128]{3,2,1,0:T(8,128)(2,1)S(1)}, u32[]{:S(2)}, u32[]{:S(2)}) collective-permute-start(bf16[16,2,16,128]{3,2,1,0:T(8,128)(2,1)S(1)} %get-tuple-element.92), channel_id=1, source_target_pairs={{0,12},{2,14},{4,0},{6,2},{8,4},{10,6},{12,8},{14,10},{1,13},{3,15... | collective-permute-start | bytes 393224 | tf_op jit(solution)/shard_map/ppermute | solution.py:183
  145.2 0.9 collective-permute-start.23
  146.1 1.1 maximum_maximum_fusion.3
  147.2 10.1 %shard_map.19.rest_0_ = f32[64,2,256,512]{3,2,1,0:T(8,128)} custom-call(bf16[16,64,512]{2,1,0:T(8,128)(2,1)} %bitcast.157, bf16[16,64,512]{2,1,0:T(8,128)(2,1)} %bitcast.162, bf16[16,64,512]{2,1,0:T(8,128)(2,1)} %bitcast.152, bf16[16,64,512]{2,1,0:T(8,128)(2,1)} %bitcast.156, f32[64,2,256,512]{3,2,1,0:T(8,128)} %shard_map.18.rest_0_), custom_call_target="tpu_custom_call", output_to_operand_aliasing={{}: (4, {})} | custom-call | flops 1073741824 | bytes 20971520 | tf_op jit(solution)/shard_map/pallas_call | solution.py:158
  157.3 0.1 broadcast.108.clone
  157.9 0.1 dynamic-slice_bitcast_fusion
  158.1 0.7 collective-permute-start.25
  158.8 4.4 %collective-permute-start.26 = (bf16[16,2,16,128]{3,2,1,0:T(8,128)(2,1)S(1)}, bf16[16,2,16,128]{3,2,1,0:T(8,128)(2,1)S(1)}, u32[]{:S(2)}, u32[]{:S(2)}) collective-permute-start(bf16[16,2,16,128]{3,2,1,0:T(8,128)(2,1)S(1)} %get-tuple-element.84), channel_id=1, source_target_pairs={{0,4},{2,6},{4,8},{6,10},{8,12},{10,14},{12,0},{14,2},{1,5},{3,7},... | collective-permute-start | bytes 393224 | tf_op jit(solution)/shard_map/ppermute | solution.py:183
  163.1 0.7 collective-permute-start.27
  163.9 1.7 collective-permute-start.28
  165.7 1.2 maximum_maximum_fusion.4
  166.9 1.4 collective-permute-start.29
  168.5 3.9 %collective-permute-start.30 = (bf16[16,2,16,128]{3,2,1,0:T(8,128)(2,1)S(1)}, bf16[16,2,16,128]{3,2,1,0:T(8,128)(2,1)S(1)}, u32[]{:S(2)}, u32[]{:S(2)}) collective-permute-start(bf16[16,2,16,128]{3,2,1,0:T(8,128)(2,1)S(1)} %get-tuple-element.80), channel_id=1, source_target_pairs={{0,12},{2,14},{4,0},{6,2},{8,4},{10,6},{12,8},{14,10},{1,13},{3,15... | collective-permute-start | bytes 393224 | tf_op jit(solution)/shard_map/ppermute | solution.py:183
  172.3 0.8 collective-permute-start.31
  173.1 1.1 maximum_maximum_fusion.5
  174.3 10.1 %shard_map.20.rest_0_ = f32[64,2,256,512]{3,2,1,0:T(8,128)} custom-call(bf16[16,64,512]{2,1,0:T(8,128)(2,1)} %bitcast.158, bf16[16,64,512]{2,1,0:T(8,128)(2,1)} %bitcast.163, bf16[16,64,512]{2,1,0:T(8,128)(2,1)} %bitcast.153, bf16[16,64,512]{2,1,0:T(8,128)(2,1)} %bitcast.155, f32[64,2,256,512]{3,2,1,0:T(8,128)} %shard_map.19.rest_0_), custom_call_target="tpu_custom_call", output_to_operand_aliasing={{}: (4, {})} | custom-call | flops 1073741824 | bytes 20971520 | tf_op jit(solution)/shard_map/pallas_call | solution.py:158
  185.1 1.2 maximum_maximum_fusion.6
  186.3 1.3 collective-permute-done.32
  187.7 1.2 maximum_maximum_fusion.7
  188.9 10.1 %shard_map.21 = f32[64,2,256,512]{3,2,1,0:T(8,128)} custom-call(bf16[16,64,512]{2,1,0:T(8,128)(2,1)} %bitcast.161, bf16[16,64,512]{2,1,0:T(8,128)(2,1)} %bitcast.164, bf16[16,64,512]{2,1,0:T(8,128)(2,1)} %bitcast.150, bf16[16,64,512]{2,1,0:T(8,128)(2,1)} %bitcast.160, f32[64,2,256,512]{3,2,1,0:T(8,128)} %shard_map.20.rest_0_), custom_call_target="tpu_custom_call", output_to_operand_aliasing={{}: (4, {})} | custom-call | flops 1073741824 | bytes 20971520 | tf_op jit(solution)/shard_map/pallas_call | solution.py:158
  (108 shorter events, 2.8 us)
Async XLA Ops:
  0.0 20.3 %collective-permute-start = (bf16[128,16384]{1,0:T(8,128)(2,1)}, bf16[128,16384]{1,0:T(8,128)(2,1)}, u32[]{:S(2)}, u32[]{:S(2)}) collective-permute-start(bf16[128,16384]{1,0:T(8,128)(2,1)} %own_ref.1), channel_id=1, source_target_pairs={{0,1},{1,2},{2,3},{4,5},{5,6},{6,7},{8,9},{9,10},{10,11},{12,13},{... | collective-permute-start | bytes 12582920 | tf_op jit(solution)/shard_map/ppermute | solution.py:17
  20.3 13.1 %copy-start.9 = (bf16[1024,1024]{1,0:T(8,128)(2,1)S(1)}, bf16[1024,1024]{1,0:T(8,128)(2,1)}, u32[]{:S(2)}) copy-start(bf16[1024,1024]{1,0:T(8,128)(2,1)} %convert_element_type.36) | copy-start | bytes 6291460
  45.0 39.7 %collective-permute-start.1 = (bf16[16,2,16,128]{3,2,1,0:T(8,128)(2,1)}, bf16[16,2,16,128]{3,2,1,0:T(8,128)(2,1)}, u32[]{:S(2)}, u32[]{:S(2)}) collective-permute-start(bf16[16,2,16,128]{3,2,1,0:T(8,128)(2,1)} %get-tuple-element.121), channel_id=1, source_target_pairs={{0,2},{2,0},{4,6},{6,4},{8,10},{10,8},{12,14},{14,12},{1,3},{3,1},... | collective-permute-start | bytes 393224 | tf_op jit(solution)/shard_map/ppermute | solution.py:183
  77.6 10.4 %collective-permute-start.2 = (bf16[16,2,16,128]{3,2,1,0:T(8,128)(2,1)}, bf16[16,2,16,128]{3,2,1,0:T(8,128)(2,1)S(1)}, u32[]{:S(2)}, u32[]{:S(2)}) collective-permute-start(bf16[16,2,16,128]{3,2,1,0:T(8,128)(2,1)} %get-tuple-element.120), channel_id=1, source_target_pairs={{0,4},{2,6},{4,8},{6,10},{8,12},{10,14},{12,0},{14,2},{1,5},{3,7},... | collective-permute-start | bytes 393224 | tf_op jit(solution)/shard_map/ppermute | solution.py:183
  79.1 9.6 %collective-permute-start.3 = (bf16[16,2,16,128]{3,2,1,0:T(8,128)(2,1)}, bf16[16,2,16,128]{3,2,1,0:T(8,128)(2,1)S(1)}, u32[]{:S(2)}, u32[]{:S(2)}) collective-permute-start(bf16[16,2,16,128]{3,2,1,0:T(8,128)(2,1)} %get-tuple-element.119), channel_id=1, source_target_pairs={{0,6},{2,4},{4,10},{6,8},{8,14},{10,12},{12,2},{14,0},{1,7},{3,5},... | collective-permute-start | bytes 393224 | tf_op jit(solution)/shard_map/ppermute | solution.py:183
  80.2 15.0 %collective-permute-start.4 = (bf16[16,2,16,128]{3,2,1,0:T(8,128)(2,1)}, bf16[16,2,16,128]{3,2,1,0:T(8,128)(2,1)S(1)}, u32[]{:S(2)}, u32[]{:S(2)}) collective-permute-start(bf16[16,2,16,128]{3,2,1,0:T(8,128)(2,1)} %get-tuple-element.118), channel_id=1, source_target_pairs={{0,8},{2,10},{4,12},{6,14},{8,0},{10,2},{12,4},{14,6},{1,9},{3,11}... | collective-permute-start | bytes 393224 | tf_op jit(solution)/shard_map/ppermute | solution.py:183
  81.7 16.3 %collective-permute-start.5 = (bf16[16,2,16,128]{3,2,1,0:T(8,128)(2,1)S(1)}, bf16[16,2,16,128]{3,2,1,0:T(8,128)(2,1)S(1)}, u32[]{:S(2)}, u32[]{:S(2)}) collective-permute-start(bf16[16,2,16,128]{3,2,1,0:T(8,128)(2,1)S(1)} %get-tuple-element.117), channel_id=1, source_target_pairs={{0,10},{2,8},{4,14},{6,12},{8,2},{10,0},{12,6},{14,4},{1,11},{3,9}... | collective-permute-start | bytes 393224 | tf_op jit(solution)/shard_map/ppermute | solution.py:183
  84.7 13.3 %collective-permute-start.6 = (bf16[16,2,16,128]{3,2,1,0:T(8,128)(2,1)S(1)}, bf16[16,2,16,128]{3,2,1,0:T(8,128)(2,1)S(1)}, u32[]{:S(2)}, u32[]{:S(2)}) collective-permute-start(bf16[16,2,16,128]{3,2,1,0:T(8,128)(2,1)S(1)} %get-tuple-element.116), channel_id=1, source_target_pairs={{0,12},{2,14},{4,0},{6,2},{8,4},{10,6},{12,8},{14,10},{1,13},{3,15... | collective-permute-start | bytes 393224 | tf_op jit(solution)/shard_map/ppermute | solution.py:183
  88.0 10.5 %collective-permute-start.7 = (bf16[16,2,16,128]{3,2,1,0:T(8,128)(2,1)S(1)}, bf16[16,2,16,128]{3,2,1,0:T(8,128)(2,1)S(1)}, u32[]{:S(2)}, u32[]{:S(2)}) collective-permute-start(bf16[16,2,16,128]{3,2,1,0:T(8,128)(2,1)S(1)} %get-tuple-element.115), channel_id=1, source_target_pairs={{0,14},{2,12},{4,2},{6,0},{8,6},{10,4},{12,10},{14,8},{1,15},{3,13... | collective-permute-start | bytes 393224 | tf_op jit(solution)/shard_map/ppermute | solution.py:183
  98.5 12.1 %copy-start.1 = (bf16[16,2,2,16,512]{4,3,2,1,0:T(8,128)(2,1)}, bf16[16,2,2,16,512]{4,3,2,1,0:T(8,128)(2,1)S(1)}, u32[]{:S(2)}) copy-start(bf16[16,2,2,16,512]{4,3,2,1,0:T(8,128)(2,1)S(1)} %bitcast_dynamic-update-slice_fusion.24) | copy-start | bytes 3145732
  98.5 13.2 %collective-permute-start.8 = (bf16[16,2,2,16,512]{4,3,2,1,0:T(8,128)(2,1)S(1)}, bf16[16,2,2,16,512]{4,3,2,1,0:T(8,128)(2,1)S(1)}, u32[]{:S(2)}, u32[]{:S(2)}) collective-permute-start(bf16[16,2,2,16,512]{4,3,2,1,0:T(8,128)(2,1)S(1)} %bitcast_dynamic-update-slice_fusion.24), channel_id=1, source_target_pairs={{0,1},{1,0},{2,3},{3,2},{4,5},{5,4},{6,7},{7,6},{8,9},{9,8},{10,11... | collective-permute-start | bytes 3145736 | tf_op jit(solution)/shard_map/ppermute | solution.py:205
  101.0 14.7 %collective-permute-start.10 = (bf16[16,2,16,128]{3,2,1,0:T(8,128)(2,1)S(1)}, bf16[16,2,16,128]{3,2,1,0:T(8,128)(2,1)S(1)}, u32[]{:S(2)}, u32[]{:S(2)}) collective-permute-start(bf16[16,2,16,128]{3,2,1,0:T(8,128)(2,1)S(1)} %get-tuple-element.108), channel_id=1, source_target_pairs={{0,4},{2,6},{4,8},{6,10},{8,12},{10,14},{12,0},{14,2},{1,5},{3,7},... | collective-permute-start | bytes 393224 | tf_op jit(solution)/shard_map/ppermute | solution.py:183
  106.7 10.1 %collective-permute-start.11 = (bf16[16,2,16,128]{3,2,1,0:T(8,128)(2,1)S(1)}, bf16[16,2,16,128]{3,2,1,0:T(8,128)(2,1)S(1)}, u32[]{:S(2)}, u32[]{:S(2)}) collective-permute-start(bf16[16,2,16,128]{3,2,1,0:T(8,128)(2,1)S(1)} %get-tuple-element.107), channel_id=1, source_target_pairs={{0,6},{2,4},{4,10},{6,8},{8,14},{10,12},{12,2},{14,0},{1,7},{3,5},... | collective-permute-start | bytes 393224 | tf_op jit(solution)/shard_map/ppermute | solution.py:183
  107.4 21.4 %collective-permute-start.12 = (bf16[16,2,16,128]{3,2,1,0:T(8,128)(2,1)}, bf16[16,2,16,128]{3,2,1,0:T(8,128)(2,1)}, u32[]{:S(2)}, u32[]{:S(2)}) collective-permute-start(bf16[16,2,16,128]{3,2,1,0:T(8,128)(2,1)} %get-tuple-element.106), channel_id=1, source_target_pairs={{0,8},{2,10},{4,12},{6,14},{8,0},{10,2},{12,4},{14,6},{1,9},{3,11}... | collective-permute-start | bytes 393224 | tf_op jit(solution)/shard_map/ppermute | solution.py:183
  109.2 19.6 %collective-permute-start.13 = (bf16[16,2,16,128]{3,2,1,0:T(8,128)(2,1)}, bf16[16,2,16,128]{3,2,1,0:T(8,128)(2,1)}, u32[]{:S(2)}, u32[]{:S(2)}) collective-permute-start(bf16[16,2,16,128]{3,2,1,0:T(8,128)(2,1)} %get-tuple-element.105), channel_id=1, source_target_pairs={{0,10},{2,8},{4,14},{6,12},{8,2},{10,0},{12,6},{14,4},{1,11},{3,9}... | collective-permute-start | bytes 393224 | tf_op jit(solution)/shard_map/ppermute | solution.py:183
  111.7 6.8 %copy-start.4 = (bf16[16,2,2,16,512]{4,3,2,1,0:T(8,128)(2,1)}, bf16[16,2,2,16,512]{4,3,2,1,0:T(8,128)(2,1)S(1)}, u32[]{:S(2)}) copy-start(bf16[16,2,2,16,512]{4,3,2,1,0:T(8,128)(2,1)S(1)} %collective-permute-done.8) | copy-start | bytes 3145732
  111.8 17.0 %collective-permute-start.14 = (bf16[16,2,16,128]{3,2,1,0:T(8,128)(2,1)}, bf16[16,2,16,128]{3,2,1,0:T(8,128)(2,1)S(1)}, u32[]{:S(2)}, u32[]{:S(2)}) collective-permute-start(bf16[16,2,16,128]{3,2,1,0:T(8,128)(2,1)} %get-tuple-element.104), channel_id=1, source_target_pairs={{0,12},{2,14},{4,0},{6,2},{8,4},{10,6},{12,8},{14,10},{1,13},{3,15... | collective-permute-start | bytes 393224 | tf_op jit(solution)/shard_map/ppermute | solution.py:183
  115.7 2.9 %copy-start.10 = (bf16[16,2,16,128]{3,2,1,0:T(8,128)(2,1)}, bf16[16,2,16,128]{3,2,1,0:T(8,128)(2,1)S(1)}, u32[]{:S(2)}) copy-start(bf16[16,2,16,128]{3,2,1,0:T(8,128)(2,1)S(1)} %collective-permute-done.10) | copy-start | bytes 393220
  115.7 13.1 %collective-permute-start.15 = (bf16[16,2,16,128]{3,2,1,0:T(8,128)(2,1)S(1)}, bf16[16,2,16,128]{3,2,1,0:T(8,128)(2,1)S(1)}, u32[]{:S(2)}, u32[]{:S(2)}) collective-permute-start(bf16[16,2,16,128]{3,2,1,0:T(8,128)(2,1)S(1)} %get-tuple-element.103), channel_id=1, source_target_pairs={{0,14},{2,12},{4,2},{6,0},{8,6},{10,4},{12,10},{14,8},{1,15},{3,13... | collective-permute-start | bytes 393224 | tf_op jit(solution)/shard_map/ppermute | solution.py:183
  116.7 1.9 copy-start.12
  116.7 12.1 %collective-permute-start.9 = (bf16[16,2,16,128]{3,2,1,0:T(8,128)(2,1)S(1)}, bf16[16,2,16,128]{3,2,1,0:T(8,128)(2,1)S(1)}, u32[]{:S(2)}, u32[]{:S(2)}) collective-permute-start(bf16[16,2,16,128]{3,2,1,0:T(8,128)(2,1)S(1)} %get-tuple-element.109), channel_id=1, source_target_pairs={{0,2},{2,0},{4,6},{6,4},{8,10},{10,8},{12,14},{14,12},{1,3},{3,1},... | collective-permute-start | bytes 393224 | tf_op jit(solution)/shard_map/ppermute | solution.py:183
  118.6 10.5 %copy-start.11 = (bf16[16,2,16,128]{3,2,1,0:T(8,128)(2,1)S(1)}, bf16[16,2,16,128]{3,2,1,0:T(8,128)(2,1)}, u32[]{:S(2)}) copy-start(bf16[16,2,16,128]{3,2,1,0:T(8,128)(2,1)} %copy-done.10) | copy-start | bytes 393220
  118.6 10.5 %copy-start.13 = (bf16[16,2,16,128]{3,2,1,0:T(8,128)(2,1)S(1)}, bf16[16,2,16,128]{3,2,1,0:T(8,128)(2,1)}, u32[]{:S(2)}) copy-start(bf16[16,2,16,128]{3,2,1,0:T(8,128)(2,1)} %copy-done.12) | copy-start | bytes 393220
  128.8 2.5 %copy-start.8 = (bf16[8,16,2,16,128]{4,3,2,1,0:T(8,128)(2,1)S(1)}, bf16[8,16,2,16,128]{4,3,2,1,0:T(8,128)(2,1)}, u32[]{:S(2)}) copy-start(bf16[8,16,2,16,128]{4,3,2,1,0:T(8,128)(2,1)} %get-tuple-element.50) | copy-start | bytes 3145732
  131.1 7.1 %copy-start.2 = (bf16[16,2,2,16,512]{4,3,2,1,0:T(8,128)(2,1)}, bf16[16,2,2,16,512]{4,3,2,1,0:T(8,128)(2,1)S(1)}, u32[]{:S(2)}) copy-start(bf16[16,2,2,16,512]{4,3,2,1,0:T(8,128)(2,1)S(1)} %bitcast_dynamic-update-slice_fusion.16) | copy-start | bytes 3145732
  131.1 8.3 %collective-permute-start.16 = (bf16[16,2,2,16,512]{4,3,2,1,0:T(8,128)(2,1)S(1)}, bf16[16,2,2,16,512]{4,3,2,1,0:T(8,128)(2,1)S(1)}, u32[]{:S(2)}, u32[]{:S(2)}) collective-permute-start(bf16[16,2,2,16,512]{4,3,2,1,0:T(8,128)(2,1)S(1)} %bitcast_dynamic-update-slice_fusion.16), channel_id=1, source_target_pairs={{0,1},{1,0},{2,3},{3,2},{4,5},{5,4},{6,7},{7,6},{8,9},{9,8},{10,11... | collective-permute-start | bytes 3145736 | tf_op jit(solution)/shard_map/ppermute | solution.py:205
  131.4 10.0 %collective-permute-start.17 = (bf16[16,2,16,128]{3,2,1,0:T(8,128)(2,1)S(1)}, bf16[16,2,16,128]{3,2,1,0:T(8,128)(2,1)S(1)}, u32[]{:S(2)}, u32[]{:S(2)}) collective-permute-start(bf16[16,2,16,128]{3,2,1,0:T(8,128)(2,1)S(1)} %get-tuple-element.97), channel_id=1, source_target_pairs={{0,2},{2,0},{4,6},{6,4},{8,10},{10,8},{12,14},{14,12},{1,3},{3,1},... | collective-permute-start | bytes 393224 | tf_op jit(solution)/shard_map/ppermute | solution.py:183
  132.7 12.5 %collective-permute-start.18 = (bf16[16,2,16,128]{3,2,1,0:T(8,128)(2,1)S(1)}, bf16[16,2,16,128]{3,2,1,0:T(8,128)(2,1)S(1)}, u32[]{:S(2)}, u32[]{:S(2)}) collective-permute-start(bf16[16,2,16,128]{3,2,1,0:T(8,128)(2,1)S(1)} %get-tuple-element.96), channel_id=1, source_target_pairs={{0,4},{2,6},{4,8},{6,10},{8,12},{10,14},{12,0},{14,2},{1,5},{3,7},... | collective-permute-start | bytes 393224 | tf_op jit(solution)/shard_map/ppermute | solution.py:183
  136.0 21.2 %collective-permute-start.19 = (bf16[16,2,16,128]{3,2,1,0:T(8,128)(2,1)S(1)}, bf16[16,2,16,128]{3,2,1,0:T(8,128)(2,1)S(1)}, u32[]{:S(2)}, u32[]{:S(2)}) collective-permute-start(bf16[16,2,16,128]{3,2,1,0:T(8,128)(2,1)S(1)} %get-tuple-element.95), channel_id=1, source_target_pairs={{0,6},{2,4},{4,10},{6,8},{8,14},{10,12},{12,2},{14,0},{1,7},{3,5},... | collective-permute-start | bytes 393224 | tf_op jit(solution)/shard_map/ppermute | solution.py:183
  136.8 20.5 %collective-permute-start.20 = (bf16[16,2,16,128]{3,2,1,0:T(8,128)(2,1)S(1)}, bf16[16,2,16,128]{3,2,1,0:T(8,128)(2,1)S(1)}, u32[]{:S(2)}, u32[]{:S(2)}) collective-permute-start(bf16[16,2,16,128]{3,2,1,0:T(8,128)(2,1)S(1)} %get-tuple-element.94), channel_id=1, source_target_pairs={{0,8},{2,10},{4,12},{6,14},{8,0},{10,2},{12,4},{14,6},{1,9},{3,11}... | collective-permute-start | bytes 393224 | tf_op jit(solution)/shard_map/ppermute | solution.py:183
  139.4 7.8 %copy-start.6 = (bf16[16,2,2,16,512]{4,3,2,1,0:T(8,128)(2,1)}, bf16[16,2,2,16,512]{4,3,2,1,0:T(8,128)(2,1)S(1)}, u32[]{:S(2)}) copy-start(bf16[16,2,2,16,512]{4,3,2,1,0:T(8,128)(2,1)S(1)} %collective-permute-done.16) | copy-start | bytes 3145732
  139.4 17.9 %collective-permute-start.21 = (bf16[16,2,16,128]{3,2,1,0:T(8,128)(2,1)S(1)}, bf16[16,2,16,128]{3,2,1,0:T(8,128)(2,1)S(1)}, u32[]{:S(2)}, u32[]{:S(2)}) collective-permute-start(bf16[16,2,16,128]{3,2,1,0:T(8,128)(2,1)S(1)} %get-tuple-element.93), channel_id=1, source_target_pairs={{0,10},{2,8},{4,14},{6,12},{8,2},{10,0},{12,6},{14,4},{1,11},{3,9}... | collective-permute-start | bytes 393224 | tf_op jit(solution)/shard_map/ppermute | solution.py:183
  141.3 15.9 %collective-permute-start.22 = (bf16[16,2,16,128]{3,2,1,0:T(8,128)(2,1)S(1)}, bf16[16,2,16,128]{3,2,1,0:T(8,128)(2,1)S(1)}, u32[]{:S(2)}, u32[]{:S(2)}) collective-permute-start(bf16[16,2,16,128]{3,2,1,0:T(8,128)(2,1)S(1)} %get-tuple-element.92), channel_id=1, source_target_pairs={{0,12},{2,14},{4,0},{6,2},{8,4},{10,6},{12,8},{14,10},{1,13},{3,15... | collective-permute-start | bytes 393224 | tf_op jit(solution)/shard_map/ppermute | solution.py:183
  145.2 12.1 %collective-permute-start.23 = (bf16[16,2,16,128]{3,2,1,0:T(8,128)(2,1)S(1)}, bf16[16,2,16,128]{3,2,1,0:T(8,128)(2,1)S(1)}, u32[]{:S(2)}, u32[]{:S(2)}) collective-permute-start(bf16[16,2,16,128]{3,2,1,0:T(8,128)(2,1)S(1)} %get-tuple-element.91), channel_id=1, source_target_pairs={{0,14},{2,12},{4,2},{6,0},{8,6},{10,4},{12,10},{14,8},{1,15},{3,13... | collective-permute-start | bytes 393224 | tf_op jit(solution)/shard_map/ppermute | solution.py:183
  157.8 7.9 %copy-start.3 = (bf16[16,2,2,16,512]{4,3,2,1,0:T(8,128)(2,1)}, bf16[16,2,2,16,512]{4,3,2,1,0:T(8,128)(2,1)S(1)}, u32[]{:S(2)}) copy-start(bf16[16,2,2,16,512]{4,3,2,1,0:T(8,128)(2,1)S(1)} %bitcast_dynamic-update-slice_fusion.8) | copy-start | bytes 3145732
  157.8 9.0 %collective-permute-start.24 = (bf16[16,2,2,16,512]{4,3,2,1,0:T(8,128)(2,1)S(1)}, bf16[16,2,2,16,512]{4,3,2,1,0:T(8,128)(2,1)S(1)}, u32[]{:S(2)}, u32[]{:S(2)}) collective-permute-start(bf16[16,2,2,16,512]{4,3,2,1,0:T(8,128)(2,1)S(1)} %bitcast_dynamic-update-slice_fusion.8), channel_id=1, source_target_pairs={{0,1},{1,0},{2,3},{3,2},{4,5},{5,4},{6,7},{7,6},{8,9},{9,8},{10,11... | collective-permute-start | bytes 3145736 | tf_op jit(solution)/shard_map/ppermute | solution.py:205
  158.1 10.4 %collective-permute-start.25 = (bf16[16,2,16,128]{3,2,1,0:T(8,128)(2,1)S(1)}, bf16[16,2,16,128]{3,2,1,0:T(8,128)(2,1)S(1)}, u32[]{:S(2)}, u32[]{:S(2)}) collective-permute-start(bf16[16,2,16,128]{3,2,1,0:T(8,128)(2,1)S(1)} %get-tuple-element.85), channel_id=1, source_target_pairs={{0,2},{2,0},{4,6},{6,4},{8,10},{10,8},{12,14},{14,12},{1,3},{3,1},... | collective-permute-start | bytes 393224 | tf_op jit(solution)/shard_map/ppermute | solution.py:183
  158.8 13.6 %collective-permute-start.26 = (bf16[16,2,16,128]{3,2,1,0:T(8,128)(2,1)S(1)}, bf16[16,2,16,128]{3,2,1,0:T(8,128)(2,1)S(1)}, u32[]{:S(2)}, u32[]{:S(2)}) collective-permute-start(bf16[16,2,16,128]{3,2,1,0:T(8,128)(2,1)S(1)} %get-tuple-element.84), channel_id=1, source_target_pairs={{0,4},{2,6},{4,8},{6,10},{8,12},{10,14},{12,0},{14,2},{1,5},{3,7},... | collective-permute-start | bytes 393224 | tf_op jit(solution)/shard_map/ppermute | solution.py:183
  163.1 21.2 %collective-permute-start.27 = (bf16[16,2,16,128]{3,2,1,0:T(8,128)(2,1)S(1)}, bf16[16,2,16,128]{3,2,1,0:T(8,128)(2,1)S(1)}, u32[]{:S(2)}, u32[]{:S(2)}) collective-permute-start(bf16[16,2,16,128]{3,2,1,0:T(8,128)(2,1)S(1)} %get-tuple-element.83), channel_id=1, source_target_pairs={{0,6},{2,4},{4,10},{6,8},{8,14},{10,12},{12,2},{14,0},{1,7},{3,5},... | collective-permute-start | bytes 393224 | tf_op jit(solution)/shard_map/ppermute | solution.py:183
  163.9 20.4 %collective-permute-start.28 = (bf16[16,2,16,128]{3,2,1,0:T(8,128)(2,1)S(1)}, bf16[16,2,16,128]{3,2,1,0:T(8,128)(2,1)S(1)}, u32[]{:S(2)}, u32[]{:S(2)}) collective-permute-start(bf16[16,2,16,128]{3,2,1,0:T(8,128)(2,1)S(1)} %get-tuple-element.82), channel_id=1, source_target_pairs={{0,8},{2,10},{4,12},{6,14},{8,0},{10,2},{12,4},{14,6},{1,9},{3,11}... | collective-permute-start | bytes 393224 | tf_op jit(solution)/shard_map/ppermute | solution.py:183
  166.9 7.4 %copy-start.5 = (bf16[16,2,2,16,512]{4,3,2,1,0:T(8,128)(2,1)}, bf16[16,2,2,16,512]{4,3,2,1,0:T(8,128)(2,1)S(1)}, u32[]{:S(2)}) copy-start(bf16[16,2,2,16,512]{4,3,2,1,0:T(8,128)(2,1)S(1)} %collective-permute-done.24) | copy-start | bytes 3145732
  166.9 17.5 %collective-permute-start.29 = (bf16[16,2,16,128]{3,2,1,0:T(8,128)(2,1)S(1)}, bf16[16,2,16,128]{3,2,1,0:T(8,128)(2,1)S(1)}, u32[]{:S(2)}, u32[]{:S(2)}) collective-permute-start(bf16[16,2,16,128]{3,2,1,0:T(8,128)(2,1)S(1)} %get-tuple-element.81), channel_id=1, source_target_pairs={{0,10},{2,8},{4,14},{6,12},{8,2},{10,0},{12,6},{14,4},{1,11},{3,9}... | collective-permute-start | bytes 393224 | tf_op jit(solution)/shard_map/ppermute | solution.py:183
  168.5 15.9 %collective-permute-start.30 = (bf16[16,2,16,128]{3,2,1,0:T(8,128)(2,1)S(1)}, bf16[16,2,16,128]{3,2,1,0:T(8,128)(2,1)S(1)}, u32[]{:S(2)}, u32[]{:S(2)}) collective-permute-start(bf16[16,2,16,128]{3,2,1,0:T(8,128)(2,1)S(1)} %get-tuple-element.80), channel_id=1, source_target_pairs={{0,12},{2,14},{4,0},{6,2},{8,4},{10,6},{12,8},{14,10},{1,13},{3,15... | collective-permute-start | bytes 393224 | tf_op jit(solution)/shard_map/ppermute | solution.py:183
  172.3 12.0 %collective-permute-start.31 = (bf16[16,2,16,128]{3,2,1,0:T(8,128)(2,1)S(1)}, bf16[16,2,16,128]{3,2,1,0:T(8,128)(2,1)S(1)}, u32[]{:S(2)}, u32[]{:S(2)}) collective-permute-start(bf16[16,2,16,128]{3,2,1,0:T(8,128)(2,1)S(1)} %get-tuple-element.79), channel_id=1, source_target_pairs={{0,14},{2,12},{4,2},{6,0},{8,6},{10,4},{12,10},{14,8},{1,15},{3,13... | collective-permute-start | bytes 393224 | tf_op jit(solution)/shard_map/ppermute | solution.py:183
  184.9 1.4 copy-start
  184.9 2.7 %collective-permute-start.32 = (bf16[16,2,2,16,512]{4,3,2,1,0:T(8,128)(2,1)S(1)}, bf16[16,2,2,16,512]{4,3,2,1,0:T(8,128)(2,1)S(1)}, u32[]{:S(2)}, u32[]{:S(2)}) collective-permute-start(bf16[16,2,2,16,512]{4,3,2,1,0:T(8,128)(2,1)S(1)} %bitcast_dynamic-update-slice_fusion), channel_id=1, source_target_pairs={{0,1},{1,0},{2,3},{3,2},{4,5},{5,4},{6,7},{7,6},{8,9},{9,8},{10,11... | collective-permute-start | bytes 3145736 | tf_op jit(solution)/shard_map/ppermute | solution.py:205
  187.6 1.3 copy-start.7
